TPU v7x, 128 devices: a whole 4x4x4 slice. The times are simulated.
128 devices in a mesh: section: 8 (over x, core), ctx: 16 (over z, y).
Axes of the slice: x: 4, y: 4, z: 4, core: 2. Of those that a mesh axis runs over, the one named last changes fastest.
Arguments:
- section_inputs: bfloat16 [8, 8192, 6144], P('section', 'ctx'), may hold values from -6 to 6
- input_gains: float32 [8, 3, 6144], P('section'), may hold values from 0.5 to 1.5
- out_gain: float32 [8, 6144], P('section'), may hold values from 0.5 to 1.5
- decay_rates: float32 [8, 48], P('section'), may hold values from 1e-05 to 0.001
- carry_state: float32 [8, 48, 128, 128], P('section'), may hold values from -48 to 48
Outputs:
- next_inputs: bfloat16 [8, 8192, 6144], P('section', 'ctx')
- end_state: float32 [8, 48, 128, 128], P('section', 'ctx')
All inputs are finite; a program needn't handle non-finite values.
Results may differ from a plain program's by a relative error of at most 0.012.
Values may be sent and summed in bfloat16 or wider, within the bound.
No kernel may reach another device: no remote copies, remote signals or barrier semaphores. Data moves between devices by JAX's collectives and lax.ppermute only.
A program may use at most 320 MiB of HBM per device.

v0:
```python
import jax
import jax.numpy as jnp
from jax import lax
from jax.sharding import PartitionSpec as P

BLOCK = 256


EPSILON = 1e-05


def entering(x, axis, combine, identity):
    size, position = (lax.axis_size(axis), lax.axis_index(axis))
    everything = jax.tree.map(lambda part: lax.all_gather(part, axis), x)
    start = jax.tree.map(
        lambda part, zero: jnp.broadcast_to(jnp.asarray(zero, part.dtype), part.shape), x, identity
    )

    def lap(k, before):
        reached = k < position
        new = combine(before, jax.tree.map(lambda part: part[k], everything))
        return jax.tree.map(lambda a, b: jnp.where(reached, a, b), new, before)

    return lax.fori_loop(0, size, lap, start)


def passed_along(value, axis, steps):
    count = lax.axis_size(axis)
    pairs = [(source, (source + steps) % count) for source in range(count)]
    return lax.ppermute(value, axis, pairs)


def combine(earlier, later):
    return (earlier[0] * later[1][:, None, None] + later[0], earlier[1] * later[1])


def on_device(section_inputs, input_gains, out_gain, decay_rates, carry_state):
    rows = section_inputs[0]
    count, width = rows.shape
    rates = decay_rates[0]
    heads = rates.shape[0]
    head_dim = width // heads
    nblocks = count // BLOCK
    wide = rows.astype(jnp.float32)
    gains = input_gains[0]
    gain_out = out_gain[0]
    queries = (
        jax.nn.silu(wide * gains[0]).astype(jnp.bfloat16).reshape(nblocks, BLOCK, heads, head_dim)
    )
    keys = (
        (jax.nn.silu(wide * gains[1]) * head_dim ** (-0.5))
        .astype(jnp.bfloat16)
        .reshape(nblocks, BLOCK, heads, head_dim)
    )
    values = (wide * gains[2]).astype(jnp.bfloat16).reshape(nblocks, BLOCK, heads, head_dim)
    position = jnp.arange(BLOCK).astype(jnp.float32)
    offset = position[:, None] - position[None, :]
    mask = jnp.where(
        offset[None] >= 0,
        jnp.exp(-rates[:, None, None] * jnp.maximum(offset, 0.0)[None]),
        jnp.float32(0.0),
    )
    tail = jnp.exp(-rates[None, :] * (BLOCK - 1 - position)[:, None])
    lead = jnp.exp(-rates[None, :] * (position + 1.0)[:, None])
    block_decay = jnp.exp(-rates * BLOCK)
    scaled_keys = (keys.astype(jnp.float32) * tail[None, :, :, None]).astype(jnp.bfloat16)
    block_states = jnp.einsum(
        "njhd,njhe->nhde", scaled_keys, values, preferred_element_type=jnp.float32
    )
    later_blocks = (nblocks - 1 - jnp.arange(nblocks)).astype(jnp.float32)
    block_weights = jnp.exp(-rates[None, :] * BLOCK * later_blocks[:, None])
    summary = jnp.sum(block_weights[:, :, None, None] * block_states, axis=0)
    shard_decay = jnp.exp(-rates * count)
    place = lax.axis_index("ctx").astype(jnp.float32)
    group_size = lax.axis_size("ctx")
    own_heads = heads // group_size
    start = lax.axis_index("ctx") * own_heads
    carry_part = lax.dynamic_slice_in_dim(carry_state[0], start, own_heads, 0)
    rate_part = lax.dynamic_slice_in_dim(rates, start, own_heads, 0)
    identity = (jnp.zeros_like(summary), jnp.ones_like(shard_decay))
    prefix, unused = entering((summary, shard_decay), "ctx", combine, identity)
    incoming = jnp.exp(-rates * count * place)[:, None, None] * carry_state[0] + prefix
    final_terms = jnp.exp(-rates * count * (group_size - 1 - place))[:, None, None] * summary
    final_part = lax.psum_scatter(
        final_terms.astype(jnp.bfloat16), "ctx", scatter_dimension=0, tiled=True
    ).astype(jnp.float32)
    end_part = final_part + jnp.exp(-rate_part * count * group_size)[:, None, None] * carry_part
    scores = jnp.einsum("nihd,njhd->nhij", queries, keys, preferred_element_type=jnp.float32)
    weights = (scores * mask[None]).astype(jnp.bfloat16)
    local_out = jnp.einsum("nhij,njhd->nihd", weights, values, preferred_element_type=jnp.float32)
    state = incoming
    pieces_out = []
    for block in range(nblocks):
        cross = jnp.einsum(
            "ihd,hde->ihe",
            queries[block],
            state.astype(jnp.bfloat16),
            preferred_element_type=jnp.float32,
        )
        total = local_out[block] + lead[:, :, None] * cross
        normed = total * lax.rsqrt(jnp.mean(total * total, axis=-1, keepdims=True) + EPSILON)
        wide_block = wide[block * BLOCK : (block + 1) * BLOCK]
        block_rows = (wide_block + normed.reshape(BLOCK, width) * gain_out).astype(jnp.bfloat16)
        pieces_out.append(block_rows[None])
        state = block_decay[:, None, None] * state + block_states[block]
    joined = jnp.concatenate(pieces_out, axis=1)
    next_rows = passed_along(joined, "section", 1)
    return (next_rows, end_part[None])


def solution(mesh):
    return jax.shard_map(
        on_device,
        mesh=mesh,
        in_specs=(
            P("section", "ctx", None),
            P("section", None, None),
            P("section", None),
            P("section", None),
            P("section", None, None, None),
        ),
        out_specs=(P("section", "ctx", None), P("section", "ctx", None, None)),
        check_vma=False,
    )
```

profile of v0, /device:TPU:0, one launch (start us, length us, event | category | flops | bytes accessed | tf_op | source)
XLA Modules:
  0.0 527.4 jit_solution(8228850008165447271)
XLA Ops:
  8.7 8.6 %copy.25 = bf16[1,512,6144]{1,2,0:T(8,128)(2,1)} copy(bf16[1,512,6144]{2,1,0:T(8,128)(2,1)} %param.7) | data formatting | bytes 12582912 | tf_op args[0]
  17.3 13.9 %reshape.270 = f32[2,256,48,128]{1,0,3,2:T(2,128)} reshape(bf16[1,512,6144]{1,2,0:T(8,128)(2,1)} %copy.25) | data formatting | bytes 18874368 | tf_op jit(solution)/shard_map/convert_element_type | solution.py:44
  31.2 19.1 %copy.26 = f32[2,256,48,128]{3,1,2,0:T(8,128)} copy(f32[2,256,48,128]{1,0,3,2:T(2,128)} %reshape.270) | data formatting | bytes 25165824 | tf_op jit(solution)/shard_map/convert_element_type | solution.py:44
  50.4 15.1 %multiply_reduce_fusion.2 = (f32[48,128,128]{2,1,0:T(8,128)}, f32[2,48,128,128]{3,2,1,0:T(8,128)}) fusion(f32[2,48]{1,0:T(2,128)S(1)} %multiply_exponential_fusion.2, f32[2,256,48,128]{3,1,2,0:T(8,128)} %copy.26, f32[48,128]{1,0:T(8,128)S(1)} %bitcast.125, f32[256,48]{0,1:T(8,128)S(1)} %get-tuple-element.142, f32[48,128]{1,0:T(8,128)S(1)} %bitcast.123, ...), kind=kOutput, calls=%fused_computation.32 | convolution fusion | flops 845414400 | bytes 34701696 | tf_op jit(solution)/shard_map/njhd,njhe->nhde/dot_general | solution.py:67
  65.6 9.1 %convert_element_type.88 = f32[1,512,6144]{1,2,0:T(8,128)} convert(bf16[1,512,6144]{1,2,0:T(8,128)(2,1)} %copy.25) | non-fusion elementwise | flops 3145728 | bytes 18874368 | tf_op jit(solution)/shard_map/convert_element_type | solution.py:44
  74.6 22.8 %all-gather.1 = f32[16,1,48]{2,1,0:T(1,128)S(1)} all-gather(f32[1,1,48]{2,1,0:T(1,128)S(1)} %get-tuple-element.140), channel_id=1, replica_groups=mesh['section'=8,'ctx'=16] {'ctx'}, dimensions={0}, use_global_device_ids=true | all-gather | bytes 3264 | tf_op jit(solution)/shard_map/all_gather | solution.py:14
  97.7 6.2 %exponential_select_fusion = f32[48,256,256]{2,1,0:T(8,128)} fusion(f32[256,256]{1,0:T(8,128)S(1)} %subtract_maximum_fusion, f32[48]{0:T(128)S(1)} %get-tuple-element.141, pred[256,256]{1,0:T(8,128)(4,1)S(1)} %subtract_compare_fusion), kind=kLoop, calls=%fused_computation.9 | loop fusion | flops 6291456 | bytes 12910784 | tf_op jit(solution)/shard_map/jit(_where)/select_n | solution.py:58
  103.9 5.6 %multiply_convert_fusion.2 = bf16[512,6144]{0,1:T(8,128)(2,1)S(1)} fusion(f32[6144]{0:T(1024)S(1)} %bitcast.120, bf16[1,512,6144]{1,2,0:T(8,128)(2,1)} %copy.25), kind=kLoop, calls=%fused_computation.6 | loop fusion | flops 22020096 | bytes 12607488 | tf_op jit(solution)/shard_map/convert_element_type | solution.py:48
  109.6 3.2 fusion.32
  112.8 26.9 %fusion.17 = f32[2,256,48,128]{1,3,2,0:T(8,128)} fusion(f32[48,256,256]{2,1,0:T(8,128)} %exponential_select_fusion, f32[2,256,48,128]{1,0,3,2:T(2,128)} %reshape.270, f32[48,128]{1,0:T(8,128)S(1)} %bitcast.121, f32[2,256,48,128]{3,1,2,0:T(8,128)} %copy.26, f32[48,128]{1,0:T(8,128)S(1)} %bitcast.126, f32[48,128]{1,0:T(8,128)S(1)} %bitcast.124), kind=kOutput, calls=%fused_computation.36 | convolution fusion | flops 3280994304 | bytes 50405376 | tf_op jit(solution)/shard_map/nhij,njhd->nihd/dot_general | solution.py:90
  139.6 211.4 %all-gather.4.cloned.1.call-done = f32[768,128,128]{2,1,0:T(8,128)} async-done(((f32[48,128,128]{2,1,0:T(8,128)}), f32[768,128,128]{2,1,0:T(8,128)}) %all-gather.4.cloned.1.call-update) | async-done | bytes 50331664 | tf_op jit(solution)/shard_map/all_gather | solution.py:14
  351.0 43.3 %while.14 = (s32[]{:T(128)}, f32[48,128,128]{2,1,0:T(8,128)S(1)}, s32[]{:T(128)}, f32[16,48]{1,0:T(8,128)S(1)}, f32[16,48,128,128]{3,2,1,0:T(8,128)}, /*index=5*/s32[]{:T(128)}, s32[]{:T(128)}) while((s32[]{:T(128)}, f32[48,128,128]{2,1,0:T(8,128)S(1)}, s32[]{:T(128)}, f32[16,48]{1,0:T(8,128)S(1)}, f32[16,48,128,128]{3,2,1,0:T(8,128)}, ...), condition=%wide.region_2.3_spmd.clone, body=%wide.region_1.2_spmd.clone.sunk | while | flops 3145732 | bytes 9437873 | solution.py:24
  353.7 2.7 fusion.37
  356.4 2.7 fusion.37
  359.1 2.7 fusion.37
  361.9 2.7 fusion.37
  364.6 2.7 fusion.37
  367.3 2.7 fusion.37
  370.0 2.7 fusion.37
  372.7 2.7 fusion.37
  375.4 2.7 fusion.37
  378.1 2.7 fusion.37
  380.8 2.7 fusion.37
  383.5 2.7 fusion.37
  394.3 6.4 %multiply_reduce_fusion.1 = (f32[256,48]{0,1:T(8,128)S(1)}, f32[256,48,128]{0,2,1:T(8,128)S(1)}) fusion(bf16[256,48,128]{0,2,1:T(8,128)(2,1)} %bitcast.116, f32[48,128,128]{2,1,0:T(8,128)S(1)} %get-tuple-element.96, f32[1,48,128,128]{3,2,1,0:T(8,128)} %param.11, f32[48]{0:T(128)S(1)} %get-tuple-element.137, f32[256,48]{0,1:T(8,128)S(1)} %get-tuple-element.143, ...), kind=kOutput, calls=%fused_computation.31 | convolution fusion | flops 411291648 | bytes 22118592 | tf_op jit(solution)/shard_map/ihd,hde->ihe/dot_general | solution.py:94
  400.8 8.3 %multiply_reduce_fusion = (f32[256,48]{0,1:T(8,128)S(1)}, f32[256,48,128]{0,2,1:T(8,128)}) fusion(bf16[256,48,128]{0,2,1:T(8,128)(2,1)S(1)} %bitcast.115, f32[2,48,128,128]{3,2,1,0:T(8,128)} %get-tuple-element.145, f32[48]{0:T(128)S(1)} %get-tuple-element.138, f32[48,128,128]{2,1,0:T(8,128)S(1)} %get-tuple-element.96, ...), kind=kOutput, calls=%fused_computation.30 | convolution fusion | flops 412864512 | bytes 25264512 | tf_op jit(solution)/shard_map/ihd,hde->ihe/dot_general | solution.py:94
  409.2 3.9 broadcast_multiply_fusion.1
  413.1 7.8 %broadcast_multiply_fusion = f32[256,48,128]{0,2,1:T(8,128)} fusion(f32[256,48,128]{0,2,1:T(8,128)} %get-tuple-element.149, f32[256,48]{0,1:T(8,128)S(1)} %add_rsqrt_fusion), kind=kLoop, calls=%fused_computation.43 | loop fusion | flops 1572864 | bytes 12632064 | tf_op jit(solution)/shard_map/mul | solution.py:101
  421.6 5.5 %fusion.11 = (bf16[256,6144]{0,1:T(8,128)(2,1)}, bf16[256,6144]{0,1:T(8,128)(2,1)}) fusion(f32[1,512,6144]{1,2,0:T(8,128)S(1)} %bitcast.114, f32[256,48,128]{0,2,1:T(8,128)S(1)} %copy-done, f32[6144]{0:T(1024)S(1)} %bitcast.122, f32[256,48,128]{0,2,1:T(8,128)} %broadcast_multiply_fusion), kind=kLoop, calls=%fused_computation.24 | loop fusion | flops 9437184 | bytes 31481856 | tf_op jit(solution)/shard_map/convert_element_type | solution.py:103
  427.2 6.1 %pad_maximum_fusion = bf16[1,512,6144]{1,2,0:T(8,128)(2,1)} fusion(bf16[1,256,6144]{1,2,0:T(8,128)(2,1)} %bitcast.118, bf16[1,256,6144]{1,2,0:T(8,128)(2,1)} %bitcast.117), kind=kLoop, calls=%fused_computation.25 | loop fusion | flops 12582912 | bytes 12582912 | tf_op jit(solution)/shard_map/concatenate | solution.py:106
  434.9 75.3 %reduce-scatter.4.cloned.1.call-done = bf16[3,128,128]{2,1,0:T(8,128)(2,1)} async-done(((bf16[48,128,128]{2,1,0:T(8,128)(2,1)}), bf16[3,128,128]{2,1,0:T(8,128)(2,1)}) %reduce-scatter.4.cloned.1.call-update) | async-done | bytes 98320
  512.0 8.6 %copy.36 = bf16[1,512,6144]{2,1,0:T(8,128)(2,1)} copy(bf16[1,512,6144]{1,2,0:T(8,128)(2,1)} %collective-permute-done) | data formatting | bytes 12582912
  (61 shorter events, 16.9 us)
Async XLA Ops:
  7.2 343.9 %all-gather.4.cloned.1.call-start = ((), (), s32[]{:S(2)}) async-start(), calls=%async_computation.1 | async-start | bytes 53477376 | tf_op jit(solution)/shard_map/all_gather | solution.py:14
  65.5 444.7 %reduce-scatter.4.cloned.1.call-start = ((), (), s32[]{:S(2)}) async-start(), calls=%async_computation.2 | async-start | bytes 1671168
  65.6 31.9 %copy-start.5 = (f32[1,48]{1,0:T(1,128)S(1)}, f32[1,48]{1,0:T(1,128)}, u32[]{:S(2)}) copy-start(f32[1,48]{1,0:T(1,128)} %param.10) | copy-start | bytes 580
  394.3 6.4 %copy-start.1 = (f32[1,48,128,128]{3,2,1,0:T(8,128)S(1)}, f32[1,48,128,128]{3,2,1,0:T(8,128)}, u32[]{:S(2)}) copy-start(f32[1,48,128,128]{3,2,1,0:T(8,128)} %param.11) | copy-start | bytes 9437188
  394.3 6.5 %copy-start.3 = (bf16[256,6144]{0,1:T(8,128)(2,1)S(1)}, bf16[256,6144]{0,1:T(8,128)(2,1)}, u32[]{:S(2)}) copy-start(bf16[256,6144]{0,1:T(8,128)(2,1)} %get-tuple-element.132) | copy-start | bytes 9437188
  409.1 11.8 %slice-start = ((s8[12582912]{0:T(1024)(128)(4,1)}), s8[4194304]{0:T(1024)(128)(4,1)S(1)}, s32[]{:S(2)}) async-start(s8[12582912]{0:T(1024)(128)(4,1)} %bitcast.113), calls=%async_computation.3 | async-start | bytes 8388608
  409.2 11.8 %slice-start.1 = ((s8[12582912]{0:T(1024)(128)(4,1)}), s8[4194304]{0:T(1024)(128)(4,1)S(1)}, s32[]{:S(2)}) async-start(s8[12582912]{0:T(1024)(128)(4,1)} %bitcast.113), calls=%async_computation.4 | async-start | bytes 8388608
  413.1 7.9 %slice-start.2 = ((s8[12582912]{0:T(1024)(128)(4,1)}), s8[4194304]{0:T(1024)(128)(4,1)S(1)}, s32[]{:S(2)}) async-start(s8[12582912]{0:T(1024)(128)(4,1)} %bitcast.113), calls=%async_computation.5 | async-start | bytes 8388608
  413.1 8.5 %copy-start = (f32[256,48,128]{0,2,1:T(8,128)S(1)}, f32[256,48,128]{0,2,1:T(8,128)}, u32[]{:S(2)}) copy-start(f32[256,48,128]{0,2,1:T(8,128)} %broadcast_multiply_fusion.1) | copy-start | bytes 18874372
  413.1 8.5 %copy-start.4 = (f32[1,6144]{1,0:T(1,128)S(1)}, f32[1,6144]{1,0:T(1,128)}, u32[]{:S(2)}) copy-start(f32[1,6144]{1,0:T(1,128)} %param.9) | copy-start | bytes 73732
  427.1 6.1 %copy-start.2 = (f32[48,128,128]{2,1,0:T(8,128)S(1)}, f32[48,128,128]{2,1,0:T(8,128)}, u32[]{:S(2)}) copy-start(f32[48,128,128]{2,1,0:T(8,128)} %get-tuple-element.144) | copy-start | bytes 9437188
  433.3 78.7 %collective-permute-start = (bf16[1,512,6144]{1,2,0:T(8,128)(2,1)}, bf16[1,512,6144]{1,2,0:T(8,128)(2,1)}, u32[]{:S(2)}, u32[]{:S(2)}) collective-permute-start(bf16[1,512,6144]{1,2,0:T(8,128)(2,1)} %pad_maximum_fusion), channel_id=1, source_target_pairs={{0,16},{16,32},{32,48},{48,64},{64,80},{80,96},{96,112},{112,0},{1... | collective-permute-start | bytes 18874376 | tf_op jit(solution)/shard_map/ppermute | solution.py:30
Sparse Core Ops, SparseCore 0:
  65.6 285.3 all-gather.3
  434.9 75.2 reduce-scatter.3
where the time goes:
time: 529 us; the launch traced here: 527 us
  waiting for transfers between devices  287 us (54%)
  other arithmetic  91.3 us (17%)
  matrix products  56.6 us (11%)
  local copies, waits for them, and re-layouts  55.1 us (10%)
  blocking collectives  22.8 us (4%)
  between operations  14.2 us (3%)
    all_gather x1, waiting for transfers between devices, entering(): everything = jax.tree.map(lambda part: lax.all_gather(part, axis), x)  211 us
    unnamed x3, waiting for transfers between devices  75.4 us
    select_n x16, other arithmetic, lap(): return jax.tree.map(lambda a, b: jnp.where(reached, a, b), new, before)  42.6 us
    convert_element_type x2, local copies, waits for them, and re-layouts, on_device(): wide = rows.astype(jnp.float32)  32.9 us
    dot_general x1, matrix products, on_device(): jnp.einsum('nhij,njhd->nihd', weights, values, preferred_element_type=jnp...  26.9 us
    all_gather x1, blocking collectives, entering(): everything = jax.tree.map(lambda part: lax.all_gather(part, axis), x)  22.8 us
    unnamed x20, local copies, waits for them, and re-layouts  18 us
    dot_general x1, matrix products, on_device(): jnp.einsum('njhd,njhe->nhde', scaled_keys, values, preferred_element_type...  15.1 us
  transfers between devices with their start and end apart: 3, of which 2 were waited for; matrix products, arithmetic and copies ran while one was open for 10% of the time, Pallas kernels for 0%

commit v1 on v0

v1 whole, which is shorter than its diff:
```python
import functools

import jax
import jax.numpy as jnp
from jax import lax
from jax.experimental import pallas as pl
from jax.experimental.pallas import tpu as pltpu
from jax.sharding import PartitionSpec as P

BLOCK = 256
EPSILON = 1e-05
HEADS_PER_STEP = 4


def _silu(v):
    return v / (1.0 + jnp.exp(-v))


def _dot_nt(a, b):
    return lax.dot_general(a, b, (((1,), (1,)), ((), ())), preferred_element_type=jnp.float32)


def _dot_tn(a, b):
    return lax.dot_general(a, b, (((0,), (0,)), ((), ())), preferred_element_type=jnp.float32)


def _dot(a, b):
    return lax.dot_general(a, b, (((1,), (0,)), ((), ())), preferred_element_type=jnp.float32)


def _block_state(keys_b, values_b, rate, pos):
    tail = jnp.exp(-rate * (BLOCK - 1 - pos))
    scaled = (keys_b.astype(jnp.float32) * tail).astype(jnp.bfloat16)
    return _dot_tn(scaled, values_b)


def _summary_kernel(rates_ref, x_ref, g_ref, o_ref, *, hg, head_dim, nblocks):
    step = pl.program_id(0)
    pos = lax.broadcasted_iota(jnp.int32, (BLOCK, 1), 0).astype(jnp.float32)
    for hh in range(hg):
        rate = jnp.full((1, 1), rates_ref[step * hg + hh], jnp.float32)
        cols = slice(hh * head_dim, (hh + 1) * head_dim)
        decay = jnp.exp(-rate * BLOCK)
        acc = None
        for b in range(nblocks):
            rows = slice(b * BLOCK, (b + 1) * BLOCK)
            x = x_ref[0, rows, cols].astype(jnp.float32)
            keys_b = (_silu(x * g_ref[0, 1:2, cols]) * head_dim ** (-0.5)).astype(jnp.bfloat16)
            values_b = (x * g_ref[0, 2:3, cols]).astype(jnp.bfloat16)
            update = _block_state(keys_b, values_b, rate, pos)
            acc = update if acc is None else decay * acc + update
        o_ref[hh] = acc


def _output_kernel(rates_ref, x_ref, g_ref, go_ref, s_ref, o_ref, *, hg, head_dim, nblocks):
    step = pl.program_id(0)
    pos = lax.broadcasted_iota(jnp.int32, (BLOCK, 1), 0).astype(jnp.float32)
    row = lax.broadcasted_iota(jnp.int32, (BLOCK, BLOCK), 0)
    col = lax.broadcasted_iota(jnp.int32, (BLOCK, BLOCK), 1)
    offset = (row - col).astype(jnp.float32)
    causal = row >= col
    for hh in range(hg):
        rate = jnp.full((1, 1), rates_ref[step * hg + hh], jnp.float32)
        cols = slice(hh * head_dim, (hh + 1) * head_dim)
        mask = jnp.where(causal, jnp.exp(-rate * jnp.maximum(offset, 0.0)), 0.0)
        lead = jnp.exp(-rate * (pos + 1.0))
        decay = jnp.exp(-rate * BLOCK)
        state = s_ref[hh]
        for b in range(nblocks):
            rows = slice(b * BLOCK, (b + 1) * BLOCK)
            x = x_ref[0, rows, cols].astype(jnp.float32)
            queries_b = _silu(x * g_ref[0, 0:1, cols]).astype(jnp.bfloat16)
            keys_b = (_silu(x * g_ref[0, 1:2, cols]) * head_dim ** (-0.5)).astype(jnp.bfloat16)
            values_b = (x * g_ref[0, 2:3, cols]).astype(jnp.bfloat16)
            scores = _dot_nt(queries_b, keys_b)
            weights = (scores * mask).astype(jnp.bfloat16)
            local = _dot(weights, values_b)
            cross = _dot(queries_b, state.astype(jnp.bfloat16))
            total = local + lead * cross
            normed = total * lax.rsqrt(jnp.mean(total * total, axis=-1, keepdims=True) + EPSILON)
            o_ref[0, rows, cols] = (x + normed * go_ref[0:1, cols]).astype(o_ref.dtype)
            if b + 1 < nblocks:
                state = decay * state + _block_state(keys_b, values_b, rate, pos)


def _summaries(rates, rows, gains, head_dim):
    _, count, width = rows.shape
    heads = width // head_dim
    hg = HEADS_PER_STEP
    cw = hg * head_dim
    kernel = functools.partial(_summary_kernel, hg=hg, head_dim=head_dim, nblocks=count // BLOCK)
    return pl.pallas_call(
        kernel,
        grid_spec=pltpu.PrefetchScalarGridSpec(
            num_scalar_prefetch=1,
            grid=(heads // hg,),
            in_specs=[
                pl.BlockSpec((1, count, cw), lambda i, r: (0, 0, i)),
                pl.BlockSpec((1, 3, cw), lambda i, r: (0, 0, i)),
            ],
            out_specs=pl.BlockSpec((hg, head_dim, head_dim), lambda i, r: (i, 0, 0)),
        ),
        out_shape=jax.ShapeDtypeStruct((heads, head_dim, head_dim), jnp.float32),
        cost_estimate=pl.CostEstimate(
            flops=2 * count * width * head_dim, transcendentals=count * width,
            bytes_accessed=count * width * 2 + heads * head_dim * head_dim * 4,
        ),
    )(rates, rows, gains)


def _outputs(rates, rows, gains, gain_out, states, head_dim):
    _, count, width = rows.shape
    heads = width // head_dim
    hg = HEADS_PER_STEP
    cw = hg * head_dim
    kernel = functools.partial(_output_kernel, hg=hg, head_dim=head_dim, nblocks=count // BLOCK)
    return pl.pallas_call(
        kernel,
        grid_spec=pltpu.PrefetchScalarGridSpec(
            num_scalar_prefetch=1,
            grid=(heads // hg,),
            in_specs=[
                pl.BlockSpec((1, count, cw), lambda i, r: (0, 0, i)),
                pl.BlockSpec((1, 3, cw), lambda i, r: (0, 0, i)),
                pl.BlockSpec((1, cw), lambda i, r: (0, i)),
                pl.BlockSpec((hg, head_dim, head_dim), lambda i, r: (i, 0, 0)),
            ],
            out_specs=pl.BlockSpec((1, count, cw), lambda i, r: (0, 0, i)),
        ),
        out_shape=jax.ShapeDtypeStruct(rows.shape, rows.dtype),
        cost_estimate=pl.CostEstimate(
            flops=8 * count * BLOCK * width, transcendentals=3 * count * width,
            bytes_accessed=2 * count * width * 2 + heads * head_dim * head_dim * 4,
        ),
    )(rates, rows, gains, gain_out, states)


def on_device(section_inputs, input_gains, out_gain, decay_rates, carry_state):
    _, count, width = section_inputs.shape
    rates = decay_rates[0]
    heads = rates.shape[0]
    head_dim = width // heads
    group_size = lax.axis_size("ctx")
    own_heads = heads // group_size
    place = lax.axis_index("ctx")

    summary = _summaries(rates, section_inputs, input_gains, head_dim)
    gathered = lax.all_to_all(summary, "ctx", 0, 0, tiled=True)
    gathered = gathered.reshape(group_size, own_heads, head_dim, head_dim)

    start = place * own_heads
    carry_part = lax.dynamic_slice_in_dim(carry_state[0], start, own_heads, 0)
    rate_part = lax.dynamic_slice_in_dim(rates, start, own_heads, 0)
    target = jnp.arange(group_size + 1)[:, None]
    source = jnp.arange(group_size)[None, :]
    gap = (target - 1 - source).astype(jnp.float32)
    weights = jnp.where(
        (source < target)[:, :, None],
        jnp.exp(-rate_part[None, None, :] * count * jnp.maximum(gap, 0.0)[:, :, None]),
        0.0,
    )
    carry_weights = jnp.exp(-rate_part[None, :] * count * target.astype(jnp.float32))
    prefixes = jnp.einsum(
        "tsh,shde->thde", weights, gathered, precision=lax.Precision.HIGHEST
    ) + carry_weights[:, :, None, None] * carry_part[None]
    end_part = prefixes[group_size]
    incoming = lax.all_to_all(
        prefixes[:group_size].reshape(heads, head_dim, head_dim), "ctx", 0, 0, tiled=True
    )

    rows_out = _outputs(rates, section_inputs, input_gains, out_gain, incoming, head_dim)
    count_s = lax.axis_size("section")
    pairs = [(src, (src + 1) % count_s) for src in range(count_s)]
    next_rows = lax.ppermute(rows_out, "section", pairs)
    return (next_rows, end_part[None])


def solution(mesh):
    return jax.shard_map(
        on_device,
        mesh=mesh,
        in_specs=(
            P("section", "ctx", None),
            P("section", None, None),
            P("section", None),
            P("section", None),
            P("section", None, None, None),
        ),
        out_specs=(P("section", "ctx", None), P("section", "ctx", None, None)),
        check_vma=False,
    )
```

time: 529 us -> 225 us (0.43)
  waiting for transfers between devices: 287 us -> 117 us
  other arithmetic: 91.3 us -> 0.17 us
  matrix products: 56.6 us -> 7.6 us
  local copies, waits for them, and re-layouts: 55.1 us -> 9.77 us
  Pallas kernels: 0 us -> 37.7 us
  blocking collectives: 22.8 us -> 43.3 us
  between operations: 14.2 us -> 0.71 us
  starting transfers between devices: 0.08 us -> 8.34 us
    all_gather x1 -> x0, waiting for transfers between devices: 211 us -> none  [entering(): everything = jax.tree.map(lambda part: lax.all_gather(part, axis), x)]
    unnamed x3 -> x0, waiting for transfers between devices: 75.4 us -> none
    ppermute x1, waiting for transfers between devices: 0.01 us -> 69.6 us  [on_device(): next_rows = lax.ppermute(rows_out, 'section', pairs)]
    dot_general x4 -> x1, matrix products: 56.6 us -> 7.6 us  [on_device(): jnp.einsum('tsh,shde->thde', weights, gathered, precision=lax.Precision.H...]
    select_n x17 -> x0, other arithmetic: 48.8 us -> none  [the longest x16 42.6 us: lap(): return jax.tree.map(lambda a, b: jnp.where(reached, a, b), new, before)]
    all_to_all x0 -> x1, waiting for transfers between devices: none -> 47.5 us  [on_device(): gathered = lax.all_to_all(summary, 'ctx', 0, 0, tiled=True)]
    all_to_all x0 -> x1, blocking collectives: none -> 43.3 us  [on_device(): lax.all_to_all(prefixes[:group_size].reshape(heads, head_dim, head_dim),...]
    pallas_call x0 -> x2, Pallas kernels: none -> 37.7 us  [the longest x1 24 us: _outputs(): pl.pallas_call(kernel, grid_spec=pltpu.PrefetchScalarGridSpec(num_scalar_...]
  transfers between devices with their start and end apart: 3 -> 2, of which waited for: 2 -> 2; matrix products, arithmetic and copies ran while one was open for 10% -> 1% of each run, Pallas kernels for 0% -> 0%
where the time goes in v1:
time: 225 us
  waiting for transfers between devices  117 us (52%)
  blocking collectives  43.3 us (19%)
  Pallas kernels  37.7 us (17%)
  local copies, waits for them, and re-layouts  9.77 us (4%)
  starting transfers between devices  8.34 us (4%)
  matrix products  7.6 us (3%)
    ppermute x1, waiting for transfers between devices, on_device(): next_rows = lax.ppermute(rows_out, 'section', pairs)  69.6 us
    all_to_all x1, waiting for transfers between devices, on_device(): gathered = lax.all_to_all(summary, 'ctx', 0, 0, tiled=True)  47.5 us
    all_to_all x1, blocking collectives, on_device(): lax.all_to_all(prefixes[:group_size].reshape(heads, head_dim, head_dim),...  43.3 us
    pallas_call x1, Pallas kernels, _outputs(): pl.pallas_call(kernel, grid_spec=pltpu.PrefetchScalarGridSpec(num_scalar_...  24 us
    pallas_call x1, Pallas kernels, _summaries(): pl.pallas_call(kernel, grid_spec=pltpu.PrefetchScalarGridSpec(num_scalar_...  13.7 us
    all_to_all x1, starting transfers between devices, on_device(): gathered = lax.all_to_all(summary, 'ctx', 0, 0, tiled=True)  8.33 us
    dot_general x1, matrix products, on_device(): jnp.einsum('tsh,shde->thde', weights, gathered, precision=lax.Precision.H...  7.6 us
    unnamed x8, local copies, waits for them, and re-layouts  6.27 us
  transfers between devices with their start and end apart: 2, of which 2 were waited for; matrix products, arithmetic and copies ran while one was open for 1% of the time, Pallas kernels for 0%

profile of v1, /device:TPU:0, one launch (start us, length us, event | category | flops | bytes accessed | tf_op | source)
XLA Modules:
  0.0 224.6 jit_solution(1490244825675554672)
XLA Ops:
  0.6 0.0 copy-start
  0.6 1.7 copy.10.g_ref
  2.4 13.7 %shard_map.68 = f32[48,128,128]{2,1,0:T(8,128)} custom-call(f32[48]{0:T(128)} %bitcast.17, bf16[1,512,6144]{2,1,0:T(8,128)(2,1)} %x_ref.3, f32[1,3,6144]{2,1,0:T(4,128)} %copy.10.g_ref), custom_call_target="tpu_custom_call" | custom-call | flops 805306368 | bytes 9437184 | tf_op jit(solution)/shard_map/pallas_call | solution.py:92
  16.0 0.0 copy-start.2
  16.0 8.3 %all-to-all-start = ((f32[48,128,128]{2,1,0:T(8,128)}), f32[48,128,128]{2,1,0:T(8,128)}, u32[]{:S(2)}, u32[]{:S(2)}) async-start(f32[48,128,128]{2,1,0:T(8,128)} %shard_map.68), calls=%async_computation | async-start | bytes 6291456 | tf_op jit(solution)/shard_map/all_to_all | solution.py:148
  24.4 0.0 copy-done.2
  24.4 0.1 multiply_bitcast_fusion
  24.5 0.0 copy-done
  24.5 0.1 multiply_exponential_fusion
  24.6 47.5 %all-to-all-done = f32[48,128,128]{2,1,0:T(8,128)} async-done(((f32[48,128,128]{2,1,0:T(8,128)}), f32[48,128,128]{2,1,0:T(8,128)}, u32[]{:S(2)}, u32[]{:S(2)}) %all-to-all-start) | async-done | bytes 3145760 | tf_op jit(solution)/shard_map/all_to_all | solution.py:148
  72.1 7.6 %bitcast_add_fusion = f32[17,3,128,128]{3,0,2,1:T(8,128)S(1)} fusion(f32[3,128,128]{2,1,0:T(8,128)S(1)} %dynamic-slice_bitcast_fusion, f32[17,3]{0,1:T(4,128)S(1)} %multiply_exponential_fusion, f32[16,3,128,128]{3,2,1,0:T(8,128)} %bitcast.1, f32[17,16]{0,1:T(8,128)S(1)} %convert_maximum_fusion, f32[3]{0:T(128)S(1)} %multiply_bitcast_fusion, ...), kind=kOutput, calls=%fused_computation | convolution fusion | flops 162104928 | bytes 6686248 | tf_op jit(solution)/shard_map/tsh,shde->thde/dot_general | solution.py:163
  79.7 0.0 copy-start.1
  79.7 0.3 slice.8
  80.0 1.8 copy-done.1
  81.8 1.0 copy.9
  82.8 43.3 %all_to_all.10.s_ref = f32[48,128,128]{2,1,0:T(8,128)} all-to-all(f32[48,128,128]{2,1,0:T(8,128)S(1)} %bitcast.15), channel_id=1, replica_groups=mesh['section'=8,'ctx'=16] {'ctx'}, dimensions={0} | all-to-all | bytes 6291456 | tf_op jit(solution)/shard_map/all_to_all | solution.py:167
  126.1 24.0 %shard_map.69 = bf16[1,512,6144]{2,1,0:T(8,128)(2,1)} custom-call(f32[48]{0:T(128)} %bitcast.18, bf16[1,512,6144]{2,1,0:T(8,128)(2,1)} %x_ref.3, f32[1,3,6144]{2,1,0:T(4,128)} %copy.10.g_ref, f32[1,6144]{1,0:T(1,128)} %go_ref.1, f32[48,128,128]{2,1,0:T(8,128)} %all_to_all.10.s_ref), custom_call_target="tpu_custom_call" | custom-call | flops 6442450944 | bytes 15728640 | tf_op jit(solution)/shard_map/pallas_call | solution.py:117
  150.1 0.0 collective-permute-start
  150.1 2.2 slice.9
  152.3 69.6 %collective-permute-done = bf16[1,512,6144]{2,1,0:T(8,128)(2,1)S(1)} collective-permute-done((bf16[1,512,6144]{2,1,0:T(8,128)(2,1)}, bf16[1,512,6144]{2,1,0:T(8,128)(2,1)S(1)}, u32[]{:S(2)}, u32[]{:S(2)}) %collective-permute-start) | collective-permute-done | bytes 6291488 | tf_op jit(solution)/shard_map/ppermute | solution.py:174
  221.9 2.7 %copy.18 = bf16[1,512,6144]{2,1,0:T(8,128)(2,1)} copy(bf16[1,512,6144]{2,1,0:T(8,128)(2,1)S(1)} %collective-permute-done) | data formatting | bytes 12582912
  (5 shorter events, 0.0 us)
Async XLA Ops:
  0.6 23.9 %copy-start = (f32[1,48,128,128]{3,2,1,0:T(8,128)S(1)}, f32[1,48,128,128]{3,2,1,0:T(8,128)}, u32[]{:S(2)}) copy-start(f32[1,48,128,128]{3,2,1,0:T(8,128)} %param.9) | copy-start | bytes 9437188
  16.0 8.4 %copy-start.2 = (f32[1,48]{1,0:T(1,128)S(1)}, f32[1,48]{1,0:T(1,128)}, u32[]{:S(2)}) copy-start(f32[1,48]{1,0:T(1,128)} %param.8) | copy-start | bytes 580
  16.0 56.1 %all-to-all-start = ((f32[48,128,128]{2,1,0:T(8,128)}), f32[48,128,128]{2,1,0:T(8,128)}, u32[]{:S(2)}, u32[]{:S(2)}) async-start(f32[48,128,128]{2,1,0:T(8,128)} %shard_map.68), calls=%async_computation | async-start | bytes 6291456 | tf_op jit(solution)/shard_map/all_to_all | solution.py:148
  79.7 2.1 copy-start.1
  150.1 71.8 %collective-permute-start = (bf16[1,512,6144]{2,1,0:T(8,128)(2,1)}, bf16[1,512,6144]{2,1,0:T(8,128)(2,1)S(1)}, u32[]{:S(2)}, u32[]{:S(2)}) collective-permute-start(bf16[1,512,6144]{2,1,0:T(8,128)(2,1)} %shard_map.69), channel_id=1, source_target_pairs={{0,16},{16,32},{32,48},{48,64},{64,80},{80,96},{96,112},{112,0},{1... | collective-permute-start | bytes 18874376 | tf_op jit(solution)/shard_map/ppermute | solution.py:174

commit v2 on v1

--- a/solution.py
+++ b/solution.py
@@ -65,7 +65,7 @@
         mask = jnp.where(causal, jnp.exp(-rate * jnp.maximum(offset, 0.0)), 0.0)
         lead = jnp.exp(-rate * (pos + 1.0))
         decay = jnp.exp(-rate * BLOCK)
-        state = s_ref[hh]
+        state = s_ref[hh].astype(jnp.float32)
         for b in range(nblocks):
             rows = slice(b * BLOCK, (b + 1) * BLOCK)
             x = x_ref[0, rows, cols].astype(jnp.float32)
@@ -143,10 +143,17 @@
     group_size = lax.axis_size("ctx")
     own_heads = heads // group_size
     place = lax.axis_index("ctx")
+    count_s = lax.axis_size("section")
+    pairs = [(src, (src + 1) % count_s) for src in range(count_s)]
+
+    prev_rows = lax.ppermute(section_inputs, "section", pairs)
+    prev_gains, prev_gain_out, prev_rates = lax.ppermute(
+        (input_gains, out_gain, decay_rates), "section", pairs
+    )
 
     summary = _summaries(rates, section_inputs, input_gains, head_dim)
-    gathered = lax.all_to_all(summary, "ctx", 0, 0, tiled=True)
-    gathered = gathered.reshape(group_size, own_heads, head_dim, head_dim)
+    gathered = lax.all_to_all(summary.astype(jnp.bfloat16), "ctx", 0, 0, tiled=True)
+    gathered = gathered.astype(jnp.float32).reshape(group_size, own_heads, head_dim, head_dim)
 
     start = place * own_heads
     carry_part = lax.dynamic_slice_in_dim(carry_state[0], start, own_heads, 0)
@@ -165,13 +172,14 @@
     ) + carry_weights[:, :, None, None] * carry_part[None]
     end_part = prefixes[group_size]
     incoming = lax.all_to_all(
-        prefixes[:group_size].reshape(heads, head_dim, head_dim), "ctx", 0, 0, tiled=True
+        prefixes[:group_size].astype(jnp.bfloat16).reshape(heads, head_dim, head_dim),
+        "ctx", 0, 0, tiled=True,
     )
+    prev_incoming = lax.ppermute(incoming, "section", pairs)
 
-    rows_out = _outputs(rates, section_inputs, input_gains, out_gain, incoming, head_dim)
-    count_s = lax.axis_size("section")
-    pairs = [(src, (src + 1) % count_s) for src in range(count_s)]
-    next_rows = lax.ppermute(rows_out, "section", pairs)
+    next_rows = _outputs(
+        prev_rates[0], prev_rows, prev_gains, prev_gain_out, prev_incoming, head_dim
+    )
     return (next_rows, end_part[None])
 
 

time: 225 us -> 134 us (0.60)
  waiting for transfers between devices: 117 us -> 46.1 us
  blocking collectives: 43.3 us -> 26 us
  local copies, waits for them, and re-layouts: 9.77 us -> 4.32 us
  matrix products: 7.6 us -> 4.03 us
  other arithmetic: 0.17 us -> 3.59 us
  starting transfers between devices: 8.34 us -> 11.4 us
    ppermute x1 -> x5, waiting for transfers between devices: 69.6 us -> 18.5 us  [the longest x3 18.5 us: on_device(): lax.ppermute((input_gains, out_gain, decay_rates), 'section', pairs)]
    all_to_all x1, waiting for transfers between devices: 47.5 us -> 27.6 us  [on_device(): lax.all_to_all(summary.astype(jnp.bfloat16), 'ctx', 0, 0, tiled=True)]
    all_to_all x1, blocking collectives: 43.3 us -> 26 us  [on_device(): lax.all_to_all(prefixes[:group_size].astype(jnp.bfloat16).reshape(heads,...]
    dot_general x1, matrix products: 7.6 us -> 4.03 us  [on_device(): jnp.einsum('tsh,shde->thde', weights, gathered, precision=lax.Precision.H...]
    convert_element_type x0 -> x1, other arithmetic: none -> 3.42 us  [on_device(): summary.astype(jnp.bfloat16)]
    unnamed x8 -> x17, local copies, waits for them, and re-layouts: 6.27 us -> 2.91 us
    ppermute x1 -> x5, starting transfers between devices: 0.01 us -> 3.21 us  [the longest x3 3.19 us: on_device(): lax.ppermute((input_gains, out_gain, decay_rates), 'section', pairs)]
  transfers between devices with their start and end apart: 2 -> 6, of which waited for: 2 -> 2; matrix products, arithmetic and copies ran while one was open for 1% -> 8% of each run, Pallas kernels for 0% -> 10%
where the time goes in v2:
time: 134 us
  waiting for transfers between devices  46.1 us (34%)
  Pallas kernels  37.6 us (28%)
  blocking collectives  26 us (19%)
  starting transfers between devices  11.4 us (9%)
  local copies, waits for them, and re-layouts  4.32 us (3%)
  matrix products  4.03 us (3%)
  other arithmetic  3.59 us (3%)
    all_to_all x1, waiting for transfers between devices, on_device(): lax.all_to_all(summary.astype(jnp.bfloat16), 'ctx', 0, 0, tiled=True)  27.6 us
    all_to_all x1, blocking collectives, on_device(): lax.all_to_all(prefixes[:group_size].astype(jnp.bfloat16).reshape(heads,...  26 us
    pallas_call x1, Pallas kernels, _outputs(): pl.pallas_call(kernel, grid_spec=pltpu.PrefetchScalarGridSpec(num_scalar_...  24 us
    ppermute x3, waiting for transfers between devices, on_device(): lax.ppermute((input_gains, out_gain, decay_rates), 'section', pairs)  18.5 us
    pallas_call x1, Pallas kernels, _summaries(): pl.pallas_call(kernel, grid_spec=pltpu.PrefetchScalarGridSpec(num_scalar_...  13.7 us
    all_to_all x1, starting transfers between devices, on_device(): lax.all_to_all(summary.astype(jnp.bfloat16), 'ctx', 0, 0, tiled=True)  8.21 us
    dot_general x1, matrix products, on_device(): jnp.einsum('tsh,shde->thde', weights, gathered, precision=lax.Precision.H...  4.03 us
    convert_element_type x1, other arithmetic, on_device(): summary.astype(jnp.bfloat16)  3.42 us
  transfers between devices with their start and end apart: 6, of which 2 were waited for; matrix products, arithmetic and copies ran while one was open for 8% of the time, Pallas kernels for 10%

profile of v2, /device:TPU:0, one launch (start us, length us, event | category | flops | bytes accessed | tf_op | source)
XLA Modules:
  0.0 133.9 jit_solution(15079900458204126967)
XLA Ops:
  0.6 0.0 copy-start
  0.6 0.0 collective-permute-start.1
  0.7 1.7 %copy.7.g_ref = f32[1,3,6144]{2,1,0:T(4,128)} copy(f32[1,3,6144]{2,0,1:T(1,128)} %param.6) | data formatting | bytes 147456 | tf_op args[1]
  2.4 13.7 %shard_map.68 = f32[48,128,128]{2,1,0:T(8,128)} custom-call(f32[48]{0:T(128)} %bitcast.18, bf16[1,512,6144]{2,1,0:T(8,128)(2,1)} %x_ref.1, f32[1,3,6144]{2,1,0:T(4,128)} %copy.7.g_ref), custom_call_target="tpu_custom_call" | custom-call | flops 805306368 | bytes 9437184 | tf_op jit(solution)/shard_map/pallas_call | solution.py:92
  16.0 3.4 %convert_element_type.20 = bf16[48,128,128]{2,1,0:T(8,128)(2,1)} convert(f32[48,128,128]{2,1,0:T(8,128)} %shard_map.68) | non-fusion elementwise | flops 786432 | bytes 4718592 | tf_op jit(solution)/shard_map/convert_element_type | solution.py:155
  19.5 8.2 %all-to-all-start = ((bf16[48,128,128]{2,1,0:T(8,128)(2,1)}), bf16[48,128,128]{2,1,0:T(8,128)(2,1)}, u32[]{:S(2)}, u32[]{:S(2)}) async-start(bf16[48,128,128]{2,1,0:T(8,128)(2,1)} %convert_element_type.20), calls=%async_computation | async-start | bytes 3145728 | tf_op jit(solution)/shard_map/all_to_all | solution.py:155
  27.7 0.0 copy-done.2
  27.7 0.1 multiply_bitcast_fusion
  27.8 0.0 copy-done
  27.8 0.1 multiply_exponential_fusion
  27.9 27.6 %all-to-all-done = bf16[48,128,128]{2,1,0:T(8,128)(2,1)} async-done(((bf16[48,128,128]{2,1,0:T(8,128)(2,1)}), bf16[48,128,128]{2,1,0:T(8,128)(2,1)}, u32[]{:S(2)}, u32[]{:S(2)}) %all-to-all-start) | async-done | bytes 1572896 | tf_op jit(solution)/shard_map/all_to_all | solution.py:155
  55.5 4.0 %bitcast_add_fusion = f32[17,3,128,128]{3,0,2,1:T(8,128)S(1)} fusion(f32[3,128,128]{2,1,0:T(8,128)S(1)} %dynamic-slice_bitcast_fusion, f32[17,3]{0,1:T(4,128)S(1)} %multiply_exponential_fusion, bf16[16,3,128,128]{3,2,1,0:T(8,128)(2,1)} %bitcast.2, f32[17,16]{0,1:T(8,128)S(1)} %convert_maximum_fusion, f32[3]{0:T(128)S(1)} %multiply_bitcast_fusion, ...), kind=kOutput, calls=%fused_computation | convolution fusion | flops 162104928 | bytes 5113384 | tf_op jit(solution)/shard_map/tsh,shde->thde/dot_general | solution.py:170
  59.6 0.2 slice.12
  59.8 0.0 copy-start.1
  59.8 0.0 copy-start.5
  59.8 0.4 copy.10
  60.2 26.0 %all_to_all.10 = bf16[48,128,128]{2,1,0:T(8,128)(2,1)S(1)} all-to-all(bf16[48,128,128]{2,1,0:T(8,128)(2,1)S(1)} %bitcast.16), channel_id=1, replica_groups=mesh['section'=8,'ctx'=16] {'ctx'}, dimensions={0} | all-to-all | bytes 3145728 | tf_op jit(solution)/shard_map/all_to_all | solution.py:174
  86.2 0.0 collective-permute-start.4
  86.2 0.0 copy-done.1
  86.2 1.6 %collective-permute-start.2 = (f32[1,3,6144]{2,1,0:T(4,128)S(1)}, f32[1,3,6144]{2,1,0:T(4,128)S(1)}, u32[]{:S(2)}, u32[]{:S(2)}) collective-permute-start(f32[1,3,6144]{2,1,0:T(4,128)S(1)} %copy-done.1), channel_id=1, source_target_pairs={{0,16},{16,32},{32,48},{48,64},{64,80},{80,96},{96,112},{112,0},{1... | collective-permute-start | bytes 221192 | tf_op jit(solution)/shard_map/ppermute | solution.py:150
  87.8 0.0 collective-permute-start.3
  87.8 1.6 %collective-permute-start = (f32[1,48]{1,0:T(1,128)S(1)}, f32[1,48]{1,0:T(1,128)S(1)}, u32[]{:S(2)}, u32[]{:S(2)}) collective-permute-start(f32[1,48]{1,0:T(1,128)S(1)} %copy-done.2), channel_id=1, source_target_pairs={{0,16},{16,32},{32,48},{48,64},{64,80},{80,96},{96,112},{112,0},{1... | collective-permute-start | bytes 584 | tf_op jit(solution)/shard_map/ppermute | solution.py:150
  89.4 0.8 slice.10
  90.2 18.5 %collective-permute-done = f32[1,48]{1,0:T(1,128)S(1)} collective-permute-done((f32[1,48]{1,0:T(1,128)S(1)}, f32[1,48]{1,0:T(1,128)S(1)}, u32[]{:S(2)}, u32[]{:S(2)}) %collective-permute-start) | collective-permute-done | bytes 224 | tf_op jit(solution)/shard_map/ppermute | solution.py:150
  108.7 0.0 collective-permute-done.3.go_ref
  108.7 0.0 collective-permute-done.2.g_ref
  108.7 0.0 collective-permute-done.4.s_ref
  108.7 0.0 copy-start.3
  108.7 1.2 copy-done.3
  109.8 0.0 collective-permute-done.1.x_ref
  109.9 0.0 copy-done.6
  109.9 24.0 %shard_map.69 = bf16[1,512,6144]{2,1,0:T(8,128)(2,1)} custom-call(f32[48]{0:T(128)} %bitcast.19, bf16[1,512,6144]{2,1,0:T(8,128)(2,1)} %collective-permute-done.1.x_ref, f32[1,3,6144]{2,1,0:T(4,128)} %copy-done.4, f32[1,6144]{1,0:T(1,128)} %copy-done.6, bf16[48,128,128]{2,1,0:T(8,128)(2,1)} %copy-done.3), custom_call_target="tpu_custom_call" | custom-call | flops 6442450944 | bytes 15728640 | tf_op jit(solution)/shard_map/pallas_call | solution.py:117
  (12 shorter events, 0.1 us)
Async XLA Ops:
  0.6 27.2 %copy-start = (f32[1,48,128,128]{3,2,1,0:T(8,128)S(1)}, f32[1,48,128,128]{3,2,1,0:T(8,128)}, u32[]{:S(2)}) copy-start(f32[1,48,128,128]{3,2,1,0:T(8,128)} %param.9) | copy-start | bytes 9437188
  0.6 109.2 %collective-permute-start.1 = (bf16[1,512,6144]{2,1,0:T(8,128)(2,1)}, bf16[1,512,6144]{2,1,0:T(8,128)(2,1)}, u32[]{:S(2)}, u32[]{:S(2)}) collective-permute-start(bf16[1,512,6144]{2,1,0:T(8,128)(2,1)} %x_ref.1), channel_id=1, source_target_pairs={{0,16},{16,32},{32,48},{48,64},{64,80},{80,96},{96,112},{112,0},{1... | collective-permute-start | bytes 18874376 | tf_op jit(solution)/shard_map/ppermute | solution.py:149
  16.0 11.7 %copy-start.2 = (f32[1,48]{1,0:T(1,128)S(1)}, f32[1,48]{1,0:T(1,128)}, u32[]{:S(2)}) copy-start(f32[1,48]{1,0:T(1,128)} %param.8) | copy-start | bytes 580
  19.5 36.1 %all-to-all-start = ((bf16[48,128,128]{2,1,0:T(8,128)(2,1)}), bf16[48,128,128]{2,1,0:T(8,128)(2,1)}, u32[]{:S(2)}, u32[]{:S(2)}) async-start(bf16[48,128,128]{2,1,0:T(8,128)(2,1)} %convert_element_type.20), calls=%async_computation | async-start | bytes 3145728 | tf_op jit(solution)/shard_map/all_to_all | solution.py:155
  59.8 26.4 %copy-start.1 = (f32[1,3,6144]{2,1,0:T(4,128)S(1)}, f32[1,3,6144]{2,1,0:T(4,128)}, u32[]{:S(2)}) copy-start(f32[1,3,6144]{2,1,0:T(4,128)} %copy.7.g_ref) | copy-start | bytes 221188
  59.8 28.0 %copy-start.5 = (f32[1,6144]{1,0:T(1,128)S(1)}, f32[1,6144]{1,0:T(1,128)}, u32[]{:S(2)}) copy-start(f32[1,6144]{1,0:T(1,128)} %param.7) | copy-start | bytes 73732
  86.2 22.5 %collective-permute-start.4 = (bf16[48,128,128]{2,1,0:T(8,128)(2,1)S(1)}, bf16[48,128,128]{2,1,0:T(8,128)(2,1)S(1)}, u32[]{:S(2)}, u32[]{:S(2)}) collective-permute-start(bf16[48,128,128]{2,1,0:T(8,128)(2,1)S(1)} %all_to_all.10), channel_id=1, source_target_pairs={{0,16},{16,32},{32,48},{48,64},{64,80},{80,96},{96,112},{112,0},{1... | collective-permute-start | bytes 4718600 | tf_op jit(solution)/shard_map/ppermute | solution.py:178
  86.2 22.5 %collective-permute-start.2 = (f32[1,3,6144]{2,1,0:T(4,128)S(1)}, f32[1,3,6144]{2,1,0:T(4,128)S(1)}, u32[]{:S(2)}, u32[]{:S(2)}) collective-permute-start(f32[1,3,6144]{2,1,0:T(4,128)S(1)} %copy-done.1), channel_id=1, source_target_pairs={{0,16},{16,32},{32,48},{48,64},{64,80},{80,96},{96,112},{112,0},{1... | collective-permute-start | bytes 221192 | tf_op jit(solution)/shard_map/ppermute | solution.py:150
  87.8 20.9 %collective-permute-start.3 = (f32[1,6144]{1,0:T(1,128)S(1)}, f32[1,6144]{1,0:T(1,128)S(1)}, u32[]{:S(2)}, u32[]{:S(2)}) collective-permute-start(f32[1,6144]{1,0:T(1,128)S(1)} %copy-done.5), channel_id=1, source_target_pairs={{0,16},{16,32},{32,48},{48,64},{64,80},{80,96},{96,112},{112,0},{1... | collective-permute-start | bytes 73736 | tf_op jit(solution)/shard_map/ppermute | solution.py:150
  87.8 20.8 %collective-permute-start = (f32[1,48]{1,0:T(1,128)S(1)}, f32[1,48]{1,0:T(1,128)S(1)}, u32[]{:S(2)}, u32[]{:S(2)}) collective-permute-start(f32[1,48]{1,0:T(1,128)S(1)} %copy-done.2), channel_id=1, source_target_pairs={{0,16},{16,32},{32,48},{48,64},{64,80},{80,96},{96,112},{112,0},{1... | collective-permute-start | bytes 584 | tf_op jit(solution)/shard_map/ppermute | solution.py:150
  108.7 1.2 copy-start.7
  108.7 1.2 copy-start.6
  108.7 1.2 copy-start.4
  108.7 1.2 copy-start.3

commit v3 on v2

--- a/solution.py
+++ b/solution.py
@@ -49,10 +49,10 @@
             values_b = (x * g_ref[0, 2:3, cols]).astype(jnp.bfloat16)
             update = _block_state(keys_b, values_b, rate, pos)
             acc = update if acc is None else decay * acc + update
-        o_ref[hh] = acc
-
-
-def _output_kernel(rates_ref, x_ref, g_ref, go_ref, s_ref, o_ref, *, hg, head_dim, nblocks):
+        o_ref[hh] = acc.astype(o_ref.dtype)
+
+
+def _local_kernel(rates_ref, x_ref, g_ref, q_ref, l_ref, r_ref, *, hg, head_dim, nblocks):
     step = pl.program_id(0)
     pos = lax.broadcasted_iota(jnp.int32, (BLOCK, 1), 0).astype(jnp.float32)
     row = lax.broadcasted_iota(jnp.int32, (BLOCK, BLOCK), 0)
@@ -63,9 +63,8 @@
         rate = jnp.full((1, 1), rates_ref[step * hg + hh], jnp.float32)
         cols = slice(hh * head_dim, (hh + 1) * head_dim)
         mask = jnp.where(causal, jnp.exp(-rate * jnp.maximum(offset, 0.0)), 0.0)
-        lead = jnp.exp(-rate * (pos + 1.0))
         decay = jnp.exp(-rate * BLOCK)
-        state = s_ref[hh].astype(jnp.float32)
+        running = None
         for b in range(nblocks):
             rows = slice(b * BLOCK, (b + 1) * BLOCK)
             x = x_ref[0, rows, cols].astype(jnp.float32)
@@ -74,13 +73,33 @@
             values_b = (x * g_ref[0, 2:3, cols]).astype(jnp.bfloat16)
             scores = _dot_nt(queries_b, keys_b)
             weights = (scores * mask).astype(jnp.bfloat16)
-            local = _dot(weights, values_b)
-            cross = _dot(queries_b, state.astype(jnp.bfloat16))
-            total = local + lead * cross
+            q_ref[0, rows, cols] = queries_b
+            l_ref[0, rows, cols] = _dot(weights, values_b)
+            if b + 1 < nblocks:
+                update = _block_state(keys_b, values_b, rate, pos)
+                running = update if running is None else decay * running + update
+                r_ref[b, hh] = running
+
+
+def _final_kernel(rates_ref, x_ref, q_ref, l_ref, r_ref, s_ref, go_ref, o_ref, *, hg, head_dim, nblocks):
+    step = pl.program_id(0)
+    pos = lax.broadcasted_iota(jnp.int32, (BLOCK, 1), 0).astype(jnp.float32)
+    for hh in range(hg):
+        rate = jnp.full((1, 1), rates_ref[step * hg + hh], jnp.float32)
+        cols = slice(hh * head_dim, (hh + 1) * head_dim)
+        lead = jnp.exp(-rate * (pos + 1.0))
+        decay = jnp.exp(-rate * BLOCK)
+        entering = s_ref[hh].astype(jnp.float32)
+        state = entering
+        for b in range(nblocks):
+            rows = slice(b * BLOCK, (b + 1) * BLOCK)
+            if b > 0:
+                state = decay * state + (r_ref[b - 1, hh] - decay * r_ref[b - 2, hh] if b > 1 else r_ref[0, hh])
+            cross = _dot(q_ref[0, rows, cols], state.astype(jnp.bfloat16))
+            total = l_ref[0, rows, cols] + lead * cross
             normed = total * lax.rsqrt(jnp.mean(total * total, axis=-1, keepdims=True) + EPSILON)
+            x = x_ref[0, rows, cols].astype(jnp.float32)
             o_ref[0, rows, cols] = (x + normed * go_ref[0:1, cols]).astype(o_ref.dtype)
-            if b + 1 < nblocks:
-                state = decay * state + _block_state(keys_b, values_b, rate, pos)
 
 
 def _summaries(rates, rows, gains, head_dim):
@@ -100,7 +119,7 @@
             ],
             out_specs=pl.BlockSpec((hg, head_dim, head_dim), lambda i, r: (i, 0, 0)),
         ),
-        out_shape=jax.ShapeDtypeStruct((heads, head_dim, head_dim), jnp.float32),
+        out_shape=jax.ShapeDtypeStruct((heads, head_dim, head_dim), jnp.bfloat16),
         cost_estimate=pl.CostEstimate(
             flops=2 * count * width * head_dim, transcendentals=count * width,
             bytes_accessed=count * width * 2 + heads * head_dim * head_dim * 4,
@@ -113,26 +132,47 @@
     heads = width // head_dim
     hg = HEADS_PER_STEP
     cw = hg * head_dim
-    kernel = functools.partial(_output_kernel, hg=hg, head_dim=head_dim, nblocks=count // BLOCK)
+    nblocks = count // BLOCK
+    row_spec = pl.BlockSpec((1, count, cw), lambda i, r: (0, 0, i))
+    run_spec = pl.BlockSpec((nblocks - 1, hg, head_dim, head_dim), lambda i, r: (0, i, 0, 0))
+    local_kernel = functools.partial(_local_kernel, hg=hg, head_dim=head_dim, nblocks=nblocks)
+    queries, local, running = pl.pallas_call(
+        local_kernel,
+        grid_spec=pltpu.PrefetchScalarGridSpec(
+            num_scalar_prefetch=1,
+            grid=(heads // hg,),
+            in_specs=[row_spec, pl.BlockSpec((1, 3, cw), lambda i, r: (0, 0, i))],
+            out_specs=[row_spec, row_spec, run_spec],
+        ),
+        out_shape=[
+            jax.ShapeDtypeStruct(rows.shape, jnp.bfloat16),
+            jax.ShapeDtypeStruct(rows.shape, jnp.float32),
+            jax.ShapeDtypeStruct((nblocks - 1, heads, head_dim, head_dim), jnp.float32),
+        ],
+        cost_estimate=pl.CostEstimate(
+            flops=6 * count * BLOCK * width, transcendentals=3 * count * width,
+            bytes_accessed=count * width * 8,
+        ),
+    )(rates, rows, gains)
+    final_kernel = functools.partial(_final_kernel, hg=hg, head_dim=head_dim, nblocks=nblocks)
     return pl.pallas_call(
-        kernel,
+        final_kernel,
         grid_spec=pltpu.PrefetchScalarGridSpec(
             num_scalar_prefetch=1,
             grid=(heads // hg,),
             in_specs=[
-                pl.BlockSpec((1, count, cw), lambda i, r: (0, 0, i)),
-                pl.BlockSpec((1, 3, cw), lambda i, r: (0, 0, i)),
+                row_spec, row_spec, row_spec, run_spec,
+                pl.BlockSpec((hg, head_dim, head_dim), lambda i, r: (i, 0, 0)),
                 pl.BlockSpec((1, cw), lambda i, r: (0, i)),
-                pl.BlockSpec((hg, head_dim, head_dim), lambda i, r: (i, 0, 0)),
             ],
-            out_specs=pl.BlockSpec((1, count, cw), lambda i, r: (0, 0, i)),
+            out_specs=row_spec,
         ),
         out_shape=jax.ShapeDtypeStruct(rows.shape, rows.dtype),
         cost_estimate=pl.CostEstimate(
-            flops=8 * count * BLOCK * width, transcendentals=3 * count * width,
-            bytes_accessed=2 * count * width * 2 + heads * head_dim * head_dim * 4,
-        ),
-    )(rates, rows, gains, gain_out, states)
+            flops=2 * count * width * head_dim, transcendentals=count * width,
+            bytes_accessed=count * width * 10,
+        ),
+    )(rates, rows, queries, local, running, states, gain_out)
 
 
 def on_device(section_inputs, input_gains, out_gain, decay_rates, carry_state):
@@ -152,7 +192,7 @@
     )
 
     summary = _summaries(rates, section_inputs, input_gains, head_dim)
-    gathered = lax.all_to_all(summary.astype(jnp.bfloat16), "ctx", 0, 0, tiled=True)
+    gathered = lax.all_to_all(summary, "ctx", 0, 0, tiled=True)
     gathered = gathered.astype(jnp.float32).reshape(group_size, own_heads, head_dim, head_dim)
 
     start = place * own_heads

time: 134 us -> 146 us (1.090)
  Pallas kernels: 37.6 us -> 51 us
  other arithmetic: 3.59 us -> 0.17 us
    pallas_call x1 -> x2, Pallas kernels: 24 us -> 37.6 us  [the longest x1 19.7 us: _outputs(): pl.pallas_call(local_kernel, grid_spec=pltpu.PrefetchScalarGridSpec(num_s...]
    convert_element_type x1 -> x0, other arithmetic: 3.42 us -> none  [on_device(): summary.astype(jnp.bfloat16)]
    unnamed x17 -> x15, local copies, waits for them, and re-layouts: 2.91 us -> 2.98 us
  transfers between devices with their start and end apart: 6 -> 6, of which waited for: 2 -> 2; matrix products, arithmetic and copies ran while one was open for 8% -> 5% of each run, Pallas kernels for 10% -> 23%
where the time goes in v3:
time: 146 us; the launch traced here: 145 us
  Pallas kernels  51 us (35%)
  waiting for transfers between devices  46.2 us (32%)
  blocking collectives  26.7 us (18%)
  starting transfers between devices  11.5 us (8%)
  local copies, waits for them, and re-layouts  4.39 us (3%)
  matrix products  4.03 us (3%)
    all_to_all x1, waiting for transfers between devices, on_device(): gathered = lax.all_to_all(summary, 'ctx', 0, 0, tiled=True)  27.6 us
    all_to_all x1, blocking collectives, on_device(): lax.all_to_all(prefixes[:group_size].astype(jnp.bfloat16).reshape(heads,...  26.7 us
    pallas_call x1, Pallas kernels, _outputs(): pl.pallas_call(local_kernel, grid_spec=pltpu.PrefetchScalarGridSpec(num_s...  19.7 us
    ppermute x3, waiting for transfers between devices, on_device(): lax.ppermute((input_gains, out_gain, decay_rates), 'section', pairs)  18.5 us
    pallas_call x1, Pallas kernels, _outputs(): pl.pallas_call(final_kernel, grid_spec=pltpu.PrefetchScalarGridSpec(num_s...  17.9 us
    pallas_call x1, Pallas kernels, _summaries(): pl.pallas_call(kernel, grid_spec=pltpu.PrefetchScalarGridSpec(num_scalar_...  13.4 us
    all_to_all x1, starting transfers between devices, on_device(): gathered = lax.all_to_all(summary, 'ctx', 0, 0, tiled=True)  8.34 us
    dot_general x1, matrix products, on_device(): jnp.einsum('tsh,shde->thde', weights, gathered, precision=lax.Precision.H...  4.03 us
  transfers between devices with their start and end apart: 6, of which 2 were waited for; matrix products, arithmetic and copies ran while one was open for 5% of the time, Pallas kernels for 23%

profile of v3, /device:TPU:0, one launch (start us, length us, event | category | flops | bytes accessed | tf_op | source)
XLA Modules:
  0.0 144.7 jit_solution(6862502130133015921)
XLA Ops:
  0.6 0.0 copy-start
  0.6 0.0 collective-permute-start.1
  0.7 1.7 %copy.7.g_ref = f32[1,3,6144]{2,1,0:T(4,128)} copy(f32[1,3,6144]{2,0,1:T(1,128)} %param.6) | data formatting | bytes 147456 | tf_op args[1]
  2.4 13.4 %shard_map.69 = bf16[48,128,128]{2,1,0:T(8,128)(2,1)} custom-call(f32[48]{0:T(128)} %bitcast.18, bf16[1,512,6144]{2,1,0:T(8,128)(2,1)} %x_ref.1, f32[1,3,6144]{2,1,0:T(4,128)} %copy.7.g_ref), custom_call_target="tpu_custom_call" | custom-call | flops 805306368 | bytes 9437184 | tf_op jit(solution)/shard_map/pallas_call | solution.py:111
  15.8 8.3 %all-to-all-start = ((bf16[48,128,128]{2,1,0:T(8,128)(2,1)}), bf16[48,128,128]{2,1,0:T(8,128)(2,1)}, u32[]{:S(2)}, u32[]{:S(2)}) async-start(bf16[48,128,128]{2,1,0:T(8,128)(2,1)} %shard_map.69), calls=%async_computation | async-start | bytes 3145728 | tf_op jit(solution)/shard_map/all_to_all | solution.py:195
  24.1 0.0 copy-done.3
  24.1 0.1 multiply_bitcast_fusion
  24.2 0.0 copy-done
  24.3 0.1 multiply_exponential_fusion
  24.4 27.6 %all-to-all-done = bf16[48,128,128]{2,1,0:T(8,128)(2,1)} async-done(((bf16[48,128,128]{2,1,0:T(8,128)(2,1)}), bf16[48,128,128]{2,1,0:T(8,128)(2,1)}, u32[]{:S(2)}, u32[]{:S(2)}) %all-to-all-start) | async-done | bytes 1572896 | tf_op jit(solution)/shard_map/all_to_all | solution.py:195
  52.0 4.0 %bitcast_add_fusion = f32[17,3,128,128]{3,0,2,1:T(8,128)S(1)} fusion(f32[3,128,128]{2,1,0:T(8,128)S(1)} %dynamic-slice_bitcast_fusion, f32[17,3]{0,1:T(4,128)S(1)} %multiply_exponential_fusion, bf16[16,3,128,128]{3,2,1,0:T(8,128)(2,1)} %bitcast.2, f32[17,16]{0,1:T(8,128)S(1)} %convert_maximum_fusion, f32[3]{0:T(128)S(1)} %multiply_bitcast_fusion, ...), kind=kOutput, calls=%fused_computation | convolution fusion | flops 162104928 | bytes 5113384 | tf_op jit(solution)/shard_map/tsh,shde->thde/dot_general | solution.py:210
  56.0 0.2 slice.12
  56.2 0.0 copy-start.1
  56.2 0.0 copy-start.6
  56.3 0.4 copy.10
  56.7 26.7 %all_to_all.10 = bf16[48,128,128]{2,1,0:T(8,128)(2,1)} all-to-all(bf16[48,128,128]{2,1,0:T(8,128)(2,1)S(1)} %bitcast.16), channel_id=1, replica_groups=mesh['section'=8,'ctx'=16] {'ctx'}, dimensions={0} | all-to-all | bytes 3145728 | tf_op jit(solution)/shard_map/all_to_all | solution.py:214
  83.4 0.0 collective-permute-start.3
  83.4 0.0 copy-done.1
  83.4 1.6 %collective-permute-start.2 = (f32[1,3,6144]{2,1,0:T(4,128)S(1)}, f32[1,3,6144]{2,1,0:T(4,128)S(1)}, u32[]{:S(2)}, u32[]{:S(2)}) collective-permute-start(f32[1,3,6144]{2,1,0:T(4,128)S(1)} %copy-done.1), channel_id=1, source_target_pairs={{0,16},{16,32},{32,48},{48,64},{64,80},{80,96},{96,112},{112,0},{1... | collective-permute-start | bytes 221192 | tf_op jit(solution)/shard_map/ppermute | solution.py:190
  85.0 0.0 collective-permute-start
  85.0 1.5 %collective-permute-start.4 = (f32[1,6144]{1,0:T(1,128)S(1)}, f32[1,6144]{1,0:T(1,128)S(1)}, u32[]{:S(2)}, u32[]{:S(2)}) collective-permute-start(f32[1,6144]{1,0:T(1,128)S(1)} %copy-done.6), channel_id=1, source_target_pairs={{0,16},{16,32},{32,48},{48,64},{64,80},{80,96},{96,112},{112,0},{1... | collective-permute-start | bytes 73736 | tf_op jit(solution)/shard_map/ppermute | solution.py:190
  86.5 0.8 slice.10
  87.3 18.5 %collective-permute-done = f32[1,48]{1,0:T(1,128)S(1)} collective-permute-done((f32[1,48]{1,0:T(1,128)S(1)}, f32[1,48]{1,0:T(1,128)S(1)}, u32[]{:S(2)}, u32[]{:S(2)}) %collective-permute-start) | collective-permute-done | bytes 224 | tf_op jit(solution)/shard_map/ppermute | solution.py:190
  105.8 0.0 collective-permute-done.2.g_ref
  105.8 0.0 collective-permute-done.1.x_ref
  105.8 0.6 copy-done.4
  106.4 0.1 copy-done.5
  106.5 19.7 %shard_map.68 = (bf16[1,512,6144]{2,1,0:T(8,128)(2,1)}, f32[1,512,6144]{2,1,0:T(8,128)}, f32[1,48,128,128]{3,2,1,0:T(8,128)}) custom-call(f32[48]{0:T(128)} %bitcast.19, bf16[1,512,6144]{2,1,0:T(8,128)(2,1)} %collective-permute-done.1.x_ref, f32[1,3,6144]{2,1,0:T(4,128)} %copy-done.5), custom_call_target="tpu_custom_call" | custom-call | flops 4831838208 | bytes 25165824 | tf_op jit(solution)/shard_map/pallas_call | solution.py:139
  126.2 0.0 collective-permute-done.4.go_ref
  126.2 0.0 collective-permute-done.3.s_ref
  126.2 0.6 copy-done.2
  126.8 17.9 %shard_map.70 = bf16[1,512,6144]{2,1,0:T(8,128)(2,1)} custom-call(f32[48]{0:T(128)} %bitcast.20, bf16[1,512,6144]{2,1,0:T(8,128)(2,1)} %collective-permute-done.1.x_ref, bf16[1,512,6144]{2,1,0:T(8,128)(2,1)} %get-tuple-element.5.q_ref, f32[1,512,6144]{2,1,0:T(8,128)} %get-tuple-element.6.l_ref, f32[1,48,128,128]{3,2,1,0:T(8,128)} %get-tuple-element.7.r_ref, ...), custom_call_target="tpu_custom_call" | custom-call | flops 805306368 | bytes 31457280 | tf_op jit(solution)/shard_map/pallas_call | solution.py:158
  (10 shorter events, 0.1 us)
Async XLA Ops:
  0.6 23.6 %copy-start = (f32[1,48,128,128]{3,2,1,0:T(8,128)S(1)}, f32[1,48,128,128]{3,2,1,0:T(8,128)}, u32[]{:S(2)}) copy-start(f32[1,48,128,128]{3,2,1,0:T(8,128)} %param.9) | copy-start | bytes 9437188
  0.6 105.2 %collective-permute-start.1 = (bf16[1,512,6144]{2,1,0:T(8,128)(2,1)}, bf16[1,512,6144]{2,1,0:T(8,128)(2,1)}, u32[]{:S(2)}, u32[]{:S(2)}) collective-permute-start(bf16[1,512,6144]{2,1,0:T(8,128)(2,1)} %x_ref.1), channel_id=1, source_target_pairs={{0,16},{16,32},{32,48},{48,64},{64,80},{80,96},{96,112},{112,0},{1... | collective-permute-start | bytes 18874376 | tf_op jit(solution)/shard_map/ppermute | solution.py:189
  15.8 8.4 %copy-start.3 = (f32[1,48]{1,0:T(1,128)S(1)}, f32[1,48]{1,0:T(1,128)}, u32[]{:S(2)}) copy-start(f32[1,48]{1,0:T(1,128)} %param.8) | copy-start | bytes 580
  15.8 36.2 %all-to-all-start = ((bf16[48,128,128]{2,1,0:T(8,128)(2,1)}), bf16[48,128,128]{2,1,0:T(8,128)(2,1)}, u32[]{:S(2)}, u32[]{:S(2)}) async-start(bf16[48,128,128]{2,1,0:T(8,128)(2,1)} %shard_map.69), calls=%async_computation | async-start | bytes 3145728 | tf_op jit(solution)/shard_map/all_to_all | solution.py:195
  56.2 27.2 %copy-start.1 = (f32[1,3,6144]{2,1,0:T(4,128)S(1)}, f32[1,3,6144]{2,1,0:T(4,128)}, u32[]{:S(2)}) copy-start(f32[1,3,6144]{2,1,0:T(4,128)} %copy.7.g_ref) | copy-start | bytes 221188
  56.2 28.8 %copy-start.6 = (f32[1,6144]{1,0:T(1,128)S(1)}, f32[1,6144]{1,0:T(1,128)}, u32[]{:S(2)}) copy-start(f32[1,6144]{1,0:T(1,128)} %param.7) | copy-start | bytes 73732
  83.4 42.8 %collective-permute-start.3 = (bf16[48,128,128]{2,1,0:T(8,128)(2,1)}, bf16[48,128,128]{2,1,0:T(8,128)(2,1)}, u32[]{:S(2)}, u32[]{:S(2)}) collective-permute-start(bf16[48,128,128]{2,1,0:T(8,128)(2,1)} %all_to_all.10), channel_id=1, source_target_pairs={{0,16},{16,32},{32,48},{48,64},{64,80},{80,96},{96,112},{112,0},{1... | collective-permute-start | bytes 4718600 | tf_op jit(solution)/shard_map/ppermute | solution.py:218
  83.4 22.4 %collective-permute-start.2 = (f32[1,3,6144]{2,1,0:T(4,128)S(1)}, f32[1,3,6144]{2,1,0:T(4,128)S(1)}, u32[]{:S(2)}, u32[]{:S(2)}) collective-permute-start(f32[1,3,6144]{2,1,0:T(4,128)S(1)} %copy-done.1), channel_id=1, source_target_pairs={{0,16},{16,32},{32,48},{48,64},{64,80},{80,96},{96,112},{112,0},{1... | collective-permute-start | bytes 221192 | tf_op jit(solution)/shard_map/ppermute | solution.py:190
  85.0 20.8 %collective-permute-start = (f32[1,48]{1,0:T(1,128)S(1)}, f32[1,48]{1,0:T(1,128)S(1)}, u32[]{:S(2)}, u32[]{:S(2)}) collective-permute-start(f32[1,48]{1,0:T(1,128)S(1)} %copy-done.3), channel_id=1, source_target_pairs={{0,16},{16,32},{32,48},{48,64},{64,80},{80,96},{96,112},{112,0},{1... | collective-permute-start | bytes 584 | tf_op jit(solution)/shard_map/ppermute | solution.py:190
  85.0 41.1 %collective-permute-start.4 = (f32[1,6144]{1,0:T(1,128)S(1)}, f32[1,6144]{1,0:T(1,128)S(1)}, u32[]{:S(2)}, u32[]{:S(2)}) collective-permute-start(f32[1,6144]{1,0:T(1,128)S(1)} %copy-done.6), channel_id=1, source_target_pairs={{0,16},{16,32},{32,48},{48,64},{64,80},{80,96},{96,112},{112,0},{1... | collective-permute-start | bytes 73736 | tf_op jit(solution)/shard_map/ppermute | solution.py:190
  105.8 0.6 copy-start.4
  105.8 0.6 copy-start.5
  126.2 0.6 copy-start.2

commit v4 on v2

--- a/solution.py
+++ b/solution.py
@@ -10,6 +10,7 @@
 BLOCK = 256
 EPSILON = 1e-05
 HEADS_PER_STEP = 4
+STATE_CHUNKS = 4
 
 
 def _silu(v):
@@ -49,11 +50,12 @@
             values_b = (x * g_ref[0, 2:3, cols]).astype(jnp.bfloat16)
             update = _block_state(keys_b, values_b, rate, pos)
             acc = update if acc is None else decay * acc + update
-        o_ref[hh] = acc
-
-
-def _output_kernel(rates_ref, x_ref, g_ref, go_ref, s_ref, o_ref, *, hg, head_dim, nblocks):
-    step = pl.program_id(0)
+        o_ref[hh] = acc.astype(o_ref.dtype)
+
+
+def _output_kernel(rates_ref, x_ref, g_ref, go_ref, s_ref, *rest, hg, head_dim, nblocks, first):
+    o_ref = rest[-1]
+    step = pl.program_id(0) + first
     pos = lax.broadcasted_iota(jnp.int32, (BLOCK, 1), 0).astype(jnp.float32)
     row = lax.broadcasted_iota(jnp.int32, (BLOCK, BLOCK), 0)
     col = lax.broadcasted_iota(jnp.int32, (BLOCK, BLOCK), 1)
@@ -100,7 +102,7 @@
             ],
             out_specs=pl.BlockSpec((hg, head_dim, head_dim), lambda i, r: (i, 0, 0)),
         ),
-        out_shape=jax.ShapeDtypeStruct((heads, head_dim, head_dim), jnp.float32),
+        out_shape=jax.ShapeDtypeStruct((heads, head_dim, head_dim), jnp.bfloat16),
         cost_estimate=pl.CostEstimate(
             flops=2 * count * width * head_dim, transcendentals=count * width,
             bytes_accessed=count * width * 2 + heads * head_dim * head_dim * 4,
@@ -108,31 +110,44 @@
     )(rates, rows, gains)
 
 
-def _outputs(rates, rows, gains, gain_out, states, head_dim):
+def _outputs(rates, rows, gains, gain_out, states, head_dim, first, previous):
     _, count, width = rows.shape
-    heads = width // head_dim
     hg = HEADS_PER_STEP
     cw = hg * head_dim
-    kernel = functools.partial(_output_kernel, hg=hg, head_dim=head_dim, nblocks=count // BLOCK)
+    steps = states.shape[0] // hg
+    base = first // hg
+    kernel = functools.partial(
+        _output_kernel, hg=hg, head_dim=head_dim, nblocks=count // BLOCK, first=base
+    )
+    row_spec = pl.BlockSpec((1, count, cw), lambda i, r: (0, 0, i + base))
+    in_specs = [
+        row_spec,
+        pl.BlockSpec((1, 3, cw), lambda i, r: (0, 0, i + base)),
+        pl.BlockSpec((1, cw), lambda i, r: (0, i + base)),
+        pl.BlockSpec((hg, head_dim, head_dim), lambda i, r: (i, 0, 0)),
+    ]
+    operands = [rates, rows, gains, gain_out, states]
+    aliases = {}
+    if previous is not None:
+        in_specs.append(pl.BlockSpec(memory_space=pl.ANY))
+        operands.append(previous)
+        aliases = {len(operands) - 1: 0}
+    share = steps * cw
     return pl.pallas_call(
         kernel,
         grid_spec=pltpu.PrefetchScalarGridSpec(
             num_scalar_prefetch=1,
-            grid=(heads // hg,),
-            in_specs=[
-                pl.BlockSpec((1, count, cw), lambda i, r: (0, 0, i)),
-                pl.BlockSpec((1, 3, cw), lambda i, r: (0, 0, i)),
-                pl.BlockSpec((1, cw), lambda i, r: (0, i)),
-                pl.BlockSpec((hg, head_dim, head_dim), lambda i, r: (i, 0, 0)),
-            ],
-            out_specs=pl.BlockSpec((1, count, cw), lambda i, r: (0, 0, i)),
+            grid=(steps,),
+            in_specs=in_specs,
+            out_specs=row_spec,
         ),
         out_shape=jax.ShapeDtypeStruct(rows.shape, rows.dtype),
+        input_output_aliases=aliases,
         cost_estimate=pl.CostEstimate(
-            flops=8 * count * BLOCK * width, transcendentals=3 * count * width,
-            bytes_accessed=2 * count * width * 2 + heads * head_dim * head_dim * 4,
-        ),
-    )(rates, rows, gains, gain_out, states)
+            flops=8 * count * BLOCK * share, transcendentals=3 * count * share,
+            bytes_accessed=2 * count * share * 2 + steps * hg * head_dim * head_dim * 2,
+        ),
+    )(*operands)
 
 
 def on_device(section_inputs, input_gains, out_gain, decay_rates, carry_state):
@@ -146,13 +161,12 @@
     count_s = lax.axis_size("section")
     pairs = [(src, (src + 1) % count_s) for src in range(count_s)]
 
-    prev_rows = lax.ppermute(section_inputs, "section", pairs)
-    prev_gains, prev_gain_out, prev_rates = lax.ppermute(
-        (input_gains, out_gain, decay_rates), "section", pairs
+    prev_rows, prev_gains, prev_gain_out, prev_rates = lax.ppermute(
+        (section_inputs, input_gains, out_gain, decay_rates), "section", pairs
     )
 
     summary = _summaries(rates, section_inputs, input_gains, head_dim)
-    gathered = lax.all_to_all(summary.astype(jnp.bfloat16), "ctx", 0, 0, tiled=True)
+    gathered = lax.all_to_all(summary, "ctx", 0, 0, tiled=True)
     gathered = gathered.astype(jnp.float32).reshape(group_size, own_heads, head_dim, head_dim)
 
     start = place * own_heads
@@ -175,11 +189,17 @@
         prefixes[:group_size].astype(jnp.bfloat16).reshape(heads, head_dim, head_dim),
         "ctx", 0, 0, tiled=True,
     )
-    prev_incoming = lax.ppermute(incoming, "section", pairs)
-
-    next_rows = _outputs(
-        prev_rates[0], prev_rows, prev_gains, prev_gain_out, prev_incoming, head_dim
-    )
+    prev_gains, prev_gain_out, prev_rates, incoming = lax.optimization_barrier(
+        (prev_gains, prev_gain_out, prev_rates, incoming)
+    )
+    chunk = heads // STATE_CHUNKS
+    next_rows = None
+    for part in range(STATE_CHUNKS):
+        piece = lax.ppermute(incoming[part * chunk : (part + 1) * chunk], "section", pairs)
+        next_rows = _outputs(
+            prev_rates[0], prev_rows, prev_gains, prev_gain_out, piece, head_dim,
+            part * chunk, next_rows,
+        )
     return (next_rows, end_part[None])
 
 

time: 134 us -> 134 us (level)
  blocking collectives: 26 us -> 0 us
  waiting for transfers between devices: 46.1 us -> 54.9 us
  Pallas kernels: 37.6 us -> 45.1 us
  local copies, waits for them, and re-layouts: 4.32 us -> 10.5 us
  starting transfers between devices: 11.4 us -> 17.5 us
  other arithmetic: 3.59 us -> 0.17 us
    all_to_all x1 -> x0, blocking collectives: 26 us -> none  [on_device(): lax.all_to_all(prefixes[:group_size].astype(jnp.bfloat16).reshape(heads,...]
    all_to_all x1 -> x2, waiting for transfers between devices: 27.6 us -> 44.1 us  [the longest x1 27.6 us: on_device(): gathered = lax.all_to_all(summary, 'ctx', 0, 0, tiled=True)]
    ppermute x5 -> x8, waiting for transfers between devices: 18.5 us -> 10.8 us  [the longest x4 7.46 us: on_device(): lax.ppermute((section_inputs, input_gains, out_gain, decay_rates), 'secti...]
    pallas_call x1 -> x4, Pallas kernels: 24 us -> 31.6 us  [_outputs(): pl.pallas_call(kernel, grid_spec=pltpu.PrefetchScalarGridSpec(num_scalar_...]
    all_to_all x1 -> x2, starting transfers between devices: 8.21 us -> 12.8 us  [the longest x1 8.21 us: on_device(): gathered = lax.all_to_all(summary, 'ctx', 0, 0, tiled=True)]
    convert_element_type x1 -> x0, other arithmetic: 3.42 us -> none  [on_device(): summary.astype(jnp.bfloat16)]
    slice x0 -> x1, local copies, waits for them, and re-layouts: none -> 2.45 us  [on_device(): incoming[part * chunk:(part + 1) * chunk]]
    ppermute x5 -> x8, starting transfers between devices: 3.21 us -> 4.7 us  [the longest x4 2.95 us: on_device(): lax.ppermute(incoming[part * chunk:(part + 1) * chunk], 'section', pairs)]
  transfers between devices with their start and end apart: 6 -> 10, of which waited for: 2 -> 4; matrix products, arithmetic and copies ran while one was open for 8% -> 9% of each run, Pallas kernels for 10% -> 28%
where the time goes in v4:
time: 134 us; the launch traced here: 133 us
  waiting for transfers between devices  54.9 us (41%)
  Pallas kernels  45.1 us (34%)
  starting transfers between devices  17.5 us (13%)
  local copies, waits for them, and re-layouts  10.5 us (8%)
  matrix products  4.03 us (3%)
    pallas_call x4, Pallas kernels, _outputs(): pl.pallas_call(kernel, grid_spec=pltpu.PrefetchScalarGridSpec(num_scalar_...  31.6 us
    all_to_all x1, waiting for transfers between devices, on_device(): gathered = lax.all_to_all(summary, 'ctx', 0, 0, tiled=True)  27.6 us
    all_to_all x1, waiting for transfers between devices, on_device(): lax.all_to_all(prefixes[:group_size].astype(jnp.bfloat16).reshape(heads,...  16.4 us
    pallas_call x1, Pallas kernels, _summaries(): pl.pallas_call(kernel, grid_spec=pltpu.PrefetchScalarGridSpec(num_scalar_...  13.5 us
    all_to_all x1, starting transfers between devices, on_device(): gathered = lax.all_to_all(summary, 'ctx', 0, 0, tiled=True)  8.21 us
    ppermute x4, waiting for transfers between devices, on_device(): lax.ppermute((section_inputs, input_gains, out_gain, decay_rates), 'secti...  7.46 us
    all_to_all x1, starting transfers between devices, on_device(): lax.all_to_all(prefixes[:group_size].astype(jnp.bfloat16).reshape(heads,...  4.59 us
    dot_general x1, matrix products, on_device(): jnp.einsum('tsh,shde->thde', weights, gathered, precision=lax.Precision.H...  4.03 us
  transfers between devices with their start and end apart: 10, of which 4 were waited for; matrix products, arithmetic and copies ran while one was open for 9% of the time, Pallas kernels for 28%

profile of v4, /device:TPU:0, one launch (start us, length us, event | category | flops | bytes accessed | tf_op | source)
XLA Modules:
  0.0 133.0 jit_solution(15566671144764987942)
XLA Ops:
  0.6 0.0 copy-start
  0.6 0.0 collective-permute-start.3
  0.7 1.7 %copy.10.g_ref = f32[1,3,6144]{2,1,0:T(4,128)} copy(f32[1,3,6144]{2,0,1:T(1,128)} %param.6) | data formatting | bytes 147456 | tf_op args[1]
  2.4 13.5 %shard_map.68 = bf16[48,128,128]{2,1,0:T(8,128)(2,1)} custom-call(f32[48]{0:T(128)} %bitcast.22, bf16[1,512,6144]{2,1,0:T(8,128)(2,1)} %x_ref.1, f32[1,3,6144]{2,1,0:T(4,128)} %copy.10.g_ref), custom_call_target="tpu_custom_call" | custom-call | flops 805306368 | bytes 9437184 | tf_op jit(solution)/shard_map/pallas_call | solution.py:94
  15.9 8.2 %all-to-all-start = ((bf16[48,128,128]{2,1,0:T(8,128)(2,1)}), bf16[48,128,128]{2,1,0:T(8,128)(2,1)}, u32[]{:S(2)}, u32[]{:S(2)}) async-start(bf16[48,128,128]{2,1,0:T(8,128)(2,1)} %shard_map.68), calls=%async_computation | async-start | bytes 3145728 | tf_op jit(solution)/shard_map/all_to_all | solution.py:169
  24.1 0.1 multiply_bitcast_fusion
  24.3 0.1 multiply_exponential_fusion
  24.4 27.6 %all-to-all-done = bf16[48,128,128]{2,1,0:T(8,128)(2,1)} async-done(((bf16[48,128,128]{2,1,0:T(8,128)(2,1)}), bf16[48,128,128]{2,1,0:T(8,128)(2,1)}, u32[]{:S(2)}, u32[]{:S(2)}) %all-to-all-start) | async-done | bytes 1572896 | tf_op jit(solution)/shard_map/all_to_all | solution.py:169
  52.0 4.0 %bitcast_add_fusion = f32[17,3,128,128]{3,0,2,1:T(8,128)S(1)} fusion(f32[3,128,128]{2,1,0:T(8,128)S(1)} %dynamic-slice_bitcast_fusion, f32[17,3]{0,1:T(4,128)S(1)} %multiply_exponential_fusion, bf16[16,3,128,128]{3,2,1,0:T(8,128)(2,1)} %bitcast.1, f32[17,16]{0,1:T(8,128)S(1)} %convert_maximum_fusion, f32[3]{0:T(128)S(1)} %multiply_bitcast_fusion, ...), kind=kOutput, calls=%fused_computation | convolution fusion | flops 162104928 | bytes 5113384 | tf_op jit(solution)/shard_map/tsh,shde->thde/dot_general | solution.py:184
  56.0 0.0 copy-start.1
  56.0 2.2 %copy-done.1 = f32[17,3,128,128]{3,0,2,1:T(8,128)} copy-done((f32[17,3,128,128]{3,0,2,1:T(8,128)}, f32[17,3,128,128]{3,0,2,1:T(8,128)S(1)}, u32[]{:S(2)}) %copy-start.1) | copy-done | bytes 3342360
  58.2 0.2 slice.28
  58.4 1.7 %copy.13 = bf16[16,3,128,128]{3,2,1,0:T(8,128)(2,1)} copy(bf16[16,3,128,128]{3,0,2,1:T(8,128)(2,1)S(1)} %slice.28) | data formatting | bytes 3145728 | tf_op jit(solution)/shard_map/slice | solution.py:189
  60.1 4.6 %all-to-all-start.1 = ((bf16[48,128,128]{2,1,0:T(8,128)(2,1)}), bf16[48,128,128]{2,1,0:T(8,128)(2,1)}, u32[]{:S(2)}, u32[]{:S(2)}) async-start(bf16[48,128,128]{2,1,0:T(8,128)(2,1)} %bitcast.16), calls=%async_computation.1 | async-start | bytes 3145728 | tf_op jit(solution)/shard_map/all_to_all | solution.py:188
  64.7 0.1 collective-permute-start
  64.8 1.5 %collective-permute-start.1 = (f32[1,6144]{1,0:T(1,128)S(1)}, f32[1,6144]{1,0:T(1,128)S(1)}, u32[]{:S(2)}, u32[]{:S(2)}) collective-permute-start(f32[1,6144]{1,0:T(1,128)S(1)} %copy-done.7), channel_id=1, source_target_pairs={{0,16},{16,32},{32,48},{48,64},{64,80},{80,96},{96,112},{112,0},{1... | collective-permute-start | bytes 73736 | tf_op jit(solution)/shard_map/ppermute | solution.py:164
  66.3 0.1 collective-permute-start.2
  66.4 7.4 %collective-permute-done.2 = f32[1,48]{1,0:T(1,128)S(1)} collective-permute-done((f32[1,48]{1,0:T(1,128)S(1)}, f32[1,48]{1,0:T(1,128)S(1)}, u32[]{:S(2)}, u32[]{:S(2)}) %collective-permute-start.2) | collective-permute-done | bytes 224 | tf_op jit(solution)/shard_map/ppermute | solution.py:164
  73.9 0.0 collective-permute-done.1.go_ref
  73.9 16.4 %all-to-all-done.1 = bf16[48,128,128]{2,1,0:T(8,128)(2,1)} async-done(((bf16[48,128,128]{2,1,0:T(8,128)(2,1)}), bf16[48,128,128]{2,1,0:T(8,128)(2,1)}, u32[]{:S(2)}, u32[]{:S(2)}) %all-to-all-start.1) | async-done | bytes 1572896 | tf_op jit(solution)/shard_map/all_to_all | solution.py:188
  90.3 2.5 %fusion.10 = (bf16[12,128,128]{2,1,0:T(8,128)(2,1)S(1)}, bf16[12,128,128]{2,1,0:T(8,128)(2,1)}, bf16[12,128,128]{2,1,0:T(8,128)(2,1)}, bf16[12,128,128]{2,1,0:T(8,128)(2,1)}) fusion(bf16[48,128,128]{2,1,0:T(8,128)(2,1)} %all-to-all-done.1), kind=kLoop, calls=%fused_computation.19 | loop fusion | bytes 3145728 | tf_op jit(solution)/shard_map/slice | solution.py:198
  92.8 1.6 %collective-permute-start.6 = (bf16[12,128,128]{2,1,0:T(8,128)(2,1)}, bf16[12,128,128]{2,1,0:T(8,128)(2,1)}, u32[]{:S(2)}, u32[]{:S(2)}) collective-permute-start(bf16[12,128,128]{2,1,0:T(8,128)(2,1)} %get-tuple-element.13), channel_id=1, source_target_pairs={{0,16},{16,32},{32,48},{48,64},{64,80},{80,96},{96,112},{112,0},{1... | collective-permute-start | bytes 1179656 | tf_op jit(solution)/shard_map/ppermute | solution.py:198
  94.4 0.0 collective-permute-start.5
  94.4 2.2 %slice.26 = f32[1,3,128,128]{3,0,2,1:T(1,128)} slice(f32[17,3,128,128]{3,0,2,1:T(8,128)} %copy-done.1), slice={[16:17], [0:3], [0:128], [0:128]} | slice | bytes 393216 | tf_op jit(solution)/shard_map/slice | solution.py:187
  96.6 1.3 collective-permute-start.4
  97.9 3.4 %collective-permute-done.7.s_ref = bf16[12,128,128]{2,1,0:T(8,128)(2,1)} collective-permute-done((bf16[12,128,128]{2,1,0:T(8,128)(2,1)S(1)}, bf16[12,128,128]{2,1,0:T(8,128)(2,1)}, u32[]{:S(2)}, u32[]{:S(2)}) %collective-permute-start.7) | collective-permute-done | bytes 393248 | tf_op jit(solution)/shard_map/ppermute | solution.py:198
  101.3 7.9 %shard_map.69.rest_0_ = bf16[1,512,6144]{2,1,0:T(8,128)(2,1)} custom-call(f32[48]{0:T(128)} %bitcast.18, bf16[1,512,6144]{2,1,0:T(8,128)(2,1)} %collective-permute-done.3.x_ref, f32[1,3,6144]{2,1,0:T(4,128)} %copy-done.2, f32[1,6144]{1,0:T(1,128)} %copy-done.4, bf16[12,128,128]{2,1,0:T(8,128)(2,1)} %collective-permute-done.7.s_ref), custom_call_target="tpu_custom_call" | custom-call | flops 1610612736 | bytes 3538944 | tf_op jit(solution)/shard_map/pallas_call | solution.py:136
  109.2 0.0 collective-permute-done.6.s_ref
  109.2 7.9 %shard_map.70.rest_0_ = bf16[1,512,6144]{2,1,0:T(8,128)(2,1)} custom-call(f32[48]{0:T(128)} %bitcast.19, bf16[1,512,6144]{2,1,0:T(8,128)(2,1)} %collective-permute-done.3.x_ref, f32[1,3,6144]{2,1,0:T(4,128)} %copy-done.2, f32[1,6144]{1,0:T(1,128)} %copy-done.4, bf16[12,128,128]{2,1,0:T(8,128)(2,1)} %collective-permute-done.6.s_ref, ...), custom_call_target="tpu_custom_call", output_to_operand_aliasing={{}: (5, {})} | custom-call | flops 1610612736 | bytes 3538944 | tf_op jit(solution)/shard_map/pallas_call | solution.py:136
  117.1 7.9 %shard_map.71.rest_0_ = bf16[1,512,6144]{2,1,0:T(8,128)(2,1)} custom-call(f32[48]{0:T(128)} %bitcast.20, bf16[1,512,6144]{2,1,0:T(8,128)(2,1)} %collective-permute-done.3.x_ref, f32[1,3,6144]{2,1,0:T(4,128)} %copy-done.2, f32[1,6144]{1,0:T(1,128)} %copy-done.4, bf16[12,128,128]{2,1,0:T(8,128)(2,1)} %collective-permute-done.5.s_ref, ...), custom_call_target="tpu_custom_call", output_to_operand_aliasing={{}: (5, {})} | custom-call | flops 1610612736 | bytes 3538944 | tf_op jit(solution)/shard_map/pallas_call | solution.py:136
  125.0 0.0 collective-permute-done.4.s_ref
  125.1 7.9 %shard_map.72 = bf16[1,512,6144]{2,1,0:T(8,128)(2,1)} custom-call(f32[48]{0:T(128)} %bitcast.21, bf16[1,512,6144]{2,1,0:T(8,128)(2,1)} %collective-permute-done.3.x_ref, f32[1,3,6144]{2,1,0:T(4,128)} %copy-done.2, f32[1,6144]{1,0:T(1,128)} %copy-done.4, bf16[12,128,128]{2,1,0:T(8,128)(2,1)} %collective-permute-done.4.s_ref, ...), custom_call_target="tpu_custom_call", output_to_operand_aliasing={{}: (5, {})} | custom-call | flops 1610612736 | bytes 3538944 | tf_op jit(solution)/shard_map/pallas_call | solution.py:136
  (22 shorter events, 0.1 us)
Async XLA Ops:
  0.6 23.6 %copy-start = (f32[1,48,128,128]{3,2,1,0:T(8,128)S(1)}, f32[1,48,128,128]{3,2,1,0:T(8,128)}, u32[]{:S(2)}) copy-start(f32[1,48,128,128]{3,2,1,0:T(8,128)} %param.9) | copy-start | bytes 9437188
  0.6 100.7 %collective-permute-start.3 = (bf16[1,512,6144]{2,1,0:T(8,128)(2,1)}, bf16[1,512,6144]{2,1,0:T(8,128)(2,1)}, u32[]{:S(2)}, u32[]{:S(2)}) collective-permute-start(bf16[1,512,6144]{2,1,0:T(8,128)(2,1)} %x_ref.1), channel_id=1, source_target_pairs={{0,16},{16,32},{32,48},{48,64},{64,80},{80,96},{96,112},{112,0},{1... | collective-permute-start | bytes 18874376 | tf_op jit(solution)/shard_map/ppermute | solution.py:164
  2.4 21.8 %copy-start.6 = (f32[1,48]{1,0:T(1,128)S(1)}, f32[1,48]{1,0:T(1,128)}, u32[]{:S(2)}) copy-start(f32[1,48]{1,0:T(1,128)} %param.8) | copy-start | bytes 580
  15.9 36.1 %all-to-all-start = ((bf16[48,128,128]{2,1,0:T(8,128)(2,1)}), bf16[48,128,128]{2,1,0:T(8,128)(2,1)}, u32[]{:S(2)}, u32[]{:S(2)}) async-start(bf16[48,128,128]{2,1,0:T(8,128)(2,1)} %shard_map.68), calls=%async_computation | async-start | bytes 3145728 | tf_op jit(solution)/shard_map/all_to_all | solution.py:169
  56.0 2.2 %copy-start.1 = (f32[17,3,128,128]{3,0,2,1:T(8,128)}, f32[17,3,128,128]{3,0,2,1:T(8,128)S(1)}, u32[]{:S(2)}) copy-start(f32[17,3,128,128]{3,0,2,1:T(8,128)S(1)} %bitcast_add_fusion) | copy-start | bytes 10027012
  58.2 6.5 %copy-start.3 = (f32[1,3,6144]{2,1,0:T(4,128)S(1)}, f32[1,3,6144]{2,1,0:T(4,128)}, u32[]{:S(2)}) copy-start(f32[1,3,6144]{2,1,0:T(4,128)} %copy.10.g_ref) | copy-start | bytes 221188
  58.2 6.6 %copy-start.7 = (f32[1,6144]{1,0:T(1,128)S(1)}, f32[1,6144]{1,0:T(1,128)}, u32[]{:S(2)}) copy-start(f32[1,6144]{1,0:T(1,128)} %param.7) | copy-start | bytes 73732
  60.1 30.2 %all-to-all-start.1 = ((bf16[48,128,128]{2,1,0:T(8,128)(2,1)}), bf16[48,128,128]{2,1,0:T(8,128)(2,1)}, u32[]{:S(2)}, u32[]{:S(2)}) async-start(bf16[48,128,128]{2,1,0:T(8,128)(2,1)} %bitcast.16), calls=%async_computation.1 | async-start | bytes 3145728 | tf_op jit(solution)/shard_map/all_to_all | solution.py:188
  64.7 9.2 %collective-permute-start = (f32[1,3,6144]{2,1,0:T(4,128)S(1)}, f32[1,3,6144]{2,1,0:T(4,128)S(1)}, u32[]{:S(2)}, u32[]{:S(2)}) collective-permute-start(f32[1,3,6144]{2,1,0:T(4,128)S(1)} %copy-done.3), channel_id=1, source_target_pairs={{0,16},{16,32},{32,48},{48,64},{64,80},{80,96},{96,112},{112,0},{1... | collective-permute-start | bytes 221192 | tf_op jit(solution)/shard_map/ppermute | solution.py:164
  64.8 9.1 %collective-permute-start.1 = (f32[1,6144]{1,0:T(1,128)S(1)}, f32[1,6144]{1,0:T(1,128)S(1)}, u32[]{:S(2)}, u32[]{:S(2)}) collective-permute-start(f32[1,6144]{1,0:T(1,128)S(1)} %copy-done.7), channel_id=1, source_target_pairs={{0,16},{16,32},{32,48},{48,64},{64,80},{80,96},{96,112},{112,0},{1... | collective-permute-start | bytes 73736 | tf_op jit(solution)/shard_map/ppermute | solution.py:164
  66.3 7.6 %collective-permute-start.2 = (f32[1,48]{1,0:T(1,128)S(1)}, f32[1,48]{1,0:T(1,128)S(1)}, u32[]{:S(2)}, u32[]{:S(2)}) collective-permute-start(f32[1,48]{1,0:T(1,128)S(1)} %copy-done.6), channel_id=1, source_target_pairs={{0,16},{16,32},{32,48},{48,64},{64,80},{80,96},{96,112},{112,0},{1... | collective-permute-start | bytes 584 | tf_op jit(solution)/shard_map/ppermute | solution.py:164
  73.9 27.4 %copy-start.5 = (f32[1,48]{1,0:T(1,128)}, f32[1,48]{1,0:T(1,128)S(1)}, u32[]{:S(2)}) copy-start(f32[1,48]{1,0:T(1,128)S(1)} %collective-permute-done.2) | copy-start | bytes 580
  73.9 27.4 %copy-start.4 = (f32[1,6144]{1,0:T(1,128)}, f32[1,6144]{1,0:T(1,128)S(1)}, u32[]{:S(2)}) copy-start(f32[1,6144]{1,0:T(1,128)S(1)} %collective-permute-done.1.go_ref) | copy-start | bytes 73732
  73.9 27.4 %copy-start.2 = (f32[1,3,6144]{2,1,0:T(4,128)}, f32[1,3,6144]{2,1,0:T(4,128)S(1)}, u32[]{:S(2)}) copy-start(f32[1,3,6144]{2,1,0:T(4,128)S(1)} %collective-permute-done.g_ref) | copy-start | bytes 221188
  92.8 8.5 %collective-permute-start.7 = (bf16[12,128,128]{2,1,0:T(8,128)(2,1)S(1)}, bf16[12,128,128]{2,1,0:T(8,128)(2,1)}, u32[]{:S(2)}, u32[]{:S(2)}) collective-permute-start(bf16[12,128,128]{2,1,0:T(8,128)(2,1)S(1)} %get-tuple-element.12), channel_id=1, source_target_pairs={{0,16},{16,32},{32,48},{48,64},{64,80},{80,96},{96,112},{112,0},{1... | collective-permute-start | bytes 1179656 | tf_op jit(solution)/shard_map/ppermute | solution.py:198
  92.8 16.4 %collective-permute-start.6 = (bf16[12,128,128]{2,1,0:T(8,128)(2,1)}, bf16[12,128,128]{2,1,0:T(8,128)(2,1)}, u32[]{:S(2)}, u32[]{:S(2)}) collective-permute-start(bf16[12,128,128]{2,1,0:T(8,128)(2,1)} %get-tuple-element.13), channel_id=1, source_target_pairs={{0,16},{16,32},{32,48},{48,64},{64,80},{80,96},{96,112},{112,0},{1... | collective-permute-start | bytes 1179656 | tf_op jit(solution)/shard_map/ppermute | solution.py:198
  94.4 22.7 %collective-permute-start.5 = (bf16[12,128,128]{2,1,0:T(8,128)(2,1)}, bf16[12,128,128]{2,1,0:T(8,128)(2,1)}, u32[]{:S(2)}, u32[]{:S(2)}) collective-permute-start(bf16[12,128,128]{2,1,0:T(8,128)(2,1)} %get-tuple-element.14), channel_id=1, source_target_pairs={{0,16},{16,32},{32,48},{48,64},{64,80},{80,96},{96,112},{112,0},{1... | collective-permute-start | bytes 1179656 | tf_op jit(solution)/shard_map/ppermute | solution.py:198
  96.6 28.4 %collective-permute-start.4 = (bf16[12,128,128]{2,1,0:T(8,128)(2,1)}, bf16[12,128,128]{2,1,0:T(8,128)(2,1)}, u32[]{:S(2)}, u32[]{:S(2)}) collective-permute-start(bf16[12,128,128]{2,1,0:T(8,128)(2,1)} %get-tuple-element.15), channel_id=1, source_target_pairs={{0,16},{16,32},{32,48},{48,64},{64,80},{80,96},{96,112},{112,0},{1... | collective-permute-start | bytes 1179656 | tf_op jit(solution)/shard_map/ppermute | solution.py:198

commit v5 on v4

--- a/solution.py
+++ b/solution.py
@@ -14,7 +14,7 @@
 
 
 def _silu(v):
-    return v / (1.0 + jnp.exp(-v))
+    return 0.5 * v * (1.0 + jnp.tanh(0.5 * v))
 
 
 def _dot_nt(a, b):
@@ -57,15 +57,15 @@
     o_ref = rest[-1]
     step = pl.program_id(0) + first
     pos = lax.broadcasted_iota(jnp.int32, (BLOCK, 1), 0).astype(jnp.float32)
+    pos_row = lax.broadcasted_iota(jnp.int32, (1, BLOCK), 1).astype(jnp.float32)
     row = lax.broadcasted_iota(jnp.int32, (BLOCK, BLOCK), 0)
     col = lax.broadcasted_iota(jnp.int32, (BLOCK, BLOCK), 1)
-    offset = (row - col).astype(jnp.float32)
     causal = row >= col
     for hh in range(hg):
         rate = jnp.full((1, 1), rates_ref[step * hg + hh], jnp.float32)
         cols = slice(hh * head_dim, (hh + 1) * head_dim)
-        mask = jnp.where(causal, jnp.exp(-rate * jnp.maximum(offset, 0.0)), 0.0)
         lead = jnp.exp(-rate * (pos + 1.0))
+        mask = jnp.where(causal, lead * jnp.exp(rate * (pos_row + 1.0)), 0.0)
         decay = jnp.exp(-rate * BLOCK)
         state = s_ref[hh].astype(jnp.float32)
         for b in range(nblocks):
@@ -172,7 +172,7 @@
     start = place * own_heads
     carry_part = lax.dynamic_slice_in_dim(carry_state[0], start, own_heads, 0)
     rate_part = lax.dynamic_slice_in_dim(rates, start, own_heads, 0)
-    target = jnp.arange(group_size + 1)[:, None]
+    target = jnp.arange(group_size)[:, None]
     source = jnp.arange(group_size)[None, :]
     gap = (target - 1 - source).astype(jnp.float32)
     weights = jnp.where(
@@ -184,9 +184,14 @@
     prefixes = jnp.einsum(
         "tsh,shde->thde", weights, gathered, precision=lax.Precision.HIGHEST
     ) + carry_weights[:, :, None, None] * carry_part[None]
-    end_part = prefixes[group_size]
+    end_weights = jnp.exp(
+        -rate_part[None, :] * count * (group_size - 1 - source[0]).astype(jnp.float32)[:, None]
+    )
+    end_part = jnp.einsum(
+        "sh,shde->hde", end_weights, gathered, precision=lax.Precision.HIGHEST
+    ) + jnp.exp(-rate_part * count * group_size)[:, None, None] * carry_part
     incoming = lax.all_to_all(
-        prefixes[:group_size].astype(jnp.bfloat16).reshape(heads, head_dim, head_dim),
+        prefixes.astype(jnp.bfloat16).reshape(heads, head_dim, head_dim),
         "ctx", 0, 0, tiled=True,
     )
     prev_gains, prev_gain_out, prev_rates, incoming = lax.optimization_barrier(

time: 134 us -> 131 us (0.978)
  local copies, waits for them, and re-layouts: 10.5 us -> 6.32 us
  other arithmetic: 0.17 us -> 1.94 us
  Pallas kernels: 45.1 us -> 43.6 us
  waiting for transfers between devices: 54.9 us -> 56.4 us
    slice x3 -> x0, local copies, waits for them, and re-layouts: 4.05 us -> none  [the longest x1 2.19 us: on_device(): end_part = prefixes[group_size]]
    ppermute x4, waiting for transfers between devices: 7.46 us -> 10.2 us  [on_device(): lax.ppermute((section_inputs, input_gains, out_gain, decay_rates), 'secti...]
    all_to_all x1, waiting for transfers between devices: 16.4 us -> 13.8 us  [on_device(): lax.all_to_all(prefixes.astype(jnp.bfloat16).reshape(heads, head_dim, hea...]
    slice x1, local copies, waits for them, and re-layouts: 2.45 us -> 0.15 us  [on_device(): incoming[part * chunk:(part + 1) * chunk]]
    dot_general x1, matrix products: 4.03 us -> 2.09 us  [on_device(): jnp.einsum('tsh,shde->thde', weights, gathered, precision=lax.Precision.H...]
    broadcast_in_dim x0 -> x1, other arithmetic: none -> 1.7 us  [on_device(): return (next_rows, end_part[None])]
    ppermute x4, waiting for transfers between devices: 3.39 us -> 5.07 us  [on_device(): lax.ppermute(incoming[part * chunk:(part + 1) * chunk], 'section', pairs)]
    convert_element_type x0 -> x1, local copies, waits for them, and re-layouts: none -> 1.55 us  [on_device(): prefixes.astype(jnp.bfloat16).reshape(heads, head_dim, head_dim)]
  transfers between devices with their start and end apart: 10 -> 10, of which waited for: 4 -> 4; matrix products, arithmetic and copies ran while one was open for 9% -> 7% of each run, Pallas kernels for 28% -> 28%
where the time goes in v5:
time: 131 us; the launch traced here: 130 us
  waiting for transfers between devices  56.4 us (43%)
  Pallas kernels  43.6 us (33%)
  starting transfers between devices  17.5 us (13%)
  local copies, waits for them, and re-layouts  6.32 us (5%)
  matrix products  3.49 us (3%)
  other arithmetic  1.94 us (1%)
    pallas_call x4, Pallas kernels, _outputs(): pl.pallas_call(kernel, grid_spec=pltpu.PrefetchScalarGridSpec(num_scalar_...  30.6 us
    all_to_all x1, waiting for transfers between devices, on_device(): gathered = lax.all_to_all(summary, 'ctx', 0, 0, tiled=True)  27.4 us
    all_to_all x1, waiting for transfers between devices, on_device(): lax.all_to_all(prefixes.astype(jnp.bfloat16).reshape(heads, head_dim, hea...  13.8 us
    pallas_call x1, Pallas kernels, _summaries(): pl.pallas_call(kernel, grid_spec=pltpu.PrefetchScalarGridSpec(num_scalar_...  13 us
    ppermute x4, waiting for transfers between devices, on_device(): lax.ppermute((section_inputs, input_gains, out_gain, decay_rates), 'secti...  10.2 us
    all_to_all x1, starting transfers between devices, on_device(): gathered = lax.all_to_all(summary, 'ctx', 0, 0, tiled=True)  8.29 us
    ppermute x4, waiting for transfers between devices, on_device(): lax.ppermute(incoming[part * chunk:(part + 1) * chunk], 'section', pairs)  5.07 us
    unnamed x21, local copies, waits for them, and re-layouts  4.62 us
  transfers between devices with their start and end apart: 10, of which 4 were waited for; matrix products, arithmetic and copies ran while one was open for 7% of the time, Pallas kernels for 28%

profile of v5, /device:TPU:0, one launch (start us, length us, event | category | flops | bytes accessed | tf_op | source)
XLA Modules:
  0.0 130.0 jit_solution(10750739879321952718)
XLA Ops:
  0.6 0.0 collective-permute-start.3
  0.7 1.6 %copy.10.g_ref = f32[1,3,6144]{2,1,0:T(4,128)} copy(f32[1,3,6144]{2,0,1:T(1,128)} %param.6) | data formatting | bytes 147456 | tf_op args[1]
  2.2 13.0 %shard_map.68 = bf16[48,128,128]{2,1,0:T(8,128)(2,1)} custom-call(f32[48]{0:T(128)} %bitcast.33, bf16[1,512,6144]{2,1,0:T(8,128)(2,1)} %x_ref.1, f32[1,3,6144]{2,1,0:T(4,128)} %copy.10.g_ref), custom_call_target="tpu_custom_call" | custom-call | flops 805306368 | bytes 9437184 | tf_op jit(solution)/shard_map/pallas_call | solution.py:94
  15.2 8.3 %all-to-all-start = ((bf16[48,128,128]{2,1,0:T(8,128)(2,1)}), bf16[48,128,128]{2,1,0:T(8,128)(2,1)S(1)}, u32[]{:S(2)}, u32[]{:S(2)}) async-start(bf16[48,128,128]{2,1,0:T(8,128)(2,1)} %shard_map.68), calls=%async_computation | async-start | bytes 3145728 | tf_op jit(solution)/shard_map/all_to_all | solution.py:169
  23.5 0.1 exponential_bitcast_fusion.1
  23.6 0.1 multiply_exponential_fusion
  23.7 0.1 convert_maximum_fusion
  23.8 27.4 %all-to-all-done = bf16[48,128,128]{2,1,0:T(8,128)(2,1)S(1)} async-done(((bf16[48,128,128]{2,1,0:T(8,128)(2,1)}), bf16[48,128,128]{2,1,0:T(8,128)(2,1)S(1)}, u32[]{:S(2)}, u32[]{:S(2)}) %all-to-all-start) | async-done | bytes 1572896 | tf_op jit(solution)/shard_map/all_to_all | solution.py:169
  51.2 1.4 %fusion.1 = f32[3,1,128,128]{3,1,2,0:T(1,128)S(1)} fusion(bf16[16,3,128,128]{3,2,1,0:T(8,128)(2,1)S(1)} %bitcast.26, f32[16,3,1,1]{0,1,2,3:T(4,128)S(1)} %get-tuple-element.17), kind=kOutput, calls=%fused_computation.2 | convolution fusion | flops 9437184 | bytes 1769664 | tf_op jit(solution)/shard_map/sh,shde->hde/dot_general | solution.py:190
  52.6 1.7 %add_bitcast_fusion = (f32[1,3,128,128]{3,2,1,0:T(8,128)}, f32[3,128,128]{2,1,0:T(8,128)S(1)}) fusion(f32[3,128,128]{2,1,0:T(8,128)S(1)} %bitcast.28, f32[3]{0:T(128)S(1)} %get-tuple-element.18, f32[1,48,128,128]{3,2,1,0:T(8,128)} %param.9, s32[]{:T(128)S(6)} %select_n.8), kind=kLoop, calls=%fused_computation.5 | loop fusion | flops 98304 | bytes 786448 | tf_op jit(solution)/shard_map/broadcast_in_dim | solution.py:208
  54.3 2.1 %fusion = bf16[16,3,128,128]{3,0,2,1:T(8,128)(2,1)S(1)} fusion(f32[3,128,128]{2,1,0:T(8,128)S(1)} %get-tuple-element.11, f32[16,3]{0,1:T(4,128)S(1)} %get-tuple-element.16, bf16[16,3,128,128]{3,2,1,0:T(8,128)(2,1)S(1)} %bitcast.27, f32[16,16]{1,0:T(8,128)S(1)} %convert_maximum_fusion, f32[3]{0:T(128)S(1)} %get-tuple-element.19, ...), kind=kOutput, calls=%fused_computation.1 | convolution fusion | flops 153355776 | bytes 3343820 | tf_op jit(solution)/shard_map/tsh,shde->thde/dot_general | solution.py:184
  56.4 1.6 %copy.13 = bf16[16,3,128,128]{3,2,1,0:T(8,128)(2,1)} copy(bf16[16,3,128,128]{3,0,2,1:T(8,128)(2,1)S(1)} %fusion) | data formatting | bytes 3145728 | tf_op jit(solution)/shard_map/convert_element_type | solution.py:194
  57.9 4.0 %all-to-all-start.1 = ((bf16[48,128,128]{2,1,0:T(8,128)(2,1)}), bf16[48,128,128]{2,1,0:T(8,128)(2,1)S(1)}, u32[]{:S(2)}, u32[]{:S(2)}) async-start(bf16[48,128,128]{2,1,0:T(8,128)(2,1)} %bitcast.7), calls=%async_computation.1 | async-start | bytes 3145728 | tf_op jit(solution)/shard_map/all_to_all | solution.py:193
  61.9 0.2 collective-permute-start
  62.1 1.4 %collective-permute-start.1 = (f32[1,6144]{1,0:T(1,128)S(1)}, f32[1,6144]{1,0:T(1,128)S(1)}, u32[]{:S(2)}, u32[]{:S(2)}) collective-permute-start(f32[1,6144]{1,0:T(1,128)S(1)} %copy-done.9), channel_id=1, source_target_pairs={{0,16},{16,32},{32,48},{48,64},{64,80},{80,96},{96,112},{112,0},{1... | collective-permute-start | bytes 73736 | tf_op jit(solution)/shard_map/ppermute | solution.py:164
  63.6 0.2 collective-permute-start.2
  63.7 10.1 %collective-permute-done.2 = f32[1,48]{1,0:T(1,128)S(1)} collective-permute-done((f32[1,48]{1,0:T(1,128)S(1)}, f32[1,48]{1,0:T(1,128)S(1)}, u32[]{:S(2)}, u32[]{:S(2)}) %collective-permute-start.2) | collective-permute-done | bytes 224 | tf_op jit(solution)/shard_map/ppermute | solution.py:164
  73.9 13.8 %all-to-all-done.1 = bf16[48,128,128]{2,1,0:T(8,128)(2,1)S(1)} async-done(((bf16[48,128,128]{2,1,0:T(8,128)(2,1)}), bf16[48,128,128]{2,1,0:T(8,128)(2,1)S(1)}, u32[]{:S(2)}, u32[]{:S(2)}) %all-to-all-start.1) | async-done | bytes 1572896 | tf_op jit(solution)/shard_map/all_to_all | solution.py:193
  87.7 0.1 fusion.14
  87.9 0.0 collective-permute-start.7
  87.9 1.6 %collective-permute-start.6 = (bf16[12,128,128]{2,1,0:T(8,128)(2,1)S(1)}, bf16[12,128,128]{2,1,0:T(8,128)(2,1)S(1)}, u32[]{:S(2)}, u32[]{:S(2)}) collective-permute-start(bf16[12,128,128]{2,1,0:T(8,128)(2,1)S(1)} %get-tuple-element.13), channel_id=1, source_target_pairs={{0,16},{16,32},{32,48},{48,64},{64,80},{80,96},{96,112},{112,0},{1... | collective-permute-start | bytes 1179656 | tf_op jit(solution)/shard_map/ppermute | solution.py:203
  89.5 0.0 collective-permute-start.5
  89.5 1.8 %collective-permute-start.4 = (bf16[12,128,128]{2,1,0:T(8,128)(2,1)S(1)}, bf16[12,128,128]{2,1,0:T(8,128)(2,1)S(1)}, u32[]{:S(2)}, u32[]{:S(2)}) collective-permute-start(bf16[12,128,128]{2,1,0:T(8,128)(2,1)S(1)} %get-tuple-element.15), channel_id=1, source_target_pairs={{0,16},{16,32},{32,48},{48,64},{64,80},{80,96},{96,112},{112,0},{1... | collective-permute-start | bytes 1179656 | tf_op jit(solution)/shard_map/ppermute | solution.py:203
  91.2 5.1 %collective-permute-done.7.s_ref = bf16[12,128,128]{2,1,0:T(8,128)(2,1)S(1)} collective-permute-done((bf16[12,128,128]{2,1,0:T(8,128)(2,1)S(1)}, bf16[12,128,128]{2,1,0:T(8,128)(2,1)S(1)}, u32[]{:S(2)}, u32[]{:S(2)}) %collective-permute-start.7) | collective-permute-done | bytes 393248 | tf_op jit(solution)/shard_map/ppermute | solution.py:203
  96.3 0.8 copy-done.2
  97.1 7.6 %shard_map.69.rest_0_ = bf16[1,512,6144]{2,1,0:T(8,128)(2,1)} custom-call(f32[48]{0:T(128)} %bitcast.29, bf16[1,512,6144]{2,1,0:T(8,128)(2,1)} %collective-permute-done.3.x_ref, f32[1,3,6144]{2,1,0:T(4,128)} %copy-done, f32[1,6144]{1,0:T(1,128)} %copy-done.6, bf16[12,128,128]{2,1,0:T(8,128)(2,1)} %copy-done.2), custom_call_target="tpu_custom_call" | custom-call | flops 1610612736 | bytes 3538944 | tf_op jit(solution)/shard_map/pallas_call | solution.py:136
  104.7 0.8 copy-done.5
  105.5 7.7 %shard_map.70.rest_0_ = bf16[1,512,6144]{2,1,0:T(8,128)(2,1)} custom-call(f32[48]{0:T(128)} %bitcast.30, bf16[1,512,6144]{2,1,0:T(8,128)(2,1)} %collective-permute-done.3.x_ref, f32[1,3,6144]{2,1,0:T(4,128)} %copy-done, f32[1,6144]{1,0:T(1,128)} %copy-done.6, bf16[12,128,128]{2,1,0:T(8,128)(2,1)} %copy-done.5, ...), custom_call_target="tpu_custom_call", output_to_operand_aliasing={{}: (5, {})} | custom-call | flops 1610612736 | bytes 3538944 | tf_op jit(solution)/shard_map/pallas_call | solution.py:136
  113.1 0.8 copy-done.4
  113.9 7.7 %shard_map.71.rest_0_ = bf16[1,512,6144]{2,1,0:T(8,128)(2,1)} custom-call(f32[48]{0:T(128)} %bitcast.31, bf16[1,512,6144]{2,1,0:T(8,128)(2,1)} %collective-permute-done.3.x_ref, f32[1,3,6144]{2,1,0:T(4,128)} %copy-done, f32[1,6144]{1,0:T(1,128)} %copy-done.6, bf16[12,128,128]{2,1,0:T(8,128)(2,1)} %copy-done.4, ...), custom_call_target="tpu_custom_call", output_to_operand_aliasing={{}: (5, {})} | custom-call | flops 1610612736 | bytes 3538944 | tf_op jit(solution)/shard_map/pallas_call | solution.py:136
  121.6 0.8 copy-done.3
  122.3 7.7 %shard_map.72 = bf16[1,512,6144]{2,1,0:T(8,128)(2,1)} custom-call(f32[48]{0:T(128)} %bitcast.32, bf16[1,512,6144]{2,1,0:T(8,128)(2,1)} %collective-permute-done.3.x_ref, f32[1,3,6144]{2,1,0:T(4,128)} %copy-done, f32[1,6144]{1,0:T(1,128)} %copy-done.6, bf16[12,128,128]{2,1,0:T(8,128)(2,1)} %copy-done.3, ...), custom_call_target="tpu_custom_call", output_to_operand_aliasing={{}: (5, {})} | custom-call | flops 1610612736 | bytes 3538944 | tf_op jit(solution)/shard_map/pallas_call | solution.py:136
  (25 shorter events, 0.1 us)
Async XLA Ops:
  0.6 95.7 %collective-permute-start.3 = (bf16[1,512,6144]{2,1,0:T(8,128)(2,1)}, bf16[1,512,6144]{2,1,0:T(8,128)(2,1)}, u32[]{:S(2)}, u32[]{:S(2)}) collective-permute-start(bf16[1,512,6144]{2,1,0:T(8,128)(2,1)} %x_ref.1), channel_id=1, source_target_pairs={{0,16},{16,32},{32,48},{48,64},{64,80},{80,96},{96,112},{112,0},{1... | collective-permute-start | bytes 18874376 | tf_op jit(solution)/shard_map/ppermute | solution.py:164
  15.2 8.3 %copy-start.8 = (f32[1,48]{1,0:T(1,128)S(1)}, f32[1,48]{1,0:T(1,128)}, u32[]{:S(2)}) copy-start(f32[1,48]{1,0:T(1,128)} %param.8) | copy-start | bytes 580
  15.2 36.0 %all-to-all-start = ((bf16[48,128,128]{2,1,0:T(8,128)(2,1)}), bf16[48,128,128]{2,1,0:T(8,128)(2,1)S(1)}, u32[]{:S(2)}, u32[]{:S(2)}) async-start(bf16[48,128,128]{2,1,0:T(8,128)(2,1)} %shard_map.68), calls=%async_computation | async-start | bytes 3145728 | tf_op jit(solution)/shard_map/all_to_all | solution.py:169
  57.9 4.0 %copy-start.1 = (f32[1,3,6144]{2,1,0:T(4,128)S(1)}, f32[1,3,6144]{2,1,0:T(4,128)}, u32[]{:S(2)}) copy-start(f32[1,3,6144]{2,1,0:T(4,128)} %copy.10.g_ref) | copy-start | bytes 221188
  57.9 4.2 %copy-start.9 = (f32[1,6144]{1,0:T(1,128)S(1)}, f32[1,6144]{1,0:T(1,128)}, u32[]{:S(2)}) copy-start(f32[1,6144]{1,0:T(1,128)} %param.7) | copy-start | bytes 73732
  57.9 29.8 %all-to-all-start.1 = ((bf16[48,128,128]{2,1,0:T(8,128)(2,1)}), bf16[48,128,128]{2,1,0:T(8,128)(2,1)S(1)}, u32[]{:S(2)}, u32[]{:S(2)}) async-start(bf16[48,128,128]{2,1,0:T(8,128)(2,1)} %bitcast.7), calls=%async_computation.1 | async-start | bytes 3145728 | tf_op jit(solution)/shard_map/all_to_all | solution.py:193
  61.9 11.9 %collective-permute-start = (f32[1,3,6144]{2,1,0:T(4,128)S(1)}, f32[1,3,6144]{2,1,0:T(4,128)S(1)}, u32[]{:S(2)}, u32[]{:S(2)}) collective-permute-start(f32[1,3,6144]{2,1,0:T(4,128)S(1)} %copy-done.1), channel_id=1, source_target_pairs={{0,16},{16,32},{32,48},{48,64},{64,80},{80,96},{96,112},{112,0},{1... | collective-permute-start | bytes 221192 | tf_op jit(solution)/shard_map/ppermute | solution.py:164
  62.1 11.7 %collective-permute-start.1 = (f32[1,6144]{1,0:T(1,128)S(1)}, f32[1,6144]{1,0:T(1,128)S(1)}, u32[]{:S(2)}, u32[]{:S(2)}) collective-permute-start(f32[1,6144]{1,0:T(1,128)S(1)} %copy-done.9), channel_id=1, source_target_pairs={{0,16},{16,32},{32,48},{48,64},{64,80},{80,96},{96,112},{112,0},{1... | collective-permute-start | bytes 73736 | tf_op jit(solution)/shard_map/ppermute | solution.py:164
  63.6 10.3 %collective-permute-start.2 = (f32[1,48]{1,0:T(1,128)S(1)}, f32[1,48]{1,0:T(1,128)S(1)}, u32[]{:S(2)}, u32[]{:S(2)}) collective-permute-start(f32[1,48]{1,0:T(1,128)S(1)} %copy-done.8), channel_id=1, source_target_pairs={{0,16},{16,32},{32,48},{48,64},{64,80},{80,96},{96,112},{112,0},{1... | collective-permute-start | bytes 584 | tf_op jit(solution)/shard_map/ppermute | solution.py:164
  73.9 14.0 %copy-start.7 = (f32[1,48]{1,0:T(1,128)}, f32[1,48]{1,0:T(1,128)S(1)}, u32[]{:S(2)}) copy-start(f32[1,48]{1,0:T(1,128)S(1)} %collective-permute-done.2) | copy-start | bytes 580
  73.9 14.0 %copy-start.6 = (f32[1,6144]{1,0:T(1,128)}, f32[1,6144]{1,0:T(1,128)S(1)}, u32[]{:S(2)}) copy-start(f32[1,6144]{1,0:T(1,128)S(1)} %collective-permute-done.1.go_ref) | copy-start | bytes 73732
  73.9 14.0 %copy-start = (f32[1,3,6144]{2,1,0:T(4,128)}, f32[1,3,6144]{2,1,0:T(4,128)S(1)}, u32[]{:S(2)}) copy-start(f32[1,3,6144]{2,1,0:T(4,128)S(1)} %collective-permute-done.g_ref) | copy-start | bytes 221188
  87.9 8.4 %collective-permute-start.7 = (bf16[12,128,128]{2,1,0:T(8,128)(2,1)S(1)}, bf16[12,128,128]{2,1,0:T(8,128)(2,1)S(1)}, u32[]{:S(2)}, u32[]{:S(2)}) collective-permute-start(bf16[12,128,128]{2,1,0:T(8,128)(2,1)S(1)} %get-tuple-element.12), channel_id=1, source_target_pairs={{0,16},{16,32},{32,48},{48,64},{64,80},{80,96},{96,112},{112,0},{1... | collective-permute-start | bytes 1179656 | tf_op jit(solution)/shard_map/ppermute | solution.py:203
  87.9 16.8 %collective-permute-start.6 = (bf16[12,128,128]{2,1,0:T(8,128)(2,1)S(1)}, bf16[12,128,128]{2,1,0:T(8,128)(2,1)S(1)}, u32[]{:S(2)}, u32[]{:S(2)}) collective-permute-start(bf16[12,128,128]{2,1,0:T(8,128)(2,1)S(1)} %get-tuple-element.13), channel_id=1, source_target_pairs={{0,16},{16,32},{32,48},{48,64},{64,80},{80,96},{96,112},{112,0},{1... | collective-permute-start | bytes 1179656 | tf_op jit(solution)/shard_map/ppermute | solution.py:203
  89.5 23.7 %collective-permute-start.5 = (bf16[12,128,128]{2,1,0:T(8,128)(2,1)S(1)}, bf16[12,128,128]{2,1,0:T(8,128)(2,1)S(1)}, u32[]{:S(2)}, u32[]{:S(2)}) collective-permute-start(bf16[12,128,128]{2,1,0:T(8,128)(2,1)S(1)} %get-tuple-element.14), channel_id=1, source_target_pairs={{0,16},{16,32},{32,48},{48,64},{64,80},{80,96},{96,112},{112,0},{1... | collective-permute-start | bytes 1179656 | tf_op jit(solution)/shard_map/ppermute | solution.py:203
  89.5 32.1 %collective-permute-start.4 = (bf16[12,128,128]{2,1,0:T(8,128)(2,1)S(1)}, bf16[12,128,128]{2,1,0:T(8,128)(2,1)S(1)}, u32[]{:S(2)}, u32[]{:S(2)}) collective-permute-start(bf16[12,128,128]{2,1,0:T(8,128)(2,1)S(1)} %get-tuple-element.15), channel_id=1, source_target_pairs={{0,16},{16,32},{32,48},{48,64},{64,80},{80,96},{96,112},{112,0},{1... | collective-permute-start | bytes 1179656 | tf_op jit(solution)/shard_map/ppermute | solution.py:203
  96.3 0.8 copy-start.2
  104.7 0.8 copy-start.5
  113.1 0.8 copy-start.4
  121.6 0.8 copy-start.3

commit v6 on v5

--- a/solution.py
+++ b/solution.py
@@ -53,9 +53,8 @@
         o_ref[hh] = acc.astype(o_ref.dtype)
 
 
-def _output_kernel(rates_ref, x_ref, g_ref, go_ref, s_ref, *rest, hg, head_dim, nblocks, first):
-    o_ref = rest[-1]
-    step = pl.program_id(0) + first
+def _local_kernel(rates_ref, x_ref, g_ref, q_ref, l_ref, r_ref, *, hg, head_dim, nblocks):
+    step = pl.program_id(0)
     pos = lax.broadcasted_iota(jnp.int32, (BLOCK, 1), 0).astype(jnp.float32)
     pos_row = lax.broadcasted_iota(jnp.int32, (1, BLOCK), 1).astype(jnp.float32)
     row = lax.broadcasted_iota(jnp.int32, (BLOCK, BLOCK), 0)
@@ -67,7 +66,7 @@
         lead = jnp.exp(-rate * (pos + 1.0))
         mask = jnp.where(causal, lead * jnp.exp(rate * (pos_row + 1.0)), 0.0)
         decay = jnp.exp(-rate * BLOCK)
-        state = s_ref[hh].astype(jnp.float32)
+        running = None
         for b in range(nblocks):
             rows = slice(b * BLOCK, (b + 1) * BLOCK)
             x = x_ref[0, rows, cols].astype(jnp.float32)
@@ -76,13 +75,36 @@
             values_b = (x * g_ref[0, 2:3, cols]).astype(jnp.bfloat16)
             scores = _dot_nt(queries_b, keys_b)
             weights = (scores * mask).astype(jnp.bfloat16)
-            local = _dot(weights, values_b)
-            cross = _dot(queries_b, state.astype(jnp.bfloat16))
-            total = local + lead * cross
+            q_ref[0, rows, cols] = queries_b
+            l_ref[0, rows, cols] = _dot(weights, values_b)
+            if b + 1 < nblocks:
+                update = _block_state(keys_b, values_b, rate, pos)
+                running = update if running is None else decay * running + update
+                r_ref[b, hh] = running
+
+
+def _final_kernel(rates_ref, x_ref, q_ref, l_ref, r_ref, s_ref, go_ref, *rest, hg, head_dim, nblocks, first):
+    o_ref = rest[-1]
+    step = pl.program_id(0) + first
+    pos = lax.broadcasted_iota(jnp.int32, (BLOCK, 1), 0).astype(jnp.float32)
+    for hh in range(hg):
+        rate = jnp.full((1, 1), rates_ref[step * hg + hh], jnp.float32)
+        cols = slice(hh * head_dim, (hh + 1) * head_dim)
+        lead = jnp.exp(-rate * (pos + 1.0))
+        decay_b = jnp.ones_like(rate)
+        entering = s_ref[hh].astype(jnp.float32)
+        for b in range(nblocks):
+            rows = slice(b * BLOCK, (b + 1) * BLOCK)
+            if b == 0:
+                state = entering
+            else:
+                decay_b = decay_b * jnp.exp(-rate * BLOCK)
+                state = decay_b * entering + r_ref[b - 1, hh]
+            cross = _dot(q_ref[0, rows, cols], state.astype(jnp.bfloat16))
+            total = l_ref[0, rows, cols] + lead * cross
             normed = total * lax.rsqrt(jnp.mean(total * total, axis=-1, keepdims=True) + EPSILON)
+            x = x_ref[0, rows, cols].astype(jnp.float32)
             o_ref[0, rows, cols] = (x + normed * go_ref[0:1, cols]).astype(o_ref.dtype)
-            if b + 1 < nblocks:
-                state = decay * state + _block_state(keys_b, values_b, rate, pos)
 
 
 def _summaries(rates, rows, gains, head_dim):
@@ -110,23 +132,53 @@
     )(rates, rows, gains)
 
 
-def _outputs(rates, rows, gains, gain_out, states, head_dim, first, previous):
+def _local_part(rates, rows, gains, head_dim):
+    _, count, width = rows.shape
+    heads = width // head_dim
+    hg = HEADS_PER_STEP
+    cw = hg * head_dim
+    nblocks = count // BLOCK
+    row_spec = pl.BlockSpec((1, count, cw), lambda i, r: (0, 0, i))
+    run_spec = pl.BlockSpec((nblocks - 1, hg, head_dim, head_dim), lambda i, r: (0, i, 0, 0))
+    kernel = functools.partial(_local_kernel, hg=hg, head_dim=head_dim, nblocks=nblocks)
+    return pl.pallas_call(
+        kernel,
+        grid_spec=pltpu.PrefetchScalarGridSpec(
+            num_scalar_prefetch=1,
+            grid=(heads // hg,),
+            in_specs=[row_spec, pl.BlockSpec((1, 3, cw), lambda i, r: (0, 0, i))],
+            out_specs=[row_spec, row_spec, run_spec],
+        ),
+        out_shape=[
+            jax.ShapeDtypeStruct(rows.shape, jnp.bfloat16),
+            jax.ShapeDtypeStruct(rows.shape, jnp.float32),
+            jax.ShapeDtypeStruct((nblocks - 1, heads, head_dim, head_dim), jnp.float32),
+        ],
+        cost_estimate=pl.CostEstimate(
+            flops=6 * count * BLOCK * width, transcendentals=3 * count * width,
+            bytes_accessed=count * width * 8,
+        ),
+    )(rates, rows, gains)
+
+
+def _outputs(rates, rows, queries, local, running, gain_out, states, head_dim, first, previous):
     _, count, width = rows.shape
     hg = HEADS_PER_STEP
     cw = hg * head_dim
+    nblocks = count // BLOCK
     steps = states.shape[0] // hg
     base = first // hg
     kernel = functools.partial(
-        _output_kernel, hg=hg, head_dim=head_dim, nblocks=count // BLOCK, first=base
+        _final_kernel, hg=hg, head_dim=head_dim, nblocks=nblocks, first=base
     )
     row_spec = pl.BlockSpec((1, count, cw), lambda i, r: (0, 0, i + base))
     in_specs = [
-        row_spec,
-        pl.BlockSpec((1, 3, cw), lambda i, r: (0, 0, i + base)),
+        row_spec, row_spec, row_spec,
+        pl.BlockSpec((nblocks - 1, hg, head_dim, head_dim), lambda i, r: (0, i + base, 0, 0)),
+        pl.BlockSpec((hg, head_dim, head_dim), lambda i, r: (i, 0, 0)),
         pl.BlockSpec((1, cw), lambda i, r: (0, i + base)),
-        pl.BlockSpec((hg, head_dim, head_dim), lambda i, r: (i, 0, 0)),
     ]
-    operands = [rates, rows, gains, gain_out, states]
+    operands = [rates, rows, queries, local, running, states, gain_out]
     aliases = {}
     if previous is not None:
         in_specs.append(pl.BlockSpec(memory_space=pl.ANY))
@@ -144,8 +196,8 @@
         out_shape=jax.ShapeDtypeStruct(rows.shape, rows.dtype),
         input_output_aliases=aliases,
         cost_estimate=pl.CostEstimate(
-            flops=8 * count * BLOCK * share, transcendentals=3 * count * share,
-            bytes_accessed=2 * count * share * 2 + steps * hg * head_dim * head_dim * 2,
+            flops=2 * count * share * head_dim, transcendentals=count * share,
+            bytes_accessed=count * share * 10,
         ),
     )(*operands)
 
@@ -161,9 +213,13 @@
     count_s = lax.axis_size("section")
     pairs = [(src, (src + 1) % count_s) for src in range(count_s)]
 
-    prev_rows, prev_gains, prev_gain_out, prev_rates = lax.ppermute(
-        (section_inputs, input_gains, out_gain, decay_rates), "section", pairs
-    )
+    prev_gains, prev_gain_out, prev_rates = lax.ppermute(
+        (input_gains, out_gain, decay_rates), "section", pairs
+    )
+    sent, prev_gains, prev_gain_out, prev_rates = lax.optimization_barrier(
+        (section_inputs, prev_gains, prev_gain_out, prev_rates)
+    )
+    prev_rows = lax.ppermute(sent, "section", pairs)
 
     summary = _summaries(rates, section_inputs, input_gains, head_dim)
     gathered = lax.all_to_all(summary, "ctx", 0, 0, tiled=True)
@@ -190,19 +246,18 @@
     end_part = jnp.einsum(
         "sh,shde->hde", end_weights, gathered, precision=lax.Precision.HIGHEST
     ) + jnp.exp(-rate_part * count * group_size)[:, None, None] * carry_part
+    queries, local, running = _local_part(prev_rates[0], prev_rows, prev_gains, head_dim)
     incoming = lax.all_to_all(
         prefixes.astype(jnp.bfloat16).reshape(heads, head_dim, head_dim),
         "ctx", 0, 0, tiled=True,
     )
-    prev_gains, prev_gain_out, prev_rates, incoming = lax.optimization_barrier(
-        (prev_gains, prev_gain_out, prev_rates, incoming)
-    )
+    incoming, queries, local, running = lax.optimization_barrier((incoming, queries, local, running))
     chunk = heads // STATE_CHUNKS
     next_rows = None
     for part in range(STATE_CHUNKS):
         piece = lax.ppermute(incoming[part * chunk : (part + 1) * chunk], "section", pairs)
         next_rows = _outputs(
-            prev_rates[0], prev_rows, prev_gains, prev_gain_out, piece, head_dim,
+            prev_rates[0], prev_rows, queries, local, running, prev_gain_out, piece, head_dim,
             part * chunk, next_rows,
         )
     return (next_rows, end_part[None])

time: 131 us -> 137 us (1.046)
  Pallas kernels: 43.6 us -> 57.9 us
  waiting for transfers between devices: 56.4 us -> 52.4 us
  starting transfers between devices: 17.5 us -> 14 us
    pallas_call x0 -> x1, Pallas kernels: none -> 19.4 us  [_local_part(): pl.pallas_call(kernel, grid_spec=pltpu.PrefetchScalarGridSpec(num_scalar_...]
    all_to_all x1, waiting for transfers between devices: 13.8 us -> 0.01 us  [on_device(): lax.all_to_all(prefixes.astype(jnp.bfloat16).reshape(heads, head_dim, hea...]
    ppermute x4, waiting for transfers between devices: 10.2 us -> 19 us  [the longest x1 14.7 us: on_device(): prev_rows = lax.ppermute(sent, 'section', pairs)]
    pallas_call x4, Pallas kernels: 30.6 us -> 25.5 us  [_outputs(): pl.pallas_call(kernel, grid_spec=pltpu.PrefetchScalarGridSpec(num_scalar_...]
    ppermute x4, starting transfers between devices: 3.36 us -> 0.49 us  [on_device(): lax.ppermute(incoming[part * chunk:(part + 1) * chunk], 'section', pairs)]
    ppermute x4, waiting for transfers between devices: 5.07 us -> 7.92 us  [on_device(): lax.ppermute(incoming[part * chunk:(part + 1) * chunk], 'section', pairs)]
    all_to_all x1, waiting for transfers between devices: 27.4 us -> 25.4 us  [on_device(): gathered = lax.all_to_all(summary, 'ctx', 0, 0, tiled=True)]
    unnamed x21 -> x19, local copies, waits for them, and re-layouts: 4.62 us -> 3.91 us
  transfers between devices with their start and end apart: 10 -> 10, of which waited for: 4 -> 4; matrix products, arithmetic and copies ran while one was open for 7% -> 5% of each run, Pallas kernels for 28% -> 38%
where the time goes in v6:
time: 137 us; the launch traced here: 136 us
  Pallas kernels  57.9 us (42%)
  waiting for transfers between devices  52.4 us (38%)
  starting transfers between devices  14 us (10%)
  local copies, waits for them, and re-layouts  5.61 us (4%)
  matrix products  3.48 us (3%)
  other arithmetic  1.94 us (1%)
    pallas_call x4, Pallas kernels, _outputs(): pl.pallas_call(kernel, grid_spec=pltpu.PrefetchScalarGridSpec(num_scalar_...  25.5 us
    all_to_all x1, waiting for transfers between devices, on_device(): gathered = lax.all_to_all(summary, 'ctx', 0, 0, tiled=True)  25.4 us
    pallas_call x1, Pallas kernels, _local_part(): pl.pallas_call(kernel, grid_spec=pltpu.PrefetchScalarGridSpec(num_scalar_...  19.4 us
    ppermute x1, waiting for transfers between devices, on_device(): prev_rows = lax.ppermute(sent, 'section', pairs)  14.7 us
    pallas_call x1, Pallas kernels, _summaries(): pl.pallas_call(kernel, grid_spec=pltpu.PrefetchScalarGridSpec(num_scalar_...  13 us
    all_to_all x1, starting transfers between devices, on_device(): gathered = lax.all_to_all(summary, 'ctx', 0, 0, tiled=True)  8.06 us
    ppermute x4, waiting for transfers between devices, on_device(): lax.ppermute(incoming[part * chunk:(part + 1) * chunk], 'section', pairs)  7.92 us
    ppermute x3, waiting for transfers between devices, on_device(): lax.ppermute((input_gains, out_gain, decay_rates), 'section', pairs)  4.32 us
  transfers between devices with their start and end apart: 10, of which 4 were waited for; matrix products, arithmetic and copies ran while one was open for 5% of the time, Pallas kernels for 38%

profile of v6, /device:TPU:0, one launch (start us, length us, event | category | flops | bytes accessed | tf_op | source)
XLA Modules:
  0.0 136.1 jit_solution(9773981561521416283)
XLA Ops:
  0.6 0.9 copy.10.g_ref
  1.6 0.0 collective-permute-start
  1.6 1.7 %collective-permute-start.1 = (f32[1,6144]{1,0:T(1,128)}, f32[1,6144]{1,0:T(1,128)S(1)}, u32[]{:S(2)}, u32[]{:S(2)}) collective-permute-start(f32[1,6144]{1,0:T(1,128)} %param.7), channel_id=1, source_target_pairs={{0,16},{16,32},{32,48},{48,64},{64,80},{80,96},{96,112},{112,0},{1... | collective-permute-start | bytes 73736 | tf_op jit(solution)/shard_map/ppermute | solution.py:216
  3.3 0.0 collective-permute-start.2
  3.3 4.3 %collective-permute-done.2 = f32[1,48]{1,0:T(1,128)S(1)} collective-permute-done((f32[1,48]{1,0:T(1,128)}, f32[1,48]{1,0:T(1,128)S(1)}, u32[]{:S(2)}, u32[]{:S(2)}) %collective-permute-start.2) | collective-permute-done | bytes 224 | tf_op jit(solution)/shard_map/ppermute | solution.py:216
  7.7 0.0 collective-permute-start.3
  7.7 13.0 %shard_map.68 = bf16[48,128,128]{2,1,0:T(8,128)(2,1)} custom-call(f32[48]{0:T(128)} %bitcast.34, bf16[1,512,6144]{2,1,0:T(8,128)(2,1)} %x_ref.1, f32[1,3,6144]{2,1,0:T(4,128)} %copy-done.5), custom_call_target="tpu_custom_call" | custom-call | flops 805306368 | bytes 9437184 | tf_op jit(solution)/shard_map/pallas_call | solution.py:116
  20.7 8.1 %all-to-all-start = ((bf16[48,128,128]{2,1,0:T(8,128)(2,1)}), bf16[48,128,128]{2,1,0:T(8,128)(2,1)S(1)}, u32[]{:S(2)}, u32[]{:S(2)}) async-start(bf16[48,128,128]{2,1,0:T(8,128)(2,1)} %shard_map.68), calls=%async_computation | async-start | bytes 3145728 | tf_op jit(solution)/shard_map/all_to_all | solution.py:225
  28.8 0.1 exponential_bitcast_fusion.1
  28.9 0.1 multiply_exponential_fusion
  28.9 0.1 convert_maximum_fusion
  29.0 25.4 %all-to-all-done = bf16[48,128,128]{2,1,0:T(8,128)(2,1)S(1)} async-done(((bf16[48,128,128]{2,1,0:T(8,128)(2,1)}), bf16[48,128,128]{2,1,0:T(8,128)(2,1)S(1)}, u32[]{:S(2)}, u32[]{:S(2)}) %all-to-all-start) | async-done | bytes 1572896 | tf_op jit(solution)/shard_map/all_to_all | solution.py:225
  54.5 1.4 %fusion.1 = f32[3,1,128,128]{3,1,2,0:T(1,128)S(1)} fusion(bf16[16,3,128,128]{3,2,1,0:T(8,128)(2,1)S(1)} %bitcast.26, f32[16,3,1,1]{0,1,2,3:T(4,128)S(1)} %get-tuple-element.31), kind=kOutput, calls=%fused_computation.2 | convolution fusion | flops 9437184 | bytes 1769664 | tf_op jit(solution)/shard_map/sh,shde->hde/dot_general | solution.py:246
  55.9 1.7 %add_bitcast_fusion = (f32[1,3,128,128]{3,2,1,0:T(8,128)}, f32[3,128,128]{2,1,0:T(8,128)S(1)}) fusion(f32[3,128,128]{2,1,0:T(8,128)S(1)} %bitcast.28, f32[3]{0:T(128)S(1)} %get-tuple-element.32, f32[1,48,128,128]{3,2,1,0:T(8,128)} %param.9, s32[]{:T(128)S(6)} %select_n.8), kind=kLoop, calls=%fused_computation.5 | loop fusion | flops 98304 | bytes 786448 | tf_op jit(solution)/shard_map/broadcast_in_dim | solution.py:263
  57.6 2.1 %fusion = bf16[16,3,128,128]{3,0,2,1:T(8,128)(2,1)S(1)} fusion(f32[3,128,128]{2,1,0:T(8,128)S(1)} %get-tuple-element.25, f32[16,3]{0,1:T(4,128)S(1)} %get-tuple-element.30, bf16[16,3,128,128]{3,2,1,0:T(8,128)(2,1)S(1)} %bitcast.27, f32[16,16]{1,0:T(8,128)S(1)} %convert_maximum_fusion, f32[3]{0:T(128)S(1)} %get-tuple-element.33, ...), kind=kOutput, calls=%fused_computation.1 | convolution fusion | flops 153355776 | bytes 3343820 | tf_op jit(solution)/shard_map/tsh,shde->thde/dot_general | solution.py:240
  59.7 1.6 %copy.13 = bf16[16,3,128,128]{3,2,1,0:T(8,128)(2,1)} copy(bf16[16,3,128,128]{3,0,2,1:T(8,128)(2,1)S(1)} %fusion) | data formatting | bytes 3145728 | tf_op jit(solution)/shard_map/convert_element_type | solution.py:251
  61.2 3.7 %all-to-all-start.1 = ((bf16[48,128,128]{2,1,0:T(8,128)(2,1)}), bf16[48,128,128]{2,1,0:T(8,128)(2,1)S(1)}, u32[]{:S(2)}, u32[]{:S(2)}) async-start(bf16[48,128,128]{2,1,0:T(8,128)(2,1)} %bitcast.8), calls=%async_computation.1 | async-start | bytes 3145728 | tf_op jit(solution)/shard_map/all_to_all | solution.py:250
  64.9 14.7 %collective-permute-done.3.x_ref = bf16[1,512,6144]{2,1,0:T(8,128)(2,1)} collective-permute-done((bf16[1,512,6144]{2,1,0:T(8,128)(2,1)}, bf16[1,512,6144]{2,1,0:T(8,128)(2,1)}, u32[]{:S(2)}, u32[]{:S(2)}) %collective-permute-start.3) | collective-permute-done | bytes 6291488 | tf_op jit(solution)/shard_map/ppermute | solution.py:222
  79.6 19.4 %shard_map.69 = (bf16[1,512,6144]{2,1,0:T(8,128)(2,1)}, f32[1,512,6144]{2,1,0:T(8,128)}, f32[1,48,128,128]{3,2,1,0:T(8,128)}) custom-call(f32[48]{0:T(128)} %bitcast.29, bf16[1,512,6144]{2,1,0:T(8,128)(2,1)} %collective-permute-done.3.x_ref, f32[1,3,6144]{2,1,0:T(4,128)} %copy-done.8), custom_call_target="tpu_custom_call" | custom-call | flops 4831838208 | bytes 25165824 | tf_op jit(solution)/shard_map/pallas_call | solution.py:144
  99.0 0.1 fusion.14
  99.1 0.0 collective-permute-start.7
  99.1 0.0 collective-permute-start.6
  99.2 0.4 collective-permute-start.4
  99.6 7.9 %collective-permute-done.7.s_ref = bf16[12,128,128]{2,1,0:T(8,128)(2,1)S(1)} collective-permute-done((bf16[12,128,128]{2,1,0:T(8,128)(2,1)S(1)}, bf16[12,128,128]{2,1,0:T(8,128)(2,1)S(1)}, u32[]{:S(2)}, u32[]{:S(2)}) %collective-permute-start.7) | collective-permute-done | bytes 393248 | tf_op jit(solution)/shard_map/ppermute | solution.py:258
  107.5 0.7 copy-done.3
  108.3 6.4 %shard_map.70.rest_0_ = bf16[1,512,6144]{2,1,0:T(8,128)(2,1)} custom-call(f32[48]{0:T(128)} %bitcast.30, bf16[1,512,6144]{2,1,0:T(8,128)(2,1)} %collective-permute-done.3.x_ref, bf16[1,512,6144]{2,1,0:T(8,128)(2,1)} %get-tuple-element.19.q_ref, f32[1,512,6144]{2,1,0:T(8,128)} %get-tuple-element.20.l_ref, f32[1,48,128,128]{3,2,1,0:T(8,128)} %get-tuple-element.21.r_ref, ...), custom_call_target="tpu_custom_call" | custom-call | flops 201326592 | bytes 7864320 | tf_op jit(solution)/shard_map/pallas_call | solution.py:188
  114.7 0.7 copy-done.2
  115.4 6.4 %shard_map.71.rest_0_ = bf16[1,512,6144]{2,1,0:T(8,128)(2,1)} custom-call(f32[48]{0:T(128)} %bitcast.31, bf16[1,512,6144]{2,1,0:T(8,128)(2,1)} %collective-permute-done.3.x_ref, bf16[1,512,6144]{2,1,0:T(8,128)(2,1)} %get-tuple-element.19.q_ref, f32[1,512,6144]{2,1,0:T(8,128)} %get-tuple-element.20.l_ref, ...), custom_call_target="tpu_custom_call", output_to_operand_aliasing={{}: (7, {})} | custom-call | flops 201326592 | bytes 7864320 | tf_op jit(solution)/shard_map/pallas_call | solution.py:188
  121.8 0.7 copy-done.1
  122.6 6.4 %shard_map.72.rest_0_ = bf16[1,512,6144]{2,1,0:T(8,128)(2,1)} custom-call(f32[48]{0:T(128)} %bitcast.32, bf16[1,512,6144]{2,1,0:T(8,128)(2,1)} %collective-permute-done.3.x_ref, bf16[1,512,6144]{2,1,0:T(8,128)(2,1)} %get-tuple-element.19.q_ref, f32[1,512,6144]{2,1,0:T(8,128)} %get-tuple-element.20.l_ref, ...), custom_call_target="tpu_custom_call", output_to_operand_aliasing={{}: (7, {})} | custom-call | flops 201326592 | bytes 7864320 | tf_op jit(solution)/shard_map/pallas_call | solution.py:188
  128.9 0.7 copy-done
  129.7 6.4 %shard_map.73 = bf16[1,512,6144]{2,1,0:T(8,128)(2,1)} custom-call(f32[48]{0:T(128)} %bitcast.33, bf16[1,512,6144]{2,1,0:T(8,128)(2,1)} %collective-permute-done.3.x_ref, bf16[1,512,6144]{2,1,0:T(8,128)(2,1)} %get-tuple-element.19.q_ref, f32[1,512,6144]{2,1,0:T(8,128)} %get-tuple-element.20.l_ref, ...), custom_call_target="tpu_custom_call", output_to_operand_aliasing={{}: (7, {})} | custom-call | flops 201326592 | bytes 7864320 | tf_op jit(solution)/shard_map/pallas_call | solution.py:188
  (24 shorter events, 0.1 us)
Async XLA Ops:
  1.6 6.1 %copy-start.5 = (f32[1,3,6144]{2,1,0:T(4,128)}, f32[1,3,6144]{2,1,0:T(4,128)S(1)}, u32[]{:S(2)}) copy-start(f32[1,3,6144]{2,1,0:T(4,128)S(1)} %copy.10.g_ref) | copy-start | bytes 221188
  1.6 6.1 %collective-permute-start = (f32[1,3,6144]{2,1,0:T(4,128)S(1)}, f32[1,3,6144]{2,1,0:T(4,128)S(1)}, u32[]{:S(2)}, u32[]{:S(2)}) collective-permute-start(f32[1,3,6144]{2,1,0:T(4,128)S(1)} %copy.10.g_ref), channel_id=1, source_target_pairs={{0,16},{16,32},{32,48},{48,64},{64,80},{80,96},{96,112},{112,0},{1... | collective-permute-start | bytes 221192 | tf_op jit(solution)/shard_map/ppermute | solution.py:216
  1.6 6.0 %collective-permute-start.1 = (f32[1,6144]{1,0:T(1,128)}, f32[1,6144]{1,0:T(1,128)S(1)}, u32[]{:S(2)}, u32[]{:S(2)}) collective-permute-start(f32[1,6144]{1,0:T(1,128)} %param.7), channel_id=1, source_target_pairs={{0,16},{16,32},{32,48},{48,64},{64,80},{80,96},{96,112},{112,0},{1... | collective-permute-start | bytes 73736 | tf_op jit(solution)/shard_map/ppermute | solution.py:216
  3.3 4.3 %collective-permute-start.2 = (f32[1,48]{1,0:T(1,128)}, f32[1,48]{1,0:T(1,128)S(1)}, u32[]{:S(2)}, u32[]{:S(2)}) collective-permute-start(f32[1,48]{1,0:T(1,128)} %param.8), channel_id=1, source_target_pairs={{0,16},{16,32},{32,48},{48,64},{64,80},{80,96},{96,112},{112,0},{1... | collective-permute-start | bytes 584 | tf_op jit(solution)/shard_map/ppermute | solution.py:216
  7.6 13.0 %copy-start.6 = (f32[1,48]{1,0:T(1,128)}, f32[1,48]{1,0:T(1,128)S(1)}, u32[]{:S(2)}) copy-start(f32[1,48]{1,0:T(1,128)S(1)} %collective-permute-done.2) | copy-start | bytes 580
  7.6 13.0 %copy-start.4 = (f32[1,6144]{1,0:T(1,128)}, f32[1,6144]{1,0:T(1,128)S(1)}, u32[]{:S(2)}) copy-start(f32[1,6144]{1,0:T(1,128)S(1)} %collective-permute-done.1.go_ref) | copy-start | bytes 73732
  7.7 13.0 %copy-start.8 = (f32[1,3,6144]{2,1,0:T(4,128)}, f32[1,3,6144]{2,1,0:T(4,128)S(1)}, u32[]{:S(2)}) copy-start(f32[1,3,6144]{2,1,0:T(4,128)S(1)} %collective-permute-done.g_ref) | copy-start | bytes 221188
  7.7 71.9 %collective-permute-start.3 = (bf16[1,512,6144]{2,1,0:T(8,128)(2,1)}, bf16[1,512,6144]{2,1,0:T(8,128)(2,1)}, u32[]{:S(2)}, u32[]{:S(2)}) collective-permute-start(bf16[1,512,6144]{2,1,0:T(8,128)(2,1)} %x_ref.1), channel_id=1, source_target_pairs={{0,16},{16,32},{32,48},{48,64},{64,80},{80,96},{96,112},{112,0},{1... | collective-permute-start | bytes 18874376 | tf_op jit(solution)/shard_map/ppermute | solution.py:222
  20.7 8.1 %copy-start.7 = (f32[1,48]{1,0:T(1,128)S(1)}, f32[1,48]{1,0:T(1,128)}, u32[]{:S(2)}) copy-start(f32[1,48]{1,0:T(1,128)} %param.8) | copy-start | bytes 580
  20.7 33.8 %all-to-all-start = ((bf16[48,128,128]{2,1,0:T(8,128)(2,1)}), bf16[48,128,128]{2,1,0:T(8,128)(2,1)S(1)}, u32[]{:S(2)}, u32[]{:S(2)}) async-start(bf16[48,128,128]{2,1,0:T(8,128)(2,1)} %shard_map.68), calls=%async_computation | async-start | bytes 3145728 | tf_op jit(solution)/shard_map/all_to_all | solution.py:225
  61.2 37.7 %all-to-all-start.1 = ((bf16[48,128,128]{2,1,0:T(8,128)(2,1)}), bf16[48,128,128]{2,1,0:T(8,128)(2,1)S(1)}, u32[]{:S(2)}, u32[]{:S(2)}) async-start(bf16[48,128,128]{2,1,0:T(8,128)(2,1)} %bitcast.8), calls=%async_computation.1 | async-start | bytes 3145728 | tf_op jit(solution)/shard_map/all_to_all | solution.py:250
  99.1 8.4 %collective-permute-start.7 = (bf16[12,128,128]{2,1,0:T(8,128)(2,1)S(1)}, bf16[12,128,128]{2,1,0:T(8,128)(2,1)S(1)}, u32[]{:S(2)}, u32[]{:S(2)}) collective-permute-start(bf16[12,128,128]{2,1,0:T(8,128)(2,1)S(1)} %get-tuple-element.26), channel_id=1, source_target_pairs={{0,16},{16,32},{32,48},{48,64},{64,80},{80,96},{96,112},{112,0},{1... | collective-permute-start | bytes 1179656 | tf_op jit(solution)/shard_map/ppermute | solution.py:258
  99.1 15.5 %collective-permute-start.6 = (bf16[12,128,128]{2,1,0:T(8,128)(2,1)S(1)}, bf16[12,128,128]{2,1,0:T(8,128)(2,1)S(1)}, u32[]{:S(2)}, u32[]{:S(2)}) collective-permute-start(bf16[12,128,128]{2,1,0:T(8,128)(2,1)S(1)} %get-tuple-element.27), channel_id=1, source_target_pairs={{0,16},{16,32},{32,48},{48,64},{64,80},{80,96},{96,112},{112,0},{1... | collective-permute-start | bytes 1179656 | tf_op jit(solution)/shard_map/ppermute | solution.py:258
  99.2 22.7 %collective-permute-start.5 = (bf16[12,128,128]{2,1,0:T(8,128)(2,1)S(1)}, bf16[12,128,128]{2,1,0:T(8,128)(2,1)S(1)}, u32[]{:S(2)}, u32[]{:S(2)}) collective-permute-start(bf16[12,128,128]{2,1,0:T(8,128)(2,1)S(1)} %get-tuple-element.28), channel_id=1, source_target_pairs={{0,16},{16,32},{32,48},{48,64},{64,80},{80,96},{96,112},{112,0},{1... | collective-permute-start | bytes 1179656 | tf_op jit(solution)/shard_map/ppermute | solution.py:258
  99.2 29.8 %collective-permute-start.4 = (bf16[12,128,128]{2,1,0:T(8,128)(2,1)S(1)}, bf16[12,128,128]{2,1,0:T(8,128)(2,1)S(1)}, u32[]{:S(2)}, u32[]{:S(2)}) collective-permute-start(bf16[12,128,128]{2,1,0:T(8,128)(2,1)S(1)} %get-tuple-element.29), channel_id=1, source_target_pairs={{0,16},{16,32},{32,48},{48,64},{64,80},{80,96},{96,112},{112,0},{1... | collective-permute-start | bytes 1179656 | tf_op jit(solution)/shard_map/ppermute | solution.py:258
  107.5 0.7 copy-start.3
  114.7 0.7 copy-start.2
  121.8 0.7 copy-start.1
  128.9 0.7 copy-start

commit v7 on v5

--- a/solution.py
+++ b/solution.py
@@ -13,8 +13,16 @@
 STATE_CHUNKS = 4
 
 
-def _silu(v):
-    return 0.5 * v * (1.0 + jnp.tanh(0.5 * v))
+def _silu_half(u):
+    return u + u * jnp.tanh(u)
+
+
+def _row_mean(v):
+    ones = jnp.full((v.shape[-1], v.shape[-1]), 1.0 / v.shape[-1], jnp.float32)
+    return lax.dot_general(
+        v, ones, (((1,), (0,)), ((), ())),
+        precision=lax.Precision.HIGHEST, preferred_element_type=jnp.float32,
+    )
 
 
 def _dot_nt(a, b):
@@ -42,11 +50,12 @@
         rate = jnp.full((1, 1), rates_ref[step * hg + hh], jnp.float32)
         cols = slice(hh * head_dim, (hh + 1) * head_dim)
         decay = jnp.exp(-rate * BLOCK)
+        half_k = 0.5 * g_ref[0, 1:2, cols]
         acc = None
         for b in range(nblocks):
             rows = slice(b * BLOCK, (b + 1) * BLOCK)
             x = x_ref[0, rows, cols].astype(jnp.float32)
-            keys_b = (_silu(x * g_ref[0, 1:2, cols]) * head_dim ** (-0.5)).astype(jnp.bfloat16)
+            keys_b = (_silu_half(x * half_k) * head_dim ** (-0.5)).astype(jnp.bfloat16)
             values_b = (x * g_ref[0, 2:3, cols]).astype(jnp.bfloat16)
             update = _block_state(keys_b, values_b, rate, pos)
             acc = update if acc is None else decay * acc + update
@@ -68,18 +77,20 @@
         mask = jnp.where(causal, lead * jnp.exp(rate * (pos_row + 1.0)), 0.0)
         decay = jnp.exp(-rate * BLOCK)
         state = s_ref[hh].astype(jnp.float32)
+        half_q = 0.5 * g_ref[0, 0:1, cols]
+        half_k = 0.5 * g_ref[0, 1:2, cols]
         for b in range(nblocks):
             rows = slice(b * BLOCK, (b + 1) * BLOCK)
             x = x_ref[0, rows, cols].astype(jnp.float32)
-            queries_b = _silu(x * g_ref[0, 0:1, cols]).astype(jnp.bfloat16)
-            keys_b = (_silu(x * g_ref[0, 1:2, cols]) * head_dim ** (-0.5)).astype(jnp.bfloat16)
+            queries_b = _silu_half(x * half_q).astype(jnp.bfloat16)
+            keys_b = (_silu_half(x * half_k) * head_dim ** (-0.5)).astype(jnp.bfloat16)
             values_b = (x * g_ref[0, 2:3, cols]).astype(jnp.bfloat16)
             scores = _dot_nt(queries_b, keys_b)
             weights = (scores * mask).astype(jnp.bfloat16)
             local = _dot(weights, values_b)
             cross = _dot(queries_b, state.astype(jnp.bfloat16))
             total = local + lead * cross
-            normed = total * lax.rsqrt(jnp.mean(total * total, axis=-1, keepdims=True) + EPSILON)
+            normed = total * lax.rsqrt(_row_mean(total * total) + EPSILON)
             o_ref[0, rows, cols] = (x + normed * go_ref[0:1, cols]).astype(o_ref.dtype)
             if b + 1 < nblocks:
                 state = decay * state + _block_state(keys_b, values_b, rate, pos)

time: 131 us -> 144 us (1.099)
  Pallas kernels: 43.6 us -> 57 us
    pallas_call x4, Pallas kernels: 30.6 us -> 44.4 us  [_outputs(): pl.pallas_call(kernel, grid_spec=pltpu.PrefetchScalarGridSpec(num_scalar_...]
  transfers between devices with their start and end apart: 10 -> 10, of which waited for: 4 -> 4; matrix products, arithmetic and copies ran while one was open for 7% -> 6% of each run, Pallas kernels for 28% -> 32%
where the time goes in v7:
time: 144 us; the launch traced here: 143 us
  Pallas kernels  57 us (40%)
  waiting for transfers between devices  56.4 us (39%)
  starting transfers between devices  17.5 us (12%)
  local copies, waits for them, and re-layouts  6.32 us (4%)
  matrix products  3.48 us (2%)
  other arithmetic  1.94 us (1%)
    pallas_call x4, Pallas kernels, _outputs(): pl.pallas_call(kernel, grid_spec=pltpu.PrefetchScalarGridSpec(num_scalar_...  44.4 us
    all_to_all x1, waiting for transfers between devices, on_device(): gathered = lax.all_to_all(summary, 'ctx', 0, 0, tiled=True)  27.4 us
    all_to_all x1, waiting for transfers between devices, on_device(): lax.all_to_all(prefixes.astype(jnp.bfloat16).reshape(heads, head_dim, hea...  13.4 us
    pallas_call x1, Pallas kernels, _summaries(): pl.pallas_call(kernel, grid_spec=pltpu.PrefetchScalarGridSpec(num_scalar_...  12.6 us
    ppermute x4, waiting for transfers between devices, on_device(): lax.ppermute((section_inputs, input_gains, out_gain, decay_rates), 'secti...  10.5 us
    all_to_all x1, starting transfers between devices, on_device(): gathered = lax.all_to_all(summary, 'ctx', 0, 0, tiled=True)  8.29 us
    ppermute x4, waiting for transfers between devices, on_device(): lax.ppermute(incoming[part * chunk:(part + 1) * chunk], 'section', pairs)  5.05 us
    unnamed x21, local copies, waits for them, and re-layouts  4.62 us
  transfers between devices with their start and end apart: 10, of which 4 were waited for; matrix products, arithmetic and copies ran while one was open for 6% of the time, Pallas kernels for 32%

profile of v7, /device:TPU:0, one launch (start us, length us, event | category | flops | bytes accessed | tf_op | source)
XLA Modules:
  0.0 143.4 jit_solution(9711207863634578826)
XLA Ops:
  0.6 0.0 collective-permute-start.3
  0.7 1.6 %copy.10.g_ref = f32[1,3,6144]{2,1,0:T(4,128)} copy(f32[1,3,6144]{2,0,1:T(1,128)} %param.6) | data formatting | bytes 147456 | tf_op args[1]
  2.2 12.6 %shard_map.68 = bf16[48,128,128]{2,1,0:T(8,128)(2,1)} custom-call(f32[48]{0:T(128)} %bitcast.33, bf16[1,512,6144]{2,1,0:T(8,128)(2,1)} %x_ref.1, f32[1,3,6144]{2,1,0:T(4,128)} %copy.10.g_ref), custom_call_target="tpu_custom_call" | custom-call | flops 805306368 | bytes 9437184 | tf_op jit(solution)/shard_map/pallas_call | solution.py:105
  14.8 8.3 %all-to-all-start = ((bf16[48,128,128]{2,1,0:T(8,128)(2,1)}), bf16[48,128,128]{2,1,0:T(8,128)(2,1)S(1)}, u32[]{:S(2)}, u32[]{:S(2)}) async-start(bf16[48,128,128]{2,1,0:T(8,128)(2,1)} %shard_map.68), calls=%async_computation | async-start | bytes 3145728 | tf_op jit(solution)/shard_map/all_to_all | solution.py:180
  23.2 0.1 exponential_bitcast_fusion.1
  23.3 0.1 multiply_exponential_fusion
  23.3 0.1 convert_maximum_fusion
  23.4 27.4 %all-to-all-done = bf16[48,128,128]{2,1,0:T(8,128)(2,1)S(1)} async-done(((bf16[48,128,128]{2,1,0:T(8,128)(2,1)}), bf16[48,128,128]{2,1,0:T(8,128)(2,1)S(1)}, u32[]{:S(2)}, u32[]{:S(2)}) %all-to-all-start) | async-done | bytes 1572896 | tf_op jit(solution)/shard_map/all_to_all | solution.py:180
  50.8 1.4 fusion.1
  52.2 1.7 %add_bitcast_fusion = (f32[1,3,128,128]{3,2,1,0:T(8,128)}, f32[3,128,128]{2,1,0:T(8,128)S(1)}) fusion(f32[3,128,128]{2,1,0:T(8,128)S(1)} %bitcast.28, f32[3]{0:T(128)S(1)} %get-tuple-element.18, f32[1,48,128,128]{3,2,1,0:T(8,128)} %param.9, s32[]{:T(128)S(6)} %select_n.8), kind=kLoop, calls=%fused_computation.5 | loop fusion | flops 98304 | bytes 786448 | tf_op jit(solution)/shard_map/broadcast_in_dim | solution.py:219
  53.9 2.1 %fusion = bf16[16,3,128,128]{3,0,2,1:T(8,128)(2,1)S(1)} fusion(f32[3,128,128]{2,1,0:T(8,128)S(1)} %get-tuple-element.11, f32[16,3]{0,1:T(4,128)S(1)} %get-tuple-element.16, bf16[16,3,128,128]{3,2,1,0:T(8,128)(2,1)S(1)} %bitcast.27, f32[16,16]{1,0:T(8,128)S(1)} %convert_maximum_fusion, f32[3]{0:T(128)S(1)} %get-tuple-element.19, ...), kind=kOutput, calls=%fused_computation.1 | convolution fusion | flops 153355776 | bytes 3343820 | tf_op jit(solution)/shard_map/tsh,shde->thde/dot_general | solution.py:195
  56.0 1.6 %copy.13 = bf16[16,3,128,128]{3,2,1,0:T(8,128)(2,1)} copy(bf16[16,3,128,128]{3,0,2,1:T(8,128)(2,1)S(1)} %fusion) | data formatting | bytes 3145728 | tf_op jit(solution)/shard_map/convert_element_type | solution.py:205
  57.6 4.0 %all-to-all-start.1 = ((bf16[48,128,128]{2,1,0:T(8,128)(2,1)}), bf16[48,128,128]{2,1,0:T(8,128)(2,1)S(1)}, u32[]{:S(2)}, u32[]{:S(2)}) async-start(bf16[48,128,128]{2,1,0:T(8,128)(2,1)} %bitcast.7), calls=%async_computation.1 | async-start | bytes 3145728 | tf_op jit(solution)/shard_map/all_to_all | solution.py:204
  61.6 0.2 collective-permute-start
  61.8 1.4 %collective-permute-start.1 = (f32[1,6144]{1,0:T(1,128)S(1)}, f32[1,6144]{1,0:T(1,128)S(1)}, u32[]{:S(2)}, u32[]{:S(2)}) collective-permute-start(f32[1,6144]{1,0:T(1,128)S(1)} %copy-done.9), channel_id=1, source_target_pairs={{0,16},{16,32},{32,48},{48,64},{64,80},{80,96},{96,112},{112,0},{1... | collective-permute-start | bytes 73736 | tf_op jit(solution)/shard_map/ppermute | solution.py:175
  63.2 0.2 collective-permute-start.2
  63.4 10.5 %collective-permute-done.2 = f32[1,48]{1,0:T(1,128)S(1)} collective-permute-done((f32[1,48]{1,0:T(1,128)S(1)}, f32[1,48]{1,0:T(1,128)S(1)}, u32[]{:S(2)}, u32[]{:S(2)}) %collective-permute-start.2) | collective-permute-done | bytes 224 | tf_op jit(solution)/shard_map/ppermute | solution.py:175
  73.9 13.4 %all-to-all-done.1 = bf16[48,128,128]{2,1,0:T(8,128)(2,1)S(1)} async-done(((bf16[48,128,128]{2,1,0:T(8,128)(2,1)}), bf16[48,128,128]{2,1,0:T(8,128)(2,1)S(1)}, u32[]{:S(2)}, u32[]{:S(2)}) %all-to-all-start.1) | async-done | bytes 1572896 | tf_op jit(solution)/shard_map/all_to_all | solution.py:204
  87.3 0.1 fusion.14
  87.5 0.0 collective-permute-start.7
  87.5 1.6 %collective-permute-start.6 = (bf16[12,128,128]{2,1,0:T(8,128)(2,1)S(1)}, bf16[12,128,128]{2,1,0:T(8,128)(2,1)S(1)}, u32[]{:S(2)}, u32[]{:S(2)}) collective-permute-start(bf16[12,128,128]{2,1,0:T(8,128)(2,1)S(1)} %get-tuple-element.13), channel_id=1, source_target_pairs={{0,16},{16,32},{32,48},{48,64},{64,80},{80,96},{96,112},{112,0},{1... | collective-permute-start | bytes 1179656 | tf_op jit(solution)/shard_map/ppermute | solution.py:214
  89.1 0.0 collective-permute-start.5
  89.2 1.7 %collective-permute-start.4 = (bf16[12,128,128]{2,1,0:T(8,128)(2,1)S(1)}, bf16[12,128,128]{2,1,0:T(8,128)(2,1)S(1)}, u32[]{:S(2)}, u32[]{:S(2)}) collective-permute-start(bf16[12,128,128]{2,1,0:T(8,128)(2,1)S(1)} %get-tuple-element.15), channel_id=1, source_target_pairs={{0,16},{16,32},{32,48},{48,64},{64,80},{80,96},{96,112},{112,0},{1... | collective-permute-start | bytes 1179656 | tf_op jit(solution)/shard_map/ppermute | solution.py:214
  90.9 5.0 %collective-permute-done.7.s_ref = bf16[12,128,128]{2,1,0:T(8,128)(2,1)S(1)} collective-permute-done((bf16[12,128,128]{2,1,0:T(8,128)(2,1)S(1)}, bf16[12,128,128]{2,1,0:T(8,128)(2,1)S(1)}, u32[]{:S(2)}, u32[]{:S(2)}) %collective-permute-start.7) | collective-permute-done | bytes 393248 | tf_op jit(solution)/shard_map/ppermute | solution.py:214
  96.0 0.8 copy-done.2
  96.7 11.1 %shard_map.69.rest_0_ = bf16[1,512,6144]{2,1,0:T(8,128)(2,1)} custom-call(f32[48]{0:T(128)} %bitcast.29, bf16[1,512,6144]{2,1,0:T(8,128)(2,1)} %collective-permute-done.3.x_ref, f32[1,3,6144]{2,1,0:T(4,128)} %copy-done, f32[1,6144]{1,0:T(1,128)} %copy-done.6, bf16[12,128,128]{2,1,0:T(8,128)(2,1)} %copy-done.2), custom_call_target="tpu_custom_call" | custom-call | flops 1610612736 | bytes 3538944 | tf_op jit(solution)/shard_map/pallas_call | solution.py:147
  107.8 0.8 copy-done.5
  108.5 11.1 %shard_map.70.rest_0_ = bf16[1,512,6144]{2,1,0:T(8,128)(2,1)} custom-call(f32[48]{0:T(128)} %bitcast.30, bf16[1,512,6144]{2,1,0:T(8,128)(2,1)} %collective-permute-done.3.x_ref, f32[1,3,6144]{2,1,0:T(4,128)} %copy-done, f32[1,6144]{1,0:T(1,128)} %copy-done.6, bf16[12,128,128]{2,1,0:T(8,128)(2,1)} %copy-done.5, ...), custom_call_target="tpu_custom_call", output_to_operand_aliasing={{}: (5, {})} | custom-call | flops 1610612736 | bytes 3538944 | tf_op jit(solution)/shard_map/pallas_call | solution.py:147
  119.7 0.8 copy-done.4
  120.4 11.1 %shard_map.71.rest_0_ = bf16[1,512,6144]{2,1,0:T(8,128)(2,1)} custom-call(f32[48]{0:T(128)} %bitcast.31, bf16[1,512,6144]{2,1,0:T(8,128)(2,1)} %collective-permute-done.3.x_ref, f32[1,3,6144]{2,1,0:T(4,128)} %copy-done, f32[1,6144]{1,0:T(1,128)} %copy-done.6, bf16[12,128,128]{2,1,0:T(8,128)(2,1)} %copy-done.4, ...), custom_call_target="tpu_custom_call", output_to_operand_aliasing={{}: (5, {})} | custom-call | flops 1610612736 | bytes 3538944 | tf_op jit(solution)/shard_map/pallas_call | solution.py:147
  131.5 0.8 copy-done.3
  132.3 11.1 %shard_map.72 = bf16[1,512,6144]{2,1,0:T(8,128)(2,1)} custom-call(f32[48]{0:T(128)} %bitcast.32, bf16[1,512,6144]{2,1,0:T(8,128)(2,1)} %collective-permute-done.3.x_ref, f32[1,3,6144]{2,1,0:T(4,128)} %copy-done, f32[1,6144]{1,0:T(1,128)} %copy-done.6, bf16[12,128,128]{2,1,0:T(8,128)(2,1)} %copy-done.3, ...), custom_call_target="tpu_custom_call", output_to_operand_aliasing={{}: (5, {})} | custom-call | flops 1610612736 | bytes 3538944 | tf_op jit(solution)/shard_map/pallas_call | solution.py:147
  (25 shorter events, 0.1 us)
Async XLA Ops:
  0.6 95.3 %collective-permute-start.3 = (bf16[1,512,6144]{2,1,0:T(8,128)(2,1)}, bf16[1,512,6144]{2,1,0:T(8,128)(2,1)}, u32[]{:S(2)}, u32[]{:S(2)}) collective-permute-start(bf16[1,512,6144]{2,1,0:T(8,128)(2,1)} %x_ref.1), channel_id=1, source_target_pairs={{0,16},{16,32},{32,48},{48,64},{64,80},{80,96},{96,112},{112,0},{1... | collective-permute-start | bytes 18874376 | tf_op jit(solution)/shard_map/ppermute | solution.py:175
  14.8 8.3 %copy-start.8 = (f32[1,48]{1,0:T(1,128)S(1)}, f32[1,48]{1,0:T(1,128)}, u32[]{:S(2)}) copy-start(f32[1,48]{1,0:T(1,128)} %param.8) | copy-start | bytes 580
  14.8 36.0 %all-to-all-start = ((bf16[48,128,128]{2,1,0:T(8,128)(2,1)}), bf16[48,128,128]{2,1,0:T(8,128)(2,1)S(1)}, u32[]{:S(2)}, u32[]{:S(2)}) async-start(bf16[48,128,128]{2,1,0:T(8,128)(2,1)} %shard_map.68), calls=%async_computation | async-start | bytes 3145728 | tf_op jit(solution)/shard_map/all_to_all | solution.py:180
  57.6 4.0 %copy-start.1 = (f32[1,3,6144]{2,1,0:T(4,128)S(1)}, f32[1,3,6144]{2,1,0:T(4,128)}, u32[]{:S(2)}) copy-start(f32[1,3,6144]{2,1,0:T(4,128)} %copy.10.g_ref) | copy-start | bytes 221188
  57.6 4.2 %copy-start.9 = (f32[1,6144]{1,0:T(1,128)S(1)}, f32[1,6144]{1,0:T(1,128)}, u32[]{:S(2)}) copy-start(f32[1,6144]{1,0:T(1,128)} %param.7) | copy-start | bytes 73732
  57.6 29.8 %all-to-all-start.1 = ((bf16[48,128,128]{2,1,0:T(8,128)(2,1)}), bf16[48,128,128]{2,1,0:T(8,128)(2,1)S(1)}, u32[]{:S(2)}, u32[]{:S(2)}) async-start(bf16[48,128,128]{2,1,0:T(8,128)(2,1)} %bitcast.7), calls=%async_computation.1 | async-start | bytes 3145728 | tf_op jit(solution)/shard_map/all_to_all | solution.py:204
  61.6 12.3 %collective-permute-start = (f32[1,3,6144]{2,1,0:T(4,128)S(1)}, f32[1,3,6144]{2,1,0:T(4,128)S(1)}, u32[]{:S(2)}, u32[]{:S(2)}) collective-permute-start(f32[1,3,6144]{2,1,0:T(4,128)S(1)} %copy-done.1), channel_id=1, source_target_pairs={{0,16},{16,32},{32,48},{48,64},{64,80},{80,96},{96,112},{112,0},{1... | collective-permute-start | bytes 221192 | tf_op jit(solution)/shard_map/ppermute | solution.py:175
  61.8 12.1 %collective-permute-start.1 = (f32[1,6144]{1,0:T(1,128)S(1)}, f32[1,6144]{1,0:T(1,128)S(1)}, u32[]{:S(2)}, u32[]{:S(2)}) collective-permute-start(f32[1,6144]{1,0:T(1,128)S(1)} %copy-done.9), channel_id=1, source_target_pairs={{0,16},{16,32},{32,48},{48,64},{64,80},{80,96},{96,112},{112,0},{1... | collective-permute-start | bytes 73736 | tf_op jit(solution)/shard_map/ppermute | solution.py:175
  63.2 10.7 %collective-permute-start.2 = (f32[1,48]{1,0:T(1,128)S(1)}, f32[1,48]{1,0:T(1,128)S(1)}, u32[]{:S(2)}, u32[]{:S(2)}) collective-permute-start(f32[1,48]{1,0:T(1,128)S(1)} %copy-done.8), channel_id=1, source_target_pairs={{0,16},{16,32},{32,48},{48,64},{64,80},{80,96},{96,112},{112,0},{1... | collective-permute-start | bytes 584 | tf_op jit(solution)/shard_map/ppermute | solution.py:175
  73.9 13.6 %copy-start.7 = (f32[1,48]{1,0:T(1,128)}, f32[1,48]{1,0:T(1,128)S(1)}, u32[]{:S(2)}) copy-start(f32[1,48]{1,0:T(1,128)S(1)} %collective-permute-done.2) | copy-start | bytes 580
  73.9 13.6 %copy-start.6 = (f32[1,6144]{1,0:T(1,128)}, f32[1,6144]{1,0:T(1,128)S(1)}, u32[]{:S(2)}) copy-start(f32[1,6144]{1,0:T(1,128)S(1)} %collective-permute-done.1.go_ref) | copy-start | bytes 73732
  73.9 13.6 %copy-start = (f32[1,3,6144]{2,1,0:T(4,128)}, f32[1,3,6144]{2,1,0:T(4,128)S(1)}, u32[]{:S(2)}) copy-start(f32[1,3,6144]{2,1,0:T(4,128)S(1)} %collective-permute-done.g_ref) | copy-start | bytes 221188
  87.5 8.4 %collective-permute-start.7 = (bf16[12,128,128]{2,1,0:T(8,128)(2,1)S(1)}, bf16[12,128,128]{2,1,0:T(8,128)(2,1)S(1)}, u32[]{:S(2)}, u32[]{:S(2)}) collective-permute-start(bf16[12,128,128]{2,1,0:T(8,128)(2,1)S(1)} %get-tuple-element.12), channel_id=1, source_target_pairs={{0,16},{16,32},{32,48},{48,64},{64,80},{80,96},{96,112},{112,0},{1... | collective-permute-start | bytes 1179656 | tf_op jit(solution)/shard_map/ppermute | solution.py:214
  87.5 20.2 %collective-permute-start.6 = (bf16[12,128,128]{2,1,0:T(8,128)(2,1)S(1)}, bf16[12,128,128]{2,1,0:T(8,128)(2,1)S(1)}, u32[]{:S(2)}, u32[]{:S(2)}) collective-permute-start(bf16[12,128,128]{2,1,0:T(8,128)(2,1)S(1)} %get-tuple-element.13), channel_id=1, source_target_pairs={{0,16},{16,32},{32,48},{48,64},{64,80},{80,96},{96,112},{112,0},{1... | collective-permute-start | bytes 1179656 | tf_op jit(solution)/shard_map/ppermute | solution.py:214
  89.1 30.5 %collective-permute-start.5 = (bf16[12,128,128]{2,1,0:T(8,128)(2,1)S(1)}, bf16[12,128,128]{2,1,0:T(8,128)(2,1)S(1)}, u32[]{:S(2)}, u32[]{:S(2)}) collective-permute-start(bf16[12,128,128]{2,1,0:T(8,128)(2,1)S(1)} %get-tuple-element.14), channel_id=1, source_target_pairs={{0,16},{16,32},{32,48},{48,64},{64,80},{80,96},{96,112},{112,0},{1... | collective-permute-start | bytes 1179656 | tf_op jit(solution)/shard_map/ppermute | solution.py:214
  89.2 42.4 %collective-permute-start.4 = (bf16[12,128,128]{2,1,0:T(8,128)(2,1)S(1)}, bf16[12,128,128]{2,1,0:T(8,128)(2,1)S(1)}, u32[]{:S(2)}, u32[]{:S(2)}) collective-permute-start(bf16[12,128,128]{2,1,0:T(8,128)(2,1)S(1)} %get-tuple-element.15), channel_id=1, source_target_pairs={{0,16},{16,32},{32,48},{48,64},{64,80},{80,96},{96,112},{112,0},{1... | collective-permute-start | bytes 1179656 | tf_op jit(solution)/shard_map/ppermute | solution.py:214
  95.9 0.8 copy-start.2
  107.8 0.8 copy-start.5
  119.7 0.8 copy-start.4
  131.5 0.8 copy-start.3

commit v8 on v5

--- a/solution.py
+++ b/solution.py
@@ -85,6 +85,45 @@
                 state = decay * state + _block_state(keys_b, values_b, rate, pos)
 
 
+def _scan_kernel(place_ref, rates_ref, s_ref, c_ref, p_ref, e_ref, *, count, own, sources):
+    for hh in range(own):
+        rate = jnp.full((1, 1), rates_ref[place_ref[0] * own + hh], jnp.float32)
+        decay = jnp.exp(-rate * count)
+        state = c_ref[0, hh]
+        for c in range(sources):
+            p_ref[c, hh] = state.astype(p_ref.dtype)
+            state = decay * state + s_ref[c, hh].astype(jnp.float32)
+        e_ref[0, hh] = state
+
+
+def _scan(place, rates, gathered, carry, count):
+    sources, own, hd, _ = gathered.shape
+    kernel = functools.partial(_scan_kernel, count=count, own=own, sources=sources)
+    return pl.pallas_call(
+        kernel,
+        grid_spec=pltpu.PrefetchScalarGridSpec(
+            num_scalar_prefetch=2,
+            grid=(1,),
+            in_specs=[
+                pl.BlockSpec((sources, own, hd, hd), lambda i, p, r: (0, 0, 0, 0)),
+                pl.BlockSpec((1, own, hd, hd), lambda i, p, r: (0, p[0], 0, 0)),
+            ],
+            out_specs=[
+                pl.BlockSpec((sources, own, hd, hd), lambda i, p, r: (0, 0, 0, 0)),
+                pl.BlockSpec((1, own, hd, hd), lambda i, p, r: (0, 0, 0, 0)),
+            ],
+        ),
+        out_shape=[
+            jax.ShapeDtypeStruct(gathered.shape, gathered.dtype),
+            jax.ShapeDtypeStruct((1, own, hd, hd), jnp.float32),
+        ],
+        cost_estimate=pl.CostEstimate(
+            flops=2 * gathered.size, transcendentals=0,
+            bytes_accessed=4 * gathered.size + 8 * own * hd * hd,
+        ),
+    )(place, rates, gathered, carry)
+
+
 def _summaries(rates, rows, gains, head_dim):
     _, count, width = rows.shape
     heads = width // head_dim
@@ -167,32 +206,12 @@
 
     summary = _summaries(rates, section_inputs, input_gains, head_dim)
     gathered = lax.all_to_all(summary, "ctx", 0, 0, tiled=True)
-    gathered = gathered.astype(jnp.float32).reshape(group_size, own_heads, head_dim, head_dim)
-
-    start = place * own_heads
-    carry_part = lax.dynamic_slice_in_dim(carry_state[0], start, own_heads, 0)
-    rate_part = lax.dynamic_slice_in_dim(rates, start, own_heads, 0)
-    target = jnp.arange(group_size)[:, None]
-    source = jnp.arange(group_size)[None, :]
-    gap = (target - 1 - source).astype(jnp.float32)
-    weights = jnp.where(
-        (source < target)[:, :, None],
-        jnp.exp(-rate_part[None, None, :] * count * jnp.maximum(gap, 0.0)[:, :, None]),
-        0.0,
-    )
-    carry_weights = jnp.exp(-rate_part[None, :] * count * target.astype(jnp.float32))
-    prefixes = jnp.einsum(
-        "tsh,shde->thde", weights, gathered, precision=lax.Precision.HIGHEST
-    ) + carry_weights[:, :, None, None] * carry_part[None]
-    end_weights = jnp.exp(
-        -rate_part[None, :] * count * (group_size - 1 - source[0]).astype(jnp.float32)[:, None]
-    )
-    end_part = jnp.einsum(
-        "sh,shde->hde", end_weights, gathered, precision=lax.Precision.HIGHEST
-    ) + jnp.exp(-rate_part * count * group_size)[:, None, None] * carry_part
+    gathered = gathered.reshape(group_size, own_heads, head_dim, head_dim)
+    prefixes, end_part = _scan(
+        place.reshape(1).astype(jnp.int32), rates, gathered, carry_state, count
+    )
     incoming = lax.all_to_all(
-        prefixes.astype(jnp.bfloat16).reshape(heads, head_dim, head_dim),
-        "ctx", 0, 0, tiled=True,
+        prefixes.reshape(heads, head_dim, head_dim), "ctx", 0, 0, tiled=True
     )
     prev_gains, prev_gain_out, prev_rates, incoming = lax.optimization_barrier(
         (prev_gains, prev_gain_out, prev_rates, incoming)
@@ -205,7 +224,7 @@
             prev_rates[0], prev_rows, prev_gains, prev_gain_out, piece, head_dim,
             part * chunk, next_rows,
         )
-    return (next_rows, end_part[None])
+    return (next_rows, end_part)
 
 
 def solution(mesh):

time: 131 us -> 129 us (0.985)
  Pallas kernels: 43.6 us -> 47.2 us
  matrix products: 3.49 us -> 0 us
  other arithmetic: 1.94 us -> 0 us
    pallas_call x0 -> x1, Pallas kernels: none -> 3.64 us  [_scan(): pl.pallas_call(kernel, grid_spec=pltpu.PrefetchScalarGridSpec(num_scalar_...]
    dot_general x2 -> x0, matrix products: 3.49 us -> none  [the longest x1 2.09 us: on_device(): jnp.einsum('tsh,shde->thde', weights, gathered, precision=lax.Precision.H...]
    ppermute x4, waiting for transfers between devices: 10.2 us -> 12.4 us  [on_device(): lax.ppermute((section_inputs, input_gains, out_gain, decay_rates), 'secti...]
    all_to_all x1, waiting for transfers between devices: 13.8 us -> 11.7 us  [on_device(): lax.all_to_all(prefixes.reshape(heads, head_dim, head_dim), 'ctx', 0, 0,...]
    broadcast_in_dim x1 -> x0, other arithmetic: 1.7 us -> none  [on_device(): return (next_rows, end_part[None])]
    convert_element_type x1 -> x0, local copies, waits for them, and re-layouts: 1.55 us -> none  [on_device(): prefixes.astype(jnp.bfloat16).reshape(heads, head_dim, head_dim)]
    unnamed x21 -> x23, local copies, waits for them, and re-layouts: 4.62 us -> 5.78 us
  transfers between devices with their start and end apart: 10 -> 10, of which waited for: 4 -> 4; matrix products, arithmetic and copies ran while one was open for 7% -> 1% of each run, Pallas kernels for 28% -> 31%
where the time goes in v8:
time: 129 us; the launch traced here: 128 us
  waiting for transfers between devices  56.8 us (44%)
  Pallas kernels  47.2 us (37%)
  starting transfers between devices  17.2 us (13%)
  local copies, waits for them, and re-layouts  5.93 us (5%)
    pallas_call x4, Pallas kernels, _outputs(): pl.pallas_call(kernel, grid_spec=pltpu.PrefetchScalarGridSpec(num_scalar_...  30.6 us
    all_to_all x1, waiting for transfers between devices, on_device(): gathered = lax.all_to_all(summary, 'ctx', 0, 0, tiled=True)  27.7 us
    pallas_call x1, Pallas kernels, _summaries(): pl.pallas_call(kernel, grid_spec=pltpu.PrefetchScalarGridSpec(num_scalar_...  13 us
    ppermute x4, waiting for transfers between devices, on_device(): lax.ppermute((section_inputs, input_gains, out_gain, decay_rates), 'secti...  12.4 us
    all_to_all x1, waiting for transfers between devices, on_device(): lax.all_to_all(prefixes.reshape(heads, head_dim, head_dim), 'ctx', 0, 0,...  11.7 us
    all_to_all x1, starting transfers between devices, on_device(): gathered = lax.all_to_all(summary, 'ctx', 0, 0, tiled=True)  8.3 us
    unnamed x23, local copies, waits for them, and re-layouts  5.78 us
    ppermute x4, waiting for transfers between devices, on_device(): lax.ppermute(incoming[part * chunk:(part + 1) * chunk], 'section', pairs)  5.06 us
  transfers between devices with their start and end apart: 10, of which 4 were waited for; matrix products, arithmetic and copies ran while one was open for 1% of the time, Pallas kernels for 31%

profile of v8, /device:TPU:0, one launch (start us, length us, event | category | flops | bytes accessed | tf_op | source)
XLA Modules:
  0.0 127.9 jit_solution(4580780695248937015)
XLA Ops:
  0.6 0.0 collective-permute-start.3
  0.7 1.6 %copy.10.g_ref = f32[1,3,6144]{2,1,0:T(4,128)} copy(f32[1,3,6144]{2,0,1:T(1,128)} %param.6) | data formatting | bytes 147456 | tf_op args[1]
  2.2 13.0 %shard_map.68 = bf16[48,128,128]{2,1,0:T(8,128)(2,1)} custom-call(f32[48]{0:T(128)} %bitcast.11, bf16[1,512,6144]{2,1,0:T(8,128)(2,1)} %x_ref.1, f32[1,3,6144]{2,1,0:T(4,128)} %copy.10.g_ref), custom_call_target="tpu_custom_call" | custom-call | flops 805306368 | bytes 9437184 | tf_op jit(solution)/shard_map/pallas_call | solution.py:133
  15.2 8.3 %all-to-all-start = ((bf16[48,128,128]{2,1,0:T(8,128)(2,1)}), bf16[48,128,128]{2,1,0:T(8,128)(2,1)S(1)}, u32[]{:S(2)}, u32[]{:S(2)}) async-start(bf16[48,128,128]{2,1,0:T(8,128)(2,1)} %shard_map.68), calls=%async_computation | async-start | bytes 3145728 | tf_op jit(solution)/shard_map/all_to_all | solution.py:208
  23.5 27.7 %all-to-all-done = bf16[48,128,128]{2,1,0:T(8,128)(2,1)S(1)} async-done(((bf16[48,128,128]{2,1,0:T(8,128)(2,1)}), bf16[48,128,128]{2,1,0:T(8,128)(2,1)S(1)}, u32[]{:S(2)}, u32[]{:S(2)}) %all-to-all-start) | async-done | bytes 1572896 | tf_op jit(solution)/shard_map/all_to_all | solution.py:208
  51.2 1.1 copy-done
  52.3 3.6 %shard_map.69 = (bf16[16,3,128,128]{3,2,1,0:T(8,128)(2,1)}, f32[1,3,128,128]{3,2,1,0:T(8,128)}) custom-call(s32[1]{0:T(128)} %bitcast.place_ref, f32[48]{0:T(128)} %bitcast.12, bf16[16,3,128,128]{3,2,1,0:T(8,128)(2,1)} %bitcast.5, f32[1,48,128,128]{3,2,1,0:T(8,128)} %c_ref.1), custom_call_target="tpu_custom_call" | custom-call | flops 1572864 | bytes 3538944 | tf_op jit(solution)/shard_map/pallas_call | solution.py:102
  56.0 3.7 %all-to-all-start.1 = ((bf16[48,128,128]{2,1,0:T(8,128)(2,1)}), bf16[48,128,128]{2,1,0:T(8,128)(2,1)S(1)}, u32[]{:S(2)}, u32[]{:S(2)}) async-start(bf16[48,128,128]{2,1,0:T(8,128)(2,1)} %bitcast.6), calls=%async_computation.1 | async-start | bytes 3145728 | tf_op jit(solution)/shard_map/all_to_all | solution.py:213
  59.7 0.2 collective-permute-start
  59.9 1.4 %collective-permute-start.1 = (f32[1,6144]{1,0:T(1,128)S(1)}, f32[1,6144]{1,0:T(1,128)S(1)}, u32[]{:S(2)}, u32[]{:S(2)}) collective-permute-start(f32[1,6144]{1,0:T(1,128)S(1)} %copy-done.10), channel_id=1, source_target_pairs={{0,16},{16,32},{32,48},{48,64},{64,80},{80,96},{96,112},{112,0},{1... | collective-permute-start | bytes 73736 | tf_op jit(solution)/shard_map/ppermute | solution.py:203
  61.3 0.2 collective-permute-start.2
  61.5 12.4 %collective-permute-done.2 = f32[1,48]{1,0:T(1,128)S(1)} collective-permute-done((f32[1,48]{1,0:T(1,128)S(1)}, f32[1,48]{1,0:T(1,128)S(1)}, u32[]{:S(2)}, u32[]{:S(2)}) %collective-permute-start.2) | collective-permute-done | bytes 224 | tf_op jit(solution)/shard_map/ppermute | solution.py:203
  73.9 0.0 collective-permute-done.1.go_ref
  73.9 0.0 collective-permute-done.g_ref
  73.9 11.7 %all-to-all-done.1 = bf16[48,128,128]{2,1,0:T(8,128)(2,1)S(1)} async-done(((bf16[48,128,128]{2,1,0:T(8,128)(2,1)}), bf16[48,128,128]{2,1,0:T(8,128)(2,1)S(1)}, u32[]{:S(2)}, u32[]{:S(2)}) %all-to-all-start.1) | async-done | bytes 1572896 | tf_op jit(solution)/shard_map/all_to_all | solution.py:213
  85.6 0.1 fusion
  85.8 0.0 collective-permute-start.7
  85.8 1.6 %collective-permute-start.6 = (bf16[12,128,128]{2,1,0:T(8,128)(2,1)S(1)}, bf16[12,128,128]{2,1,0:T(8,128)(2,1)S(1)}, u32[]{:S(2)}, u32[]{:S(2)}) collective-permute-start(bf16[12,128,128]{2,1,0:T(8,128)(2,1)S(1)} %get-tuple-element.15), channel_id=1, source_target_pairs={{0,16},{16,32},{32,48},{48,64},{64,80},{80,96},{96,112},{112,0},{1... | collective-permute-start | bytes 1179656 | tf_op jit(solution)/shard_map/ppermute | solution.py:222
  87.4 0.0 collective-permute-start.5
  87.4 1.7 %collective-permute-start.4 = (bf16[12,128,128]{2,1,0:T(8,128)(2,1)S(1)}, bf16[12,128,128]{2,1,0:T(8,128)(2,1)S(1)}, u32[]{:S(2)}, u32[]{:S(2)}) collective-permute-start(bf16[12,128,128]{2,1,0:T(8,128)(2,1)S(1)} %get-tuple-element.17), channel_id=1, source_target_pairs={{0,16},{16,32},{32,48},{48,64},{64,80},{80,96},{96,112},{112,0},{1... | collective-permute-start | bytes 1179656 | tf_op jit(solution)/shard_map/ppermute | solution.py:222
  89.1 5.1 %collective-permute-done.7.s_ref = bf16[12,128,128]{2,1,0:T(8,128)(2,1)S(1)} collective-permute-done((bf16[12,128,128]{2,1,0:T(8,128)(2,1)S(1)}, bf16[12,128,128]{2,1,0:T(8,128)(2,1)S(1)}, u32[]{:S(2)}, u32[]{:S(2)}) %collective-permute-start.7) | collective-permute-done | bytes 393248 | tf_op jit(solution)/shard_map/ppermute | solution.py:222
  94.2 0.0 collective-permute-done.3.x_ref
  94.2 0.7 copy-done.3
  94.9 7.6 %shard_map.70.rest_0_ = bf16[1,512,6144]{2,1,0:T(8,128)(2,1)} custom-call(f32[48]{0:T(128)} %bitcast.7, bf16[1,512,6144]{2,1,0:T(8,128)(2,1)} %collective-permute-done.3.x_ref, f32[1,3,6144]{2,1,0:T(4,128)} %copy-done.1, f32[1,6144]{1,0:T(1,128)} %copy-done.7, bf16[12,128,128]{2,1,0:T(8,128)(2,1)} %copy-done.3), custom_call_target="tpu_custom_call" | custom-call | flops 1610612736 | bytes 3538944 | tf_op jit(solution)/shard_map/pallas_call | solution.py:175
  102.6 0.8 copy-done.6
  103.4 7.7 %shard_map.71.rest_0_ = bf16[1,512,6144]{2,1,0:T(8,128)(2,1)} custom-call(f32[48]{0:T(128)} %bitcast.8, bf16[1,512,6144]{2,1,0:T(8,128)(2,1)} %collective-permute-done.3.x_ref, f32[1,3,6144]{2,1,0:T(4,128)} %copy-done.1, f32[1,6144]{1,0:T(1,128)} %copy-done.7, bf16[12,128,128]{2,1,0:T(8,128)(2,1)} %copy-done.6, ...), custom_call_target="tpu_custom_call", output_to_operand_aliasing={{}: (5, {})} | custom-call | flops 1610612736 | bytes 3538944 | tf_op jit(solution)/shard_map/pallas_call | solution.py:175
  111.0 0.0 collective-permute-done.5.s_ref
  111.0 0.8 copy-done.5
  111.8 7.7 %shard_map.72.rest_0_ = bf16[1,512,6144]{2,1,0:T(8,128)(2,1)} custom-call(f32[48]{0:T(128)} %bitcast.9, bf16[1,512,6144]{2,1,0:T(8,128)(2,1)} %collective-permute-done.3.x_ref, f32[1,3,6144]{2,1,0:T(4,128)} %copy-done.1, f32[1,6144]{1,0:T(1,128)} %copy-done.7, bf16[12,128,128]{2,1,0:T(8,128)(2,1)} %copy-done.5, ...), custom_call_target="tpu_custom_call", output_to_operand_aliasing={{}: (5, {})} | custom-call | flops 1610612736 | bytes 3538944 | tf_op jit(solution)/shard_map/pallas_call | solution.py:175
  119.5 0.0 collective-permute-done.4.s_ref
  119.5 0.8 copy-done.4
  120.2 7.7 %shard_map.73 = bf16[1,512,6144]{2,1,0:T(8,128)(2,1)} custom-call(f32[48]{0:T(128)} %bitcast.10, bf16[1,512,6144]{2,1,0:T(8,128)(2,1)} %collective-permute-done.3.x_ref, f32[1,3,6144]{2,1,0:T(4,128)} %copy-done.1, f32[1,6144]{1,0:T(1,128)} %copy-done.7, bf16[12,128,128]{2,1,0:T(8,128)(2,1)} %copy-done.4, ...), custom_call_target="tpu_custom_call", output_to_operand_aliasing={{}: (5, {})} | custom-call | flops 1610612736 | bytes 3538944 | tf_op jit(solution)/shard_map/pallas_call | solution.py:175
  (18 shorter events, 0.0 us)
Async XLA Ops:
  0.6 93.6 %collective-permute-start.3 = (bf16[1,512,6144]{2,1,0:T(8,128)(2,1)}, bf16[1,512,6144]{2,1,0:T(8,128)(2,1)}, u32[]{:S(2)}, u32[]{:S(2)}) collective-permute-start(bf16[1,512,6144]{2,1,0:T(8,128)(2,1)} %x_ref.1), channel_id=1, source_target_pairs={{0,16},{16,32},{32,48},{48,64},{64,80},{80,96},{96,112},{112,0},{1... | collective-permute-start | bytes 18874376 | tf_op jit(solution)/shard_map/ppermute | solution.py:203
  15.2 44.5 %copy-start.2 = (f32[1,3,6144]{2,1,0:T(4,128)S(1)}, f32[1,3,6144]{2,1,0:T(4,128)}, u32[]{:S(2)}) copy-start(f32[1,3,6144]{2,1,0:T(4,128)} %copy.10.g_ref) | copy-start | bytes 221188
  15.2 44.7 %copy-start.10 = (f32[1,6144]{1,0:T(1,128)S(1)}, f32[1,6144]{1,0:T(1,128)}, u32[]{:S(2)}) copy-start(f32[1,6144]{1,0:T(1,128)} %param.7) | copy-start | bytes 73732
  15.2 46.1 %copy-start.9 = (f32[1,48]{1,0:T(1,128)S(1)}, f32[1,48]{1,0:T(1,128)}, u32[]{:S(2)}) copy-start(f32[1,48]{1,0:T(1,128)} %param.8) | copy-start | bytes 580
  15.2 36.0 %all-to-all-start = ((bf16[48,128,128]{2,1,0:T(8,128)(2,1)}), bf16[48,128,128]{2,1,0:T(8,128)(2,1)S(1)}, u32[]{:S(2)}, u32[]{:S(2)}) async-start(bf16[48,128,128]{2,1,0:T(8,128)(2,1)} %shard_map.68), calls=%async_computation | async-start | bytes 3145728 | tf_op jit(solution)/shard_map/all_to_all | solution.py:208
  51.2 1.1 copy-start
  56.0 29.6 %all-to-all-start.1 = ((bf16[48,128,128]{2,1,0:T(8,128)(2,1)}), bf16[48,128,128]{2,1,0:T(8,128)(2,1)S(1)}, u32[]{:S(2)}, u32[]{:S(2)}) async-start(bf16[48,128,128]{2,1,0:T(8,128)(2,1)} %bitcast.6), calls=%async_computation.1 | async-start | bytes 3145728 | tf_op jit(solution)/shard_map/all_to_all | solution.py:213
  59.7 14.2 %collective-permute-start = (f32[1,3,6144]{2,1,0:T(4,128)S(1)}, f32[1,3,6144]{2,1,0:T(4,128)S(1)}, u32[]{:S(2)}, u32[]{:S(2)}) collective-permute-start(f32[1,3,6144]{2,1,0:T(4,128)S(1)} %copy-done.2), channel_id=1, source_target_pairs={{0,16},{16,32},{32,48},{48,64},{64,80},{80,96},{96,112},{112,0},{1... | collective-permute-start | bytes 221192 | tf_op jit(solution)/shard_map/ppermute | solution.py:203
  59.9 14.0 %collective-permute-start.1 = (f32[1,6144]{1,0:T(1,128)S(1)}, f32[1,6144]{1,0:T(1,128)S(1)}, u32[]{:S(2)}, u32[]{:S(2)}) collective-permute-start(f32[1,6144]{1,0:T(1,128)S(1)} %copy-done.10), channel_id=1, source_target_pairs={{0,16},{16,32},{32,48},{48,64},{64,80},{80,96},{96,112},{112,0},{1... | collective-permute-start | bytes 73736 | tf_op jit(solution)/shard_map/ppermute | solution.py:203
  61.3 12.6 %collective-permute-start.2 = (f32[1,48]{1,0:T(1,128)S(1)}, f32[1,48]{1,0:T(1,128)S(1)}, u32[]{:S(2)}, u32[]{:S(2)}) collective-permute-start(f32[1,48]{1,0:T(1,128)S(1)} %copy-done.9), channel_id=1, source_target_pairs={{0,16},{16,32},{32,48},{48,64},{64,80},{80,96},{96,112},{112,0},{1... | collective-permute-start | bytes 584 | tf_op jit(solution)/shard_map/ppermute | solution.py:203
  73.9 20.3 %copy-start.8 = (f32[1,48]{1,0:T(1,128)}, f32[1,48]{1,0:T(1,128)S(1)}, u32[]{:S(2)}) copy-start(f32[1,48]{1,0:T(1,128)S(1)} %collective-permute-done.2) | copy-start | bytes 580
  73.9 20.3 %copy-start.7 = (f32[1,6144]{1,0:T(1,128)}, f32[1,6144]{1,0:T(1,128)S(1)}, u32[]{:S(2)}) copy-start(f32[1,6144]{1,0:T(1,128)S(1)} %collective-permute-done.1.go_ref) | copy-start | bytes 73732
  73.9 20.3 %copy-start.1 = (f32[1,3,6144]{2,1,0:T(4,128)}, f32[1,3,6144]{2,1,0:T(4,128)S(1)}, u32[]{:S(2)}) copy-start(f32[1,3,6144]{2,1,0:T(4,128)S(1)} %collective-permute-done.g_ref) | copy-start | bytes 221188
  85.8 8.4 %collective-permute-start.7 = (bf16[12,128,128]{2,1,0:T(8,128)(2,1)S(1)}, bf16[12,128,128]{2,1,0:T(8,128)(2,1)S(1)}, u32[]{:S(2)}, u32[]{:S(2)}) collective-permute-start(bf16[12,128,128]{2,1,0:T(8,128)(2,1)S(1)} %get-tuple-element.14), channel_id=1, source_target_pairs={{0,16},{16,32},{32,48},{48,64},{64,80},{80,96},{96,112},{112,0},{1... | collective-permute-start | bytes 1179656 | tf_op jit(solution)/shard_map/ppermute | solution.py:222
  85.8 16.8 %collective-permute-start.6 = (bf16[12,128,128]{2,1,0:T(8,128)(2,1)S(1)}, bf16[12,128,128]{2,1,0:T(8,128)(2,1)S(1)}, u32[]{:S(2)}, u32[]{:S(2)}) collective-permute-start(bf16[12,128,128]{2,1,0:T(8,128)(2,1)S(1)} %get-tuple-element.15), channel_id=1, source_target_pairs={{0,16},{16,32},{32,48},{48,64},{64,80},{80,96},{96,112},{112,0},{1... | collective-permute-start | bytes 1179656 | tf_op jit(solution)/shard_map/ppermute | solution.py:222
  87.4 23.7 %collective-permute-start.5 = (bf16[12,128,128]{2,1,0:T(8,128)(2,1)S(1)}, bf16[12,128,128]{2,1,0:T(8,128)(2,1)S(1)}, u32[]{:S(2)}, u32[]{:S(2)}) collective-permute-start(bf16[12,128,128]{2,1,0:T(8,128)(2,1)S(1)} %get-tuple-element.16), channel_id=1, source_target_pairs={{0,16},{16,32},{32,48},{48,64},{64,80},{80,96},{96,112},{112,0},{1... | collective-permute-start | bytes 1179656 | tf_op jit(solution)/shard_map/ppermute | solution.py:222
  87.4 32.1 %collective-permute-start.4 = (bf16[12,128,128]{2,1,0:T(8,128)(2,1)S(1)}, bf16[12,128,128]{2,1,0:T(8,128)(2,1)S(1)}, u32[]{:S(2)}, u32[]{:S(2)}) collective-permute-start(bf16[12,128,128]{2,1,0:T(8,128)(2,1)S(1)} %get-tuple-element.17), channel_id=1, source_target_pairs={{0,16},{16,32},{32,48},{48,64},{64,80},{80,96},{96,112},{112,0},{1... | collective-permute-start | bytes 1179656 | tf_op jit(solution)/shard_map/ppermute | solution.py:222
  94.2 0.8 copy-start.3
  102.6 0.8 copy-start.6
  111.0 0.8 copy-start.5
  119.5 0.8 copy-start.4

commit v9 on v8

--- a/solution.py
+++ b/solution.py
@@ -13,8 +13,15 @@
 STATE_CHUNKS = 4
 
 
-def _silu(v):
-    return 0.5 * v * (1.0 + jnp.tanh(0.5 * v))
+def _silu_half(u):
+    return u + u * jnp.tanh(u)
+
+
+def _row_mean(v):
+    ones = jnp.full((v.shape[-1], v.shape[-1]), 1.0 / v.shape[-1], jnp.bfloat16)
+    high = v.astype(jnp.bfloat16)
+    low = (v - high.astype(jnp.float32)).astype(jnp.bfloat16)
+    return _dot(high, ones) + _dot(low, ones)
 
 
 def _dot_nt(a, b):
@@ -42,11 +49,12 @@
         rate = jnp.full((1, 1), rates_ref[step * hg + hh], jnp.float32)
         cols = slice(hh * head_dim, (hh + 1) * head_dim)
         decay = jnp.exp(-rate * BLOCK)
+        half_k = 0.5 * g_ref[0, 1:2, cols]
         acc = None
         for b in range(nblocks):
             rows = slice(b * BLOCK, (b + 1) * BLOCK)
             x = x_ref[0, rows, cols].astype(jnp.float32)
-            keys_b = (_silu(x * g_ref[0, 1:2, cols]) * head_dim ** (-0.5)).astype(jnp.bfloat16)
+            keys_b = (_silu_half(x * half_k) * head_dim ** (-0.5)).astype(jnp.bfloat16)
             values_b = (x * g_ref[0, 2:3, cols]).astype(jnp.bfloat16)
             update = _block_state(keys_b, values_b, rate, pos)
             acc = update if acc is None else decay * acc + update
@@ -68,18 +76,20 @@
         mask = jnp.where(causal, lead * jnp.exp(rate * (pos_row + 1.0)), 0.0)
         decay = jnp.exp(-rate * BLOCK)
         state = s_ref[hh].astype(jnp.float32)
+        half_q = 0.5 * g_ref[0, 0:1, cols]
+        half_k = 0.5 * g_ref[0, 1:2, cols]
         for b in range(nblocks):
             rows = slice(b * BLOCK, (b + 1) * BLOCK)
             x = x_ref[0, rows, cols].astype(jnp.float32)
-            queries_b = _silu(x * g_ref[0, 0:1, cols]).astype(jnp.bfloat16)
-            keys_b = (_silu(x * g_ref[0, 1:2, cols]) * head_dim ** (-0.5)).astype(jnp.bfloat16)
+            queries_b = _silu_half(x * half_q).astype(jnp.bfloat16)
+            keys_b = (_silu_half(x * half_k) * head_dim ** (-0.5)).astype(jnp.bfloat16)
             values_b = (x * g_ref[0, 2:3, cols]).astype(jnp.bfloat16)
             scores = _dot_nt(queries_b, keys_b)
             weights = (scores * mask).astype(jnp.bfloat16)
             local = _dot(weights, values_b)
             cross = _dot(queries_b, state.astype(jnp.bfloat16))
             total = local + lead * cross
-            normed = total * lax.rsqrt(jnp.mean(total * total, axis=-1, keepdims=True) + EPSILON)
+            normed = total * lax.rsqrt(_row_mean(total * total) + EPSILON)
             o_ref[0, rows, cols] = (x + normed * go_ref[0:1, cols]).astype(o_ref.dtype)
             if b + 1 < nblocks:
                 state = decay * state + _block_state(keys_b, values_b, rate, pos)

time: 129 us -> 140 us (1.085)
  Pallas kernels: 47.2 us -> 58.2 us
    pallas_call x4, Pallas kernels: 30.6 us -> 42 us  [_outputs(): pl.pallas_call(kernel, grid_spec=pltpu.PrefetchScalarGridSpec(num_scalar_...]
  transfers between devices with their start and end apart: 10 -> 10, of which waited for: 4 -> 4; matrix products, arithmetic and copies ran while one was open for 1% -> 1% of each run, Pallas kernels for 31% -> 34%
where the time goes in v9:
time: 140 us; the launch traced here: 139 us
  Pallas kernels  58.2 us (42%)
  waiting for transfers between devices  56.8 us (41%)
  starting transfers between devices  17.2 us (12%)
  local copies, waits for them, and re-layouts  5.93 us (4%)
    pallas_call x4, Pallas kernels, _outputs(): pl.pallas_call(kernel, grid_spec=pltpu.PrefetchScalarGridSpec(num_scalar_...  42 us
    all_to_all x1, waiting for transfers between devices, on_device(): gathered = lax.all_to_all(summary, 'ctx', 0, 0, tiled=True)  27.7 us
    ppermute x4, waiting for transfers between devices, on_device(): lax.ppermute((section_inputs, input_gains, out_gain, decay_rates), 'secti...  12.8 us
    pallas_call x1, Pallas kernels, _summaries(): pl.pallas_call(kernel, grid_spec=pltpu.PrefetchScalarGridSpec(num_scalar_...  12.6 us
    all_to_all x1, waiting for transfers between devices, on_device(): lax.all_to_all(prefixes.reshape(heads, head_dim, head_dim), 'ctx', 0, 0,...  11.4 us
    all_to_all x1, starting transfers between devices, on_device(): gathered = lax.all_to_all(summary, 'ctx', 0, 0, tiled=True)  8.3 us
    unnamed x23, local copies, waits for them, and re-layouts  5.78 us
    ppermute x4, waiting for transfers between devices, on_device(): lax.ppermute(incoming[part * chunk:(part + 1) * chunk], 'section', pairs)  5.07 us
  transfers between devices with their start and end apart: 10, of which 4 were waited for; matrix products, arithmetic and copies ran while one was open for 1% of the time, Pallas kernels for 34%

profile of v9, /device:TPU:0, one launch (start us, length us, event | category | flops | bytes accessed | tf_op | source)
XLA Modules:
  0.0 138.9 jit_solution(4537652792196956393)
XLA Ops:
  0.6 0.0 collective-permute-start.3
  0.7 1.6 %copy.10.g_ref = f32[1,3,6144]{2,1,0:T(4,128)} copy(f32[1,3,6144]{2,0,1:T(1,128)} %param.6) | data formatting | bytes 147456 | tf_op args[1]
  2.2 12.6 %shard_map.68 = bf16[48,128,128]{2,1,0:T(8,128)(2,1)} custom-call(f32[48]{0:T(128)} %bitcast.11, bf16[1,512,6144]{2,1,0:T(8,128)(2,1)} %x_ref.1, f32[1,3,6144]{2,1,0:T(4,128)} %copy.10.g_ref), custom_call_target="tpu_custom_call" | custom-call | flops 805306368 | bytes 9437184 | tf_op jit(solution)/shard_map/pallas_call | solution.py:143
  14.9 8.3 %all-to-all-start = ((bf16[48,128,128]{2,1,0:T(8,128)(2,1)}), bf16[48,128,128]{2,1,0:T(8,128)(2,1)S(1)}, u32[]{:S(2)}, u32[]{:S(2)}) async-start(bf16[48,128,128]{2,1,0:T(8,128)(2,1)} %shard_map.68), calls=%async_computation | async-start | bytes 3145728 | tf_op jit(solution)/shard_map/all_to_all | solution.py:218
  23.2 27.7 %all-to-all-done = bf16[48,128,128]{2,1,0:T(8,128)(2,1)S(1)} async-done(((bf16[48,128,128]{2,1,0:T(8,128)(2,1)}), bf16[48,128,128]{2,1,0:T(8,128)(2,1)S(1)}, u32[]{:S(2)}, u32[]{:S(2)}) %all-to-all-start) | async-done | bytes 1572896 | tf_op jit(solution)/shard_map/all_to_all | solution.py:218
  50.8 1.1 copy-done
  52.0 3.6 %shard_map.69 = (bf16[16,3,128,128]{3,2,1,0:T(8,128)(2,1)}, f32[1,3,128,128]{3,2,1,0:T(8,128)}) custom-call(s32[1]{0:T(128)} %bitcast.place_ref, f32[48]{0:T(128)} %bitcast.12, bf16[16,3,128,128]{3,2,1,0:T(8,128)(2,1)} %bitcast.5, f32[1,48,128,128]{3,2,1,0:T(8,128)} %c_ref.1), custom_call_target="tpu_custom_call" | custom-call | flops 1572864 | bytes 3538944 | tf_op jit(solution)/shard_map/pallas_call | solution.py:112
  55.6 3.7 %all-to-all-start.1 = ((bf16[48,128,128]{2,1,0:T(8,128)(2,1)}), bf16[48,128,128]{2,1,0:T(8,128)(2,1)S(1)}, u32[]{:S(2)}, u32[]{:S(2)}) async-start(bf16[48,128,128]{2,1,0:T(8,128)(2,1)} %bitcast.6), calls=%async_computation.1 | async-start | bytes 3145728 | tf_op jit(solution)/shard_map/all_to_all | solution.py:223
  59.3 0.2 collective-permute-start
  59.5 1.4 %collective-permute-start.1 = (f32[1,6144]{1,0:T(1,128)S(1)}, f32[1,6144]{1,0:T(1,128)S(1)}, u32[]{:S(2)}, u32[]{:S(2)}) collective-permute-start(f32[1,6144]{1,0:T(1,128)S(1)} %copy-done.10), channel_id=1, source_target_pairs={{0,16},{16,32},{32,48},{48,64},{64,80},{80,96},{96,112},{112,0},{1... | collective-permute-start | bytes 73736 | tf_op jit(solution)/shard_map/ppermute | solution.py:213
  61.0 0.2 collective-permute-start.2
  61.1 12.7 %collective-permute-done.2 = f32[1,48]{1,0:T(1,128)S(1)} collective-permute-done((f32[1,48]{1,0:T(1,128)S(1)}, f32[1,48]{1,0:T(1,128)S(1)}, u32[]{:S(2)}, u32[]{:S(2)}) %collective-permute-start.2) | collective-permute-done | bytes 224 | tf_op jit(solution)/shard_map/ppermute | solution.py:213
  73.9 0.0 collective-permute-done.1.go_ref
  73.9 11.4 %all-to-all-done.1 = bf16[48,128,128]{2,1,0:T(8,128)(2,1)S(1)} async-done(((bf16[48,128,128]{2,1,0:T(8,128)(2,1)}), bf16[48,128,128]{2,1,0:T(8,128)(2,1)S(1)}, u32[]{:S(2)}, u32[]{:S(2)}) %all-to-all-start.1) | async-done | bytes 1572896 | tf_op jit(solution)/shard_map/all_to_all | solution.py:223
  85.3 0.1 fusion
  85.4 0.0 collective-permute-start.7
  85.4 1.6 %collective-permute-start.6 = (bf16[12,128,128]{2,1,0:T(8,128)(2,1)S(1)}, bf16[12,128,128]{2,1,0:T(8,128)(2,1)S(1)}, u32[]{:S(2)}, u32[]{:S(2)}) collective-permute-start(bf16[12,128,128]{2,1,0:T(8,128)(2,1)S(1)} %get-tuple-element.15), channel_id=1, source_target_pairs={{0,16},{16,32},{32,48},{48,64},{64,80},{80,96},{96,112},{112,0},{1... | collective-permute-start | bytes 1179656 | tf_op jit(solution)/shard_map/ppermute | solution.py:232
  87.0 0.0 collective-permute-start.5
  87.1 1.7 %collective-permute-start.4 = (bf16[12,128,128]{2,1,0:T(8,128)(2,1)S(1)}, bf16[12,128,128]{2,1,0:T(8,128)(2,1)S(1)}, u32[]{:S(2)}, u32[]{:S(2)}) collective-permute-start(bf16[12,128,128]{2,1,0:T(8,128)(2,1)S(1)} %get-tuple-element.17), channel_id=1, source_target_pairs={{0,16},{16,32},{32,48},{48,64},{64,80},{80,96},{96,112},{112,0},{1... | collective-permute-start | bytes 1179656 | tf_op jit(solution)/shard_map/ppermute | solution.py:232
  88.8 5.1 %collective-permute-done.7.s_ref = bf16[12,128,128]{2,1,0:T(8,128)(2,1)S(1)} collective-permute-done((bf16[12,128,128]{2,1,0:T(8,128)(2,1)S(1)}, bf16[12,128,128]{2,1,0:T(8,128)(2,1)S(1)}, u32[]{:S(2)}, u32[]{:S(2)}) %collective-permute-start.7) | collective-permute-done | bytes 393248 | tf_op jit(solution)/shard_map/ppermute | solution.py:232
  93.8 0.0 collective-permute-done.3.x_ref
  93.9 0.7 copy-done.3
  94.6 10.5 %shard_map.70.rest_0_ = bf16[1,512,6144]{2,1,0:T(8,128)(2,1)} custom-call(f32[48]{0:T(128)} %bitcast.7, bf16[1,512,6144]{2,1,0:T(8,128)(2,1)} %collective-permute-done.3.x_ref, f32[1,3,6144]{2,1,0:T(4,128)} %copy-done.1, f32[1,6144]{1,0:T(1,128)} %copy-done.7, bf16[12,128,128]{2,1,0:T(8,128)(2,1)} %copy-done.3), custom_call_target="tpu_custom_call" | custom-call | flops 1610612736 | bytes 3538944 | tf_op jit(solution)/shard_map/pallas_call | solution.py:185
  105.1 0.0 collective-permute-done.6.s_ref
  105.1 0.8 copy-done.6
  105.9 10.5 %shard_map.71.rest_0_ = bf16[1,512,6144]{2,1,0:T(8,128)(2,1)} custom-call(f32[48]{0:T(128)} %bitcast.8, bf16[1,512,6144]{2,1,0:T(8,128)(2,1)} %collective-permute-done.3.x_ref, f32[1,3,6144]{2,1,0:T(4,128)} %copy-done.1, f32[1,6144]{1,0:T(1,128)} %copy-done.7, bf16[12,128,128]{2,1,0:T(8,128)(2,1)} %copy-done.6, ...), custom_call_target="tpu_custom_call", output_to_operand_aliasing={{}: (5, {})} | custom-call | flops 1610612736 | bytes 3538944 | tf_op jit(solution)/shard_map/pallas_call | solution.py:185
  116.4 0.0 collective-permute-done.5.s_ref
  116.4 0.8 copy-done.5
  117.1 10.5 %shard_map.72.rest_0_ = bf16[1,512,6144]{2,1,0:T(8,128)(2,1)} custom-call(f32[48]{0:T(128)} %bitcast.9, bf16[1,512,6144]{2,1,0:T(8,128)(2,1)} %collective-permute-done.3.x_ref, f32[1,3,6144]{2,1,0:T(4,128)} %copy-done.1, f32[1,6144]{1,0:T(1,128)} %copy-done.7, bf16[12,128,128]{2,1,0:T(8,128)(2,1)} %copy-done.5, ...), custom_call_target="tpu_custom_call", output_to_operand_aliasing={{}: (5, {})} | custom-call | flops 1610612736 | bytes 3538944 | tf_op jit(solution)/shard_map/pallas_call | solution.py:185
  127.6 0.0 collective-permute-done.4.s_ref
  127.6 0.8 copy-done.4
  128.4 10.5 %shard_map.73 = bf16[1,512,6144]{2,1,0:T(8,128)(2,1)} custom-call(f32[48]{0:T(128)} %bitcast.10, bf16[1,512,6144]{2,1,0:T(8,128)(2,1)} %collective-permute-done.3.x_ref, f32[1,3,6144]{2,1,0:T(4,128)} %copy-done.1, f32[1,6144]{1,0:T(1,128)} %copy-done.7, bf16[12,128,128]{2,1,0:T(8,128)(2,1)} %copy-done.4, ...), custom_call_target="tpu_custom_call", output_to_operand_aliasing={{}: (5, {})} | custom-call | flops 1610612736 | bytes 3538944 | tf_op jit(solution)/shard_map/pallas_call | solution.py:185
  (18 shorter events, 0.0 us)
Async XLA Ops:
  0.6 93.2 %collective-permute-start.3 = (bf16[1,512,6144]{2,1,0:T(8,128)(2,1)}, bf16[1,512,6144]{2,1,0:T(8,128)(2,1)}, u32[]{:S(2)}, u32[]{:S(2)}) collective-permute-start(bf16[1,512,6144]{2,1,0:T(8,128)(2,1)} %x_ref.1), channel_id=1, source_target_pairs={{0,16},{16,32},{32,48},{48,64},{64,80},{80,96},{96,112},{112,0},{1... | collective-permute-start | bytes 18874376 | tf_op jit(solution)/shard_map/ppermute | solution.py:213
  14.8 44.5 %copy-start.2 = (f32[1,3,6144]{2,1,0:T(4,128)S(1)}, f32[1,3,6144]{2,1,0:T(4,128)}, u32[]{:S(2)}) copy-start(f32[1,3,6144]{2,1,0:T(4,128)} %copy.10.g_ref) | copy-start | bytes 221188
  14.8 44.7 %copy-start.10 = (f32[1,6144]{1,0:T(1,128)S(1)}, f32[1,6144]{1,0:T(1,128)}, u32[]{:S(2)}) copy-start(f32[1,6144]{1,0:T(1,128)} %param.7) | copy-start | bytes 73732
  14.9 46.1 %copy-start.9 = (f32[1,48]{1,0:T(1,128)S(1)}, f32[1,48]{1,0:T(1,128)}, u32[]{:S(2)}) copy-start(f32[1,48]{1,0:T(1,128)} %param.8) | copy-start | bytes 580
  14.9 36.0 %all-to-all-start = ((bf16[48,128,128]{2,1,0:T(8,128)(2,1)}), bf16[48,128,128]{2,1,0:T(8,128)(2,1)S(1)}, u32[]{:S(2)}, u32[]{:S(2)}) async-start(bf16[48,128,128]{2,1,0:T(8,128)(2,1)} %shard_map.68), calls=%async_computation | async-start | bytes 3145728 | tf_op jit(solution)/shard_map/all_to_all | solution.py:218
  50.8 1.1 copy-start
  55.6 29.6 %all-to-all-start.1 = ((bf16[48,128,128]{2,1,0:T(8,128)(2,1)}), bf16[48,128,128]{2,1,0:T(8,128)(2,1)S(1)}, u32[]{:S(2)}, u32[]{:S(2)}) async-start(bf16[48,128,128]{2,1,0:T(8,128)(2,1)} %bitcast.6), calls=%async_computation.1 | async-start | bytes 3145728 | tf_op jit(solution)/shard_map/all_to_all | solution.py:223
  59.3 14.5 %collective-permute-start = (f32[1,3,6144]{2,1,0:T(4,128)S(1)}, f32[1,3,6144]{2,1,0:T(4,128)S(1)}, u32[]{:S(2)}, u32[]{:S(2)}) collective-permute-start(f32[1,3,6144]{2,1,0:T(4,128)S(1)} %copy-done.2), channel_id=1, source_target_pairs={{0,16},{16,32},{32,48},{48,64},{64,80},{80,96},{96,112},{112,0},{1... | collective-permute-start | bytes 221192 | tf_op jit(solution)/shard_map/ppermute | solution.py:213
  59.5 14.4 %collective-permute-start.1 = (f32[1,6144]{1,0:T(1,128)S(1)}, f32[1,6144]{1,0:T(1,128)S(1)}, u32[]{:S(2)}, u32[]{:S(2)}) collective-permute-start(f32[1,6144]{1,0:T(1,128)S(1)} %copy-done.10), channel_id=1, source_target_pairs={{0,16},{16,32},{32,48},{48,64},{64,80},{80,96},{96,112},{112,0},{1... | collective-permute-start | bytes 73736 | tf_op jit(solution)/shard_map/ppermute | solution.py:213
  61.0 12.9 %collective-permute-start.2 = (f32[1,48]{1,0:T(1,128)S(1)}, f32[1,48]{1,0:T(1,128)S(1)}, u32[]{:S(2)}, u32[]{:S(2)}) collective-permute-start(f32[1,48]{1,0:T(1,128)S(1)} %copy-done.9), channel_id=1, source_target_pairs={{0,16},{16,32},{32,48},{48,64},{64,80},{80,96},{96,112},{112,0},{1... | collective-permute-start | bytes 584 | tf_op jit(solution)/shard_map/ppermute | solution.py:213
  73.9 20.0 %copy-start.8 = (f32[1,48]{1,0:T(1,128)}, f32[1,48]{1,0:T(1,128)S(1)}, u32[]{:S(2)}) copy-start(f32[1,48]{1,0:T(1,128)S(1)} %collective-permute-done.2) | copy-start | bytes 580
  73.9 20.0 %copy-start.7 = (f32[1,6144]{1,0:T(1,128)}, f32[1,6144]{1,0:T(1,128)S(1)}, u32[]{:S(2)}) copy-start(f32[1,6144]{1,0:T(1,128)S(1)} %collective-permute-done.1.go_ref) | copy-start | bytes 73732
  73.9 20.0 %copy-start.1 = (f32[1,3,6144]{2,1,0:T(4,128)}, f32[1,3,6144]{2,1,0:T(4,128)S(1)}, u32[]{:S(2)}) copy-start(f32[1,3,6144]{2,1,0:T(4,128)S(1)} %collective-permute-done.g_ref) | copy-start | bytes 221188
  85.4 8.4 %collective-permute-start.7 = (bf16[12,128,128]{2,1,0:T(8,128)(2,1)S(1)}, bf16[12,128,128]{2,1,0:T(8,128)(2,1)S(1)}, u32[]{:S(2)}, u32[]{:S(2)}) collective-permute-start(bf16[12,128,128]{2,1,0:T(8,128)(2,1)S(1)} %get-tuple-element.14), channel_id=1, source_target_pairs={{0,16},{16,32},{32,48},{48,64},{64,80},{80,96},{96,112},{112,0},{1... | collective-permute-start | bytes 1179656 | tf_op jit(solution)/shard_map/ppermute | solution.py:232
  85.4 19.6 %collective-permute-start.6 = (bf16[12,128,128]{2,1,0:T(8,128)(2,1)S(1)}, bf16[12,128,128]{2,1,0:T(8,128)(2,1)S(1)}, u32[]{:S(2)}, u32[]{:S(2)}) collective-permute-start(bf16[12,128,128]{2,1,0:T(8,128)(2,1)S(1)} %get-tuple-element.15), channel_id=1, source_target_pairs={{0,16},{16,32},{32,48},{48,64},{64,80},{80,96},{96,112},{112,0},{1... | collective-permute-start | bytes 1179656 | tf_op jit(solution)/shard_map/ppermute | solution.py:232
  87.0 29.3 %collective-permute-start.5 = (bf16[12,128,128]{2,1,0:T(8,128)(2,1)S(1)}, bf16[12,128,128]{2,1,0:T(8,128)(2,1)S(1)}, u32[]{:S(2)}, u32[]{:S(2)}) collective-permute-start(bf16[12,128,128]{2,1,0:T(8,128)(2,1)S(1)} %get-tuple-element.16), channel_id=1, source_target_pairs={{0,16},{16,32},{32,48},{48,64},{64,80},{80,96},{96,112},{112,0},{1... | collective-permute-start | bytes 1179656 | tf_op jit(solution)/shard_map/ppermute | solution.py:232
  87.1 40.6 %collective-permute-start.4 = (bf16[12,128,128]{2,1,0:T(8,128)(2,1)S(1)}, bf16[12,128,128]{2,1,0:T(8,128)(2,1)S(1)}, u32[]{:S(2)}, u32[]{:S(2)}) collective-permute-start(bf16[12,128,128]{2,1,0:T(8,128)(2,1)S(1)} %get-tuple-element.17), channel_id=1, source_target_pairs={{0,16},{16,32},{32,48},{48,64},{64,80},{80,96},{96,112},{112,0},{1... | collective-permute-start | bytes 1179656 | tf_op jit(solution)/shard_map/ppermute | solution.py:232
  93.8 0.8 copy-start.3
  105.1 0.8 copy-start.6
  116.4 0.8 copy-start.5
  127.6 0.8 copy-start.4

commit v10 on v8

--- a/solution.py
+++ b/solution.py
@@ -9,7 +9,7 @@
 
 BLOCK = 256
 EPSILON = 1e-05
-HEADS_PER_STEP = 4
+HEADS_PER_STEP = 6
 STATE_CHUNKS = 4
 
 

time: 129 us -> 126 us (0.977)
  Pallas kernels: 47.2 us -> 44.9 us
    pallas_call x1, Pallas kernels: 13 us -> 11.1 us  [_summaries(): pl.pallas_call(kernel, grid_spec=pltpu.PrefetchScalarGridSpec(num_scalar_...]
    all_to_all x1, waiting for transfers between devices: 11.7 us -> 9.87 us  [on_device(): lax.all_to_all(prefixes.reshape(heads, head_dim, head_dim), 'ctx', 0, 0,...]
    ppermute x4, waiting for transfers between devices: 12.4 us -> 14.2 us  [on_device(): lax.ppermute((section_inputs, input_gains, out_gain, decay_rates), 'secti...]
  transfers between devices with their start and end apart: 10 -> 10, of which waited for: 4 -> 4; matrix products, arithmetic and copies ran while one was open for 1% -> 1% of each run, Pallas kernels for 31% -> 30%
where the time goes in v10:
time: 126 us
  waiting for transfers between devices  56.8 us (45%)
  Pallas kernels  44.9 us (36%)
  starting transfers between devices  17.2 us (14%)
  local copies, waits for them, and re-layouts  5.93 us (5%)
    pallas_call x4, Pallas kernels, _outputs(): pl.pallas_call(kernel, grid_spec=pltpu.PrefetchScalarGridSpec(num_scalar_...  30.1 us
    all_to_all x1, waiting for transfers between devices, on_device(): gathered = lax.all_to_all(summary, 'ctx', 0, 0, tiled=True)  27.7 us
    ppermute x4, waiting for transfers between devices, on_device(): lax.ppermute((section_inputs, input_gains, out_gain, decay_rates), 'secti...  14.2 us
    pallas_call x1, Pallas kernels, _summaries(): pl.pallas_call(kernel, grid_spec=pltpu.PrefetchScalarGridSpec(num_scalar_...  11.1 us
    all_to_all x1, waiting for transfers between devices, on_device(): lax.all_to_all(prefixes.reshape(heads, head_dim, head_dim), 'ctx', 0, 0,...  9.87 us
    all_to_all x1, starting transfers between devices, on_device(): gathered = lax.all_to_all(summary, 'ctx', 0, 0, tiled=True)  8.3 us
    unnamed x23, local copies, waits for them, and re-layouts  5.78 us
    ppermute x4, waiting for transfers between devices, on_device(): lax.ppermute(incoming[part * chunk:(part + 1) * chunk], 'section', pairs)  5.06 us
  transfers between devices with their start and end apart: 10, of which 4 were waited for; matrix products, arithmetic and copies ran while one was open for 1% of the time, Pallas kernels for 30%

profile of v10, /device:TPU:0, one launch (start us, length us, event | category | flops | bytes accessed | tf_op | source)
XLA Modules:
  0.0 125.6 jit_solution(6329715684357835698)
XLA Ops:
  0.6 0.0 collective-permute-start.3
  0.7 1.6 %copy.10.g_ref = f32[1,3,6144]{2,1,0:T(4,128)} copy(f32[1,3,6144]{2,0,1:T(1,128)} %param.6) | data formatting | bytes 147456 | tf_op args[1]
  2.2 11.1 %shard_map.68 = bf16[48,128,128]{2,1,0:T(8,128)(2,1)} custom-call(f32[48]{0:T(128)} %bitcast.11, bf16[1,512,6144]{2,1,0:T(8,128)(2,1)} %x_ref.1, f32[1,3,6144]{2,1,0:T(4,128)} %copy.10.g_ref), custom_call_target="tpu_custom_call" | custom-call | flops 805306368 | bytes 9437184 | tf_op jit(solution)/shard_map/pallas_call | solution.py:133
  13.4 8.3 %all-to-all-start = ((bf16[48,128,128]{2,1,0:T(8,128)(2,1)}), bf16[48,128,128]{2,1,0:T(8,128)(2,1)S(1)}, u32[]{:S(2)}, u32[]{:S(2)}) async-start(bf16[48,128,128]{2,1,0:T(8,128)(2,1)} %shard_map.68), calls=%async_computation | async-start | bytes 3145728 | tf_op jit(solution)/shard_map/all_to_all | solution.py:208
  21.7 27.7 %all-to-all-done = bf16[48,128,128]{2,1,0:T(8,128)(2,1)S(1)} async-done(((bf16[48,128,128]{2,1,0:T(8,128)(2,1)}), bf16[48,128,128]{2,1,0:T(8,128)(2,1)S(1)}, u32[]{:S(2)}, u32[]{:S(2)}) %all-to-all-start) | async-done | bytes 1572896 | tf_op jit(solution)/shard_map/all_to_all | solution.py:208
  49.3 1.1 copy-done
  50.5 3.6 %shard_map.69 = (bf16[16,3,128,128]{3,2,1,0:T(8,128)(2,1)}, f32[1,3,128,128]{3,2,1,0:T(8,128)}) custom-call(s32[1]{0:T(128)} %bitcast.place_ref, f32[48]{0:T(128)} %bitcast.12, bf16[16,3,128,128]{3,2,1,0:T(8,128)(2,1)} %bitcast.5, f32[1,48,128,128]{3,2,1,0:T(8,128)} %c_ref.1), custom_call_target="tpu_custom_call" | custom-call | flops 1572864 | bytes 3538944 | tf_op jit(solution)/shard_map/pallas_call | solution.py:102
  54.1 3.7 %all-to-all-start.1 = ((bf16[48,128,128]{2,1,0:T(8,128)(2,1)}), bf16[48,128,128]{2,1,0:T(8,128)(2,1)S(1)}, u32[]{:S(2)}, u32[]{:S(2)}) async-start(bf16[48,128,128]{2,1,0:T(8,128)(2,1)} %bitcast.6), calls=%async_computation.1 | async-start | bytes 3145728 | tf_op jit(solution)/shard_map/all_to_all | solution.py:213
  57.8 0.2 collective-permute-start
  58.0 1.4 %collective-permute-start.1 = (f32[1,6144]{1,0:T(1,128)S(1)}, f32[1,6144]{1,0:T(1,128)S(1)}, u32[]{:S(2)}, u32[]{:S(2)}) collective-permute-start(f32[1,6144]{1,0:T(1,128)S(1)} %copy-done.10), channel_id=1, source_target_pairs={{0,16},{16,32},{32,48},{48,64},{64,80},{80,96},{96,112},{112,0},{1... | collective-permute-start | bytes 73736 | tf_op jit(solution)/shard_map/ppermute | solution.py:203
  59.5 0.2 collective-permute-start.2
  59.6 14.2 %collective-permute-done.2 = f32[1,48]{1,0:T(1,128)S(1)} collective-permute-done((f32[1,48]{1,0:T(1,128)S(1)}, f32[1,48]{1,0:T(1,128)S(1)}, u32[]{:S(2)}, u32[]{:S(2)}) %collective-permute-start.2) | collective-permute-done | bytes 224 | tf_op jit(solution)/shard_map/ppermute | solution.py:203
  73.9 0.0 collective-permute-done.1.go_ref
  73.9 0.0 collective-permute-done.g_ref
  73.9 9.9 %all-to-all-done.1 = bf16[48,128,128]{2,1,0:T(8,128)(2,1)S(1)} async-done(((bf16[48,128,128]{2,1,0:T(8,128)(2,1)}), bf16[48,128,128]{2,1,0:T(8,128)(2,1)S(1)}, u32[]{:S(2)}, u32[]{:S(2)}) %all-to-all-start.1) | async-done | bytes 1572896 | tf_op jit(solution)/shard_map/all_to_all | solution.py:213
  83.8 0.1 fusion
  83.9 0.0 collective-permute-start.7
  83.9 1.6 %collective-permute-start.6 = (bf16[12,128,128]{2,1,0:T(8,128)(2,1)S(1)}, bf16[12,128,128]{2,1,0:T(8,128)(2,1)S(1)}, u32[]{:S(2)}, u32[]{:S(2)}) collective-permute-start(bf16[12,128,128]{2,1,0:T(8,128)(2,1)S(1)} %get-tuple-element.15), channel_id=1, source_target_pairs={{0,16},{16,32},{32,48},{48,64},{64,80},{80,96},{96,112},{112,0},{1... | collective-permute-start | bytes 1179656 | tf_op jit(solution)/shard_map/ppermute | solution.py:222
  85.5 0.0 collective-permute-start.5
  85.6 1.7 %collective-permute-start.4 = (bf16[12,128,128]{2,1,0:T(8,128)(2,1)S(1)}, bf16[12,128,128]{2,1,0:T(8,128)(2,1)S(1)}, u32[]{:S(2)}, u32[]{:S(2)}) collective-permute-start(bf16[12,128,128]{2,1,0:T(8,128)(2,1)S(1)} %get-tuple-element.17), channel_id=1, source_target_pairs={{0,16},{16,32},{32,48},{48,64},{64,80},{80,96},{96,112},{112,0},{1... | collective-permute-start | bytes 1179656 | tf_op jit(solution)/shard_map/ppermute | solution.py:222
  87.3 5.0 %collective-permute-done.7.s_ref = bf16[12,128,128]{2,1,0:T(8,128)(2,1)S(1)} collective-permute-done((bf16[12,128,128]{2,1,0:T(8,128)(2,1)S(1)}, bf16[12,128,128]{2,1,0:T(8,128)(2,1)S(1)}, u32[]{:S(2)}, u32[]{:S(2)}) %collective-permute-start.7) | collective-permute-done | bytes 393248 | tf_op jit(solution)/shard_map/ppermute | solution.py:222
  92.4 0.7 copy-done.3
  93.1 7.5 %shard_map.70.rest_0_ = bf16[1,512,6144]{2,1,0:T(8,128)(2,1)} custom-call(f32[48]{0:T(128)} %bitcast.7, bf16[1,512,6144]{2,1,0:T(8,128)(2,1)} %collective-permute-done.3.x_ref, f32[1,3,6144]{2,1,0:T(4,128)} %copy-done.1, f32[1,6144]{1,0:T(1,128)} %copy-done.7, bf16[12,128,128]{2,1,0:T(8,128)(2,1)} %copy-done.3), custom_call_target="tpu_custom_call" | custom-call | flops 1610612736 | bytes 3538944 | tf_op jit(solution)/shard_map/pallas_call | solution.py:175
  100.6 0.0 collective-permute-done.6.s_ref
  100.6 0.8 copy-done.6
  101.4 7.5 %shard_map.71.rest_0_ = bf16[1,512,6144]{2,1,0:T(8,128)(2,1)} custom-call(f32[48]{0:T(128)} %bitcast.8, bf16[1,512,6144]{2,1,0:T(8,128)(2,1)} %collective-permute-done.3.x_ref, f32[1,3,6144]{2,1,0:T(4,128)} %copy-done.1, f32[1,6144]{1,0:T(1,128)} %copy-done.7, bf16[12,128,128]{2,1,0:T(8,128)(2,1)} %copy-done.6, ...), custom_call_target="tpu_custom_call", output_to_operand_aliasing={{}: (5, {})} | custom-call | flops 1610612736 | bytes 3538944 | tf_op jit(solution)/shard_map/pallas_call | solution.py:175
  108.9 0.0 collective-permute-done.5.s_ref
  109.0 0.8 copy-done.5
  109.7 7.5 %shard_map.72.rest_0_ = bf16[1,512,6144]{2,1,0:T(8,128)(2,1)} custom-call(f32[48]{0:T(128)} %bitcast.9, bf16[1,512,6144]{2,1,0:T(8,128)(2,1)} %collective-permute-done.3.x_ref, f32[1,3,6144]{2,1,0:T(4,128)} %copy-done.1, f32[1,6144]{1,0:T(1,128)} %copy-done.7, bf16[12,128,128]{2,1,0:T(8,128)(2,1)} %copy-done.5, ...), custom_call_target="tpu_custom_call", output_to_operand_aliasing={{}: (5, {})} | custom-call | flops 1610612736 | bytes 3538944 | tf_op jit(solution)/shard_map/pallas_call | solution.py:175
  117.3 0.0 collective-permute-done.4.s_ref
  117.3 0.8 copy-done.4
  118.0 7.5 %shard_map.73 = bf16[1,512,6144]{2,1,0:T(8,128)(2,1)} custom-call(f32[48]{0:T(128)} %bitcast.10, bf16[1,512,6144]{2,1,0:T(8,128)(2,1)} %collective-permute-done.3.x_ref, f32[1,3,6144]{2,1,0:T(4,128)} %copy-done.1, f32[1,6144]{1,0:T(1,128)} %copy-done.7, bf16[12,128,128]{2,1,0:T(8,128)(2,1)} %copy-done.4, ...), custom_call_target="tpu_custom_call", output_to_operand_aliasing={{}: (5, {})} | custom-call | flops 1610612736 | bytes 3538944 | tf_op jit(solution)/shard_map/pallas_call | solution.py:175
  (18 shorter events, 0.0 us)
Async XLA Ops:
  0.6 91.7 %collective-permute-start.3 = (bf16[1,512,6144]{2,1,0:T(8,128)(2,1)}, bf16[1,512,6144]{2,1,0:T(8,128)(2,1)}, u32[]{:S(2)}, u32[]{:S(2)}) collective-permute-start(bf16[1,512,6144]{2,1,0:T(8,128)(2,1)} %x_ref.1), channel_id=1, source_target_pairs={{0,16},{16,32},{32,48},{48,64},{64,80},{80,96},{96,112},{112,0},{1... | collective-permute-start | bytes 18874376 | tf_op jit(solution)/shard_map/ppermute | solution.py:203
  13.4 44.5 %copy-start.2 = (f32[1,3,6144]{2,1,0:T(4,128)S(1)}, f32[1,3,6144]{2,1,0:T(4,128)}, u32[]{:S(2)}) copy-start(f32[1,3,6144]{2,1,0:T(4,128)} %copy.10.g_ref) | copy-start | bytes 221188
  13.4 44.7 %copy-start.10 = (f32[1,6144]{1,0:T(1,128)S(1)}, f32[1,6144]{1,0:T(1,128)}, u32[]{:S(2)}) copy-start(f32[1,6144]{1,0:T(1,128)} %param.7) | copy-start | bytes 73732
  13.4 46.1 %copy-start.9 = (f32[1,48]{1,0:T(1,128)S(1)}, f32[1,48]{1,0:T(1,128)}, u32[]{:S(2)}) copy-start(f32[1,48]{1,0:T(1,128)} %param.8) | copy-start | bytes 580
  13.4 36.0 %all-to-all-start = ((bf16[48,128,128]{2,1,0:T(8,128)(2,1)}), bf16[48,128,128]{2,1,0:T(8,128)(2,1)S(1)}, u32[]{:S(2)}, u32[]{:S(2)}) async-start(bf16[48,128,128]{2,1,0:T(8,128)(2,1)} %shard_map.68), calls=%async_computation | async-start | bytes 3145728 | tf_op jit(solution)/shard_map/all_to_all | solution.py:208
  49.3 1.1 copy-start
  54.1 29.6 %all-to-all-start.1 = ((bf16[48,128,128]{2,1,0:T(8,128)(2,1)}), bf16[48,128,128]{2,1,0:T(8,128)(2,1)S(1)}, u32[]{:S(2)}, u32[]{:S(2)}) async-start(bf16[48,128,128]{2,1,0:T(8,128)(2,1)} %bitcast.6), calls=%async_computation.1 | async-start | bytes 3145728 | tf_op jit(solution)/shard_map/all_to_all | solution.py:213
  57.8 16.0 %collective-permute-start = (f32[1,3,6144]{2,1,0:T(4,128)S(1)}, f32[1,3,6144]{2,1,0:T(4,128)S(1)}, u32[]{:S(2)}, u32[]{:S(2)}) collective-permute-start(f32[1,3,6144]{2,1,0:T(4,128)S(1)} %copy-done.2), channel_id=1, source_target_pairs={{0,16},{16,32},{32,48},{48,64},{64,80},{80,96},{96,112},{112,0},{1... | collective-permute-start | bytes 221192 | tf_op jit(solution)/shard_map/ppermute | solution.py:203
  58.0 15.9 %collective-permute-start.1 = (f32[1,6144]{1,0:T(1,128)S(1)}, f32[1,6144]{1,0:T(1,128)S(1)}, u32[]{:S(2)}, u32[]{:S(2)}) collective-permute-start(f32[1,6144]{1,0:T(1,128)S(1)} %copy-done.10), channel_id=1, source_target_pairs={{0,16},{16,32},{32,48},{48,64},{64,80},{80,96},{96,112},{112,0},{1... | collective-permute-start | bytes 73736 | tf_op jit(solution)/shard_map/ppermute | solution.py:203
  59.5 14.4 %collective-permute-start.2 = (f32[1,48]{1,0:T(1,128)S(1)}, f32[1,48]{1,0:T(1,128)S(1)}, u32[]{:S(2)}, u32[]{:S(2)}) collective-permute-start(f32[1,48]{1,0:T(1,128)S(1)} %copy-done.9), channel_id=1, source_target_pairs={{0,16},{16,32},{32,48},{48,64},{64,80},{80,96},{96,112},{112,0},{1... | collective-permute-start | bytes 584 | tf_op jit(solution)/shard_map/ppermute | solution.py:203
  73.9 18.5 %copy-start.8 = (f32[1,48]{1,0:T(1,128)}, f32[1,48]{1,0:T(1,128)S(1)}, u32[]{:S(2)}) copy-start(f32[1,48]{1,0:T(1,128)S(1)} %collective-permute-done.2) | copy-start | bytes 580
  73.9 18.5 %copy-start.7 = (f32[1,6144]{1,0:T(1,128)}, f32[1,6144]{1,0:T(1,128)S(1)}, u32[]{:S(2)}) copy-start(f32[1,6144]{1,0:T(1,128)S(1)} %collective-permute-done.1.go_ref) | copy-start | bytes 73732
  73.9 18.5 %copy-start.1 = (f32[1,3,6144]{2,1,0:T(4,128)}, f32[1,3,6144]{2,1,0:T(4,128)S(1)}, u32[]{:S(2)}) copy-start(f32[1,3,6144]{2,1,0:T(4,128)S(1)} %collective-permute-done.g_ref) | copy-start | bytes 221188
  83.9 8.4 %collective-permute-start.7 = (bf16[12,128,128]{2,1,0:T(8,128)(2,1)S(1)}, bf16[12,128,128]{2,1,0:T(8,128)(2,1)S(1)}, u32[]{:S(2)}, u32[]{:S(2)}) collective-permute-start(bf16[12,128,128]{2,1,0:T(8,128)(2,1)S(1)} %get-tuple-element.14), channel_id=1, source_target_pairs={{0,16},{16,32},{32,48},{48,64},{64,80},{80,96},{96,112},{112,0},{1... | collective-permute-start | bytes 1179656 | tf_op jit(solution)/shard_map/ppermute | solution.py:222
  83.9 16.7 %collective-permute-start.6 = (bf16[12,128,128]{2,1,0:T(8,128)(2,1)S(1)}, bf16[12,128,128]{2,1,0:T(8,128)(2,1)S(1)}, u32[]{:S(2)}, u32[]{:S(2)}) collective-permute-start(bf16[12,128,128]{2,1,0:T(8,128)(2,1)S(1)} %get-tuple-element.15), channel_id=1, source_target_pairs={{0,16},{16,32},{32,48},{48,64},{64,80},{80,96},{96,112},{112,0},{1... | collective-permute-start | bytes 1179656 | tf_op jit(solution)/shard_map/ppermute | solution.py:222
  85.5 23.4 %collective-permute-start.5 = (bf16[12,128,128]{2,1,0:T(8,128)(2,1)S(1)}, bf16[12,128,128]{2,1,0:T(8,128)(2,1)S(1)}, u32[]{:S(2)}, u32[]{:S(2)}) collective-permute-start(bf16[12,128,128]{2,1,0:T(8,128)(2,1)S(1)} %get-tuple-element.16), channel_id=1, source_target_pairs={{0,16},{16,32},{32,48},{48,64},{64,80},{80,96},{96,112},{112,0},{1... | collective-permute-start | bytes 1179656 | tf_op jit(solution)/shard_map/ppermute | solution.py:222
  85.6 31.7 %collective-permute-start.4 = (bf16[12,128,128]{2,1,0:T(8,128)(2,1)S(1)}, bf16[12,128,128]{2,1,0:T(8,128)(2,1)S(1)}, u32[]{:S(2)}, u32[]{:S(2)}) collective-permute-start(bf16[12,128,128]{2,1,0:T(8,128)(2,1)S(1)} %get-tuple-element.17), channel_id=1, source_target_pairs={{0,16},{16,32},{32,48},{48,64},{64,80},{80,96},{96,112},{112,0},{1... | collective-permute-start | bytes 1179656 | tf_op jit(solution)/shard_map/ppermute | solution.py:222
  92.3 0.8 copy-start.3
  100.6 0.8 copy-start.6
  108.9 0.8 copy-start.5
  117.3 0.8 copy-start.4

commit v11 on v10

--- a/solution.py
+++ b/solution.py
@@ -10,6 +10,7 @@
 BLOCK = 256
 EPSILON = 1e-05
 HEADS_PER_STEP = 6
+SUMMARY_HEADS_PER_STEP = 12
 STATE_CHUNKS = 4
 
 
@@ -127,7 +128,7 @@
 def _summaries(rates, rows, gains, head_dim):
     _, count, width = rows.shape
     heads = width // head_dim
-    hg = HEADS_PER_STEP
+    hg = SUMMARY_HEADS_PER_STEP
     cw = hg * head_dim
     kernel = functools.partial(_summary_kernel, hg=hg, head_dim=head_dim, nblocks=count // BLOCK)
     return pl.pallas_call(

time: 126 us -> 125 us (level)
  transfers between devices with their start and end apart: 10 -> 10, of which waited for: 4 -> 4; matrix products, arithmetic and copies ran while one was open for 1% -> 1% of each run, Pallas kernels for 30% -> 29%
where the time goes in v11:
time: 125 us
  waiting for transfers between devices  56.7 us (45%)
  Pallas kernels  43.9 us (35%)
  starting transfers between devices  17.4 us (14%)
  local copies, waits for them, and re-layouts  5.93 us (5%)
    pallas_call x4, Pallas kernels, _outputs(): pl.pallas_call(kernel, grid_spec=pltpu.PrefetchScalarGridSpec(num_scalar_...  30.2 us
    all_to_all x1, waiting for transfers between devices, on_device(): gathered = lax.all_to_all(summary, 'ctx', 0, 0, tiled=True)  27.7 us
    ppermute x4, waiting for transfers between devices, on_device(): lax.ppermute((section_inputs, input_gains, out_gain, decay_rates), 'secti...  15.1 us
    pallas_call x1, Pallas kernels, _summaries(): pl.pallas_call(kernel, grid_spec=pltpu.PrefetchScalarGridSpec(num_scalar_...  10.1 us
    all_to_all x1, waiting for transfers between devices, on_device(): lax.all_to_all(prefixes.reshape(heads, head_dim, head_dim), 'ctx', 0, 0,...  8.88 us
    all_to_all x1, starting transfers between devices, on_device(): gathered = lax.all_to_all(summary, 'ctx', 0, 0, tiled=True)  8.3 us
    unnamed x23, local copies, waits for them, and re-layouts  5.78 us
    ppermute x4, waiting for transfers between devices, on_device(): lax.ppermute(incoming[part * chunk:(part + 1) * chunk], 'section', pairs)  5.06 us
  transfers between devices with their start and end apart: 10, of which 4 were waited for; matrix products, arithmetic and copies ran while one was open for 1% of the time, Pallas kernels for 29%

profile of v11, /device:TPU:0, one launch (start us, length us, event | category | flops | bytes accessed | tf_op | source)
XLA Modules:
  0.0 124.6 jit_solution(5916701792953682998)
XLA Ops:
  0.6 0.0 collective-permute-start.3
  0.7 1.6 %copy.10.g_ref = f32[1,3,6144]{2,1,0:T(4,128)} copy(f32[1,3,6144]{2,0,1:T(1,128)} %param.6) | data formatting | bytes 147456 | tf_op args[1]
  2.2 10.1 %shard_map.68 = bf16[48,128,128]{2,1,0:T(8,128)(2,1)} custom-call(f32[48]{0:T(128)} %bitcast.11, bf16[1,512,6144]{2,1,0:T(8,128)(2,1)} %x_ref.1, f32[1,3,6144]{2,1,0:T(4,128)} %copy.10.g_ref), custom_call_target="tpu_custom_call" | custom-call | flops 805306368 | bytes 9437184 | tf_op jit(solution)/shard_map/pallas_call | solution.py:134
  12.4 8.3 %all-to-all-start = ((bf16[48,128,128]{2,1,0:T(8,128)(2,1)}), bf16[48,128,128]{2,1,0:T(8,128)(2,1)S(1)}, u32[]{:S(2)}, u32[]{:S(2)}) async-start(bf16[48,128,128]{2,1,0:T(8,128)(2,1)} %shard_map.68), calls=%async_computation | async-start | bytes 3145728 | tf_op jit(solution)/shard_map/all_to_all | solution.py:209
  20.7 27.7 %all-to-all-done = bf16[48,128,128]{2,1,0:T(8,128)(2,1)S(1)} async-done(((bf16[48,128,128]{2,1,0:T(8,128)(2,1)}), bf16[48,128,128]{2,1,0:T(8,128)(2,1)S(1)}, u32[]{:S(2)}, u32[]{:S(2)}) %all-to-all-start) | async-done | bytes 1572896 | tf_op jit(solution)/shard_map/all_to_all | solution.py:209
  48.3 1.1 copy-done
  49.5 3.6 %shard_map.69 = (bf16[16,3,128,128]{3,2,1,0:T(8,128)(2,1)}, f32[1,3,128,128]{3,2,1,0:T(8,128)}) custom-call(s32[1]{0:T(128)} %bitcast.place_ref, f32[48]{0:T(128)} %bitcast.12, bf16[16,3,128,128]{3,2,1,0:T(8,128)(2,1)} %bitcast.5, f32[1,48,128,128]{3,2,1,0:T(8,128)} %c_ref.1), custom_call_target="tpu_custom_call" | custom-call | flops 1572864 | bytes 3538944 | tf_op jit(solution)/shard_map/pallas_call | solution.py:103
  53.1 3.9 %all-to-all-start.1 = ((bf16[48,128,128]{2,1,0:T(8,128)(2,1)}), bf16[48,128,128]{2,1,0:T(8,128)(2,1)S(1)}, u32[]{:S(2)}, u32[]{:S(2)}) async-start(bf16[48,128,128]{2,1,0:T(8,128)(2,1)} %bitcast.6), calls=%async_computation.1 | async-start | bytes 3145728 | tf_op jit(solution)/shard_map/all_to_all | solution.py:214
  57.0 0.2 collective-permute-start
  57.2 1.4 %collective-permute-start.1 = (f32[1,6144]{1,0:T(1,128)S(1)}, f32[1,6144]{1,0:T(1,128)S(1)}, u32[]{:S(2)}, u32[]{:S(2)}) collective-permute-start(f32[1,6144]{1,0:T(1,128)S(1)} %copy-done.10), channel_id=1, source_target_pairs={{0,16},{16,32},{32,48},{48,64},{64,80},{80,96},{96,112},{112,0},{1... | collective-permute-start | bytes 73736 | tf_op jit(solution)/shard_map/ppermute | solution.py:204
  58.6 0.2 collective-permute-start.2
  58.8 15.1 %collective-permute-done.2 = f32[1,48]{1,0:T(1,128)S(1)} collective-permute-done((f32[1,48]{1,0:T(1,128)S(1)}, f32[1,48]{1,0:T(1,128)S(1)}, u32[]{:S(2)}, u32[]{:S(2)}) %collective-permute-start.2) | collective-permute-done | bytes 224 | tf_op jit(solution)/shard_map/ppermute | solution.py:204
  73.9 0.0 collective-permute-done.1.go_ref
  73.9 0.0 collective-permute-done.g_ref
  73.9 8.9 %all-to-all-done.1 = bf16[48,128,128]{2,1,0:T(8,128)(2,1)S(1)} async-done(((bf16[48,128,128]{2,1,0:T(8,128)(2,1)}), bf16[48,128,128]{2,1,0:T(8,128)(2,1)S(1)}, u32[]{:S(2)}, u32[]{:S(2)}) %all-to-all-start.1) | async-done | bytes 1572896 | tf_op jit(solution)/shard_map/all_to_all | solution.py:214
  82.8 0.1 fusion
  82.9 0.0 collective-permute-start.7
  82.9 1.6 %collective-permute-start.6 = (bf16[12,128,128]{2,1,0:T(8,128)(2,1)S(1)}, bf16[12,128,128]{2,1,0:T(8,128)(2,1)S(1)}, u32[]{:S(2)}, u32[]{:S(2)}) collective-permute-start(bf16[12,128,128]{2,1,0:T(8,128)(2,1)S(1)} %get-tuple-element.15), channel_id=1, source_target_pairs={{0,16},{16,32},{32,48},{48,64},{64,80},{80,96},{96,112},{112,0},{1... | collective-permute-start | bytes 1179656 | tf_op jit(solution)/shard_map/ppermute | solution.py:223
  84.6 0.0 collective-permute-start.5
  84.6 1.7 %collective-permute-start.4 = (bf16[12,128,128]{2,1,0:T(8,128)(2,1)S(1)}, bf16[12,128,128]{2,1,0:T(8,128)(2,1)S(1)}, u32[]{:S(2)}, u32[]{:S(2)}) collective-permute-start(bf16[12,128,128]{2,1,0:T(8,128)(2,1)S(1)} %get-tuple-element.17), channel_id=1, source_target_pairs={{0,16},{16,32},{32,48},{48,64},{64,80},{80,96},{96,112},{112,0},{1... | collective-permute-start | bytes 1179656 | tf_op jit(solution)/shard_map/ppermute | solution.py:223
  86.3 5.0 %collective-permute-done.7.s_ref = bf16[12,128,128]{2,1,0:T(8,128)(2,1)S(1)} collective-permute-done((bf16[12,128,128]{2,1,0:T(8,128)(2,1)S(1)}, bf16[12,128,128]{2,1,0:T(8,128)(2,1)S(1)}, u32[]{:S(2)}, u32[]{:S(2)}) %collective-permute-start.7) | collective-permute-done | bytes 393248 | tf_op jit(solution)/shard_map/ppermute | solution.py:223
  91.3 0.0 collective-permute-done.3.x_ref
  91.4 0.7 copy-done.3
  92.1 7.5 %shard_map.70.rest_0_ = bf16[1,512,6144]{2,1,0:T(8,128)(2,1)} custom-call(f32[48]{0:T(128)} %bitcast.7, bf16[1,512,6144]{2,1,0:T(8,128)(2,1)} %collective-permute-done.3.x_ref, f32[1,3,6144]{2,1,0:T(4,128)} %copy-done.1, f32[1,6144]{1,0:T(1,128)} %copy-done.7, bf16[12,128,128]{2,1,0:T(8,128)(2,1)} %copy-done.3), custom_call_target="tpu_custom_call" | custom-call | flops 1610612736 | bytes 3538944 | tf_op jit(solution)/shard_map/pallas_call | solution.py:176
  99.6 0.0 collective-permute-done.6.s_ref
  99.6 0.8 copy-done.6
  100.4 7.5 %shard_map.71.rest_0_ = bf16[1,512,6144]{2,1,0:T(8,128)(2,1)} custom-call(f32[48]{0:T(128)} %bitcast.8, bf16[1,512,6144]{2,1,0:T(8,128)(2,1)} %collective-permute-done.3.x_ref, f32[1,3,6144]{2,1,0:T(4,128)} %copy-done.1, f32[1,6144]{1,0:T(1,128)} %copy-done.7, bf16[12,128,128]{2,1,0:T(8,128)(2,1)} %copy-done.6, ...), custom_call_target="tpu_custom_call", output_to_operand_aliasing={{}: (5, {})} | custom-call | flops 1610612736 | bytes 3538944 | tf_op jit(solution)/shard_map/pallas_call | solution.py:176
  108.0 0.0 collective-permute-done.5.s_ref
  108.0 0.8 copy-done.5
  108.7 7.5 %shard_map.72.rest_0_ = bf16[1,512,6144]{2,1,0:T(8,128)(2,1)} custom-call(f32[48]{0:T(128)} %bitcast.9, bf16[1,512,6144]{2,1,0:T(8,128)(2,1)} %collective-permute-done.3.x_ref, f32[1,3,6144]{2,1,0:T(4,128)} %copy-done.1, f32[1,6144]{1,0:T(1,128)} %copy-done.7, bf16[12,128,128]{2,1,0:T(8,128)(2,1)} %copy-done.5, ...), custom_call_target="tpu_custom_call", output_to_operand_aliasing={{}: (5, {})} | custom-call | flops 1610612736 | bytes 3538944 | tf_op jit(solution)/shard_map/pallas_call | solution.py:176
  116.3 0.8 copy-done.4
  117.0 7.5 %shard_map.73 = bf16[1,512,6144]{2,1,0:T(8,128)(2,1)} custom-call(f32[48]{0:T(128)} %bitcast.10, bf16[1,512,6144]{2,1,0:T(8,128)(2,1)} %collective-permute-done.3.x_ref, f32[1,3,6144]{2,1,0:T(4,128)} %copy-done.1, f32[1,6144]{1,0:T(1,128)} %copy-done.7, bf16[12,128,128]{2,1,0:T(8,128)(2,1)} %copy-done.4, ...), custom_call_target="tpu_custom_call", output_to_operand_aliasing={{}: (5, {})} | custom-call | flops 1610612736 | bytes 3538944 | tf_op jit(solution)/shard_map/pallas_call | solution.py:176
  (18 shorter events, 0.0 us)
Async XLA Ops:
  0.6 90.7 %collective-permute-start.3 = (bf16[1,512,6144]{2,1,0:T(8,128)(2,1)}, bf16[1,512,6144]{2,1,0:T(8,128)(2,1)}, u32[]{:S(2)}, u32[]{:S(2)}) collective-permute-start(bf16[1,512,6144]{2,1,0:T(8,128)(2,1)} %x_ref.1), channel_id=1, source_target_pairs={{0,16},{16,32},{32,48},{48,64},{64,80},{80,96},{96,112},{112,0},{1... | collective-permute-start | bytes 18874376 | tf_op jit(solution)/shard_map/ppermute | solution.py:204
  12.4 44.7 %copy-start.2 = (f32[1,3,6144]{2,1,0:T(4,128)S(1)}, f32[1,3,6144]{2,1,0:T(4,128)}, u32[]{:S(2)}) copy-start(f32[1,3,6144]{2,1,0:T(4,128)} %copy.10.g_ref) | copy-start | bytes 221188
  12.4 44.8 %copy-start.10 = (f32[1,6144]{1,0:T(1,128)S(1)}, f32[1,6144]{1,0:T(1,128)}, u32[]{:S(2)}) copy-start(f32[1,6144]{1,0:T(1,128)} %param.7) | copy-start | bytes 73732
  12.4 46.3 %copy-start.9 = (f32[1,48]{1,0:T(1,128)S(1)}, f32[1,48]{1,0:T(1,128)}, u32[]{:S(2)}) copy-start(f32[1,48]{1,0:T(1,128)} %param.8) | copy-start | bytes 580
  12.4 36.0 %all-to-all-start = ((bf16[48,128,128]{2,1,0:T(8,128)(2,1)}), bf16[48,128,128]{2,1,0:T(8,128)(2,1)S(1)}, u32[]{:S(2)}, u32[]{:S(2)}) async-start(bf16[48,128,128]{2,1,0:T(8,128)(2,1)} %shard_map.68), calls=%async_computation | async-start | bytes 3145728 | tf_op jit(solution)/shard_map/all_to_all | solution.py:209
  48.3 1.1 copy-start
  53.1 29.6 %all-to-all-start.1 = ((bf16[48,128,128]{2,1,0:T(8,128)(2,1)}), bf16[48,128,128]{2,1,0:T(8,128)(2,1)S(1)}, u32[]{:S(2)}, u32[]{:S(2)}) async-start(bf16[48,128,128]{2,1,0:T(8,128)(2,1)} %bitcast.6), calls=%async_computation.1 | async-start | bytes 3145728 | tf_op jit(solution)/shard_map/all_to_all | solution.py:214
  57.0 16.8 %collective-permute-start = (f32[1,3,6144]{2,1,0:T(4,128)S(1)}, f32[1,3,6144]{2,1,0:T(4,128)S(1)}, u32[]{:S(2)}, u32[]{:S(2)}) collective-permute-start(f32[1,3,6144]{2,1,0:T(4,128)S(1)} %copy-done.2), channel_id=1, source_target_pairs={{0,16},{16,32},{32,48},{48,64},{64,80},{80,96},{96,112},{112,0},{1... | collective-permute-start | bytes 221192 | tf_op jit(solution)/shard_map/ppermute | solution.py:204
  57.2 16.7 %collective-permute-start.1 = (f32[1,6144]{1,0:T(1,128)S(1)}, f32[1,6144]{1,0:T(1,128)S(1)}, u32[]{:S(2)}, u32[]{:S(2)}) collective-permute-start(f32[1,6144]{1,0:T(1,128)S(1)} %copy-done.10), channel_id=1, source_target_pairs={{0,16},{16,32},{32,48},{48,64},{64,80},{80,96},{96,112},{112,0},{1... | collective-permute-start | bytes 73736 | tf_op jit(solution)/shard_map/ppermute | solution.py:204
  58.6 15.2 %collective-permute-start.2 = (f32[1,48]{1,0:T(1,128)S(1)}, f32[1,48]{1,0:T(1,128)S(1)}, u32[]{:S(2)}, u32[]{:S(2)}) collective-permute-start(f32[1,48]{1,0:T(1,128)S(1)} %copy-done.9), channel_id=1, source_target_pairs={{0,16},{16,32},{32,48},{48,64},{64,80},{80,96},{96,112},{112,0},{1... | collective-permute-start | bytes 584 | tf_op jit(solution)/shard_map/ppermute | solution.py:204
  73.9 17.5 %copy-start.8 = (f32[1,48]{1,0:T(1,128)}, f32[1,48]{1,0:T(1,128)S(1)}, u32[]{:S(2)}) copy-start(f32[1,48]{1,0:T(1,128)S(1)} %collective-permute-done.2) | copy-start | bytes 580
  73.9 17.5 %copy-start.7 = (f32[1,6144]{1,0:T(1,128)}, f32[1,6144]{1,0:T(1,128)S(1)}, u32[]{:S(2)}) copy-start(f32[1,6144]{1,0:T(1,128)S(1)} %collective-permute-done.1.go_ref) | copy-start | bytes 73732
  73.9 17.5 %copy-start.1 = (f32[1,3,6144]{2,1,0:T(4,128)}, f32[1,3,6144]{2,1,0:T(4,128)S(1)}, u32[]{:S(2)}) copy-start(f32[1,3,6144]{2,1,0:T(4,128)S(1)} %collective-permute-done.g_ref) | copy-start | bytes 221188
  82.9 8.4 %collective-permute-start.7 = (bf16[12,128,128]{2,1,0:T(8,128)(2,1)S(1)}, bf16[12,128,128]{2,1,0:T(8,128)(2,1)S(1)}, u32[]{:S(2)}, u32[]{:S(2)}) collective-permute-start(bf16[12,128,128]{2,1,0:T(8,128)(2,1)S(1)} %get-tuple-element.14), channel_id=1, source_target_pairs={{0,16},{16,32},{32,48},{48,64},{64,80},{80,96},{96,112},{112,0},{1... | collective-permute-start | bytes 1179656 | tf_op jit(solution)/shard_map/ppermute | solution.py:223
  82.9 16.7 %collective-permute-start.6 = (bf16[12,128,128]{2,1,0:T(8,128)(2,1)S(1)}, bf16[12,128,128]{2,1,0:T(8,128)(2,1)S(1)}, u32[]{:S(2)}, u32[]{:S(2)}) collective-permute-start(bf16[12,128,128]{2,1,0:T(8,128)(2,1)S(1)} %get-tuple-element.15), channel_id=1, source_target_pairs={{0,16},{16,32},{32,48},{48,64},{64,80},{80,96},{96,112},{112,0},{1... | collective-permute-start | bytes 1179656 | tf_op jit(solution)/shard_map/ppermute | solution.py:223
  84.6 23.4 %collective-permute-start.5 = (bf16[12,128,128]{2,1,0:T(8,128)(2,1)S(1)}, bf16[12,128,128]{2,1,0:T(8,128)(2,1)S(1)}, u32[]{:S(2)}, u32[]{:S(2)}) collective-permute-start(bf16[12,128,128]{2,1,0:T(8,128)(2,1)S(1)} %get-tuple-element.16), channel_id=1, source_target_pairs={{0,16},{16,32},{32,48},{48,64},{64,80},{80,96},{96,112},{112,0},{1... | collective-permute-start | bytes 1179656 | tf_op jit(solution)/shard_map/ppermute | solution.py:223
  84.6 31.7 %collective-permute-start.4 = (bf16[12,128,128]{2,1,0:T(8,128)(2,1)S(1)}, bf16[12,128,128]{2,1,0:T(8,128)(2,1)S(1)}, u32[]{:S(2)}, u32[]{:S(2)}) collective-permute-start(bf16[12,128,128]{2,1,0:T(8,128)(2,1)S(1)} %get-tuple-element.17), channel_id=1, source_target_pairs={{0,16},{16,32},{32,48},{48,64},{64,80},{80,96},{96,112},{112,0},{1... | collective-permute-start | bytes 1179656 | tf_op jit(solution)/shard_map/ppermute | solution.py:223
  91.3 0.8 copy-start.3
  99.6 0.8 copy-start.6
  108.0 0.8 copy-start.5
  116.3 0.8 copy-start.4

commit v12 on v11

--- a/solution.py
+++ b/solution.py
@@ -77,9 +77,11 @@
             values_b = (x * g_ref[0, 2:3, cols]).astype(jnp.bfloat16)
             scores = _dot_nt(queries_b, keys_b)
             weights = (scores * mask).astype(jnp.bfloat16)
-            local = _dot(weights, values_b)
-            cross = _dot(queries_b, state.astype(jnp.bfloat16))
-            total = local + lead * cross
+            scaled_q = (queries_b.astype(jnp.float32) * lead).astype(jnp.bfloat16)
+            total = _dot(
+                jnp.concatenate([weights, scaled_q], axis=1),
+                jnp.concatenate([values_b, state.astype(jnp.bfloat16)], axis=0),
+            )
             normed = total * lax.rsqrt(jnp.mean(total * total, axis=-1, keepdims=True) + EPSILON)
             o_ref[0, rows, cols] = (x + normed * go_ref[0:1, cols]).astype(o_ref.dtype)
             if b + 1 < nblocks:

time: 125 us -> 127 us (1.016)
  Pallas kernels: 43.9 us -> 45.8 us
    pallas_call x4, Pallas kernels: 30.2 us -> 32 us  [_outputs(): pl.pallas_call(kernel, grid_spec=pltpu.PrefetchScalarGridSpec(num_scalar_...]
  transfers between devices with their start and end apart: 10 -> 10, of which waited for: 4 -> 4; matrix products, arithmetic and copies ran while one was open for 1% -> 1% of each run, Pallas kernels for 29% -> 30%
where the time goes in v12:
time: 127 us; the launch traced here: 126 us
  waiting for transfers between devices  56.7 us (45%)
  Pallas kernels  45.8 us (36%)
  starting transfers between devices  17.4 us (14%)
  local copies, waits for them, and re-layouts  5.93 us (5%)
    pallas_call x4, Pallas kernels, _outputs(): pl.pallas_call(kernel, grid_spec=pltpu.PrefetchScalarGridSpec(num_scalar_...  32 us
    all_to_all x1, waiting for transfers between devices, on_device(): gathered = lax.all_to_all(summary, 'ctx', 0, 0, tiled=True)  27.7 us
    ppermute x4, waiting for transfers between devices, on_device(): lax.ppermute((section_inputs, input_gains, out_gain, decay_rates), 'secti...  15.1 us
    pallas_call x1, Pallas kernels, _summaries(): pl.pallas_call(kernel, grid_spec=pltpu.PrefetchScalarGridSpec(num_scalar_...  10.1 us
    all_to_all x1, waiting for transfers between devices, on_device(): lax.all_to_all(prefixes.reshape(heads, head_dim, head_dim), 'ctx', 0, 0,...  8.88 us
    all_to_all x1, starting transfers between devices, on_device(): gathered = lax.all_to_all(summary, 'ctx', 0, 0, tiled=True)  8.3 us
    unnamed x23, local copies, waits for them, and re-layouts  5.78 us
    ppermute x4, waiting for transfers between devices, on_device(): lax.ppermute(incoming[part * chunk:(part + 1) * chunk], 'section', pairs)  5.06 us
  transfers between devices with their start and end apart: 10, of which 4 were waited for; matrix products, arithmetic and copies ran while one was open for 1% of the time, Pallas kernels for 30%

profile of v12, /device:TPU:0, one launch (start us, length us, event | category | flops | bytes accessed | tf_op | source)
XLA Modules:
  0.0 126.4 jit_solution(8873000677581714288)
XLA Ops:
  0.6 0.0 collective-permute-start.3
  0.7 1.6 %copy.10.g_ref = f32[1,3,6144]{2,1,0:T(4,128)} copy(f32[1,3,6144]{2,0,1:T(1,128)} %param.6) | data formatting | bytes 147456 | tf_op args[1]
  2.2 10.1 %shard_map.68 = bf16[48,128,128]{2,1,0:T(8,128)(2,1)} custom-call(f32[48]{0:T(128)} %bitcast.11, bf16[1,512,6144]{2,1,0:T(8,128)(2,1)} %x_ref.1, f32[1,3,6144]{2,1,0:T(4,128)} %copy.10.g_ref), custom_call_target="tpu_custom_call" | custom-call | flops 805306368 | bytes 9437184 | tf_op jit(solution)/shard_map/pallas_call | solution.py:136
  12.4 8.3 %all-to-all-start = ((bf16[48,128,128]{2,1,0:T(8,128)(2,1)}), bf16[48,128,128]{2,1,0:T(8,128)(2,1)S(1)}, u32[]{:S(2)}, u32[]{:S(2)}) async-start(bf16[48,128,128]{2,1,0:T(8,128)(2,1)} %shard_map.68), calls=%async_computation | async-start | bytes 3145728 | tf_op jit(solution)/shard_map/all_to_all | solution.py:211
  20.7 27.7 %all-to-all-done = bf16[48,128,128]{2,1,0:T(8,128)(2,1)S(1)} async-done(((bf16[48,128,128]{2,1,0:T(8,128)(2,1)}), bf16[48,128,128]{2,1,0:T(8,128)(2,1)S(1)}, u32[]{:S(2)}, u32[]{:S(2)}) %all-to-all-start) | async-done | bytes 1572896 | tf_op jit(solution)/shard_map/all_to_all | solution.py:211
  48.3 1.1 copy-done
  49.5 3.6 %shard_map.69 = (bf16[16,3,128,128]{3,2,1,0:T(8,128)(2,1)}, f32[1,3,128,128]{3,2,1,0:T(8,128)}) custom-call(s32[1]{0:T(128)} %bitcast.place_ref, f32[48]{0:T(128)} %bitcast.12, bf16[16,3,128,128]{3,2,1,0:T(8,128)(2,1)} %bitcast.5, f32[1,48,128,128]{3,2,1,0:T(8,128)} %c_ref.1), custom_call_target="tpu_custom_call" | custom-call | flops 1572864 | bytes 3538944 | tf_op jit(solution)/shard_map/pallas_call | solution.py:105
  53.1 3.9 %all-to-all-start.1 = ((bf16[48,128,128]{2,1,0:T(8,128)(2,1)}), bf16[48,128,128]{2,1,0:T(8,128)(2,1)S(1)}, u32[]{:S(2)}, u32[]{:S(2)}) async-start(bf16[48,128,128]{2,1,0:T(8,128)(2,1)} %bitcast.6), calls=%async_computation.1 | async-start | bytes 3145728 | tf_op jit(solution)/shard_map/all_to_all | solution.py:216
  57.0 0.2 collective-permute-start
  57.2 1.4 %collective-permute-start.1 = (f32[1,6144]{1,0:T(1,128)S(1)}, f32[1,6144]{1,0:T(1,128)S(1)}, u32[]{:S(2)}, u32[]{:S(2)}) collective-permute-start(f32[1,6144]{1,0:T(1,128)S(1)} %copy-done.10), channel_id=1, source_target_pairs={{0,16},{16,32},{32,48},{48,64},{64,80},{80,96},{96,112},{112,0},{1... | collective-permute-start | bytes 73736 | tf_op jit(solution)/shard_map/ppermute | solution.py:206
  58.6 0.2 collective-permute-start.2
  58.8 15.1 %collective-permute-done.2 = f32[1,48]{1,0:T(1,128)S(1)} collective-permute-done((f32[1,48]{1,0:T(1,128)S(1)}, f32[1,48]{1,0:T(1,128)S(1)}, u32[]{:S(2)}, u32[]{:S(2)}) %collective-permute-start.2) | collective-permute-done | bytes 224 | tf_op jit(solution)/shard_map/ppermute | solution.py:206
  73.9 0.0 collective-permute-done.1.go_ref
  73.9 0.0 collective-permute-done.g_ref
  73.9 8.9 %all-to-all-done.1 = bf16[48,128,128]{2,1,0:T(8,128)(2,1)S(1)} async-done(((bf16[48,128,128]{2,1,0:T(8,128)(2,1)}), bf16[48,128,128]{2,1,0:T(8,128)(2,1)S(1)}, u32[]{:S(2)}, u32[]{:S(2)}) %all-to-all-start.1) | async-done | bytes 1572896 | tf_op jit(solution)/shard_map/all_to_all | solution.py:216
  82.8 0.1 fusion
  82.9 0.0 collective-permute-start.7
  82.9 1.6 %collective-permute-start.6 = (bf16[12,128,128]{2,1,0:T(8,128)(2,1)S(1)}, bf16[12,128,128]{2,1,0:T(8,128)(2,1)S(1)}, u32[]{:S(2)}, u32[]{:S(2)}) collective-permute-start(bf16[12,128,128]{2,1,0:T(8,128)(2,1)S(1)} %get-tuple-element.15), channel_id=1, source_target_pairs={{0,16},{16,32},{32,48},{48,64},{64,80},{80,96},{96,112},{112,0},{1... | collective-permute-start | bytes 1179656 | tf_op jit(solution)/shard_map/ppermute | solution.py:225
  84.6 0.0 collective-permute-start.5
  84.6 1.7 %collective-permute-start.4 = (bf16[12,128,128]{2,1,0:T(8,128)(2,1)S(1)}, bf16[12,128,128]{2,1,0:T(8,128)(2,1)S(1)}, u32[]{:S(2)}, u32[]{:S(2)}) collective-permute-start(bf16[12,128,128]{2,1,0:T(8,128)(2,1)S(1)} %get-tuple-element.17), channel_id=1, source_target_pairs={{0,16},{16,32},{32,48},{48,64},{64,80},{80,96},{96,112},{112,0},{1... | collective-permute-start | bytes 1179656 | tf_op jit(solution)/shard_map/ppermute | solution.py:225
  86.3 5.0 %collective-permute-done.7.s_ref = bf16[12,128,128]{2,1,0:T(8,128)(2,1)S(1)} collective-permute-done((bf16[12,128,128]{2,1,0:T(8,128)(2,1)S(1)}, bf16[12,128,128]{2,1,0:T(8,128)(2,1)S(1)}, u32[]{:S(2)}, u32[]{:S(2)}) %collective-permute-start.7) | collective-permute-done | bytes 393248 | tf_op jit(solution)/shard_map/ppermute | solution.py:225
  91.3 0.0 collective-permute-done.3.x_ref
  91.4 0.7 copy-done.3
  92.1 8.0 %shard_map.70.rest_0_ = bf16[1,512,6144]{2,1,0:T(8,128)(2,1)} custom-call(f32[48]{0:T(128)} %bitcast.7, bf16[1,512,6144]{2,1,0:T(8,128)(2,1)} %collective-permute-done.3.x_ref, f32[1,3,6144]{2,1,0:T(4,128)} %copy-done.1, f32[1,6144]{1,0:T(1,128)} %copy-done.7, bf16[12,128,128]{2,1,0:T(8,128)(2,1)} %copy-done.3), custom_call_target="tpu_custom_call" | custom-call | flops 1610612736 | bytes 3538944 | tf_op jit(solution)/shard_map/pallas_call | solution.py:178
  100.1 0.0 collective-permute-done.6.s_ref
  100.1 0.8 copy-done.6
  100.9 8.0 %shard_map.71.rest_0_ = bf16[1,512,6144]{2,1,0:T(8,128)(2,1)} custom-call(f32[48]{0:T(128)} %bitcast.8, bf16[1,512,6144]{2,1,0:T(8,128)(2,1)} %collective-permute-done.3.x_ref, f32[1,3,6144]{2,1,0:T(4,128)} %copy-done.1, f32[1,6144]{1,0:T(1,128)} %copy-done.7, bf16[12,128,128]{2,1,0:T(8,128)(2,1)} %copy-done.6, ...), custom_call_target="tpu_custom_call", output_to_operand_aliasing={{}: (5, {})} | custom-call | flops 1610612736 | bytes 3538944 | tf_op jit(solution)/shard_map/pallas_call | solution.py:178
  108.9 0.0 collective-permute-done.5.s_ref
  108.9 0.8 copy-done.5
  109.6 8.0 %shard_map.72.rest_0_ = bf16[1,512,6144]{2,1,0:T(8,128)(2,1)} custom-call(f32[48]{0:T(128)} %bitcast.9, bf16[1,512,6144]{2,1,0:T(8,128)(2,1)} %collective-permute-done.3.x_ref, f32[1,3,6144]{2,1,0:T(4,128)} %copy-done.1, f32[1,6144]{1,0:T(1,128)} %copy-done.7, bf16[12,128,128]{2,1,0:T(8,128)(2,1)} %copy-done.5, ...), custom_call_target="tpu_custom_call", output_to_operand_aliasing={{}: (5, {})} | custom-call | flops 1610612736 | bytes 3538944 | tf_op jit(solution)/shard_map/pallas_call | solution.py:178
  117.7 0.8 copy-done.4
  118.4 8.0 %shard_map.73 = bf16[1,512,6144]{2,1,0:T(8,128)(2,1)} custom-call(f32[48]{0:T(128)} %bitcast.10, bf16[1,512,6144]{2,1,0:T(8,128)(2,1)} %collective-permute-done.3.x_ref, f32[1,3,6144]{2,1,0:T(4,128)} %copy-done.1, f32[1,6144]{1,0:T(1,128)} %copy-done.7, bf16[12,128,128]{2,1,0:T(8,128)(2,1)} %copy-done.4, ...), custom_call_target="tpu_custom_call", output_to_operand_aliasing={{}: (5, {})} | custom-call | flops 1610612736 | bytes 3538944 | tf_op jit(solution)/shard_map/pallas_call | solution.py:178
  (18 shorter events, 0.0 us)
Async XLA Ops:
  0.6 90.7 %collective-permute-start.3 = (bf16[1,512,6144]{2,1,0:T(8,128)(2,1)}, bf16[1,512,6144]{2,1,0:T(8,128)(2,1)}, u32[]{:S(2)}, u32[]{:S(2)}) collective-permute-start(bf16[1,512,6144]{2,1,0:T(8,128)(2,1)} %x_ref.1), channel_id=1, source_target_pairs={{0,16},{16,32},{32,48},{48,64},{64,80},{80,96},{96,112},{112,0},{1... | collective-permute-start | bytes 18874376 | tf_op jit(solution)/shard_map/ppermute | solution.py:206
  12.4 44.7 %copy-start.2 = (f32[1,3,6144]{2,1,0:T(4,128)S(1)}, f32[1,3,6144]{2,1,0:T(4,128)}, u32[]{:S(2)}) copy-start(f32[1,3,6144]{2,1,0:T(4,128)} %copy.10.g_ref) | copy-start | bytes 221188
  12.4 44.8 %copy-start.10 = (f32[1,6144]{1,0:T(1,128)S(1)}, f32[1,6144]{1,0:T(1,128)}, u32[]{:S(2)}) copy-start(f32[1,6144]{1,0:T(1,128)} %param.7) | copy-start | bytes 73732
  12.4 46.3 %copy-start.9 = (f32[1,48]{1,0:T(1,128)S(1)}, f32[1,48]{1,0:T(1,128)}, u32[]{:S(2)}) copy-start(f32[1,48]{1,0:T(1,128)} %param.8) | copy-start | bytes 580
  12.4 36.0 %all-to-all-start = ((bf16[48,128,128]{2,1,0:T(8,128)(2,1)}), bf16[48,128,128]{2,1,0:T(8,128)(2,1)S(1)}, u32[]{:S(2)}, u32[]{:S(2)}) async-start(bf16[48,128,128]{2,1,0:T(8,128)(2,1)} %shard_map.68), calls=%async_computation | async-start | bytes 3145728 | tf_op jit(solution)/shard_map/all_to_all | solution.py:211
  48.3 1.1 copy-start
  53.1 29.6 %all-to-all-start.1 = ((bf16[48,128,128]{2,1,0:T(8,128)(2,1)}), bf16[48,128,128]{2,1,0:T(8,128)(2,1)S(1)}, u32[]{:S(2)}, u32[]{:S(2)}) async-start(bf16[48,128,128]{2,1,0:T(8,128)(2,1)} %bitcast.6), calls=%async_computation.1 | async-start | bytes 3145728 | tf_op jit(solution)/shard_map/all_to_all | solution.py:216
  57.0 16.8 %collective-permute-start = (f32[1,3,6144]{2,1,0:T(4,128)S(1)}, f32[1,3,6144]{2,1,0:T(4,128)S(1)}, u32[]{:S(2)}, u32[]{:S(2)}) collective-permute-start(f32[1,3,6144]{2,1,0:T(4,128)S(1)} %copy-done.2), channel_id=1, source_target_pairs={{0,16},{16,32},{32,48},{48,64},{64,80},{80,96},{96,112},{112,0},{1... | collective-permute-start | bytes 221192 | tf_op jit(solution)/shard_map/ppermute | solution.py:206
  57.2 16.7 %collective-permute-start.1 = (f32[1,6144]{1,0:T(1,128)S(1)}, f32[1,6144]{1,0:T(1,128)S(1)}, u32[]{:S(2)}, u32[]{:S(2)}) collective-permute-start(f32[1,6144]{1,0:T(1,128)S(1)} %copy-done.10), channel_id=1, source_target_pairs={{0,16},{16,32},{32,48},{48,64},{64,80},{80,96},{96,112},{112,0},{1... | collective-permute-start | bytes 73736 | tf_op jit(solution)/shard_map/ppermute | solution.py:206
  58.6 15.2 %collective-permute-start.2 = (f32[1,48]{1,0:T(1,128)S(1)}, f32[1,48]{1,0:T(1,128)S(1)}, u32[]{:S(2)}, u32[]{:S(2)}) collective-permute-start(f32[1,48]{1,0:T(1,128)S(1)} %copy-done.9), channel_id=1, source_target_pairs={{0,16},{16,32},{32,48},{48,64},{64,80},{80,96},{96,112},{112,0},{1... | collective-permute-start | bytes 584 | tf_op jit(solution)/shard_map/ppermute | solution.py:206
  73.9 17.5 %copy-start.8 = (f32[1,48]{1,0:T(1,128)}, f32[1,48]{1,0:T(1,128)S(1)}, u32[]{:S(2)}) copy-start(f32[1,48]{1,0:T(1,128)S(1)} %collective-permute-done.2) | copy-start | bytes 580
  73.9 17.5 %copy-start.7 = (f32[1,6144]{1,0:T(1,128)}, f32[1,6144]{1,0:T(1,128)S(1)}, u32[]{:S(2)}) copy-start(f32[1,6144]{1,0:T(1,128)S(1)} %collective-permute-done.1.go_ref) | copy-start | bytes 73732
  73.9 17.5 %copy-start.1 = (f32[1,3,6144]{2,1,0:T(4,128)}, f32[1,3,6144]{2,1,0:T(4,128)S(1)}, u32[]{:S(2)}) copy-start(f32[1,3,6144]{2,1,0:T(4,128)S(1)} %collective-permute-done.g_ref) | copy-start | bytes 221188
  82.9 8.4 %collective-permute-start.7 = (bf16[12,128,128]{2,1,0:T(8,128)(2,1)S(1)}, bf16[12,128,128]{2,1,0:T(8,128)(2,1)S(1)}, u32[]{:S(2)}, u32[]{:S(2)}) collective-permute-start(bf16[12,128,128]{2,1,0:T(8,128)(2,1)S(1)} %get-tuple-element.14), channel_id=1, source_target_pairs={{0,16},{16,32},{32,48},{48,64},{64,80},{80,96},{96,112},{112,0},{1... | collective-permute-start | bytes 1179656 | tf_op jit(solution)/shard_map/ppermute | solution.py:225
  82.9 17.2 %collective-permute-start.6 = (bf16[12,128,128]{2,1,0:T(8,128)(2,1)S(1)}, bf16[12,128,128]{2,1,0:T(8,128)(2,1)S(1)}, u32[]{:S(2)}, u32[]{:S(2)}) collective-permute-start(bf16[12,128,128]{2,1,0:T(8,128)(2,1)S(1)} %get-tuple-element.15), channel_id=1, source_target_pairs={{0,16},{16,32},{32,48},{48,64},{64,80},{80,96},{96,112},{112,0},{1... | collective-permute-start | bytes 1179656 | tf_op jit(solution)/shard_map/ppermute | solution.py:225
  84.6 24.3 %collective-permute-start.5 = (bf16[12,128,128]{2,1,0:T(8,128)(2,1)S(1)}, bf16[12,128,128]{2,1,0:T(8,128)(2,1)S(1)}, u32[]{:S(2)}, u32[]{:S(2)}) collective-permute-start(bf16[12,128,128]{2,1,0:T(8,128)(2,1)S(1)} %get-tuple-element.16), channel_id=1, source_target_pairs={{0,16},{16,32},{32,48},{48,64},{64,80},{80,96},{96,112},{112,0},{1... | collective-permute-start | bytes 1179656 | tf_op jit(solution)/shard_map/ppermute | solution.py:225
  84.6 33.1 %collective-permute-start.4 = (bf16[12,128,128]{2,1,0:T(8,128)(2,1)S(1)}, bf16[12,128,128]{2,1,0:T(8,128)(2,1)S(1)}, u32[]{:S(2)}, u32[]{:S(2)}) collective-permute-start(bf16[12,128,128]{2,1,0:T(8,128)(2,1)S(1)} %get-tuple-element.17), channel_id=1, source_target_pairs={{0,16},{16,32},{32,48},{48,64},{64,80},{80,96},{96,112},{112,0},{1... | collective-permute-start | bytes 1179656 | tf_op jit(solution)/shard_map/ppermute | solution.py:225
  91.3 0.8 copy-start.3
  100.1 0.8 copy-start.6
  108.9 0.8 copy-start.5
  117.7 0.8 copy-start.4

commit v13 on v11

--- a/solution.py
+++ b/solution.py
@@ -87,14 +87,13 @@
 
 
 def _scan_kernel(place_ref, rates_ref, s_ref, c_ref, p_ref, e_ref, *, count, own, sources):
-    for hh in range(own):
-        rate = jnp.full((1, 1), rates_ref[place_ref[0] * own + hh], jnp.float32)
-        decay = jnp.exp(-rate * count)
-        state = c_ref[0, hh]
-        for c in range(sources):
-            p_ref[c, hh] = state.astype(p_ref.dtype)
-            state = decay * state + s_ref[c, hh].astype(jnp.float32)
-        e_ref[0, hh] = state
+    rate = jnp.full((1, 1), rates_ref[place_ref[0] * own + pl.program_id(0)], jnp.float32)
+    decay = jnp.exp(-rate * count)
+    state = c_ref[0, 0]
+    for c in range(sources):
+        p_ref[c, 0] = state.astype(p_ref.dtype)
+        state = decay * state + s_ref[c, 0].astype(jnp.float32)
+    e_ref[0, 0] = state
 
 
 def _scan(place, rates, gathered, carry, count):
@@ -104,14 +103,14 @@
         kernel,
         grid_spec=pltpu.PrefetchScalarGridSpec(
             num_scalar_prefetch=2,
-            grid=(1,),
+            grid=(own,),
             in_specs=[
-                pl.BlockSpec((sources, own, hd, hd), lambda i, p, r: (0, 0, 0, 0)),
-                pl.BlockSpec((1, own, hd, hd), lambda i, p, r: (0, p[0], 0, 0)),
+                pl.BlockSpec((sources, 1, hd, hd), lambda i, p, r: (0, i, 0, 0)),
+                pl.BlockSpec((1, 1, hd, hd), lambda i, p, r: (0, p[0] * own + i, 0, 0)),
             ],
             out_specs=[
-                pl.BlockSpec((sources, own, hd, hd), lambda i, p, r: (0, 0, 0, 0)),
-                pl.BlockSpec((1, own, hd, hd), lambda i, p, r: (0, 0, 0, 0)),
+                pl.BlockSpec((sources, 1, hd, hd), lambda i, p, r: (0, i, 0, 0)),
+                pl.BlockSpec((1, 1, hd, hd), lambda i, p, r: (0, i, 0, 0)),
             ],
         ),
         out_shape=[

time: 125 us -> 126 us (level)
  transfers between devices with their start and end apart: 10 -> 10, of which waited for: 4 -> 4; matrix products, arithmetic and copies ran while one was open for 1% -> 1% of each run, Pallas kernels for 29% -> 30%
where the time goes in v13:
time: 126 us; the launch traced here: 125 us
  waiting for transfers between devices  56.7 us (45%)
  Pallas kernels  44.6 us (35%)
  starting transfers between devices  17.4 us (14%)
  local copies, waits for them, and re-layouts  5.93 us (5%)
    pallas_call x4, Pallas kernels, _outputs(): pl.pallas_call(kernel, grid_spec=pltpu.PrefetchScalarGridSpec(num_scalar_...  30.2 us
    all_to_all x1, waiting for transfers between devices, on_device(): gathered = lax.all_to_all(summary, 'ctx', 0, 0, tiled=True)  27.7 us
    ppermute x4, waiting for transfers between devices, on_device(): lax.ppermute((section_inputs, input_gains, out_gain, decay_rates), 'secti...  14.4 us
    pallas_call x1, Pallas kernels, _summaries(): pl.pallas_call(kernel, grid_spec=pltpu.PrefetchScalarGridSpec(num_scalar_...  10.1 us
    all_to_all x1, waiting for transfers between devices, on_device(): lax.all_to_all(prefixes.reshape(heads, head_dim, head_dim), 'ctx', 0, 0,...  9.53 us
    all_to_all x1, starting transfers between devices, on_device(): gathered = lax.all_to_all(summary, 'ctx', 0, 0, tiled=True)  8.3 us
    unnamed x23, local copies, waits for them, and re-layouts  5.78 us
    ppermute x4, waiting for transfers between devices, on_device(): lax.ppermute(incoming[part * chunk:(part + 1) * chunk], 'section', pairs)  5.06 us
  transfers between devices with their start and end apart: 10, of which 4 were waited for; matrix products, arithmetic and copies ran while one was open for 1% of the time, Pallas kernels for 30%

profile of v13, /device:TPU:0, one launch (start us, length us, event | category | flops | bytes accessed | tf_op | source)
XLA Modules:
  0.0 125.2 jit_solution(11501991338015031517)
XLA Ops:
  0.6 0.0 collective-permute-start.3
  0.7 1.6 %copy.10.g_ref = f32[1,3,6144]{2,1,0:T(4,128)} copy(f32[1,3,6144]{2,0,1:T(1,128)} %param.6) | data formatting | bytes 147456 | tf_op args[1]
  2.2 10.1 %shard_map.68 = bf16[48,128,128]{2,1,0:T(8,128)(2,1)} custom-call(f32[48]{0:T(128)} %bitcast.11, bf16[1,512,6144]{2,1,0:T(8,128)(2,1)} %x_ref.1, f32[1,3,6144]{2,1,0:T(4,128)} %copy.10.g_ref), custom_call_target="tpu_custom_call" | custom-call | flops 805306368 | bytes 9437184 | tf_op jit(solution)/shard_map/pallas_call | solution.py:133
  12.4 8.3 %all-to-all-start = ((bf16[48,128,128]{2,1,0:T(8,128)(2,1)}), bf16[48,128,128]{2,1,0:T(8,128)(2,1)S(1)}, u32[]{:S(2)}, u32[]{:S(2)}) async-start(bf16[48,128,128]{2,1,0:T(8,128)(2,1)} %shard_map.68), calls=%async_computation | async-start | bytes 3145728 | tf_op jit(solution)/shard_map/all_to_all | solution.py:208
  20.7 27.7 %all-to-all-done = bf16[48,128,128]{2,1,0:T(8,128)(2,1)S(1)} async-done(((bf16[48,128,128]{2,1,0:T(8,128)(2,1)}), bf16[48,128,128]{2,1,0:T(8,128)(2,1)S(1)}, u32[]{:S(2)}, u32[]{:S(2)}) %all-to-all-start) | async-done | bytes 1572896 | tf_op jit(solution)/shard_map/all_to_all | solution.py:208
  48.3 1.1 copy-done
  49.5 4.3 %shard_map.69 = (bf16[16,3,128,128]{3,2,1,0:T(8,128)(2,1)}, f32[1,3,128,128]{3,2,1,0:T(8,128)}) custom-call(s32[1]{0:T(128)} %bitcast.place_ref, f32[48]{0:T(128)} %bitcast.12, bf16[16,3,128,128]{3,2,1,0:T(8,128)(2,1)} %bitcast.5, f32[1,48,128,128]{3,2,1,0:T(8,128)} %c_ref.1), custom_call_target="tpu_custom_call" | custom-call | flops 1572864 | bytes 3538944 | tf_op jit(solution)/shard_map/pallas_call | solution.py:102
  53.8 3.9 %all-to-all-start.1 = ((bf16[48,128,128]{2,1,0:T(8,128)(2,1)}), bf16[48,128,128]{2,1,0:T(8,128)(2,1)S(1)}, u32[]{:S(2)}, u32[]{:S(2)}) async-start(bf16[48,128,128]{2,1,0:T(8,128)(2,1)} %bitcast.6), calls=%async_computation.1 | async-start | bytes 3145728 | tf_op jit(solution)/shard_map/all_to_all | solution.py:213
  57.7 0.2 collective-permute-start
  57.9 1.4 %collective-permute-start.1 = (f32[1,6144]{1,0:T(1,128)S(1)}, f32[1,6144]{1,0:T(1,128)S(1)}, u32[]{:S(2)}, u32[]{:S(2)}) collective-permute-start(f32[1,6144]{1,0:T(1,128)S(1)} %copy-done.10), channel_id=1, source_target_pairs={{0,16},{16,32},{32,48},{48,64},{64,80},{80,96},{96,112},{112,0},{1... | collective-permute-start | bytes 73736 | tf_op jit(solution)/shard_map/ppermute | solution.py:203
  59.3 0.2 collective-permute-start.2
  59.5 14.4 %collective-permute-done.2 = f32[1,48]{1,0:T(1,128)S(1)} collective-permute-done((f32[1,48]{1,0:T(1,128)S(1)}, f32[1,48]{1,0:T(1,128)S(1)}, u32[]{:S(2)}, u32[]{:S(2)}) %collective-permute-start.2) | collective-permute-done | bytes 224 | tf_op jit(solution)/shard_map/ppermute | solution.py:203
  73.9 0.0 collective-permute-done.1.go_ref
  73.9 0.0 collective-permute-done.g_ref
  73.9 9.5 %all-to-all-done.1 = bf16[48,128,128]{2,1,0:T(8,128)(2,1)S(1)} async-done(((bf16[48,128,128]{2,1,0:T(8,128)(2,1)}), bf16[48,128,128]{2,1,0:T(8,128)(2,1)S(1)}, u32[]{:S(2)}, u32[]{:S(2)}) %all-to-all-start.1) | async-done | bytes 1572896 | tf_op jit(solution)/shard_map/all_to_all | solution.py:213
  83.4 0.1 fusion
  83.6 0.0 collective-permute-start.7
  83.6 1.6 %collective-permute-start.6 = (bf16[12,128,128]{2,1,0:T(8,128)(2,1)S(1)}, bf16[12,128,128]{2,1,0:T(8,128)(2,1)S(1)}, u32[]{:S(2)}, u32[]{:S(2)}) collective-permute-start(bf16[12,128,128]{2,1,0:T(8,128)(2,1)S(1)} %get-tuple-element.15), channel_id=1, source_target_pairs={{0,16},{16,32},{32,48},{48,64},{64,80},{80,96},{96,112},{112,0},{1... | collective-permute-start | bytes 1179656 | tf_op jit(solution)/shard_map/ppermute | solution.py:222
  85.2 0.0 collective-permute-start.5
  85.2 1.7 %collective-permute-start.4 = (bf16[12,128,128]{2,1,0:T(8,128)(2,1)S(1)}, bf16[12,128,128]{2,1,0:T(8,128)(2,1)S(1)}, u32[]{:S(2)}, u32[]{:S(2)}) collective-permute-start(bf16[12,128,128]{2,1,0:T(8,128)(2,1)S(1)} %get-tuple-element.17), channel_id=1, source_target_pairs={{0,16},{16,32},{32,48},{48,64},{64,80},{80,96},{96,112},{112,0},{1... | collective-permute-start | bytes 1179656 | tf_op jit(solution)/shard_map/ppermute | solution.py:222
  87.0 5.0 %collective-permute-done.7.s_ref = bf16[12,128,128]{2,1,0:T(8,128)(2,1)S(1)} collective-permute-done((bf16[12,128,128]{2,1,0:T(8,128)(2,1)S(1)}, bf16[12,128,128]{2,1,0:T(8,128)(2,1)S(1)}, u32[]{:S(2)}, u32[]{:S(2)}) %collective-permute-start.7) | collective-permute-done | bytes 393248 | tf_op jit(solution)/shard_map/ppermute | solution.py:222
  92.0 0.0 collective-permute-done.3.x_ref
  92.0 0.7 copy-done.3
  92.8 7.5 %shard_map.70.rest_0_ = bf16[1,512,6144]{2,1,0:T(8,128)(2,1)} custom-call(f32[48]{0:T(128)} %bitcast.7, bf16[1,512,6144]{2,1,0:T(8,128)(2,1)} %collective-permute-done.3.x_ref, f32[1,3,6144]{2,1,0:T(4,128)} %copy-done.1, f32[1,6144]{1,0:T(1,128)} %copy-done.7, bf16[12,128,128]{2,1,0:T(8,128)(2,1)} %copy-done.3), custom_call_target="tpu_custom_call" | custom-call | flops 1610612736 | bytes 3538944 | tf_op jit(solution)/shard_map/pallas_call | solution.py:175
  100.3 0.8 copy-done.6
  101.1 7.5 %shard_map.71.rest_0_ = bf16[1,512,6144]{2,1,0:T(8,128)(2,1)} custom-call(f32[48]{0:T(128)} %bitcast.8, bf16[1,512,6144]{2,1,0:T(8,128)(2,1)} %collective-permute-done.3.x_ref, f32[1,3,6144]{2,1,0:T(4,128)} %copy-done.1, f32[1,6144]{1,0:T(1,128)} %copy-done.7, bf16[12,128,128]{2,1,0:T(8,128)(2,1)} %copy-done.6, ...), custom_call_target="tpu_custom_call", output_to_operand_aliasing={{}: (5, {})} | custom-call | flops 1610612736 | bytes 3538944 | tf_op jit(solution)/shard_map/pallas_call | solution.py:175
  108.6 0.0 collective-permute-done.5.s_ref
  108.6 0.8 copy-done.5
  109.4 7.5 %shard_map.72.rest_0_ = bf16[1,512,6144]{2,1,0:T(8,128)(2,1)} custom-call(f32[48]{0:T(128)} %bitcast.9, bf16[1,512,6144]{2,1,0:T(8,128)(2,1)} %collective-permute-done.3.x_ref, f32[1,3,6144]{2,1,0:T(4,128)} %copy-done.1, f32[1,6144]{1,0:T(1,128)} %copy-done.7, bf16[12,128,128]{2,1,0:T(8,128)(2,1)} %copy-done.5, ...), custom_call_target="tpu_custom_call", output_to_operand_aliasing={{}: (5, {})} | custom-call | flops 1610612736 | bytes 3538944 | tf_op jit(solution)/shard_map/pallas_call | solution.py:175
  116.9 0.0 collective-permute-done.4.s_ref
  116.9 0.8 copy-done.4
  117.7 7.5 %shard_map.73 = bf16[1,512,6144]{2,1,0:T(8,128)(2,1)} custom-call(f32[48]{0:T(128)} %bitcast.10, bf16[1,512,6144]{2,1,0:T(8,128)(2,1)} %collective-permute-done.3.x_ref, f32[1,3,6144]{2,1,0:T(4,128)} %copy-done.1, f32[1,6144]{1,0:T(1,128)} %copy-done.7, bf16[12,128,128]{2,1,0:T(8,128)(2,1)} %copy-done.4, ...), custom_call_target="tpu_custom_call", output_to_operand_aliasing={{}: (5, {})} | custom-call | flops 1610612736 | bytes 3538944 | tf_op jit(solution)/shard_map/pallas_call | solution.py:175
  (18 shorter events, 0.0 us)
Async XLA Ops:
  0.6 91.4 %collective-permute-start.3 = (bf16[1,512,6144]{2,1,0:T(8,128)(2,1)}, bf16[1,512,6144]{2,1,0:T(8,128)(2,1)}, u32[]{:S(2)}, u32[]{:S(2)}) collective-permute-start(bf16[1,512,6144]{2,1,0:T(8,128)(2,1)} %x_ref.1), channel_id=1, source_target_pairs={{0,16},{16,32},{32,48},{48,64},{64,80},{80,96},{96,112},{112,0},{1... | collective-permute-start | bytes 18874376 | tf_op jit(solution)/shard_map/ppermute | solution.py:203
  12.4 45.3 %copy-start.2 = (f32[1,3,6144]{2,1,0:T(4,128)S(1)}, f32[1,3,6144]{2,1,0:T(4,128)}, u32[]{:S(2)}) copy-start(f32[1,3,6144]{2,1,0:T(4,128)} %copy.10.g_ref) | copy-start | bytes 221188
  12.4 45.5 %copy-start.10 = (f32[1,6144]{1,0:T(1,128)S(1)}, f32[1,6144]{1,0:T(1,128)}, u32[]{:S(2)}) copy-start(f32[1,6144]{1,0:T(1,128)} %param.7) | copy-start | bytes 73732
  12.4 46.9 %copy-start.9 = (f32[1,48]{1,0:T(1,128)S(1)}, f32[1,48]{1,0:T(1,128)}, u32[]{:S(2)}) copy-start(f32[1,48]{1,0:T(1,128)} %param.8) | copy-start | bytes 580
  12.4 36.0 %all-to-all-start = ((bf16[48,128,128]{2,1,0:T(8,128)(2,1)}), bf16[48,128,128]{2,1,0:T(8,128)(2,1)S(1)}, u32[]{:S(2)}, u32[]{:S(2)}) async-start(bf16[48,128,128]{2,1,0:T(8,128)(2,1)} %shard_map.68), calls=%async_computation | async-start | bytes 3145728 | tf_op jit(solution)/shard_map/all_to_all | solution.py:208
  48.3 1.1 copy-start
  53.8 29.6 %all-to-all-start.1 = ((bf16[48,128,128]{2,1,0:T(8,128)(2,1)}), bf16[48,128,128]{2,1,0:T(8,128)(2,1)S(1)}, u32[]{:S(2)}, u32[]{:S(2)}) async-start(bf16[48,128,128]{2,1,0:T(8,128)(2,1)} %bitcast.6), calls=%async_computation.1 | async-start | bytes 3145728 | tf_op jit(solution)/shard_map/all_to_all | solution.py:213
  57.7 16.2 %collective-permute-start = (f32[1,3,6144]{2,1,0:T(4,128)S(1)}, f32[1,3,6144]{2,1,0:T(4,128)S(1)}, u32[]{:S(2)}, u32[]{:S(2)}) collective-permute-start(f32[1,3,6144]{2,1,0:T(4,128)S(1)} %copy-done.2), channel_id=1, source_target_pairs={{0,16},{16,32},{32,48},{48,64},{64,80},{80,96},{96,112},{112,0},{1... | collective-permute-start | bytes 221192 | tf_op jit(solution)/shard_map/ppermute | solution.py:203
  57.9 16.0 %collective-permute-start.1 = (f32[1,6144]{1,0:T(1,128)S(1)}, f32[1,6144]{1,0:T(1,128)S(1)}, u32[]{:S(2)}, u32[]{:S(2)}) collective-permute-start(f32[1,6144]{1,0:T(1,128)S(1)} %copy-done.10), channel_id=1, source_target_pairs={{0,16},{16,32},{32,48},{48,64},{64,80},{80,96},{96,112},{112,0},{1... | collective-permute-start | bytes 73736 | tf_op jit(solution)/shard_map/ppermute | solution.py:203
  59.3 14.6 %collective-permute-start.2 = (f32[1,48]{1,0:T(1,128)S(1)}, f32[1,48]{1,0:T(1,128)S(1)}, u32[]{:S(2)}, u32[]{:S(2)}) collective-permute-start(f32[1,48]{1,0:T(1,128)S(1)} %copy-done.9), channel_id=1, source_target_pairs={{0,16},{16,32},{32,48},{48,64},{64,80},{80,96},{96,112},{112,0},{1... | collective-permute-start | bytes 584 | tf_op jit(solution)/shard_map/ppermute | solution.py:203
  73.9 18.1 %copy-start.8 = (f32[1,48]{1,0:T(1,128)}, f32[1,48]{1,0:T(1,128)S(1)}, u32[]{:S(2)}) copy-start(f32[1,48]{1,0:T(1,128)S(1)} %collective-permute-done.2) | copy-start | bytes 580
  73.9 18.1 %copy-start.7 = (f32[1,6144]{1,0:T(1,128)}, f32[1,6144]{1,0:T(1,128)S(1)}, u32[]{:S(2)}) copy-start(f32[1,6144]{1,0:T(1,128)S(1)} %collective-permute-done.1.go_ref) | copy-start | bytes 73732
  73.9 18.1 %copy-start.1 = (f32[1,3,6144]{2,1,0:T(4,128)}, f32[1,3,6144]{2,1,0:T(4,128)S(1)}, u32[]{:S(2)}) copy-start(f32[1,3,6144]{2,1,0:T(4,128)S(1)} %collective-permute-done.g_ref) | copy-start | bytes 221188
  83.6 8.4 %collective-permute-start.7 = (bf16[12,128,128]{2,1,0:T(8,128)(2,1)S(1)}, bf16[12,128,128]{2,1,0:T(8,128)(2,1)S(1)}, u32[]{:S(2)}, u32[]{:S(2)}) collective-permute-start(bf16[12,128,128]{2,1,0:T(8,128)(2,1)S(1)} %get-tuple-element.14), channel_id=1, source_target_pairs={{0,16},{16,32},{32,48},{48,64},{64,80},{80,96},{96,112},{112,0},{1... | collective-permute-start | bytes 1179656 | tf_op jit(solution)/shard_map/ppermute | solution.py:222
  83.6 16.7 %collective-permute-start.6 = (bf16[12,128,128]{2,1,0:T(8,128)(2,1)S(1)}, bf16[12,128,128]{2,1,0:T(8,128)(2,1)S(1)}, u32[]{:S(2)}, u32[]{:S(2)}) collective-permute-start(bf16[12,128,128]{2,1,0:T(8,128)(2,1)S(1)} %get-tuple-element.15), channel_id=1, source_target_pairs={{0,16},{16,32},{32,48},{48,64},{64,80},{80,96},{96,112},{112,0},{1... | collective-permute-start | bytes 1179656 | tf_op jit(solution)/shard_map/ppermute | solution.py:222
  85.2 23.4 %collective-permute-start.5 = (bf16[12,128,128]{2,1,0:T(8,128)(2,1)S(1)}, bf16[12,128,128]{2,1,0:T(8,128)(2,1)S(1)}, u32[]{:S(2)}, u32[]{:S(2)}) collective-permute-start(bf16[12,128,128]{2,1,0:T(8,128)(2,1)S(1)} %get-tuple-element.16), channel_id=1, source_target_pairs={{0,16},{16,32},{32,48},{48,64},{64,80},{80,96},{96,112},{112,0},{1... | collective-permute-start | bytes 1179656 | tf_op jit(solution)/shard_map/ppermute | solution.py:222
  85.2 31.7 %collective-permute-start.4 = (bf16[12,128,128]{2,1,0:T(8,128)(2,1)S(1)}, bf16[12,128,128]{2,1,0:T(8,128)(2,1)S(1)}, u32[]{:S(2)}, u32[]{:S(2)}) collective-permute-start(bf16[12,128,128]{2,1,0:T(8,128)(2,1)S(1)} %get-tuple-element.17), channel_id=1, source_target_pairs={{0,16},{16,32},{32,48},{48,64},{64,80},{80,96},{96,112},{112,0},{1... | collective-permute-start | bytes 1179656 | tf_op jit(solution)/shard_map/ppermute | solution.py:222
  92.0 0.8 copy-start.3
  100.3 0.8 copy-start.6
  108.6 0.8 copy-start.5
  116.9 0.8 copy-start.4

commit v14 on v11

--- a/solution.py
+++ b/solution.py
@@ -10,7 +10,7 @@
 BLOCK = 256
 EPSILON = 1e-05
 HEADS_PER_STEP = 6
-SUMMARY_HEADS_PER_STEP = 12
+SUMMARY_HEADS_PER_STEP = 16
 STATE_CHUNKS = 4
 
 

time: 125 us -> 125 us (level)
  no operation moved by 1% of the time
where the time goes in v14:
time: 125 us
  waiting for transfers between devices  56.7 us (45%)
  Pallas kernels  44.1 us (35%)
  starting transfers between devices  17.3 us (14%)
  local copies, waits for them, and re-layouts  5.93 us (5%)
    pallas_call x4, Pallas kernels, _outputs(): pl.pallas_call(kernel, grid_spec=pltpu.PrefetchScalarGridSpec(num_scalar_...  30.2 us
    all_to_all x1, waiting for transfers between devices, on_device(): gathered = lax.all_to_all(summary, 'ctx', 0, 0, tiled=True)  27.7 us
    ppermute x4, waiting for transfers between devices, on_device(): lax.ppermute((section_inputs, input_gains, out_gain, decay_rates), 'secti...  14.8 us
    pallas_call x1, Pallas kernels, _summaries(): pl.pallas_call(kernel, grid_spec=pltpu.PrefetchScalarGridSpec(num_scalar_...  10.3 us
    all_to_all x1, waiting for transfers between devices, on_device(): lax.all_to_all(prefixes.reshape(heads, head_dim, head_dim), 'ctx', 0, 0,...  9.09 us
    all_to_all x1, starting transfers between devices, on_device(): gathered = lax.all_to_all(summary, 'ctx', 0, 0, tiled=True)  8.3 us
    unnamed x23, local copies, waits for them, and re-layouts  5.78 us
    ppermute x4, waiting for transfers between devices, on_device(): lax.ppermute(incoming[part * chunk:(part + 1) * chunk], 'section', pairs)  5.07 us
  transfers between devices with their start and end apart: 10, of which 4 were waited for; matrix products, arithmetic and copies ran while one was open for 1% of the time, Pallas kernels for 29%

profile of v14, /device:TPU:0, one launch (start us, length us, event | category | flops | bytes accessed | tf_op | source)
XLA Modules:
  0.0 124.8 jit_solution(5202473990344428270)
XLA Ops:
  0.6 0.0 collective-permute-start.3
  0.7 1.6 %copy.10.g_ref = f32[1,3,6144]{2,1,0:T(4,128)} copy(f32[1,3,6144]{2,0,1:T(1,128)} %param.6) | data formatting | bytes 147456 | tf_op args[1]
  2.2 10.3 %shard_map.68 = bf16[48,128,128]{2,1,0:T(8,128)(2,1)} custom-call(f32[48]{0:T(128)} %bitcast.11, bf16[1,512,6144]{2,1,0:T(8,128)(2,1)} %x_ref.1, f32[1,3,6144]{2,1,0:T(4,128)} %copy.10.g_ref), custom_call_target="tpu_custom_call" | custom-call | flops 805306368 | bytes 9437184 | tf_op jit(solution)/shard_map/pallas_call | solution.py:134
  12.6 8.3 %all-to-all-start = ((bf16[48,128,128]{2,1,0:T(8,128)(2,1)}), bf16[48,128,128]{2,1,0:T(8,128)(2,1)S(1)}, u32[]{:S(2)}, u32[]{:S(2)}) async-start(bf16[48,128,128]{2,1,0:T(8,128)(2,1)} %shard_map.68), calls=%async_computation | async-start | bytes 3145728 | tf_op jit(solution)/shard_map/all_to_all | solution.py:209
  20.9 27.7 %all-to-all-done = bf16[48,128,128]{2,1,0:T(8,128)(2,1)S(1)} async-done(((bf16[48,128,128]{2,1,0:T(8,128)(2,1)}), bf16[48,128,128]{2,1,0:T(8,128)(2,1)S(1)}, u32[]{:S(2)}, u32[]{:S(2)}) %all-to-all-start) | async-done | bytes 1572896 | tf_op jit(solution)/shard_map/all_to_all | solution.py:209
  48.6 1.1 copy-done
  49.7 3.6 %shard_map.69 = (bf16[16,3,128,128]{3,2,1,0:T(8,128)(2,1)}, f32[1,3,128,128]{3,2,1,0:T(8,128)}) custom-call(s32[1]{0:T(128)} %bitcast.place_ref, f32[48]{0:T(128)} %bitcast.12, bf16[16,3,128,128]{3,2,1,0:T(8,128)(2,1)} %bitcast.5, f32[1,48,128,128]{3,2,1,0:T(8,128)} %c_ref.1), custom_call_target="tpu_custom_call" | custom-call | flops 1572864 | bytes 3538944 | tf_op jit(solution)/shard_map/pallas_call | solution.py:103
  53.3 3.9 %all-to-all-start.1 = ((bf16[48,128,128]{2,1,0:T(8,128)(2,1)}), bf16[48,128,128]{2,1,0:T(8,128)(2,1)S(1)}, u32[]{:S(2)}, u32[]{:S(2)}) async-start(bf16[48,128,128]{2,1,0:T(8,128)(2,1)} %bitcast.6), calls=%async_computation.1 | async-start | bytes 3145728 | tf_op jit(solution)/shard_map/all_to_all | solution.py:214
  57.2 0.2 collective-permute-start
  57.4 1.4 %collective-permute-start.1 = (f32[1,6144]{1,0:T(1,128)S(1)}, f32[1,6144]{1,0:T(1,128)S(1)}, u32[]{:S(2)}, u32[]{:S(2)}) collective-permute-start(f32[1,6144]{1,0:T(1,128)S(1)} %copy-done.10), channel_id=1, source_target_pairs={{0,16},{16,32},{32,48},{48,64},{64,80},{80,96},{96,112},{112,0},{1... | collective-permute-start | bytes 73736 | tf_op jit(solution)/shard_map/ppermute | solution.py:204
  58.9 0.2 collective-permute-start.2
  59.0 14.8 %collective-permute-done.2 = f32[1,48]{1,0:T(1,128)S(1)} collective-permute-done((f32[1,48]{1,0:T(1,128)S(1)}, f32[1,48]{1,0:T(1,128)S(1)}, u32[]{:S(2)}, u32[]{:S(2)}) %collective-permute-start.2) | collective-permute-done | bytes 224 | tf_op jit(solution)/shard_map/ppermute | solution.py:204
  73.9 0.0 collective-permute-done.1.go_ref
  73.9 0.0 collective-permute-done.g_ref
  73.9 9.1 %all-to-all-done.1 = bf16[48,128,128]{2,1,0:T(8,128)(2,1)S(1)} async-done(((bf16[48,128,128]{2,1,0:T(8,128)(2,1)}), bf16[48,128,128]{2,1,0:T(8,128)(2,1)S(1)}, u32[]{:S(2)}, u32[]{:S(2)}) %all-to-all-start.1) | async-done | bytes 1572896 | tf_op jit(solution)/shard_map/all_to_all | solution.py:214
  83.0 0.1 fusion
  83.1 0.0 collective-permute-start.7
  83.2 1.6 %collective-permute-start.6 = (bf16[12,128,128]{2,1,0:T(8,128)(2,1)S(1)}, bf16[12,128,128]{2,1,0:T(8,128)(2,1)S(1)}, u32[]{:S(2)}, u32[]{:S(2)}) collective-permute-start(bf16[12,128,128]{2,1,0:T(8,128)(2,1)S(1)} %get-tuple-element.15), channel_id=1, source_target_pairs={{0,16},{16,32},{32,48},{48,64},{64,80},{80,96},{96,112},{112,0},{1... | collective-permute-start | bytes 1179656 | tf_op jit(solution)/shard_map/ppermute | solution.py:223
  84.8 0.0 collective-permute-start.5
  84.8 1.7 %collective-permute-start.4 = (bf16[12,128,128]{2,1,0:T(8,128)(2,1)S(1)}, bf16[12,128,128]{2,1,0:T(8,128)(2,1)S(1)}, u32[]{:S(2)}, u32[]{:S(2)}) collective-permute-start(bf16[12,128,128]{2,1,0:T(8,128)(2,1)S(1)} %get-tuple-element.17), channel_id=1, source_target_pairs={{0,16},{16,32},{32,48},{48,64},{64,80},{80,96},{96,112},{112,0},{1... | collective-permute-start | bytes 1179656 | tf_op jit(solution)/shard_map/ppermute | solution.py:223
  86.5 5.1 %collective-permute-done.7.s_ref = bf16[12,128,128]{2,1,0:T(8,128)(2,1)S(1)} collective-permute-done((bf16[12,128,128]{2,1,0:T(8,128)(2,1)S(1)}, bf16[12,128,128]{2,1,0:T(8,128)(2,1)S(1)}, u32[]{:S(2)}, u32[]{:S(2)}) %collective-permute-start.7) | collective-permute-done | bytes 393248 | tf_op jit(solution)/shard_map/ppermute | solution.py:223
  91.6 0.0 collective-permute-done.3.x_ref
  91.6 0.7 copy-done.3
  92.3 7.5 %shard_map.70.rest_0_ = bf16[1,512,6144]{2,1,0:T(8,128)(2,1)} custom-call(f32[48]{0:T(128)} %bitcast.7, bf16[1,512,6144]{2,1,0:T(8,128)(2,1)} %collective-permute-done.3.x_ref, f32[1,3,6144]{2,1,0:T(4,128)} %copy-done.1, f32[1,6144]{1,0:T(1,128)} %copy-done.7, bf16[12,128,128]{2,1,0:T(8,128)(2,1)} %copy-done.3), custom_call_target="tpu_custom_call" | custom-call | flops 1610612736 | bytes 3538944 | tf_op jit(solution)/shard_map/pallas_call | solution.py:176
  99.9 0.0 collective-permute-done.6.s_ref
  99.9 0.8 copy-done.6
  100.6 7.5 %shard_map.71.rest_0_ = bf16[1,512,6144]{2,1,0:T(8,128)(2,1)} custom-call(f32[48]{0:T(128)} %bitcast.8, bf16[1,512,6144]{2,1,0:T(8,128)(2,1)} %collective-permute-done.3.x_ref, f32[1,3,6144]{2,1,0:T(4,128)} %copy-done.1, f32[1,6144]{1,0:T(1,128)} %copy-done.7, bf16[12,128,128]{2,1,0:T(8,128)(2,1)} %copy-done.6, ...), custom_call_target="tpu_custom_call", output_to_operand_aliasing={{}: (5, {})} | custom-call | flops 1610612736 | bytes 3538944 | tf_op jit(solution)/shard_map/pallas_call | solution.py:176
  108.2 0.8 copy-done.5
  108.9 7.5 %shard_map.72.rest_0_ = bf16[1,512,6144]{2,1,0:T(8,128)(2,1)} custom-call(f32[48]{0:T(128)} %bitcast.9, bf16[1,512,6144]{2,1,0:T(8,128)(2,1)} %collective-permute-done.3.x_ref, f32[1,3,6144]{2,1,0:T(4,128)} %copy-done.1, f32[1,6144]{1,0:T(1,128)} %copy-done.7, bf16[12,128,128]{2,1,0:T(8,128)(2,1)} %copy-done.5, ...), custom_call_target="tpu_custom_call", output_to_operand_aliasing={{}: (5, {})} | custom-call | flops 1610612736 | bytes 3538944 | tf_op jit(solution)/shard_map/pallas_call | solution.py:176
  116.5 0.0 collective-permute-done.4.s_ref
  116.5 0.8 copy-done.4
  117.3 7.5 %shard_map.73 = bf16[1,512,6144]{2,1,0:T(8,128)(2,1)} custom-call(f32[48]{0:T(128)} %bitcast.10, bf16[1,512,6144]{2,1,0:T(8,128)(2,1)} %collective-permute-done.3.x_ref, f32[1,3,6144]{2,1,0:T(4,128)} %copy-done.1, f32[1,6144]{1,0:T(1,128)} %copy-done.7, bf16[12,128,128]{2,1,0:T(8,128)(2,1)} %copy-done.4, ...), custom_call_target="tpu_custom_call", output_to_operand_aliasing={{}: (5, {})} | custom-call | flops 1610612736 | bytes 3538944 | tf_op jit(solution)/shard_map/pallas_call | solution.py:176
  (18 shorter events, 0.0 us)
Async XLA Ops:
  0.6 90.9 %collective-permute-start.3 = (bf16[1,512,6144]{2,1,0:T(8,128)(2,1)}, bf16[1,512,6144]{2,1,0:T(8,128)(2,1)}, u32[]{:S(2)}, u32[]{:S(2)}) collective-permute-start(bf16[1,512,6144]{2,1,0:T(8,128)(2,1)} %x_ref.1), channel_id=1, source_target_pairs={{0,16},{16,32},{32,48},{48,64},{64,80},{80,96},{96,112},{112,0},{1... | collective-permute-start | bytes 18874376 | tf_op jit(solution)/shard_map/ppermute | solution.py:204
  12.6 44.7 %copy-start.2 = (f32[1,3,6144]{2,1,0:T(4,128)S(1)}, f32[1,3,6144]{2,1,0:T(4,128)}, u32[]{:S(2)}) copy-start(f32[1,3,6144]{2,1,0:T(4,128)} %copy.10.g_ref) | copy-start | bytes 221188
  12.6 44.8 %copy-start.10 = (f32[1,6144]{1,0:T(1,128)S(1)}, f32[1,6144]{1,0:T(1,128)}, u32[]{:S(2)}) copy-start(f32[1,6144]{1,0:T(1,128)} %param.7) | copy-start | bytes 73732
  12.6 46.3 %copy-start.9 = (f32[1,48]{1,0:T(1,128)S(1)}, f32[1,48]{1,0:T(1,128)}, u32[]{:S(2)}) copy-start(f32[1,48]{1,0:T(1,128)} %param.8) | copy-start | bytes 580
  12.6 36.0 %all-to-all-start = ((bf16[48,128,128]{2,1,0:T(8,128)(2,1)}), bf16[48,128,128]{2,1,0:T(8,128)(2,1)S(1)}, u32[]{:S(2)}, u32[]{:S(2)}) async-start(bf16[48,128,128]{2,1,0:T(8,128)(2,1)} %shard_map.68), calls=%async_computation | async-start | bytes 3145728 | tf_op jit(solution)/shard_map/all_to_all | solution.py:209
  48.6 1.1 copy-start
  53.3 29.6 %all-to-all-start.1 = ((bf16[48,128,128]{2,1,0:T(8,128)(2,1)}), bf16[48,128,128]{2,1,0:T(8,128)(2,1)S(1)}, u32[]{:S(2)}, u32[]{:S(2)}) async-start(bf16[48,128,128]{2,1,0:T(8,128)(2,1)} %bitcast.6), calls=%async_computation.1 | async-start | bytes 3145728 | tf_op jit(solution)/shard_map/all_to_all | solution.py:214
  57.2 16.6 %collective-permute-start = (f32[1,3,6144]{2,1,0:T(4,128)S(1)}, f32[1,3,6144]{2,1,0:T(4,128)S(1)}, u32[]{:S(2)}, u32[]{:S(2)}) collective-permute-start(f32[1,3,6144]{2,1,0:T(4,128)S(1)} %copy-done.2), channel_id=1, source_target_pairs={{0,16},{16,32},{32,48},{48,64},{64,80},{80,96},{96,112},{112,0},{1... | collective-permute-start | bytes 221192 | tf_op jit(solution)/shard_map/ppermute | solution.py:204
  57.4 16.4 %collective-permute-start.1 = (f32[1,6144]{1,0:T(1,128)S(1)}, f32[1,6144]{1,0:T(1,128)S(1)}, u32[]{:S(2)}, u32[]{:S(2)}) collective-permute-start(f32[1,6144]{1,0:T(1,128)S(1)} %copy-done.10), channel_id=1, source_target_pairs={{0,16},{16,32},{32,48},{48,64},{64,80},{80,96},{96,112},{112,0},{1... | collective-permute-start | bytes 73736 | tf_op jit(solution)/shard_map/ppermute | solution.py:204
  58.9 15.0 %collective-permute-start.2 = (f32[1,48]{1,0:T(1,128)S(1)}, f32[1,48]{1,0:T(1,128)S(1)}, u32[]{:S(2)}, u32[]{:S(2)}) collective-permute-start(f32[1,48]{1,0:T(1,128)S(1)} %copy-done.9), channel_id=1, source_target_pairs={{0,16},{16,32},{32,48},{48,64},{64,80},{80,96},{96,112},{112,0},{1... | collective-permute-start | bytes 584 | tf_op jit(solution)/shard_map/ppermute | solution.py:204
  73.9 17.7 %copy-start.8 = (f32[1,48]{1,0:T(1,128)}, f32[1,48]{1,0:T(1,128)S(1)}, u32[]{:S(2)}) copy-start(f32[1,48]{1,0:T(1,128)S(1)} %collective-permute-done.2) | copy-start | bytes 580
  73.9 17.7 %copy-start.7 = (f32[1,6144]{1,0:T(1,128)}, f32[1,6144]{1,0:T(1,128)S(1)}, u32[]{:S(2)}) copy-start(f32[1,6144]{1,0:T(1,128)S(1)} %collective-permute-done.1.go_ref) | copy-start | bytes 73732
  73.9 17.7 %copy-start.1 = (f32[1,3,6144]{2,1,0:T(4,128)}, f32[1,3,6144]{2,1,0:T(4,128)S(1)}, u32[]{:S(2)}) copy-start(f32[1,3,6144]{2,1,0:T(4,128)S(1)} %collective-permute-done.g_ref) | copy-start | bytes 221188
  83.1 8.4 %collective-permute-start.7 = (bf16[12,128,128]{2,1,0:T(8,128)(2,1)S(1)}, bf16[12,128,128]{2,1,0:T(8,128)(2,1)S(1)}, u32[]{:S(2)}, u32[]{:S(2)}) collective-permute-start(bf16[12,128,128]{2,1,0:T(8,128)(2,1)S(1)} %get-tuple-element.14), channel_id=1, source_target_pairs={{0,16},{16,32},{32,48},{48,64},{64,80},{80,96},{96,112},{112,0},{1... | collective-permute-start | bytes 1179656 | tf_op jit(solution)/shard_map/ppermute | solution.py:223
  83.2 16.7 %collective-permute-start.6 = (bf16[12,128,128]{2,1,0:T(8,128)(2,1)S(1)}, bf16[12,128,128]{2,1,0:T(8,128)(2,1)S(1)}, u32[]{:S(2)}, u32[]{:S(2)}) collective-permute-start(bf16[12,128,128]{2,1,0:T(8,128)(2,1)S(1)} %get-tuple-element.15), channel_id=1, source_target_pairs={{0,16},{16,32},{32,48},{48,64},{64,80},{80,96},{96,112},{112,0},{1... | collective-permute-start | bytes 1179656 | tf_op jit(solution)/shard_map/ppermute | solution.py:223
  84.8 23.4 %collective-permute-start.5 = (bf16[12,128,128]{2,1,0:T(8,128)(2,1)S(1)}, bf16[12,128,128]{2,1,0:T(8,128)(2,1)S(1)}, u32[]{:S(2)}, u32[]{:S(2)}) collective-permute-start(bf16[12,128,128]{2,1,0:T(8,128)(2,1)S(1)} %get-tuple-element.16), channel_id=1, source_target_pairs={{0,16},{16,32},{32,48},{48,64},{64,80},{80,96},{96,112},{112,0},{1... | collective-permute-start | bytes 1179656 | tf_op jit(solution)/shard_map/ppermute | solution.py:223
  84.8 31.7 %collective-permute-start.4 = (bf16[12,128,128]{2,1,0:T(8,128)(2,1)S(1)}, bf16[12,128,128]{2,1,0:T(8,128)(2,1)S(1)}, u32[]{:S(2)}, u32[]{:S(2)}) collective-permute-start(bf16[12,128,128]{2,1,0:T(8,128)(2,1)S(1)} %get-tuple-element.17), channel_id=1, source_target_pairs={{0,16},{16,32},{32,48},{48,64},{64,80},{80,96},{96,112},{112,0},{1... | collective-permute-start | bytes 1179656 | tf_op jit(solution)/shard_map/ppermute | solution.py:223
  91.6 0.8 copy-start.3
  99.9 0.8 copy-start.6
  108.2 0.8 copy-start.5
  116.5 0.8 copy-start.4

commit v15 on v11

--- a/solution.py
+++ b/solution.py
@@ -36,7 +36,7 @@
     return _dot_tn(scaled, values_b)
 
 
-def _summary_kernel(rates_ref, x_ref, g_ref, o_ref, *, hg, head_dim, nblocks):
+def _summary_kernel(rates_ref, x_ref, gk_ref, gv_ref, o_ref, *, hg, head_dim, nblocks):
     step = pl.program_id(0)
     pos = lax.broadcasted_iota(jnp.int32, (BLOCK, 1), 0).astype(jnp.float32)
     for hh in range(hg):
@@ -47,14 +47,14 @@
         for b in range(nblocks):
             rows = slice(b * BLOCK, (b + 1) * BLOCK)
             x = x_ref[0, rows, cols].astype(jnp.float32)
-            keys_b = (_silu(x * g_ref[0, 1:2, cols]) * head_dim ** (-0.5)).astype(jnp.bfloat16)
-            values_b = (x * g_ref[0, 2:3, cols]).astype(jnp.bfloat16)
+            keys_b = (_silu(x * gk_ref[0:1, cols]) * head_dim ** (-0.5)).astype(jnp.bfloat16)
+            values_b = (x * gv_ref[0:1, cols]).astype(jnp.bfloat16)
             update = _block_state(keys_b, values_b, rate, pos)
             acc = update if acc is None else decay * acc + update
         o_ref[hh] = acc.astype(o_ref.dtype)
 
 
-def _output_kernel(rates_ref, x_ref, g_ref, go_ref, s_ref, *rest, hg, head_dim, nblocks, first):
+def _output_kernel(rates_ref, x_ref, gq_ref, gk_ref, gv_ref, go_ref, s_ref, *rest, hg, head_dim, nblocks, first):
     o_ref = rest[-1]
     step = pl.program_id(0) + first
     pos = lax.broadcasted_iota(jnp.int32, (BLOCK, 1), 0).astype(jnp.float32)
@@ -72,9 +72,9 @@
         for b in range(nblocks):
             rows = slice(b * BLOCK, (b + 1) * BLOCK)
             x = x_ref[0, rows, cols].astype(jnp.float32)
-            queries_b = _silu(x * g_ref[0, 0:1, cols]).astype(jnp.bfloat16)
-            keys_b = (_silu(x * g_ref[0, 1:2, cols]) * head_dim ** (-0.5)).astype(jnp.bfloat16)
-            values_b = (x * g_ref[0, 2:3, cols]).astype(jnp.bfloat16)
+            queries_b = _silu(x * gq_ref[0:1, cols]).astype(jnp.bfloat16)
+            keys_b = (_silu(x * gk_ref[0:1, cols]) * head_dim ** (-0.5)).astype(jnp.bfloat16)
+            values_b = (x * gv_ref[0:1, cols]).astype(jnp.bfloat16)
             scores = _dot_nt(queries_b, keys_b)
             weights = (scores * mask).astype(jnp.bfloat16)
             local = _dot(weights, values_b)
@@ -130,6 +130,7 @@
     heads = width // head_dim
     hg = SUMMARY_HEADS_PER_STEP
     cw = hg * head_dim
+    per_row = width // cw
     kernel = functools.partial(_summary_kernel, hg=hg, head_dim=head_dim, nblocks=count // BLOCK)
     return pl.pallas_call(
         kernel,
@@ -138,7 +139,8 @@
             grid=(heads // hg,),
             in_specs=[
                 pl.BlockSpec((1, count, cw), lambda i, r: (0, 0, i)),
-                pl.BlockSpec((1, 3, cw), lambda i, r: (0, 0, i)),
+                pl.BlockSpec((1, cw), lambda i, r: (0, i + per_row)),
+                pl.BlockSpec((1, cw), lambda i, r: (0, i + 2 * per_row)),
             ],
             out_specs=pl.BlockSpec((hg, head_dim, head_dim), lambda i, r: (i, 0, 0)),
         ),
@@ -147,7 +149,7 @@
             flops=2 * count * width * head_dim, transcendentals=count * width,
             bytes_accessed=count * width * 2 + heads * head_dim * head_dim * 4,
         ),
-    )(rates, rows, gains)
+    )(rates, rows, gains, gains)
 
 
 def _outputs(rates, rows, gains, gain_out, states, head_dim, first, previous):
@@ -160,13 +162,16 @@
         _output_kernel, hg=hg, head_dim=head_dim, nblocks=count // BLOCK, first=base
     )
     row_spec = pl.BlockSpec((1, count, cw), lambda i, r: (0, 0, i + base))
+    per_row = width // cw
     in_specs = [
         row_spec,
-        pl.BlockSpec((1, 3, cw), lambda i, r: (0, 0, i + base)),
+        pl.BlockSpec((1, cw), lambda i, r: (0, i + base)),
+        pl.BlockSpec((1, cw), lambda i, r: (0, i + base + per_row)),
+        pl.BlockSpec((1, cw), lambda i, r: (0, i + base + 2 * per_row)),
         pl.BlockSpec((1, cw), lambda i, r: (0, i + base)),
         pl.BlockSpec((hg, head_dim, head_dim), lambda i, r: (i, 0, 0)),
     ]
-    operands = [rates, rows, gains, gain_out, states]
+    operands = [rates, rows, gains, gains, gains, gain_out, states]
     aliases = {}
     if previous is not None:
         in_specs.append(pl.BlockSpec(memory_space=pl.ANY))
@@ -201,11 +206,12 @@
     count_s = lax.axis_size("section")
     pairs = [(src, (src + 1) % count_s) for src in range(count_s)]
 
+    flat_gains = input_gains.reshape(1, -1)
     prev_rows, prev_gains, prev_gain_out, prev_rates = lax.ppermute(
-        (section_inputs, input_gains, out_gain, decay_rates), "section", pairs
-    )
-
-    summary = _summaries(rates, section_inputs, input_gains, head_dim)
+        (section_inputs, flat_gains, out_gain, decay_rates), "section", pairs
+    )
+
+    summary = _summaries(rates, section_inputs, flat_gains, head_dim)
     gathered = lax.all_to_all(summary, "ctx", 0, 0, tiled=True)
     gathered = gathered.reshape(group_size, own_heads, head_dim, head_dim)
     prefixes, end_part = _scan(

time: 125 us -> 124 us (level)
  local copies, waits for them, and re-layouts: 5.93 us -> 4.3 us
    unnamed x23 -> x22, local copies, waits for them, and re-layouts: 5.78 us -> 4.2 us
  transfers between devices with their start and end apart: 10 -> 10, of which waited for: 4 -> 4; matrix products, arithmetic and copies ran while one was open for 1% -> 0% of each run, Pallas kernels for 29% -> 30%
where the time goes in v15:
time: 124 us; the launch traced here: 123 us
  waiting for transfers between devices  56.6 us (46%)
  Pallas kernels  44 us (35%)
  starting transfers between devices  17.4 us (14%)
  local copies, waits for them, and re-layouts  4.3 us (3%)
    pallas_call x4, Pallas kernels, _outputs(): pl.pallas_call(kernel, grid_spec=pltpu.PrefetchScalarGridSpec(num_scalar_...  30.2 us
    all_to_all x1, waiting for transfers between devices, on_device(): gathered = lax.all_to_all(summary, 'ctx', 0, 0, tiled=True)  27.7 us
    ppermute x4, waiting for transfers between devices, on_device(): lax.ppermute((section_inputs, flat_gains, out_gain, decay_rates), 'sectio...  16.3 us
    pallas_call x1, Pallas kernels, _summaries(): pl.pallas_call(kernel, grid_spec=pltpu.PrefetchScalarGridSpec(num_scalar_...  10.2 us
    all_to_all x1, starting transfers between devices, on_device(): gathered = lax.all_to_all(summary, 'ctx', 0, 0, tiled=True)  8.31 us
    all_to_all x1, waiting for transfers between devices, on_device(): lax.all_to_all(prefixes.reshape(heads, head_dim, head_dim), 'ctx', 0, 0,...  7.63 us
    ppermute x4, waiting for transfers between devices, on_device(): lax.ppermute(incoming[part * chunk:(part + 1) * chunk], 'section', pairs)  5.05 us
    unnamed x22, local copies, waits for them, and re-layouts  4.2 us
  transfers between devices with their start and end apart: 10, of which 4 were waited for; matrix products, arithmetic and copies ran while one was open for 0% of the time, Pallas kernels for 30%

profile of v15, /device:TPU:0, one launch (start us, length us, event | category | flops | bytes accessed | tf_op | source)
XLA Modules:
  0.0 123.1 jit_solution(17440599350590353426)
XLA Ops:
  0.6 0.0 collective-permute-start.3
  0.7 10.2 %shard_map.68 = bf16[48,128,128]{2,1,0:T(8,128)(2,1)} custom-call(f32[48]{0:T(128)} %bitcast.15, bf16[1,512,6144]{2,1,0:T(8,128)(2,1)} %x_ref.1, f32[1,18432]{1,0:T(1,128)} %bitcast.8, f32[1,18432]{1,0:T(1,128)} %bitcast.9), custom_call_target="tpu_custom_call" | custom-call | flops 805306368 | bytes 9437184 | tf_op jit(solution)/shard_map/pallas_call | solution.py:135
  10.9 8.3 %all-to-all-start = ((bf16[48,128,128]{2,1,0:T(8,128)(2,1)}), bf16[48,128,128]{2,1,0:T(8,128)(2,1)S(1)}, u32[]{:S(2)}, u32[]{:S(2)}) async-start(bf16[48,128,128]{2,1,0:T(8,128)(2,1)} %shard_map.68), calls=%async_computation | async-start | bytes 3145728 | tf_op jit(solution)/shard_map/all_to_all | solution.py:215
  19.2 27.7 %all-to-all-done = bf16[48,128,128]{2,1,0:T(8,128)(2,1)S(1)} async-done(((bf16[48,128,128]{2,1,0:T(8,128)(2,1)}), bf16[48,128,128]{2,1,0:T(8,128)(2,1)S(1)}, u32[]{:S(2)}, u32[]{:S(2)}) %all-to-all-start) | async-done | bytes 1572896 | tf_op jit(solution)/shard_map/all_to_all | solution.py:215
  46.9 1.1 copy-done.1
  48.0 3.6 %shard_map.69 = (bf16[16,3,128,128]{3,2,1,0:T(8,128)(2,1)}, f32[1,3,128,128]{3,2,1,0:T(8,128)}) custom-call(s32[1]{0:T(128)} %bitcast.1.place_ref, f32[48]{0:T(128)} %bitcast.16, bf16[16,3,128,128]{3,2,1,0:T(8,128)(2,1)} %bitcast.6, f32[1,48,128,128]{3,2,1,0:T(8,128)} %c_ref.1), custom_call_target="tpu_custom_call" | custom-call | flops 1572864 | bytes 3538944 | tf_op jit(solution)/shard_map/pallas_call | solution.py:103
  51.6 3.9 %all-to-all-start.1 = ((bf16[48,128,128]{2,1,0:T(8,128)(2,1)}), bf16[48,128,128]{2,1,0:T(8,128)(2,1)S(1)}, u32[]{:S(2)}, u32[]{:S(2)}) async-start(bf16[48,128,128]{2,1,0:T(8,128)(2,1)} %bitcast.7), calls=%async_computation.1 | async-start | bytes 3145728 | tf_op jit(solution)/shard_map/all_to_all | solution.py:220
  55.5 0.2 collective-permute-start
  55.7 1.4 %collective-permute-start.1 = (f32[1,6144]{1,0:T(1,128)S(1)}, f32[1,6144]{1,0:T(1,128)S(1)}, u32[]{:S(2)}, u32[]{:S(2)}) collective-permute-start(f32[1,6144]{1,0:T(1,128)S(1)} %copy-done.10), channel_id=1, source_target_pairs={{0,16},{16,32},{32,48},{48,64},{64,80},{80,96},{96,112},{112,0},{1... | collective-permute-start | bytes 73736 | tf_op jit(solution)/shard_map/ppermute | solution.py:210
  57.2 0.2 collective-permute-start.2
  57.3 16.3 %collective-permute-done.2 = f32[1,48]{1,0:T(1,128)S(1)} collective-permute-done((f32[1,48]{1,0:T(1,128)S(1)}, f32[1,48]{1,0:T(1,128)S(1)}, u32[]{:S(2)}, u32[]{:S(2)}) %collective-permute-start.2) | collective-permute-done | bytes 224 | tf_op jit(solution)/shard_map/ppermute | solution.py:210
  73.6 0.0 collective-permute-done.1.go_ref
  73.6 0.0 collective-permute-done.gq_ref.gk_ref.gv_ref
  73.6 7.6 %all-to-all-done.1 = bf16[48,128,128]{2,1,0:T(8,128)(2,1)S(1)} async-done(((bf16[48,128,128]{2,1,0:T(8,128)(2,1)}), bf16[48,128,128]{2,1,0:T(8,128)(2,1)S(1)}, u32[]{:S(2)}, u32[]{:S(2)}) %all-to-all-start.1) | async-done | bytes 1572896 | tf_op jit(solution)/shard_map/all_to_all | solution.py:220
  81.3 0.1 fusion
  81.4 0.0 collective-permute-start.7
  81.4 1.6 %collective-permute-start.6 = (bf16[12,128,128]{2,1,0:T(8,128)(2,1)S(1)}, bf16[12,128,128]{2,1,0:T(8,128)(2,1)S(1)}, u32[]{:S(2)}, u32[]{:S(2)}) collective-permute-start(bf16[12,128,128]{2,1,0:T(8,128)(2,1)S(1)} %get-tuple-element.15), channel_id=1, source_target_pairs={{0,16},{16,32},{32,48},{48,64},{64,80},{80,96},{96,112},{112,0},{1... | collective-permute-start | bytes 1179656 | tf_op jit(solution)/shard_map/ppermute | solution.py:229
  83.0 0.0 collective-permute-start.5
  83.0 1.7 %collective-permute-start.4 = (bf16[12,128,128]{2,1,0:T(8,128)(2,1)S(1)}, bf16[12,128,128]{2,1,0:T(8,128)(2,1)S(1)}, u32[]{:S(2)}, u32[]{:S(2)}) collective-permute-start(bf16[12,128,128]{2,1,0:T(8,128)(2,1)S(1)} %get-tuple-element.17), channel_id=1, source_target_pairs={{0,16},{16,32},{32,48},{48,64},{64,80},{80,96},{96,112},{112,0},{1... | collective-permute-start | bytes 1179656 | tf_op jit(solution)/shard_map/ppermute | solution.py:229
  84.8 5.0 %collective-permute-done.7.s_ref = bf16[12,128,128]{2,1,0:T(8,128)(2,1)S(1)} collective-permute-done((bf16[12,128,128]{2,1,0:T(8,128)(2,1)S(1)}, bf16[12,128,128]{2,1,0:T(8,128)(2,1)S(1)}, u32[]{:S(2)}, u32[]{:S(2)}) %collective-permute-start.7) | collective-permute-done | bytes 393248 | tf_op jit(solution)/shard_map/ppermute | solution.py:229
  89.8 0.0 collective-permute-done.3.x_ref
  89.8 0.7 copy-done.3
  90.6 7.5 %shard_map.70.rest_0_ = bf16[1,512,6144]{2,1,0:T(8,128)(2,1)} custom-call(f32[48]{0:T(128)} %bitcast.11, bf16[1,512,6144]{2,1,0:T(8,128)(2,1)} %collective-permute-done.3.x_ref, f32[1,18432]{1,0:T(1,128)} %copy-done, f32[1,18432]{1,0:T(1,128)} %copy-done, f32[1,18432]{1,0:T(1,128)} %copy-done, f32[1,6144]{1,0:T(1,128)} %copy-done.2, ...), custom_call_target="tpu_custom_call" | custom-call | flops 1610612736 | bytes 3538944 | tf_op jit(solution)/shard_map/pallas_call | solution.py:181
  98.1 0.0 collective-permute-done.6.s_ref
  98.1 0.8 copy-done.6
  98.9 7.6 %shard_map.71.rest_0_ = bf16[1,512,6144]{2,1,0:T(8,128)(2,1)} custom-call(f32[48]{0:T(128)} %bitcast.12, bf16[1,512,6144]{2,1,0:T(8,128)(2,1)} %collective-permute-done.3.x_ref, f32[1,18432]{1,0:T(1,128)} %copy-done, f32[1,18432]{1,0:T(1,128)} %copy-done, f32[1,18432]{1,0:T(1,128)} %copy-done, f32[1,6144]{1,0:T(1,128)} %copy-done.2, ...), custom_call_target="tpu_custom_call", output_to_operand_aliasing={{}: (7, {})} | custom-call | flops 1610612736 | bytes 3538944 | tf_op jit(solution)/shard_map/pallas_call | solution.py:181
  106.4 0.0 collective-permute-done.5.s_ref
  106.4 0.8 copy-done.5
  107.2 7.6 %shard_map.72.rest_0_ = bf16[1,512,6144]{2,1,0:T(8,128)(2,1)} custom-call(f32[48]{0:T(128)} %bitcast.13, bf16[1,512,6144]{2,1,0:T(8,128)(2,1)} %collective-permute-done.3.x_ref, f32[1,18432]{1,0:T(1,128)} %copy-done, f32[1,18432]{1,0:T(1,128)} %copy-done, f32[1,18432]{1,0:T(1,128)} %copy-done, f32[1,6144]{1,0:T(1,128)} %copy-done.2, ...), custom_call_target="tpu_custom_call", output_to_operand_aliasing={{}: (7, {})} | custom-call | flops 1610612736 | bytes 3538944 | tf_op jit(solution)/shard_map/pallas_call | solution.py:181
  114.8 0.0 collective-permute-done.4.s_ref
  114.8 0.8 copy-done.4
  115.5 7.5 %shard_map.73 = bf16[1,512,6144]{2,1,0:T(8,128)(2,1)} custom-call(f32[48]{0:T(128)} %bitcast.14, bf16[1,512,6144]{2,1,0:T(8,128)(2,1)} %collective-permute-done.3.x_ref, f32[1,18432]{1,0:T(1,128)} %copy-done, f32[1,18432]{1,0:T(1,128)} %copy-done, f32[1,18432]{1,0:T(1,128)} %copy-done, f32[1,6144]{1,0:T(1,128)} %copy-done.2, ...), custom_call_target="tpu_custom_call", output_to_operand_aliasing={{}: (7, {})} | custom-call | flops 1610612736 | bytes 3538944 | tf_op jit(solution)/shard_map/pallas_call | solution.py:181
  (17 shorter events, 0.0 us)
Async XLA Ops:
  0.6 89.2 %collective-permute-start.3 = (bf16[1,512,6144]{2,1,0:T(8,128)(2,1)}, bf16[1,512,6144]{2,1,0:T(8,128)(2,1)}, u32[]{:S(2)}, u32[]{:S(2)}) collective-permute-start(bf16[1,512,6144]{2,1,0:T(8,128)(2,1)} %x_ref.1), channel_id=1, source_target_pairs={{0,16},{16,32},{32,48},{48,64},{64,80},{80,96},{96,112},{112,0},{1... | collective-permute-start | bytes 18874376 | tf_op jit(solution)/shard_map/ppermute | solution.py:210
  10.9 44.7 %copy-start.7 = (f32[1,3,6144]{2,0,1:T(1,128)S(1)}, f32[1,3,6144]{2,0,1:T(1,128)}, u32[]{:S(2)}) copy-start(f32[1,3,6144]{2,0,1:T(1,128)} %param.6) | copy-start | bytes 221188
  10.9 44.9 %copy-start.10 = (f32[1,6144]{1,0:T(1,128)S(1)}, f32[1,6144]{1,0:T(1,128)}, u32[]{:S(2)}) copy-start(f32[1,6144]{1,0:T(1,128)} %param.7) | copy-start | bytes 73732
  10.9 46.3 %copy-start.9 = (f32[1,48]{1,0:T(1,128)S(1)}, f32[1,48]{1,0:T(1,128)}, u32[]{:S(2)}) copy-start(f32[1,48]{1,0:T(1,128)} %param.8) | copy-start | bytes 580
  10.9 36.0 %all-to-all-start = ((bf16[48,128,128]{2,1,0:T(8,128)(2,1)}), bf16[48,128,128]{2,1,0:T(8,128)(2,1)S(1)}, u32[]{:S(2)}, u32[]{:S(2)}) async-start(bf16[48,128,128]{2,1,0:T(8,128)(2,1)} %shard_map.68), calls=%async_computation | async-start | bytes 3145728 | tf_op jit(solution)/shard_map/all_to_all | solution.py:215
  46.9 1.1 copy-start.1
  51.6 29.6 %all-to-all-start.1 = ((bf16[48,128,128]{2,1,0:T(8,128)(2,1)}), bf16[48,128,128]{2,1,0:T(8,128)(2,1)S(1)}, u32[]{:S(2)}, u32[]{:S(2)}) async-start(bf16[48,128,128]{2,1,0:T(8,128)(2,1)} %bitcast.7), calls=%async_computation.1 | async-start | bytes 3145728 | tf_op jit(solution)/shard_map/all_to_all | solution.py:220
  55.5 18.1 %collective-permute-start = (f32[1,18432]{1,0:T(1,128)S(1)}, f32[1,18432]{1,0:T(1,128)S(1)}, u32[]{:S(2)}, u32[]{:S(2)}) collective-permute-start(f32[1,18432]{1,0:T(1,128)S(1)} %bitcast.10), channel_id=1, source_target_pairs={{0,16},{16,32},{32,48},{48,64},{64,80},{80,96},{96,112},{112,0},{1... | collective-permute-start | bytes 221192 | tf_op jit(solution)/shard_map/ppermute | solution.py:210
  55.7 17.9 %collective-permute-start.1 = (f32[1,6144]{1,0:T(1,128)S(1)}, f32[1,6144]{1,0:T(1,128)S(1)}, u32[]{:S(2)}, u32[]{:S(2)}) collective-permute-start(f32[1,6144]{1,0:T(1,128)S(1)} %copy-done.10), channel_id=1, source_target_pairs={{0,16},{16,32},{32,48},{48,64},{64,80},{80,96},{96,112},{112,0},{1... | collective-permute-start | bytes 73736 | tf_op jit(solution)/shard_map/ppermute | solution.py:210
  57.2 16.4 %collective-permute-start.2 = (f32[1,48]{1,0:T(1,128)S(1)}, f32[1,48]{1,0:T(1,128)S(1)}, u32[]{:S(2)}, u32[]{:S(2)}) collective-permute-start(f32[1,48]{1,0:T(1,128)S(1)} %copy-done.9), channel_id=1, source_target_pairs={{0,16},{16,32},{32,48},{48,64},{64,80},{80,96},{96,112},{112,0},{1... | collective-permute-start | bytes 584 | tf_op jit(solution)/shard_map/ppermute | solution.py:210
  73.6 16.2 %copy-start.8 = (f32[1,48]{1,0:T(1,128)}, f32[1,48]{1,0:T(1,128)S(1)}, u32[]{:S(2)}) copy-start(f32[1,48]{1,0:T(1,128)S(1)} %collective-permute-done.2) | copy-start | bytes 580
  73.6 16.2 %copy-start.2 = (f32[1,6144]{1,0:T(1,128)}, f32[1,6144]{1,0:T(1,128)S(1)}, u32[]{:S(2)}) copy-start(f32[1,6144]{1,0:T(1,128)S(1)} %collective-permute-done.1.go_ref) | copy-start | bytes 73732
  73.6 16.2 %copy-start = (f32[1,18432]{1,0:T(1,128)}, f32[1,18432]{1,0:T(1,128)S(1)}, u32[]{:S(2)}) copy-start(f32[1,18432]{1,0:T(1,128)S(1)} %collective-permute-done.gq_ref.gk_ref.gv_ref) | copy-start | bytes 221188
  81.4 8.4 %collective-permute-start.7 = (bf16[12,128,128]{2,1,0:T(8,128)(2,1)S(1)}, bf16[12,128,128]{2,1,0:T(8,128)(2,1)S(1)}, u32[]{:S(2)}, u32[]{:S(2)}) collective-permute-start(bf16[12,128,128]{2,1,0:T(8,128)(2,1)S(1)} %get-tuple-element.14), channel_id=1, source_target_pairs={{0,16},{16,32},{32,48},{48,64},{64,80},{80,96},{96,112},{112,0},{1... | collective-permute-start | bytes 1179656 | tf_op jit(solution)/shard_map/ppermute | solution.py:229
  81.4 16.7 %collective-permute-start.6 = (bf16[12,128,128]{2,1,0:T(8,128)(2,1)S(1)}, bf16[12,128,128]{2,1,0:T(8,128)(2,1)S(1)}, u32[]{:S(2)}, u32[]{:S(2)}) collective-permute-start(bf16[12,128,128]{2,1,0:T(8,128)(2,1)S(1)} %get-tuple-element.15), channel_id=1, source_target_pairs={{0,16},{16,32},{32,48},{48,64},{64,80},{80,96},{96,112},{112,0},{1... | collective-permute-start | bytes 1179656 | tf_op jit(solution)/shard_map/ppermute | solution.py:229
  83.0 23.4 %collective-permute-start.5 = (bf16[12,128,128]{2,1,0:T(8,128)(2,1)S(1)}, bf16[12,128,128]{2,1,0:T(8,128)(2,1)S(1)}, u32[]{:S(2)}, u32[]{:S(2)}) collective-permute-start(bf16[12,128,128]{2,1,0:T(8,128)(2,1)S(1)} %get-tuple-element.16), channel_id=1, source_target_pairs={{0,16},{16,32},{32,48},{48,64},{64,80},{80,96},{96,112},{112,0},{1... | collective-permute-start | bytes 1179656 | tf_op jit(solution)/shard_map/ppermute | solution.py:229
  83.0 31.7 %collective-permute-start.4 = (bf16[12,128,128]{2,1,0:T(8,128)(2,1)S(1)}, bf16[12,128,128]{2,1,0:T(8,128)(2,1)S(1)}, u32[]{:S(2)}, u32[]{:S(2)}) collective-permute-start(bf16[12,128,128]{2,1,0:T(8,128)(2,1)S(1)} %get-tuple-element.17), channel_id=1, source_target_pairs={{0,16},{16,32},{32,48},{48,64},{64,80},{80,96},{96,112},{112,0},{1... | collective-permute-start | bytes 1179656 | tf_op jit(solution)/shard_map/ppermute | solution.py:229
  89.8 0.8 copy-start.3
  98.1 0.8 copy-start.6
  106.4 0.8 copy-start.5
  114.8 0.8 copy-start.4

commit v16 on v15

--- a/solution.py
+++ b/solution.py
@@ -11,7 +11,7 @@
 EPSILON = 1e-05
 HEADS_PER_STEP = 6
 SUMMARY_HEADS_PER_STEP = 12
-STATE_CHUNKS = 4
+STATE_CHUNKS = 2
 
 
 def _silu(v):

time: 124 us -> 121 us (0.976)
  waiting for transfers between devices: 56.6 us -> 62.8 us
  Pallas kernels: 44 us -> 38.8 us
  starting transfers between devices: 17.4 us -> 15.3 us
    ppermute x4 -> x2, waiting for transfers between devices: 5.05 us -> 11 us  [on_device(): lax.ppermute(incoming[part * chunk:(part + 1) * chunk], 'section', pairs)]
    pallas_call x4 -> x2, Pallas kernels: 30.2 us -> 24.8 us  [_outputs(): pl.pallas_call(kernel, grid_spec=pltpu.PrefetchScalarGridSpec(num_scalar_...]
    ppermute x4 -> x2, starting transfers between devices: 3.37 us -> 1.6 us  [on_device(): lax.ppermute(incoming[part * chunk:(part + 1) * chunk], 'section', pairs)]
    unnamed x22 -> x18, local copies, waits for them, and re-layouts: 4.2 us -> 2.96 us
  transfers between devices with their start and end apart: 10 -> 8, of which waited for: 4 -> 4; matrix products, arithmetic and copies ran while one was open for 0% -> 0% of each run, Pallas kernels for 30% -> 22%
where the time goes in v16:
time: 121 us
  waiting for transfers between devices  62.8 us (52%)
  Pallas kernels  38.8 us (32%)
  starting transfers between devices  15.3 us (13%)
  local copies, waits for them, and re-layouts  3.13 us (3%)
    all_to_all x1, waiting for transfers between devices, on_device(): gathered = lax.all_to_all(summary, 'ctx', 0, 0, tiled=True)  27.7 us
    pallas_call x2, Pallas kernels, _outputs(): pl.pallas_call(kernel, grid_spec=pltpu.PrefetchScalarGridSpec(num_scalar_...  24.8 us
    ppermute x4, waiting for transfers between devices, on_device(): lax.ppermute((section_inputs, flat_gains, out_gain, decay_rates), 'sectio...  16.5 us
    ppermute x2, waiting for transfers between devices, on_device(): lax.ppermute(incoming[part * chunk:(part + 1) * chunk], 'section', pairs)  11 us
    pallas_call x1, Pallas kernels, _summaries(): pl.pallas_call(kernel, grid_spec=pltpu.PrefetchScalarGridSpec(num_scalar_...  10.2 us
    all_to_all x1, starting transfers between devices, on_device(): gathered = lax.all_to_all(summary, 'ctx', 0, 0, tiled=True)  8.16 us
    all_to_all x1, waiting for transfers between devices, on_device(): lax.all_to_all(prefixes.reshape(heads, head_dim, head_dim), 'ctx', 0, 0,...  7.63 us
    pallas_call x1, Pallas kernels, _scan(): pl.pallas_call(kernel, grid_spec=pltpu.PrefetchScalarGridSpec(num_scalar_...  3.77 us
  transfers between devices with their start and end apart: 8, of which 4 were waited for; matrix products, arithmetic and copies ran while one was open for 0% of the time, Pallas kernels for 22%

profile of v16, /device:TPU:0, one launch (start us, length us, event | category | flops | bytes accessed | tf_op | source)
XLA Modules:
  0.0 120.7 jit_solution(15622809497363234533)
XLA Ops:
  0.6 0.0 collective-permute-start.3
  0.7 10.2 %shard_map.68 = bf16[48,128,128]{2,1,0:T(8,128)(2,1)} custom-call(f32[48]{0:T(128)} %bitcast.13, bf16[1,512,6144]{2,1,0:T(8,128)(2,1)} %x_ref.1, f32[1,18432]{1,0:T(1,128)} %bitcast.8, f32[1,18432]{1,0:T(1,128)} %bitcast.9), custom_call_target="tpu_custom_call" | custom-call | flops 805306368 | bytes 9437184 | tf_op jit(solution)/shard_map/pallas_call | solution.py:135
  10.9 8.2 %all-to-all-start = ((bf16[48,128,128]{2,1,0:T(8,128)(2,1)}), bf16[48,128,128]{2,1,0:T(8,128)(2,1)S(1)}, u32[]{:S(2)}, u32[]{:S(2)}) async-start(bf16[48,128,128]{2,1,0:T(8,128)(2,1)} %shard_map.68), calls=%async_computation | async-start | bytes 3145728 | tf_op jit(solution)/shard_map/all_to_all | solution.py:215
  19.0 27.7 %all-to-all-done = bf16[48,128,128]{2,1,0:T(8,128)(2,1)S(1)} async-done(((bf16[48,128,128]{2,1,0:T(8,128)(2,1)}), bf16[48,128,128]{2,1,0:T(8,128)(2,1)S(1)}, u32[]{:S(2)}, u32[]{:S(2)}) %all-to-all-start) | async-done | bytes 1572896 | tf_op jit(solution)/shard_map/all_to_all | solution.py:215
  46.7 0.0 copy-start
  46.7 1.1 copy-done
  47.8 3.8 %shard_map.69 = (bf16[16,3,128,128]{3,2,1,0:T(8,128)(2,1)}, f32[1,3,128,128]{3,2,1,0:T(8,128)}) custom-call(s32[1]{0:T(128)} %bitcast.1.place_ref, f32[48]{0:T(128)} %bitcast.14, bf16[16,3,128,128]{3,2,1,0:T(8,128)(2,1)} %bitcast.6, f32[1,48,128,128]{3,2,1,0:T(8,128)} %c_ref.1), custom_call_target="tpu_custom_call" | custom-call | flops 1572864 | bytes 3538944 | tf_op jit(solution)/shard_map/pallas_call | solution.py:103
  51.6 3.7 %all-to-all-start.1 = ((bf16[48,128,128]{2,1,0:T(8,128)(2,1)}), bf16[48,128,128]{2,1,0:T(8,128)(2,1)S(1)}, u32[]{:S(2)}, u32[]{:S(2)}) async-start(bf16[48,128,128]{2,1,0:T(8,128)(2,1)} %bitcast.7), calls=%async_computation.1 | async-start | bytes 3145728 | tf_op jit(solution)/shard_map/all_to_all | solution.py:220
  55.3 0.0 copy-done.4
  55.3 0.2 collective-permute-start
  55.5 0.0 copy-done.8
  55.5 1.5 %collective-permute-start.1 = (f32[1,6144]{1,0:T(1,128)S(1)}, f32[1,6144]{1,0:T(1,128)S(1)}, u32[]{:S(2)}, u32[]{:S(2)}) collective-permute-start(f32[1,6144]{1,0:T(1,128)S(1)} %copy-done.8), channel_id=1, source_target_pairs={{0,16},{16,32},{32,48},{48,64},{64,80},{80,96},{96,112},{112,0},{1... | collective-permute-start | bytes 73736 | tf_op jit(solution)/shard_map/ppermute | solution.py:210
  57.0 0.0 copy-done.7
  57.0 0.2 collective-permute-start.2
  57.1 16.5 %collective-permute-done.2 = f32[1,48]{1,0:T(1,128)S(1)} collective-permute-done((f32[1,48]{1,0:T(1,128)S(1)}, f32[1,48]{1,0:T(1,128)S(1)}, u32[]{:S(2)}, u32[]{:S(2)}) %collective-permute-start.2) | collective-permute-done | bytes 224 | tf_op jit(solution)/shard_map/ppermute | solution.py:210
  73.6 0.0 collective-permute-done.1.go_ref
  73.6 0.0 collective-permute-done.gq_ref.gk_ref.gv_ref
  73.6 0.0 copy-start.1
  73.6 7.6 %all-to-all-done.1 = bf16[48,128,128]{2,1,0:T(8,128)(2,1)S(1)} async-done(((bf16[48,128,128]{2,1,0:T(8,128)(2,1)}), bf16[48,128,128]{2,1,0:T(8,128)(2,1)S(1)}, u32[]{:S(2)}, u32[]{:S(2)}) %all-to-all-start.1) | async-done | bytes 1572896 | tf_op jit(solution)/shard_map/all_to_all | solution.py:220
  81.3 0.2 fusion
  81.4 0.0 collective-permute-start.5
  81.5 1.6 %collective-permute-start.4 = (bf16[24,128,128]{2,1,0:T(8,128)(2,1)S(1)}, bf16[24,128,128]{2,1,0:T(8,128)(2,1)S(1)}, u32[]{:S(2)}, u32[]{:S(2)}) collective-permute-start(bf16[24,128,128]{2,1,0:T(8,128)(2,1)S(1)} %get-tuple-element.15), channel_id=1, source_target_pairs={{0,16},{16,32},{32,48},{48,64},{64,80},{80,96},{96,112},{112,0},{1... | collective-permute-start | bytes 2359304 | tf_op jit(solution)/shard_map/ppermute | solution.py:229
  83.0 11.0 %collective-permute-done.5.s_ref = bf16[24,128,128]{2,1,0:T(8,128)(2,1)S(1)} collective-permute-done((bf16[24,128,128]{2,1,0:T(8,128)(2,1)S(1)}, bf16[24,128,128]{2,1,0:T(8,128)(2,1)S(1)}, u32[]{:S(2)}, u32[]{:S(2)}) %collective-permute-start.5) | collective-permute-done | bytes 786464 | tf_op jit(solution)/shard_map/ppermute | solution.py:229
  94.1 0.0 collective-permute-done.3.x_ref
  94.1 0.0 copy-done.6
  94.1 0.0 copy-done.5
  94.1 0.0 copy-done.1
  94.1 0.9 copy-done.3
  95.0 12.4 %shard_map.70.rest_0_ = bf16[1,512,6144]{2,1,0:T(8,128)(2,1)} custom-call(f32[48]{0:T(128)} %bitcast.11, bf16[1,512,6144]{2,1,0:T(8,128)(2,1)} %collective-permute-done.3.x_ref, f32[1,18432]{1,0:T(1,128)} %copy-done.1, f32[1,18432]{1,0:T(1,128)} %copy-done.1, f32[1,18432]{1,0:T(1,128)} %copy-done.1, f32[1,6144]{1,0:T(1,128)} %copy-done.5, ...), custom_call_target="tpu_custom_call" | custom-call | flops 3221225472 | bytes 7077888 | tf_op jit(solution)/shard_map/pallas_call | solution.py:181
  107.4 0.0 collective-permute-done.4.s_ref
  107.4 0.9 copy-done.2
  108.3 12.4 %shard_map.71 = bf16[1,512,6144]{2,1,0:T(8,128)(2,1)} custom-call(f32[48]{0:T(128)} %bitcast.12, bf16[1,512,6144]{2,1,0:T(8,128)(2,1)} %collective-permute-done.3.x_ref, f32[1,18432]{1,0:T(1,128)} %copy-done.1, f32[1,18432]{1,0:T(1,128)} %copy-done.1, f32[1,18432]{1,0:T(1,128)} %copy-done.1, f32[1,6144]{1,0:T(1,128)} %copy-done.5, ...), custom_call_target="tpu_custom_call", output_to_operand_aliasing={{}: (7, {})} | custom-call | flops 3221225472 | bytes 7077888 | tf_op jit(solution)/shard_map/pallas_call | solution.py:181
  (7 shorter events, 0.0 us)
Async XLA Ops:
  0.6 93.4 %collective-permute-start.3 = (bf16[1,512,6144]{2,1,0:T(8,128)(2,1)}, bf16[1,512,6144]{2,1,0:T(8,128)(2,1)}, u32[]{:S(2)}, u32[]{:S(2)}) collective-permute-start(bf16[1,512,6144]{2,1,0:T(8,128)(2,1)} %x_ref.1), channel_id=1, source_target_pairs={{0,16},{16,32},{32,48},{48,64},{64,80},{80,96},{96,112},{112,0},{1... | collective-permute-start | bytes 18874376 | tf_op jit(solution)/shard_map/ppermute | solution.py:210
  10.9 35.8 %all-to-all-start = ((bf16[48,128,128]{2,1,0:T(8,128)(2,1)}), bf16[48,128,128]{2,1,0:T(8,128)(2,1)S(1)}, u32[]{:S(2)}, u32[]{:S(2)}) async-start(bf16[48,128,128]{2,1,0:T(8,128)(2,1)} %shard_map.68), calls=%async_computation | async-start | bytes 3145728 | tf_op jit(solution)/shard_map/all_to_all | solution.py:215
  46.7 1.1 copy-start
  47.8 7.5 %copy-start.4 = (f32[1,3,6144]{2,0,1:T(1,128)S(1)}, f32[1,3,6144]{2,0,1:T(1,128)}, u32[]{:S(2)}) copy-start(f32[1,3,6144]{2,0,1:T(1,128)} %param.6) | copy-start | bytes 221188
  47.8 7.7 %copy-start.8 = (f32[1,6144]{1,0:T(1,128)S(1)}, f32[1,6144]{1,0:T(1,128)}, u32[]{:S(2)}) copy-start(f32[1,6144]{1,0:T(1,128)} %param.7) | copy-start | bytes 73732
  47.8 9.1 %copy-start.7 = (f32[1,48]{1,0:T(1,128)S(1)}, f32[1,48]{1,0:T(1,128)}, u32[]{:S(2)}) copy-start(f32[1,48]{1,0:T(1,128)} %param.8) | copy-start | bytes 580
  51.6 29.6 %all-to-all-start.1 = ((bf16[48,128,128]{2,1,0:T(8,128)(2,1)}), bf16[48,128,128]{2,1,0:T(8,128)(2,1)S(1)}, u32[]{:S(2)}, u32[]{:S(2)}) async-start(bf16[48,128,128]{2,1,0:T(8,128)(2,1)} %bitcast.7), calls=%async_computation.1 | async-start | bytes 3145728 | tf_op jit(solution)/shard_map/all_to_all | solution.py:220
  55.3 18.3 %collective-permute-start = (f32[1,18432]{1,0:T(1,128)S(1)}, f32[1,18432]{1,0:T(1,128)S(1)}, u32[]{:S(2)}, u32[]{:S(2)}) collective-permute-start(f32[1,18432]{1,0:T(1,128)S(1)} %bitcast.10), channel_id=1, source_target_pairs={{0,16},{16,32},{32,48},{48,64},{64,80},{80,96},{96,112},{112,0},{1... | collective-permute-start | bytes 221192 | tf_op jit(solution)/shard_map/ppermute | solution.py:210
  55.5 18.1 %collective-permute-start.1 = (f32[1,6144]{1,0:T(1,128)S(1)}, f32[1,6144]{1,0:T(1,128)S(1)}, u32[]{:S(2)}, u32[]{:S(2)}) collective-permute-start(f32[1,6144]{1,0:T(1,128)S(1)} %copy-done.8), channel_id=1, source_target_pairs={{0,16},{16,32},{32,48},{48,64},{64,80},{80,96},{96,112},{112,0},{1... | collective-permute-start | bytes 73736 | tf_op jit(solution)/shard_map/ppermute | solution.py:210
  57.0 16.6 %collective-permute-start.2 = (f32[1,48]{1,0:T(1,128)S(1)}, f32[1,48]{1,0:T(1,128)S(1)}, u32[]{:S(2)}, u32[]{:S(2)}) collective-permute-start(f32[1,48]{1,0:T(1,128)S(1)} %copy-done.7), channel_id=1, source_target_pairs={{0,16},{16,32},{32,48},{48,64},{64,80},{80,96},{96,112},{112,0},{1... | collective-permute-start | bytes 584 | tf_op jit(solution)/shard_map/ppermute | solution.py:210
  73.6 20.5 %copy-start.6 = (f32[1,48]{1,0:T(1,128)}, f32[1,48]{1,0:T(1,128)S(1)}, u32[]{:S(2)}) copy-start(f32[1,48]{1,0:T(1,128)S(1)} %collective-permute-done.2) | copy-start | bytes 580
  73.6 20.5 %copy-start.5 = (f32[1,6144]{1,0:T(1,128)}, f32[1,6144]{1,0:T(1,128)S(1)}, u32[]{:S(2)}) copy-start(f32[1,6144]{1,0:T(1,128)S(1)} %collective-permute-done.1.go_ref) | copy-start | bytes 73732
  73.6 20.5 %copy-start.1 = (f32[1,18432]{1,0:T(1,128)}, f32[1,18432]{1,0:T(1,128)S(1)}, u32[]{:S(2)}) copy-start(f32[1,18432]{1,0:T(1,128)S(1)} %collective-permute-done.gq_ref.gk_ref.gv_ref) | copy-start | bytes 221188
  81.4 12.6 %collective-permute-start.5 = (bf16[24,128,128]{2,1,0:T(8,128)(2,1)S(1)}, bf16[24,128,128]{2,1,0:T(8,128)(2,1)S(1)}, u32[]{:S(2)}, u32[]{:S(2)}) collective-permute-start(bf16[24,128,128]{2,1,0:T(8,128)(2,1)S(1)} %get-tuple-element.14), channel_id=1, source_target_pairs={{0,16},{16,32},{32,48},{48,64},{64,80},{80,96},{96,112},{112,0},{1... | collective-permute-start | bytes 2359304 | tf_op jit(solution)/shard_map/ppermute | solution.py:229
  81.5 25.9 %collective-permute-start.4 = (bf16[24,128,128]{2,1,0:T(8,128)(2,1)S(1)}, bf16[24,128,128]{2,1,0:T(8,128)(2,1)S(1)}, u32[]{:S(2)}, u32[]{:S(2)}) collective-permute-start(bf16[24,128,128]{2,1,0:T(8,128)(2,1)S(1)} %get-tuple-element.15), channel_id=1, source_target_pairs={{0,16},{16,32},{32,48},{48,64},{64,80},{80,96},{96,112},{112,0},{1... | collective-permute-start | bytes 2359304 | tf_op jit(solution)/shard_map/ppermute | solution.py:229
  94.1 0.9 copy-start.3
  107.4 0.9 copy-start.2

commit v17 on v16

--- a/solution.py
+++ b/solution.py
@@ -11,7 +11,7 @@
 EPSILON = 1e-05
 HEADS_PER_STEP = 6
 SUMMARY_HEADS_PER_STEP = 12
-STATE_CHUNKS = 2
+FIRST_CHUNK_STEPS = 3
 
 
 def _silu(v):
@@ -223,13 +223,14 @@
     prev_gains, prev_gain_out, prev_rates, incoming = lax.optimization_barrier(
         (prev_gains, prev_gain_out, prev_rates, incoming)
     )
-    chunk = heads // STATE_CHUNKS
+    first_chunk = min(FIRST_CHUNK_STEPS * HEADS_PER_STEP, heads)
+    bounds = [0, first_chunk, heads] if first_chunk < heads else [0, heads]
     next_rows = None
-    for part in range(STATE_CHUNKS):
-        piece = lax.ppermute(incoming[part * chunk : (part + 1) * chunk], "section", pairs)
+    for lo, hi in zip(bounds[:-1], bounds[1:]):
+        piece = lax.ppermute(incoming[lo:hi], "section", pairs)
         next_rows = _outputs(
             prev_rates[0], prev_rows, prev_gains, prev_gain_out, piece, head_dim,
-            part * chunk, next_rows,
+            lo, next_rows,
         )
     return (next_rows, end_part)
 

time: 121 us -> 131 us (1.083)
  waiting for transfers between devices: 62.8 us -> 71.4 us
    ppermute x2, waiting for transfers between devices: 11 us -> 19.6 us  [on_device(): piece = lax.ppermute(incoming[lo:hi], 'section', pairs)]
  transfers between devices with their start and end apart: 8 -> 8, of which waited for: 4 -> 4; matrix products, arithmetic and copies ran while one was open for 0% -> 1% of each run, Pallas kernels for 22% -> 18%
where the time goes in v17:
time: 131 us; the launch traced here: 130 us
  waiting for transfers between devices  71.4 us (55%)
  Pallas kernels  38.8 us (30%)
  starting transfers between devices  15.3 us (12%)
  local copies, waits for them, and re-layouts  4.02 us (3%)
    all_to_all x1, waiting for transfers between devices, on_device(): gathered = lax.all_to_all(summary, 'ctx', 0, 0, tiled=True)  27.7 us
    pallas_call x2, Pallas kernels, _outputs(): pl.pallas_call(kernel, grid_spec=pltpu.PrefetchScalarGridSpec(num_scalar_...  24.8 us
    ppermute x2, waiting for transfers between devices, on_device(): piece = lax.ppermute(incoming[lo:hi], 'section', pairs)  19.6 us
    ppermute x4, waiting for transfers between devices, on_device(): lax.ppermute((section_inputs, flat_gains, out_gain, decay_rates), 'sectio...  16.5 us
    pallas_call x1, Pallas kernels, _summaries(): pl.pallas_call(kernel, grid_spec=pltpu.PrefetchScalarGridSpec(num_scalar_...  10.2 us
    all_to_all x1, starting transfers between devices, on_device(): gathered = lax.all_to_all(summary, 'ctx', 0, 0, tiled=True)  8.16 us
    all_to_all x1, waiting for transfers between devices, on_device(): lax.all_to_all(prefixes.reshape(heads, head_dim, head_dim), 'ctx', 0, 0,...  7.63 us
    pallas_call x1, Pallas kernels, _scan(): pl.pallas_call(kernel, grid_spec=pltpu.PrefetchScalarGridSpec(num_scalar_...  3.77 us
  transfers between devices with their start and end apart: 8, of which 4 were waited for; matrix products, arithmetic and copies ran while one was open for 1% of the time, Pallas kernels for 18%

profile of v17, /device:TPU:0, one launch (start us, length us, event | category | flops | bytes accessed | tf_op | source)
XLA Modules:
  0.0 130.2 jit_solution(8334008227307600692)
XLA Ops:
  0.6 0.0 collective-permute-start.3
  0.7 10.2 %shard_map.68 = bf16[48,128,128]{2,1,0:T(8,128)(2,1)} custom-call(f32[48]{0:T(128)} %bitcast.13, bf16[1,512,6144]{2,1,0:T(8,128)(2,1)} %x_ref.1, f32[1,18432]{1,0:T(1,128)} %bitcast.8, f32[1,18432]{1,0:T(1,128)} %bitcast.9), custom_call_target="tpu_custom_call" | custom-call | flops 805306368 | bytes 9437184 | tf_op jit(solution)/shard_map/pallas_call | solution.py:135
  10.9 8.2 %all-to-all-start = ((bf16[48,128,128]{2,1,0:T(8,128)(2,1)}), bf16[48,128,128]{2,1,0:T(8,128)(2,1)S(1)}, u32[]{:S(2)}, u32[]{:S(2)}) async-start(bf16[48,128,128]{2,1,0:T(8,128)(2,1)} %shard_map.68), calls=%async_computation | async-start | bytes 3145728 | tf_op jit(solution)/shard_map/all_to_all | solution.py:215
  19.0 27.7 %all-to-all-done = bf16[48,128,128]{2,1,0:T(8,128)(2,1)S(1)} async-done(((bf16[48,128,128]{2,1,0:T(8,128)(2,1)}), bf16[48,128,128]{2,1,0:T(8,128)(2,1)S(1)}, u32[]{:S(2)}, u32[]{:S(2)}) %all-to-all-start) | async-done | bytes 1572896 | tf_op jit(solution)/shard_map/all_to_all | solution.py:215
  46.7 0.0 copy-start
  46.7 1.1 copy-done
  47.8 3.8 %shard_map.69 = (bf16[16,3,128,128]{3,2,1,0:T(8,128)(2,1)}, f32[1,3,128,128]{3,2,1,0:T(8,128)}) custom-call(s32[1]{0:T(128)} %bitcast.1.place_ref, f32[48]{0:T(128)} %bitcast.14, bf16[16,3,128,128]{3,2,1,0:T(8,128)(2,1)} %bitcast.6, f32[1,48,128,128]{3,2,1,0:T(8,128)} %c_ref.1), custom_call_target="tpu_custom_call" | custom-call | flops 1572864 | bytes 3538944 | tf_op jit(solution)/shard_map/pallas_call | solution.py:103
  51.6 3.7 %all-to-all-start.1 = ((bf16[48,128,128]{2,1,0:T(8,128)(2,1)}), bf16[48,128,128]{2,1,0:T(8,128)(2,1)S(1)}, u32[]{:S(2)}, u32[]{:S(2)}) async-start(bf16[48,128,128]{2,1,0:T(8,128)(2,1)} %bitcast.7), calls=%async_computation.1 | async-start | bytes 3145728 | tf_op jit(solution)/shard_map/all_to_all | solution.py:220
  55.3 0.0 copy-done.4
  55.3 0.2 collective-permute-start
  55.5 0.0 copy-done.8
  55.5 1.5 %collective-permute-start.1 = (f32[1,6144]{1,0:T(1,128)S(1)}, f32[1,6144]{1,0:T(1,128)S(1)}, u32[]{:S(2)}, u32[]{:S(2)}) collective-permute-start(f32[1,6144]{1,0:T(1,128)S(1)} %copy-done.8), channel_id=1, source_target_pairs={{0,16},{16,32},{32,48},{48,64},{64,80},{80,96},{96,112},{112,0},{1... | collective-permute-start | bytes 73736 | tf_op jit(solution)/shard_map/ppermute | solution.py:210
  57.0 0.0 copy-done.7
  57.0 0.2 collective-permute-start.2
  57.1 16.5 %collective-permute-done.2 = f32[1,48]{1,0:T(1,128)S(1)} collective-permute-done((f32[1,48]{1,0:T(1,128)S(1)}, f32[1,48]{1,0:T(1,128)S(1)}, u32[]{:S(2)}, u32[]{:S(2)}) %collective-permute-start.2) | collective-permute-done | bytes 224 | tf_op jit(solution)/shard_map/ppermute | solution.py:210
  73.6 0.0 collective-permute-done.1.go_ref
  73.6 0.0 collective-permute-done.gq_ref.gk_ref.gv_ref
  73.6 0.0 copy-start.1
  73.6 7.6 %all-to-all-done.1 = bf16[48,128,128]{2,1,0:T(8,128)(2,1)S(1)} async-done(((bf16[48,128,128]{2,1,0:T(8,128)(2,1)}), bf16[48,128,128]{2,1,0:T(8,128)(2,1)S(1)}, u32[]{:S(2)}, u32[]{:S(2)}) %all-to-all-start.1) | async-done | bytes 1572896 | tf_op jit(solution)/shard_map/all_to_all | solution.py:220
  81.3 1.0 slice.6
  82.3 0.0 collective-permute-start.4
  82.4 1.6 %collective-permute-start.5 = (bf16[18,128,128]{2,1,0:T(8,128)(2,1)S(1)}, bf16[18,128,128]{2,1,0:T(8,128)(2,1)S(1)}, u32[]{:S(2)}, u32[]{:S(2)}) collective-permute-start(bf16[18,128,128]{2,1,0:T(8,128)(2,1)S(1)} %slice.7), channel_id=1, source_target_pairs={{0,16},{16,32},{32,48},{48,64},{64,80},{80,96},{96,112},{112,0},{1... | collective-permute-start | bytes 1769480 | tf_op jit(solution)/shard_map/ppermute | solution.py:230
  84.0 19.6 %collective-permute-done.5.s_ref = bf16[18,128,128]{2,1,0:T(8,128)(2,1)S(1)} collective-permute-done((bf16[18,128,128]{2,1,0:T(8,128)(2,1)S(1)}, bf16[18,128,128]{2,1,0:T(8,128)(2,1)S(1)}, u32[]{:S(2)}, u32[]{:S(2)}) %collective-permute-start.5) | collective-permute-done | bytes 589856 | tf_op jit(solution)/shard_map/ppermute | solution.py:230
  103.6 0.0 collective-permute-done.3.x_ref
  103.6 0.0 copy-done.6
  103.6 0.0 copy-done.5
  103.6 0.0 copy-done.1
  103.6 0.8 copy-done.3
  104.4 10.0 %shard_map.70.rest_0_ = bf16[1,512,6144]{2,1,0:T(8,128)(2,1)} custom-call(f32[48]{0:T(128)} %bitcast.11, bf16[1,512,6144]{2,1,0:T(8,128)(2,1)} %collective-permute-done.3.x_ref, f32[1,18432]{1,0:T(1,128)} %copy-done.1, f32[1,18432]{1,0:T(1,128)} %copy-done.1, f32[1,18432]{1,0:T(1,128)} %copy-done.1, f32[1,6144]{1,0:T(1,128)} %copy-done.5, ...), custom_call_target="tpu_custom_call" | custom-call | flops 2415919104 | bytes 5308416 | tf_op jit(solution)/shard_map/pallas_call | solution.py:181
  114.4 0.0 collective-permute-done.4.s_ref
  114.4 1.0 copy-done.2
  115.3 14.9 %shard_map.71 = bf16[1,512,6144]{2,1,0:T(8,128)(2,1)} custom-call(f32[48]{0:T(128)} %bitcast.12, bf16[1,512,6144]{2,1,0:T(8,128)(2,1)} %collective-permute-done.3.x_ref, f32[1,18432]{1,0:T(1,128)} %copy-done.1, f32[1,18432]{1,0:T(1,128)} %copy-done.1, f32[1,18432]{1,0:T(1,128)} %copy-done.1, f32[1,6144]{1,0:T(1,128)} %copy-done.5, ...), custom_call_target="tpu_custom_call", output_to_operand_aliasing={{}: (7, {})} | custom-call | flops 4026531840 | bytes 8847360 | tf_op jit(solution)/shard_map/pallas_call | solution.py:181
  (8 shorter events, 0.0 us)
Async XLA Ops:
  0.6 102.9 %collective-permute-start.3 = (bf16[1,512,6144]{2,1,0:T(8,128)(2,1)}, bf16[1,512,6144]{2,1,0:T(8,128)(2,1)}, u32[]{:S(2)}, u32[]{:S(2)}) collective-permute-start(bf16[1,512,6144]{2,1,0:T(8,128)(2,1)} %x_ref.1), channel_id=1, source_target_pairs={{0,16},{16,32},{32,48},{48,64},{64,80},{80,96},{96,112},{112,0},{1... | collective-permute-start | bytes 18874376 | tf_op jit(solution)/shard_map/ppermute | solution.py:210
  10.9 35.8 %all-to-all-start = ((bf16[48,128,128]{2,1,0:T(8,128)(2,1)}), bf16[48,128,128]{2,1,0:T(8,128)(2,1)S(1)}, u32[]{:S(2)}, u32[]{:S(2)}) async-start(bf16[48,128,128]{2,1,0:T(8,128)(2,1)} %shard_map.68), calls=%async_computation | async-start | bytes 3145728 | tf_op jit(solution)/shard_map/all_to_all | solution.py:215
  46.7 1.1 copy-start
  47.8 7.5 %copy-start.4 = (f32[1,3,6144]{2,0,1:T(1,128)S(1)}, f32[1,3,6144]{2,0,1:T(1,128)}, u32[]{:S(2)}) copy-start(f32[1,3,6144]{2,0,1:T(1,128)} %param.6) | copy-start | bytes 221188
  47.8 7.7 %copy-start.8 = (f32[1,6144]{1,0:T(1,128)S(1)}, f32[1,6144]{1,0:T(1,128)}, u32[]{:S(2)}) copy-start(f32[1,6144]{1,0:T(1,128)} %param.7) | copy-start | bytes 73732
  47.8 9.1 %copy-start.7 = (f32[1,48]{1,0:T(1,128)S(1)}, f32[1,48]{1,0:T(1,128)}, u32[]{:S(2)}) copy-start(f32[1,48]{1,0:T(1,128)} %param.8) | copy-start | bytes 580
  51.6 29.6 %all-to-all-start.1 = ((bf16[48,128,128]{2,1,0:T(8,128)(2,1)}), bf16[48,128,128]{2,1,0:T(8,128)(2,1)S(1)}, u32[]{:S(2)}, u32[]{:S(2)}) async-start(bf16[48,128,128]{2,1,0:T(8,128)(2,1)} %bitcast.7), calls=%async_computation.1 | async-start | bytes 3145728 | tf_op jit(solution)/shard_map/all_to_all | solution.py:220
  55.3 18.3 %collective-permute-start = (f32[1,18432]{1,0:T(1,128)S(1)}, f32[1,18432]{1,0:T(1,128)S(1)}, u32[]{:S(2)}, u32[]{:S(2)}) collective-permute-start(f32[1,18432]{1,0:T(1,128)S(1)} %bitcast.10), channel_id=1, source_target_pairs={{0,16},{16,32},{32,48},{48,64},{64,80},{80,96},{96,112},{112,0},{1... | collective-permute-start | bytes 221192 | tf_op jit(solution)/shard_map/ppermute | solution.py:210
  55.5 18.1 %collective-permute-start.1 = (f32[1,6144]{1,0:T(1,128)S(1)}, f32[1,6144]{1,0:T(1,128)S(1)}, u32[]{:S(2)}, u32[]{:S(2)}) collective-permute-start(f32[1,6144]{1,0:T(1,128)S(1)} %copy-done.8), channel_id=1, source_target_pairs={{0,16},{16,32},{32,48},{48,64},{64,80},{80,96},{96,112},{112,0},{1... | collective-permute-start | bytes 73736 | tf_op jit(solution)/shard_map/ppermute | solution.py:210
  57.0 16.6 %collective-permute-start.2 = (f32[1,48]{1,0:T(1,128)S(1)}, f32[1,48]{1,0:T(1,128)S(1)}, u32[]{:S(2)}, u32[]{:S(2)}) collective-permute-start(f32[1,48]{1,0:T(1,128)S(1)} %copy-done.7), channel_id=1, source_target_pairs={{0,16},{16,32},{32,48},{48,64},{64,80},{80,96},{96,112},{112,0},{1... | collective-permute-start | bytes 584 | tf_op jit(solution)/shard_map/ppermute | solution.py:210
  73.6 30.0 %copy-start.6 = (f32[1,48]{1,0:T(1,128)}, f32[1,48]{1,0:T(1,128)S(1)}, u32[]{:S(2)}) copy-start(f32[1,48]{1,0:T(1,128)S(1)} %collective-permute-done.2) | copy-start | bytes 580
  73.6 30.0 %copy-start.5 = (f32[1,6144]{1,0:T(1,128)}, f32[1,6144]{1,0:T(1,128)S(1)}, u32[]{:S(2)}) copy-start(f32[1,6144]{1,0:T(1,128)S(1)} %collective-permute-done.1.go_ref) | copy-start | bytes 73732
  73.6 30.0 %copy-start.1 = (f32[1,18432]{1,0:T(1,128)}, f32[1,18432]{1,0:T(1,128)S(1)}, u32[]{:S(2)}) copy-start(f32[1,18432]{1,0:T(1,128)S(1)} %collective-permute-done.gq_ref.gk_ref.gv_ref) | copy-start | bytes 221188
  82.3 32.1 %collective-permute-start.4 = (bf16[30,128,128]{2,1,0:T(8,128)(2,1)}, bf16[30,128,128]{2,1,0:T(8,128)(2,1)S(1)}, u32[]{:S(2)}, u32[]{:S(2)}) collective-permute-start(bf16[30,128,128]{2,1,0:T(8,128)(2,1)} %slice.6), channel_id=1, source_target_pairs={{0,16},{16,32},{32,48},{48,64},{64,80},{80,96},{96,112},{112,0},{1... | collective-permute-start | bytes 2949128 | tf_op jit(solution)/shard_map/ppermute | solution.py:230
  82.4 21.2 %collective-permute-start.5 = (bf16[18,128,128]{2,1,0:T(8,128)(2,1)S(1)}, bf16[18,128,128]{2,1,0:T(8,128)(2,1)S(1)}, u32[]{:S(2)}, u32[]{:S(2)}) collective-permute-start(bf16[18,128,128]{2,1,0:T(8,128)(2,1)S(1)} %slice.7), channel_id=1, source_target_pairs={{0,16},{16,32},{32,48},{48,64},{64,80},{80,96},{96,112},{112,0},{1... | collective-permute-start | bytes 1769480 | tf_op jit(solution)/shard_map/ppermute | solution.py:230
  103.6 0.8 copy-start.3
  114.4 1.0 copy-start.2

commit v18 on v16

--- a/solution.py
+++ b/solution.py
@@ -9,7 +9,7 @@
 
 BLOCK = 256
 EPSILON = 1e-05
-HEADS_PER_STEP = 6
+HEADS_PER_STEP = 12
 SUMMARY_HEADS_PER_STEP = 12
 STATE_CHUNKS = 2
 

time: 121 us -> 121 us (level)
  no operation moved by 1% of the time
where the time goes in v18:
time: 121 us
  waiting for transfers between devices  62.6 us (52%)
  Pallas kernels  38.9 us (32%)
  starting transfers between devices  15.5 us (13%)
  local copies, waits for them, and re-layouts  3.13 us (3%)
    all_to_all x1, waiting for transfers between devices, on_device(): gathered = lax.all_to_all(summary, 'ctx', 0, 0, tiled=True)  27.7 us
    pallas_call x2, Pallas kernels, _outputs(): pl.pallas_call(kernel, grid_spec=pltpu.PrefetchScalarGridSpec(num_scalar_...  24.9 us
    ppermute x4, waiting for transfers between devices, on_device(): lax.ppermute((section_inputs, flat_gains, out_gain, decay_rates), 'sectio...  16.3 us
    ppermute x2, waiting for transfers between devices, on_device(): lax.ppermute(incoming[part * chunk:(part + 1) * chunk], 'section', pairs)  11 us
    pallas_call x1, Pallas kernels, _summaries(): pl.pallas_call(kernel, grid_spec=pltpu.PrefetchScalarGridSpec(num_scalar_...  10.2 us
    all_to_all x1, starting transfers between devices, on_device(): gathered = lax.all_to_all(summary, 'ctx', 0, 0, tiled=True)  8.17 us
    all_to_all x1, waiting for transfers between devices, on_device(): lax.all_to_all(prefixes.reshape(heads, head_dim, head_dim), 'ctx', 0, 0,...  7.62 us
    all_to_all x1, starting transfers between devices, on_device(): lax.all_to_all(prefixes.reshape(heads, head_dim, head_dim), 'ctx', 0, 0,...  3.89 us
  transfers between devices with their start and end apart: 8, of which 4 were waited for; matrix products, arithmetic and copies ran while one was open for 0% of the time, Pallas kernels for 22%

profile of v18, /device:TPU:0, one launch (start us, length us, event | category | flops | bytes accessed | tf_op | source)
XLA Modules:
  0.0 120.8 jit_solution(13238983427893180876)
XLA Ops:
  0.6 0.0 collective-permute-start.3
  0.7 10.2 %shard_map.68 = bf16[48,128,128]{2,1,0:T(8,128)(2,1)} custom-call(f32[48]{0:T(128)} %bitcast.13, bf16[1,512,6144]{2,1,0:T(8,128)(2,1)} %x_ref.1, f32[1,18432]{1,0:T(1,128)} %bitcast.8, f32[1,18432]{1,0:T(1,128)} %bitcast.9), custom_call_target="tpu_custom_call" | custom-call | flops 805306368 | bytes 9437184 | tf_op jit(solution)/shard_map/pallas_call | solution.py:135
  10.9 8.2 %all-to-all-start = ((bf16[48,128,128]{2,1,0:T(8,128)(2,1)}), bf16[48,128,128]{2,1,0:T(8,128)(2,1)S(1)}, u32[]{:S(2)}, u32[]{:S(2)}) async-start(bf16[48,128,128]{2,1,0:T(8,128)(2,1)} %shard_map.68), calls=%async_computation | async-start | bytes 3145728 | tf_op jit(solution)/shard_map/all_to_all | solution.py:215
  19.0 27.7 %all-to-all-done = bf16[48,128,128]{2,1,0:T(8,128)(2,1)S(1)} async-done(((bf16[48,128,128]{2,1,0:T(8,128)(2,1)}), bf16[48,128,128]{2,1,0:T(8,128)(2,1)S(1)}, u32[]{:S(2)}, u32[]{:S(2)}) %all-to-all-start) | async-done | bytes 1572896 | tf_op jit(solution)/shard_map/all_to_all | solution.py:215
  46.7 0.0 copy-start
  46.7 1.1 copy-done
  47.9 3.8 %shard_map.69 = (bf16[16,3,128,128]{3,2,1,0:T(8,128)(2,1)}, f32[1,3,128,128]{3,2,1,0:T(8,128)}) custom-call(s32[1]{0:T(128)} %bitcast.1.place_ref, f32[48]{0:T(128)} %bitcast.14, bf16[16,3,128,128]{3,2,1,0:T(8,128)(2,1)} %bitcast.6, f32[1,48,128,128]{3,2,1,0:T(8,128)} %c_ref.1), custom_call_target="tpu_custom_call" | custom-call | flops 1572864 | bytes 3538944 | tf_op jit(solution)/shard_map/pallas_call | solution.py:103
  51.6 3.9 %all-to-all-start.1 = ((bf16[48,128,128]{2,1,0:T(8,128)(2,1)}), bf16[48,128,128]{2,1,0:T(8,128)(2,1)S(1)}, u32[]{:S(2)}, u32[]{:S(2)}) async-start(bf16[48,128,128]{2,1,0:T(8,128)(2,1)} %bitcast.7), calls=%async_computation.1 | async-start | bytes 3145728 | tf_op jit(solution)/shard_map/all_to_all | solution.py:220
  55.5 0.0 copy-done.4
  55.5 0.2 collective-permute-start
  55.7 0.0 copy-done.8
  55.7 1.4 %collective-permute-start.1 = (f32[1,6144]{1,0:T(1,128)S(1)}, f32[1,6144]{1,0:T(1,128)S(1)}, u32[]{:S(2)}, u32[]{:S(2)}) collective-permute-start(f32[1,6144]{1,0:T(1,128)S(1)} %copy-done.8), channel_id=1, source_target_pairs={{0,16},{16,32},{32,48},{48,64},{64,80},{80,96},{96,112},{112,0},{1... | collective-permute-start | bytes 73736 | tf_op jit(solution)/shard_map/ppermute | solution.py:210
  57.1 0.0 copy-done.7
  57.1 0.2 collective-permute-start.2
  57.3 16.3 %collective-permute-done.2 = f32[1,48]{1,0:T(1,128)S(1)} collective-permute-done((f32[1,48]{1,0:T(1,128)S(1)}, f32[1,48]{1,0:T(1,128)S(1)}, u32[]{:S(2)}, u32[]{:S(2)}) %collective-permute-start.2) | collective-permute-done | bytes 224 | tf_op jit(solution)/shard_map/ppermute | solution.py:210
  73.6 0.0 collective-permute-done.1.go_ref
  73.6 0.0 collective-permute-done.gq_ref.gk_ref.gv_ref
  73.6 0.0 copy-start.1
  73.6 7.6 %all-to-all-done.1 = bf16[48,128,128]{2,1,0:T(8,128)(2,1)S(1)} async-done(((bf16[48,128,128]{2,1,0:T(8,128)(2,1)}), bf16[48,128,128]{2,1,0:T(8,128)(2,1)S(1)}, u32[]{:S(2)}, u32[]{:S(2)}) %all-to-all-start.1) | async-done | bytes 1572896 | tf_op jit(solution)/shard_map/all_to_all | solution.py:220
  81.2 0.2 fusion
  81.4 0.0 collective-permute-start.5
  81.4 1.6 %collective-permute-start.4 = (bf16[24,128,128]{2,1,0:T(8,128)(2,1)S(1)}, bf16[24,128,128]{2,1,0:T(8,128)(2,1)S(1)}, u32[]{:S(2)}, u32[]{:S(2)}) collective-permute-start(bf16[24,128,128]{2,1,0:T(8,128)(2,1)S(1)} %get-tuple-element.15), channel_id=1, source_target_pairs={{0,16},{16,32},{32,48},{48,64},{64,80},{80,96},{96,112},{112,0},{1... | collective-permute-start | bytes 2359304 | tf_op jit(solution)/shard_map/ppermute | solution.py:229
  83.1 11.0 %collective-permute-done.5.s_ref = bf16[24,128,128]{2,1,0:T(8,128)(2,1)S(1)} collective-permute-done((bf16[24,128,128]{2,1,0:T(8,128)(2,1)S(1)}, bf16[24,128,128]{2,1,0:T(8,128)(2,1)S(1)}, u32[]{:S(2)}, u32[]{:S(2)}) %collective-permute-start.5) | collective-permute-done | bytes 786464 | tf_op jit(solution)/shard_map/ppermute | solution.py:229
  94.1 0.0 collective-permute-done.3.x_ref
  94.1 0.0 copy-done.6
  94.1 0.0 copy-done.5
  94.1 0.0 copy-done.1
  94.1 0.9 copy-done.3
  95.0 12.4 %shard_map.70.rest_0_ = bf16[1,512,6144]{2,1,0:T(8,128)(2,1)} custom-call(f32[48]{0:T(128)} %bitcast.11, bf16[1,512,6144]{2,1,0:T(8,128)(2,1)} %collective-permute-done.3.x_ref, f32[1,18432]{1,0:T(1,128)} %copy-done.1, f32[1,18432]{1,0:T(1,128)} %copy-done.1, f32[1,18432]{1,0:T(1,128)} %copy-done.1, f32[1,6144]{1,0:T(1,128)} %copy-done.5, ...), custom_call_target="tpu_custom_call" | custom-call | flops 3221225472 | bytes 7077888 | tf_op jit(solution)/shard_map/pallas_call | solution.py:181
  107.4 0.0 collective-permute-done.4.s_ref
  107.4 0.9 copy-done.2
  108.3 12.4 %shard_map.71 = bf16[1,512,6144]{2,1,0:T(8,128)(2,1)} custom-call(f32[48]{0:T(128)} %bitcast.12, bf16[1,512,6144]{2,1,0:T(8,128)(2,1)} %collective-permute-done.3.x_ref, f32[1,18432]{1,0:T(1,128)} %copy-done.1, f32[1,18432]{1,0:T(1,128)} %copy-done.1, f32[1,18432]{1,0:T(1,128)} %copy-done.1, f32[1,6144]{1,0:T(1,128)} %copy-done.5, ...), custom_call_target="tpu_custom_call", output_to_operand_aliasing={{}: (7, {})} | custom-call | flops 3221225472 | bytes 7077888 | tf_op jit(solution)/shard_map/pallas_call | solution.py:181
  (7 shorter events, 0.0 us)
Async XLA Ops:
  0.6 93.4 %collective-permute-start.3 = (bf16[1,512,6144]{2,1,0:T(8,128)(2,1)}, bf16[1,512,6144]{2,1,0:T(8,128)(2,1)}, u32[]{:S(2)}, u32[]{:S(2)}) collective-permute-start(bf16[1,512,6144]{2,1,0:T(8,128)(2,1)} %x_ref.1), channel_id=1, source_target_pairs={{0,16},{16,32},{32,48},{48,64},{64,80},{80,96},{96,112},{112,0},{1... | collective-permute-start | bytes 18874376 | tf_op jit(solution)/shard_map/ppermute | solution.py:210
  10.9 35.8 %all-to-all-start = ((bf16[48,128,128]{2,1,0:T(8,128)(2,1)}), bf16[48,128,128]{2,1,0:T(8,128)(2,1)S(1)}, u32[]{:S(2)}, u32[]{:S(2)}) async-start(bf16[48,128,128]{2,1,0:T(8,128)(2,1)} %shard_map.68), calls=%async_computation | async-start | bytes 3145728 | tf_op jit(solution)/shard_map/all_to_all | solution.py:215
  46.7 1.1 copy-start
  47.8 7.7 %copy-start.4 = (f32[1,3,6144]{2,0,1:T(1,128)S(1)}, f32[1,3,6144]{2,0,1:T(1,128)}, u32[]{:S(2)}) copy-start(f32[1,3,6144]{2,0,1:T(1,128)} %param.6) | copy-start | bytes 221188
  47.9 7.8 %copy-start.8 = (f32[1,6144]{1,0:T(1,128)S(1)}, f32[1,6144]{1,0:T(1,128)}, u32[]{:S(2)}) copy-start(f32[1,6144]{1,0:T(1,128)} %param.7) | copy-start | bytes 73732
  47.9 9.3 %copy-start.7 = (f32[1,48]{1,0:T(1,128)S(1)}, f32[1,48]{1,0:T(1,128)}, u32[]{:S(2)}) copy-start(f32[1,48]{1,0:T(1,128)} %param.8) | copy-start | bytes 580
  51.6 29.6 %all-to-all-start.1 = ((bf16[48,128,128]{2,1,0:T(8,128)(2,1)}), bf16[48,128,128]{2,1,0:T(8,128)(2,1)S(1)}, u32[]{:S(2)}, u32[]{:S(2)}) async-start(bf16[48,128,128]{2,1,0:T(8,128)(2,1)} %bitcast.7), calls=%async_computation.1 | async-start | bytes 3145728 | tf_op jit(solution)/shard_map/all_to_all | solution.py:220
  55.5 18.1 %collective-permute-start = (f32[1,18432]{1,0:T(1,128)S(1)}, f32[1,18432]{1,0:T(1,128)S(1)}, u32[]{:S(2)}, u32[]{:S(2)}) collective-permute-start(f32[1,18432]{1,0:T(1,128)S(1)} %bitcast.10), channel_id=1, source_target_pairs={{0,16},{16,32},{32,48},{48,64},{64,80},{80,96},{96,112},{112,0},{1... | collective-permute-start | bytes 221192 | tf_op jit(solution)/shard_map/ppermute | solution.py:210
  55.7 17.9 %collective-permute-start.1 = (f32[1,6144]{1,0:T(1,128)S(1)}, f32[1,6144]{1,0:T(1,128)S(1)}, u32[]{:S(2)}, u32[]{:S(2)}) collective-permute-start(f32[1,6144]{1,0:T(1,128)S(1)} %copy-done.8), channel_id=1, source_target_pairs={{0,16},{16,32},{32,48},{48,64},{64,80},{80,96},{96,112},{112,0},{1... | collective-permute-start | bytes 73736 | tf_op jit(solution)/shard_map/ppermute | solution.py:210
  57.1 16.5 %collective-permute-start.2 = (f32[1,48]{1,0:T(1,128)S(1)}, f32[1,48]{1,0:T(1,128)S(1)}, u32[]{:S(2)}, u32[]{:S(2)}) collective-permute-start(f32[1,48]{1,0:T(1,128)S(1)} %copy-done.7), channel_id=1, source_target_pairs={{0,16},{16,32},{32,48},{48,64},{64,80},{80,96},{96,112},{112,0},{1... | collective-permute-start | bytes 584 | tf_op jit(solution)/shard_map/ppermute | solution.py:210
  73.6 20.5 %copy-start.6 = (f32[1,48]{1,0:T(1,128)}, f32[1,48]{1,0:T(1,128)S(1)}, u32[]{:S(2)}) copy-start(f32[1,48]{1,0:T(1,128)S(1)} %collective-permute-done.2) | copy-start | bytes 580
  73.6 20.5 %copy-start.5 = (f32[1,6144]{1,0:T(1,128)}, f32[1,6144]{1,0:T(1,128)S(1)}, u32[]{:S(2)}) copy-start(f32[1,6144]{1,0:T(1,128)S(1)} %collective-permute-done.1.go_ref) | copy-start | bytes 73732
  73.6 20.5 %copy-start.1 = (f32[1,18432]{1,0:T(1,128)}, f32[1,18432]{1,0:T(1,128)S(1)}, u32[]{:S(2)}) copy-start(f32[1,18432]{1,0:T(1,128)S(1)} %collective-permute-done.gq_ref.gk_ref.gv_ref) | copy-start | bytes 221188
  81.4 12.6 %collective-permute-start.5 = (bf16[24,128,128]{2,1,0:T(8,128)(2,1)S(1)}, bf16[24,128,128]{2,1,0:T(8,128)(2,1)S(1)}, u32[]{:S(2)}, u32[]{:S(2)}) collective-permute-start(bf16[24,128,128]{2,1,0:T(8,128)(2,1)S(1)} %get-tuple-element.14), channel_id=1, source_target_pairs={{0,16},{16,32},{32,48},{48,64},{64,80},{80,96},{96,112},{112,0},{1... | collective-permute-start | bytes 2359304 | tf_op jit(solution)/shard_map/ppermute | solution.py:229
  81.4 26.0 %collective-permute-start.4 = (bf16[24,128,128]{2,1,0:T(8,128)(2,1)S(1)}, bf16[24,128,128]{2,1,0:T(8,128)(2,1)S(1)}, u32[]{:S(2)}, u32[]{:S(2)}) collective-permute-start(bf16[24,128,128]{2,1,0:T(8,128)(2,1)S(1)} %get-tuple-element.15), channel_id=1, source_target_pairs={{0,16},{16,32},{32,48},{48,64},{64,80},{80,96},{96,112},{112,0},{1... | collective-permute-start | bytes 2359304 | tf_op jit(solution)/shard_map/ppermute | solution.py:229
  94.1 0.9 copy-start.3
  107.4 0.9 copy-start.2

commit v19 on v18

--- a/solution.py
+++ b/solution.py
@@ -9,9 +9,9 @@
 
 BLOCK = 256
 EPSILON = 1e-05
-HEADS_PER_STEP = 12
+HEADS_PER_STEP = 8
 SUMMARY_HEADS_PER_STEP = 12
-STATE_CHUNKS = 2
+STATE_CHUNKS = 3
 
 
 def _silu(v):

time: 121 us -> 122 us (level)
  waiting for transfers between devices: 62.6 us -> 59.8 us
  Pallas kernels: 38.9 us -> 41.5 us
    ppermute x2 -> x3, waiting for transfers between devices: 11 us -> 8.18 us  [on_device(): lax.ppermute(incoming[part * chunk:(part + 1) * chunk], 'section', pairs)]
    pallas_call x2 -> x3, Pallas kernels: 24.9 us -> 27.5 us  [_outputs(): pl.pallas_call(kernel, grid_spec=pltpu.PrefetchScalarGridSpec(num_scalar_...]
    unnamed x18 -> x20, local copies, waits for them, and re-layouts: 2.96 us -> 3.52 us
  transfers between devices with their start and end apart: 8 -> 9, of which waited for: 4 -> 4; matrix products, arithmetic and copies ran while one was open for 0% -> 0% of each run, Pallas kernels for 22% -> 27%
where the time goes in v19:
time: 122 us; the launch traced here: 121 us
  waiting for transfers between devices  59.8 us (49%)
  Pallas kernels  41.5 us (34%)
  starting transfers between devices  15.5 us (13%)
  local copies, waits for them, and re-layouts  3.68 us (3%)
    all_to_all x1, waiting for transfers between devices, on_device(): gathered = lax.all_to_all(summary, 'ctx', 0, 0, tiled=True)  27.7 us
    pallas_call x3, Pallas kernels, _outputs(): pl.pallas_call(kernel, grid_spec=pltpu.PrefetchScalarGridSpec(num_scalar_...  27.5 us
    ppermute x4, waiting for transfers between devices, on_device(): lax.ppermute((section_inputs, flat_gains, out_gain, decay_rates), 'sectio...  16.3 us
    pallas_call x1, Pallas kernels, _summaries(): pl.pallas_call(kernel, grid_spec=pltpu.PrefetchScalarGridSpec(num_scalar_...  10.2 us
    ppermute x3, waiting for transfers between devices, on_device(): lax.ppermute(incoming[part * chunk:(part + 1) * chunk], 'section', pairs)  8.18 us
    all_to_all x1, starting transfers between devices, on_device(): gathered = lax.all_to_all(summary, 'ctx', 0, 0, tiled=True)  8.17 us
    all_to_all x1, waiting for transfers between devices, on_device(): lax.all_to_all(prefixes.reshape(heads, head_dim, head_dim), 'ctx', 0, 0,...  7.62 us
    all_to_all x1, starting transfers between devices, on_device(): lax.all_to_all(prefixes.reshape(heads, head_dim, head_dim), 'ctx', 0, 0,...  3.89 us
  transfers between devices with their start and end apart: 9, of which 4 were waited for; matrix products, arithmetic and copies ran while one was open for 0% of the time, Pallas kernels for 27%

profile of v19, /device:TPU:0, one launch (start us, length us, event | category | flops | bytes accessed | tf_op | source)
XLA Modules:
  0.0 121.2 jit_solution(1627702746952013221)
XLA Ops:
  0.6 0.0 collective-permute-start.3
  0.7 10.2 %shard_map.68 = bf16[48,128,128]{2,1,0:T(8,128)(2,1)} custom-call(f32[48]{0:T(128)} %bitcast.14, bf16[1,512,6144]{2,1,0:T(8,128)(2,1)} %x_ref.1, f32[1,18432]{1,0:T(1,128)} %bitcast.8, f32[1,18432]{1,0:T(1,128)} %bitcast.9), custom_call_target="tpu_custom_call" | custom-call | flops 805306368 | bytes 9437184 | tf_op jit(solution)/shard_map/pallas_call | solution.py:135
  10.9 8.2 %all-to-all-start = ((bf16[48,128,128]{2,1,0:T(8,128)(2,1)}), bf16[48,128,128]{2,1,0:T(8,128)(2,1)S(1)}, u32[]{:S(2)}, u32[]{:S(2)}) async-start(bf16[48,128,128]{2,1,0:T(8,128)(2,1)} %shard_map.68), calls=%async_computation | async-start | bytes 3145728 | tf_op jit(solution)/shard_map/all_to_all | solution.py:215
  19.0 27.7 %all-to-all-done = bf16[48,128,128]{2,1,0:T(8,128)(2,1)S(1)} async-done(((bf16[48,128,128]{2,1,0:T(8,128)(2,1)}), bf16[48,128,128]{2,1,0:T(8,128)(2,1)S(1)}, u32[]{:S(2)}, u32[]{:S(2)}) %all-to-all-start) | async-done | bytes 1572896 | tf_op jit(solution)/shard_map/all_to_all | solution.py:215
  46.7 1.1 copy-done
  47.9 3.8 %shard_map.69 = (bf16[16,3,128,128]{3,2,1,0:T(8,128)(2,1)}, f32[1,3,128,128]{3,2,1,0:T(8,128)}) custom-call(s32[1]{0:T(128)} %bitcast.1.place_ref, f32[48]{0:T(128)} %bitcast.15, bf16[16,3,128,128]{3,2,1,0:T(8,128)(2,1)} %bitcast.6, f32[1,48,128,128]{3,2,1,0:T(8,128)} %c_ref.1), custom_call_target="tpu_custom_call" | custom-call | flops 1572864 | bytes 3538944 | tf_op jit(solution)/shard_map/pallas_call | solution.py:103
  51.6 3.9 %all-to-all-start.1 = ((bf16[48,128,128]{2,1,0:T(8,128)(2,1)}), bf16[48,128,128]{2,1,0:T(8,128)(2,1)S(1)}, u32[]{:S(2)}, u32[]{:S(2)}) async-start(bf16[48,128,128]{2,1,0:T(8,128)(2,1)} %bitcast.7), calls=%async_computation.1 | async-start | bytes 3145728 | tf_op jit(solution)/shard_map/all_to_all | solution.py:220
  55.5 0.0 copy-done.5
  55.5 0.2 collective-permute-start
  55.7 1.4 %collective-permute-start.1 = (f32[1,6144]{1,0:T(1,128)S(1)}, f32[1,6144]{1,0:T(1,128)S(1)}, u32[]{:S(2)}, u32[]{:S(2)}) collective-permute-start(f32[1,6144]{1,0:T(1,128)S(1)} %copy-done.9), channel_id=1, source_target_pairs={{0,16},{16,32},{32,48},{48,64},{64,80},{80,96},{96,112},{112,0},{1... | collective-permute-start | bytes 73736 | tf_op jit(solution)/shard_map/ppermute | solution.py:210
  57.1 0.2 collective-permute-start.2
  57.3 16.3 %collective-permute-done.2 = f32[1,48]{1,0:T(1,128)S(1)} collective-permute-done((f32[1,48]{1,0:T(1,128)S(1)}, f32[1,48]{1,0:T(1,128)S(1)}, u32[]{:S(2)}, u32[]{:S(2)}) %collective-permute-start.2) | collective-permute-done | bytes 224 | tf_op jit(solution)/shard_map/ppermute | solution.py:210
  73.6 0.0 collective-permute-done.1.go_ref
  73.6 0.0 collective-permute-done.gq_ref.gk_ref.gv_ref
  73.6 7.6 %all-to-all-done.1 = bf16[48,128,128]{2,1,0:T(8,128)(2,1)S(1)} async-done(((bf16[48,128,128]{2,1,0:T(8,128)(2,1)}), bf16[48,128,128]{2,1,0:T(8,128)(2,1)S(1)}, u32[]{:S(2)}, u32[]{:S(2)}) %all-to-all-start.1) | async-done | bytes 1572896 | tf_op jit(solution)/shard_map/all_to_all | solution.py:220
  81.2 0.2 fusion
  81.4 0.0 collective-permute-start.6
  81.4 1.6 %collective-permute-start.5 = (bf16[16,128,128]{2,1,0:T(8,128)(2,1)S(1)}, bf16[16,128,128]{2,1,0:T(8,128)(2,1)S(1)}, u32[]{:S(2)}, u32[]{:S(2)}) collective-permute-start(bf16[16,128,128]{2,1,0:T(8,128)(2,1)S(1)} %get-tuple-element.15), channel_id=1, source_target_pairs={{0,16},{16,32},{32,48},{48,64},{64,80},{80,96},{96,112},{112,0},{1... | collective-permute-start | bytes 1572872 | tf_op jit(solution)/shard_map/ppermute | solution.py:229
  83.1 0.0 collective-permute-start.4
  83.1 8.2 %collective-permute-done.6.s_ref = bf16[16,128,128]{2,1,0:T(8,128)(2,1)S(1)} collective-permute-done((bf16[16,128,128]{2,1,0:T(8,128)(2,1)S(1)}, bf16[16,128,128]{2,1,0:T(8,128)(2,1)S(1)}, u32[]{:S(2)}, u32[]{:S(2)}) %collective-permute-start.6) | collective-permute-done | bytes 524320 | tf_op jit(solution)/shard_map/ppermute | solution.py:229
  91.2 0.0 collective-permute-done.3.x_ref
  91.3 0.0 copy-done.7
  91.3 0.0 copy-done.6
  91.3 0.0 copy-done.1
  91.3 0.8 copy-done.4
  92.0 9.2 %shard_map.70.rest_0_ = bf16[1,512,6144]{2,1,0:T(8,128)(2,1)} custom-call(f32[48]{0:T(128)} %bitcast.11, bf16[1,512,6144]{2,1,0:T(8,128)(2,1)} %collective-permute-done.3.x_ref, f32[1,18432]{1,0:T(1,128)} %copy-done.1, f32[1,18432]{1,0:T(1,128)} %copy-done.1, f32[1,18432]{1,0:T(1,128)} %copy-done.1, f32[1,6144]{1,0:T(1,128)} %copy-done.6, ...), custom_call_target="tpu_custom_call" | custom-call | flops 2147483648 | bytes 4718592 | tf_op jit(solution)/shard_map/pallas_call | solution.py:181
  101.2 0.0 collective-permute-done.5.s_ref
  101.2 0.8 copy-done.3
  102.0 9.2 %shard_map.71.rest_0_ = bf16[1,512,6144]{2,1,0:T(8,128)(2,1)} custom-call(f32[48]{0:T(128)} %bitcast.12, bf16[1,512,6144]{2,1,0:T(8,128)(2,1)} %collective-permute-done.3.x_ref, f32[1,18432]{1,0:T(1,128)} %copy-done.1, f32[1,18432]{1,0:T(1,128)} %copy-done.1, f32[1,18432]{1,0:T(1,128)} %copy-done.1, ...), custom_call_target="tpu_custom_call", output_to_operand_aliasing={{}: (7, {})} | custom-call | flops 2147483648 | bytes 4718592 | tf_op jit(solution)/shard_map/pallas_call | solution.py:181
  111.2 0.0 collective-permute-done.4.s_ref
  111.2 0.8 copy-done.2
  112.0 9.2 %shard_map.72 = bf16[1,512,6144]{2,1,0:T(8,128)(2,1)} custom-call(f32[48]{0:T(128)} %bitcast.13, bf16[1,512,6144]{2,1,0:T(8,128)(2,1)} %collective-permute-done.3.x_ref, f32[1,18432]{1,0:T(1,128)} %copy-done.1, f32[1,18432]{1,0:T(1,128)} %copy-done.1, f32[1,18432]{1,0:T(1,128)} %copy-done.1, f32[1,6144]{1,0:T(1,128)} %copy-done.6, ...), custom_call_target="tpu_custom_call", output_to_operand_aliasing={{}: (7, {})} | custom-call | flops 2147483648 | bytes 4718592 | tf_op jit(solution)/shard_map/pallas_call | solution.py:181
  (12 shorter events, 0.0 us)
Async XLA Ops:
  0.6 90.6 %collective-permute-start.3 = (bf16[1,512,6144]{2,1,0:T(8,128)(2,1)}, bf16[1,512,6144]{2,1,0:T(8,128)(2,1)}, u32[]{:S(2)}, u32[]{:S(2)}) collective-permute-start(bf16[1,512,6144]{2,1,0:T(8,128)(2,1)} %x_ref.1), channel_id=1, source_target_pairs={{0,16},{16,32},{32,48},{48,64},{64,80},{80,96},{96,112},{112,0},{1... | collective-permute-start | bytes 18874376 | tf_op jit(solution)/shard_map/ppermute | solution.py:210
  10.9 35.8 %all-to-all-start = ((bf16[48,128,128]{2,1,0:T(8,128)(2,1)}), bf16[48,128,128]{2,1,0:T(8,128)(2,1)S(1)}, u32[]{:S(2)}, u32[]{:S(2)}) async-start(bf16[48,128,128]{2,1,0:T(8,128)(2,1)} %shard_map.68), calls=%async_computation | async-start | bytes 3145728 | tf_op jit(solution)/shard_map/all_to_all | solution.py:215
  46.7 1.1 copy-start
  47.8 7.7 %copy-start.5 = (f32[1,3,6144]{2,0,1:T(1,128)S(1)}, f32[1,3,6144]{2,0,1:T(1,128)}, u32[]{:S(2)}) copy-start(f32[1,3,6144]{2,0,1:T(1,128)} %param.6) | copy-start | bytes 221188
  47.9 7.8 %copy-start.9 = (f32[1,6144]{1,0:T(1,128)S(1)}, f32[1,6144]{1,0:T(1,128)}, u32[]{:S(2)}) copy-start(f32[1,6144]{1,0:T(1,128)} %param.7) | copy-start | bytes 73732
  47.9 9.3 %copy-start.8 = (f32[1,48]{1,0:T(1,128)S(1)}, f32[1,48]{1,0:T(1,128)}, u32[]{:S(2)}) copy-start(f32[1,48]{1,0:T(1,128)} %param.8) | copy-start | bytes 580
  51.6 29.6 %all-to-all-start.1 = ((bf16[48,128,128]{2,1,0:T(8,128)(2,1)}), bf16[48,128,128]{2,1,0:T(8,128)(2,1)S(1)}, u32[]{:S(2)}, u32[]{:S(2)}) async-start(bf16[48,128,128]{2,1,0:T(8,128)(2,1)} %bitcast.7), calls=%async_computation.1 | async-start | bytes 3145728 | tf_op jit(solution)/shard_map/all_to_all | solution.py:220
  55.5 18.1 %collective-permute-start = (f32[1,18432]{1,0:T(1,128)S(1)}, f32[1,18432]{1,0:T(1,128)S(1)}, u32[]{:S(2)}, u32[]{:S(2)}) collective-permute-start(f32[1,18432]{1,0:T(1,128)S(1)} %bitcast.10), channel_id=1, source_target_pairs={{0,16},{16,32},{32,48},{48,64},{64,80},{80,96},{96,112},{112,0},{1... | collective-permute-start | bytes 221192 | tf_op jit(solution)/shard_map/ppermute | solution.py:210
  55.7 17.9 %collective-permute-start.1 = (f32[1,6144]{1,0:T(1,128)S(1)}, f32[1,6144]{1,0:T(1,128)S(1)}, u32[]{:S(2)}, u32[]{:S(2)}) collective-permute-start(f32[1,6144]{1,0:T(1,128)S(1)} %copy-done.9), channel_id=1, source_target_pairs={{0,16},{16,32},{32,48},{48,64},{64,80},{80,96},{96,112},{112,0},{1... | collective-permute-start | bytes 73736 | tf_op jit(solution)/shard_map/ppermute | solution.py:210
  57.1 16.5 %collective-permute-start.2 = (f32[1,48]{1,0:T(1,128)S(1)}, f32[1,48]{1,0:T(1,128)S(1)}, u32[]{:S(2)}, u32[]{:S(2)}) collective-permute-start(f32[1,48]{1,0:T(1,128)S(1)} %copy-done.8), channel_id=1, source_target_pairs={{0,16},{16,32},{32,48},{48,64},{64,80},{80,96},{96,112},{112,0},{1... | collective-permute-start | bytes 584 | tf_op jit(solution)/shard_map/ppermute | solution.py:210
  73.6 17.6 %copy-start.7 = (f32[1,48]{1,0:T(1,128)}, f32[1,48]{1,0:T(1,128)S(1)}, u32[]{:S(2)}) copy-start(f32[1,48]{1,0:T(1,128)S(1)} %collective-permute-done.2) | copy-start | bytes 580
  73.6 17.6 %copy-start.6 = (f32[1,6144]{1,0:T(1,128)}, f32[1,6144]{1,0:T(1,128)S(1)}, u32[]{:S(2)}) copy-start(f32[1,6144]{1,0:T(1,128)S(1)} %collective-permute-done.1.go_ref) | copy-start | bytes 73732
  73.6 17.7 %copy-start.1 = (f32[1,18432]{1,0:T(1,128)}, f32[1,18432]{1,0:T(1,128)S(1)}, u32[]{:S(2)}) copy-start(f32[1,18432]{1,0:T(1,128)S(1)} %collective-permute-done.gq_ref.gk_ref.gv_ref) | copy-start | bytes 221188
  81.4 9.8 %collective-permute-start.6 = (bf16[16,128,128]{2,1,0:T(8,128)(2,1)S(1)}, bf16[16,128,128]{2,1,0:T(8,128)(2,1)S(1)}, u32[]{:S(2)}, u32[]{:S(2)}) collective-permute-start(bf16[16,128,128]{2,1,0:T(8,128)(2,1)S(1)} %get-tuple-element.14), channel_id=1, source_target_pairs={{0,16},{16,32},{32,48},{48,64},{64,80},{80,96},{96,112},{112,0},{1... | collective-permute-start | bytes 1572872 | tf_op jit(solution)/shard_map/ppermute | solution.py:229
  81.4 19.8 %collective-permute-start.5 = (bf16[16,128,128]{2,1,0:T(8,128)(2,1)S(1)}, bf16[16,128,128]{2,1,0:T(8,128)(2,1)S(1)}, u32[]{:S(2)}, u32[]{:S(2)}) collective-permute-start(bf16[16,128,128]{2,1,0:T(8,128)(2,1)S(1)} %get-tuple-element.15), channel_id=1, source_target_pairs={{0,16},{16,32},{32,48},{48,64},{64,80},{80,96},{96,112},{112,0},{1... | collective-permute-start | bytes 1572872 | tf_op jit(solution)/shard_map/ppermute | solution.py:229
  83.1 28.2 %collective-permute-start.4 = (bf16[16,128,128]{2,1,0:T(8,128)(2,1)S(1)}, bf16[16,128,128]{2,1,0:T(8,128)(2,1)S(1)}, u32[]{:S(2)}, u32[]{:S(2)}) collective-permute-start(bf16[16,128,128]{2,1,0:T(8,128)(2,1)S(1)} %get-tuple-element.16), channel_id=1, source_target_pairs={{0,16},{16,32},{32,48},{48,64},{64,80},{80,96},{96,112},{112,0},{1... | collective-permute-start | bytes 1572872 | tf_op jit(solution)/shard_map/ppermute | solution.py:229
  91.2 0.8 copy-start.4
  101.2 0.8 copy-start.3
  111.2 0.8 copy-start.2
